TPU v7x, 1024 devices: a whole 8x8x8 slice. The times are simulated.
1024 devices in a mesh: space: 128 (over z, y_hi, x), chan: 4 (over y_lo), dp: 2 (over core).
Axes of the slice: x: 8, y: 8 (y_hi: 2, y_lo: 4; y = y_hi * 4 + y_lo), z: 8, core: 2. Of those that a mesh axis runs over, the one named last changes fastest.
Arguments:
- volume: bfloat16 [2, 256, 16, 128, 256], P('dp', 'space', None, 'chan'), may hold values from -6 to 6
- kernel: bfloat16 [27, 128, 128], P(None, 'chan'), may hold values from -0.109375 to 0.109375
- cotangent: bfloat16 [2, 128, 8, 128, 128], P('dp', 'space', None, 'chan'), may hold values from -12 to 12
Outputs:
- response: bfloat16 [2, 128, 8, 128, 128], P('dp', 'space', None, 'chan')
- volume_grad: bfloat16 [2, 256, 16, 128, 256], P('dp', 'space', None, 'chan')
All inputs are finite; a program needn't handle non-finite values.
Results may differ from a plain program's by a relative error of at most 0.001.
Values may be sent and summed in bfloat16 or wider, within the bound.
No kernel may reach another device: no remote copies, remote signals or barrier semaphores. Data moves between devices by JAX's collectives and lax.ppermute only.
A program may use at most 32 MiB of HBM per device.

v0:
```python
import jax
import jax.numpy as jnp
from jax import lax
from jax.sharding import PartitionSpec as P


def from_behind(block, axis, distance):
    devices = range(lax.axis_size(axis))
    route = [(i - distance, i) for i in devices if i - distance in devices]
    return lax.ppermute(block, axis, route)


def shift_front(values, axis):
    widths = [(0, 0)] * values.ndim
    widths[axis] = (1, 0)
    return jnp.pad(lax.slice_in_dim(values, 0, values.shape[axis] - 1, 1, axis), widths)


def shift_back(values, axis):
    widths = [(0, 0)] * values.ndim
    widths[axis] = (0, 1)
    return jnp.pad(lax.slice_in_dim(values, 1, values.shape[axis], 1, axis), widths)


def transposed_phases(source, taps):
    shift_row = shift_back(source, 2)
    shift_col = shift_back(source, 4)
    shift_both = shift_back(shift_row, 4)
    sources = {(0, 0): source, (1, 0): shift_row, (0, 1): shift_col, (1, 1): shift_both}
    phases = {}
    for row_tap in range(3):
        for col_tap in range(3):
            picked = sources[int(row_tap == 0), int(col_tap == 0)]
            term = jnp.einsum(
                "bdhew,ce->bdhcw",
                picked,
                taps[row_tap, col_tap],
                preferred_element_type=jnp.float32,
            )
            place = (0 if row_tap == 1 else 1, 0 if col_tap == 1 else 1)
            phases[place] = term if place not in phases else phases[place] + term
    upper = jnp.stack([phases[0, 0], phases[0, 1]], axis=4)
    lower = jnp.stack([phases[1, 0], phases[1, 1]], axis=4)
    return jnp.stack([upper, lower], axis=3)


def per_device(volume, kernel, cotangent):
    count, planes_in, rows_in, chans_in, cols_in = volume.shape
    planes_out = planes_in // 2
    rows_out = rows_in // 2
    cols_out = cols_in // 2
    chans_out = kernel.shape[2]
    below = from_behind(volume[:, -1:], "space", 1)
    extended = jnp.concatenate([below, volume, jnp.zeros_like(below)], axis=1)
    extended = extended.reshape(count, planes_out + 1, 2, rows_out, 2, chans_in, cols_out, 2)
    extended = jnp.moveaxis(extended, 7, 6)
    column_sets = [
        shift_front(extended[:, :, :, :, :, :, 1], 6),
        extended[:, :, :, :, :, :, 0],
        extended[:, :, :, :, :, :, 1],
    ]
    partial_sum = jnp.zeros((count, planes_out, rows_out, chans_out, cols_out), jnp.float32)
    for col_tap in range(3):
        columns = column_sets[col_tap]
        depth_sets = [columns[:, :planes_out, 0], columns[:, :planes_out, 1], columns[:, 1:, 0]]
        for depth_tap in range(3):
            slab = depth_sets[depth_tap]
            row_sets = [shift_front(slab[:, :, :, 1], 2), slab[:, :, :, 0], slab[:, :, :, 1]]
            for row_tap in range(3):
                index = 9 * depth_tap + 3 * row_tap + col_tap
                partial_sum = partial_sum + jnp.einsum(
                    "bdhcw,ce->bdhew",
                    row_sets[row_tap],
                    kernel[index],
                    preferred_element_type=jnp.float32,
                )
    response = lax.psum_scatter(partial_sum, "chan", scatter_dimension=3, tiled=True).astype(
        jnp.bfloat16
    )
    full_cot = lax.all_gather(cotangent, "chan", axis=3, tiled=True)
    taps = kernel.reshape(3, 3, 3, chans_in, chans_out)
    even_planes = transposed_phases(full_cot, taps[1])
    edge = transposed_phases(full_cot, taps[0])
    from_above = from_behind(edge, "space", -1)
    odd_planes = from_above + transposed_phases(full_cot, taps[2])
    both = jnp.stack([even_planes, odd_planes], axis=2).astype(jnp.bfloat16)
    both = jnp.moveaxis(both, 6, 7)
    volume_grad = both.reshape(count, planes_in, rows_in, chans_in, cols_in)
    return (response, volume_grad)


def solution(mesh):
    placed = (
        P("dp", "space", None, "chan", None),
        P(None, "chan", None),
        P("dp", "space", None, "chan", None),
    )
    return jax.shard_map(
        per_device,
        mesh=mesh,
        in_specs=placed,
        out_specs=(P("dp", "space", None, "chan", None), P("dp", "space", None, "chan", None)),
        check_vma=False,
    )
```

profile of v0, /device:TPU:2, one launch (start us, length us, event | category | flops | bytes accessed | tf_op | source)
XLA Modules:
  0.0 117.4 jit_solution(10770903671336900619)
XLA Ops:
  7.2 1.0 slice.319
  8.2 3.4 %collective-permute-start = (bf16[1,1,16,32,256]{4,3,2,1,0:T(8,128)(2,1)S(1)}, bf16[1,1,16,32,256]{4,3,2,1,0:T(8,128)(2,1)S(1)}, u32[]{:S(2)}, u32[]{:S(2)}) collective-permute-start(bf16[1,1,16,32,256]{4,3,2,1,0:T(8,128)(2,1)S(1)} %slice.319), channel_id=1, source_target_pairs={{0,8},{8,16},{16,24},{24,32},{32,40},{40,48},{48,56},{56,64},{64,7... | collective-permute-start | bytes 786440 | tf_op jit(solution)/shard_map/ppermute | solution.py:10
  11.6 1.0 fusion.214
  12.6 14.6 %all_gather.3 = bf16[1,1,8,128,128]{4,3,2,1,0:T(8,128)(2,1)S(1)} all-gather(bf16[1,1,8,32,128]{4,3,2,1,0:T(8,128)(2,1)} %param.5), channel_id=1, replica_groups=mesh['space'=128,'chan'=4,'dp'=2] {'chan'}, dimensions={3}, use_global_device_ids=true | all-gather | bytes 327680 | tf_op jit(solution)/shard_map/all_gather | solution.py:80
  28.8 0.2 fusion.30
  29.1 16.4 %collective-permute-start.1 = (f32[1,1,8,2,32,2,128]{6,4,2,5,3,1,0:T(8,128)S(1)}, f32[1,1,8,2,32,2,128]{6,4,2,5,3,1,0:T(8,128)S(1)}, u32[]{:S(2)}, u32[]{:S(2)}) collective-permute-start(f32[1,1,8,2,32,2,128]{6,4,2,5,3,1,0:T(8,128)S(1)} %pad_maximum_fusion), channel_id=1, source_target_pairs={{8,0},{16,8},{24,16},{32,24},{40,32},{48,40},{56,48},{64,56},{72,6... | collective-permute-start | bytes 1572872 | tf_op jit(solution)/shard_map/ppermute | solution.py:10
  45.5 0.8 fusion.36
  47.4 0.8 fusion.38
  48.3 0.8 fusion.37
  49.4 0.8 fusion.39
  50.2 0.8 fusion.22
  51.4 3.1 %copy.11 = bf16[1,4,16,32,256]{3,4,2,1,0:T(8,128)(2,1)} copy(bf16[1,4,16,32,256]{4,3,2,1,0:T(8,128)(2,1)S(1)} %maximum_maximum_fusion) | data formatting | bytes 2097152 | tf_op jit(solution)/shard_map/concatenate | solution.py:54
  54.5 9.2 %copy.12 = bf16[1,2,2,8,2,32,128,2]{6,5,3,4,2,1,7,0:T(8,128)(2,1)S(1)} copy(bf16[1,2,2,8,2,32,128,2]{5,7,6,4,3,2,1,0:T(2,128)(2,1)} %bitcast.700) | data formatting | bytes 2097152 | tf_op jit(solution)/shard_map/reshape | solution.py:55
  63.9 0.3 convolution_bitcast_fusion.6
  64.2 0.3 convolution_bitcast_fusion.7
  64.4 0.3 convolution_bitcast_fusion
  64.7 0.3 convolution_bitcast_fusion.1
  65.0 0.3 convolution_bitcast_fusion.3
  65.2 0.3 convolution_bitcast_fusion.4
  65.5 0.3 convolution_bitcast_fusion.9
  65.8 0.2 fusion.92
  66.1 0.3 fusion.116
  66.3 0.3 convolution_add_fusion.13
  66.6 0.3 convolution_add_fusion.12
  66.9 0.3 convolution_add_fusion.11
  67.2 0.3 convolution_add_fusion.10
  67.4 0.3 convolution_add_fusion.9
  67.7 0.3 convolution_add_fusion.8
  68.0 0.3 convolution_add_fusion.7
  68.3 0.3 convolution_add_fusion.6
  68.5 0.3 convolution_add_fusion.5
  68.8 0.3 convolution_add_fusion.4
  69.1 0.3 convolution_add_fusion.3
  69.3 0.3 convolution_add_fusion.2
  69.6 0.3 convolution_add_fusion.1
  69.9 0.3 fusion.2
  70.1 0.2 convolution_bitcast_fusion.5
  70.4 0.3 convolution_bitcast_fusion.2
  70.7 0.3 convolution_bitcast_fusion.8
  70.9 0.3 fusion.1
  71.2 0.4 fusion.14
  71.7 1.0 copy.13
  73.0 0.2 fusion.27
  73.6 1.5 %copy.14 = bf16[1,1,2,8,2,32,128,2]{5,7,6,4,3,2,1,0:T(2,128)(2,1)S(1)} copy(bf16[1,1,2,8,2,32,128,2]{6,5,3,7,4,2,1,0:T(8,128)(2,1)S(1)} %maximum_bitcast_fusion) | data formatting | bytes 1048576 | tf_op jit(solution)/shard_map/transpose | solution.py:87
  75.1 1.5 %copy.16 = bf16[1,2,16,32,256]{4,3,2,1,0:T(8,128)(2,1)} copy(bf16[1,2,16,32,256]{3,4,2,1,0:T(8,128)(2,1)S(1)} %bitcast.701) | data formatting | bytes 1048576
  76.6 32.4 %reduce-scatter.2.cloned.1.call-done = f32[1,1,8,32,128]{4,2,1,0,3:T(8,128)} async-done(((f32[1,1,8,128,128]{4,2,1,0,3:T(8,128)}), f32[1,1,8,32,128]{4,2,1,0,3:T(8,128)}) %reduce-scatter.2.cloned.1.call-update) | async-done | bytes 131088 | tf_op jit(solution)/shard_map/reduce_scatter | solution.py:77
  109.0 0.9 convert_element_type.35
  109.9 0.6 copy.15
  (84 shorter events, 4.4 us)
Async XLA Ops:
  7.2 101.8 %reduce-scatter.2.cloned.1.call-start = ((), (), s32[]{:S(2)}) async-start(), calls=%async_computation.1 | async-start | bytes 655360 | tf_op jit(solution)/shard_map/reduce_scatter | solution.py:77
  8.2 43.1 %collective-permute-start = (bf16[1,1,16,32,256]{4,3,2,1,0:T(8,128)(2,1)S(1)}, bf16[1,1,16,32,256]{4,3,2,1,0:T(8,128)(2,1)S(1)}, u32[]{:S(2)}, u32[]{:S(2)}) collective-permute-start(bf16[1,1,16,32,256]{4,3,2,1,0:T(8,128)(2,1)S(1)} %slice.319), channel_id=1, source_target_pairs={{0,8},{8,16},{16,24},{24,32},{32,40},{40,48},{48,56},{56,64},{64,7... | collective-permute-start | bytes 786440 | tf_op jit(solution)/shard_map/ppermute | solution.py:10
  29.0 22.3 %copy-start = (bf16[1,2,16,32,256]{4,3,2,1,0:T(8,128)(2,1)S(1)}, bf16[1,2,16,32,256]{4,3,2,1,0:T(8,128)(2,1)}, u32[]{:S(2)}) copy-start(bf16[1,2,16,32,256]{4,3,2,1,0:T(8,128)(2,1)} %param.3) | copy-start | bytes 1572868
  29.1 44.3 %collective-permute-start.1 = (f32[1,1,8,2,32,2,128]{6,4,2,5,3,1,0:T(8,128)S(1)}, f32[1,1,8,2,32,2,128]{6,4,2,5,3,1,0:T(8,128)S(1)}, u32[]{:S(2)}, u32[]{:S(2)}) collective-permute-start(f32[1,1,8,2,32,2,128]{6,4,2,5,3,1,0:T(8,128)S(1)} %pad_maximum_fusion), channel_id=1, source_target_pairs={{8,0},{16,8},{24,16},{32,24},{40,32},{48,40},{56,48},{64,56},{72,6... | collective-permute-start | bytes 1572872 | tf_op jit(solution)/shard_map/ppermute | solution.py:10
  54.5 9.4 %copy-start.1 = (bf16[27,32,128]{2,1,0:T(8,128)(2,1)S(1)}, bf16[27,32,128]{2,1,0:T(8,128)(2,1)}, u32[]{:S(2)}) copy-start(bf16[27,32,128]{2,1,0:T(8,128)(2,1)} %param.4) | copy-start | bytes 663556
  63.9 2.7 %copy-start.7 = (bf16[1,1,8,32,128]{4,3,2,1,0:T(8,128)(2,1)}, bf16[1,1,8,32,128]{4,3,2,1,0:T(8,128)(2,1)S(1)}, u32[]{:S(2)}) copy-start(bf16[1,1,8,32,128]{4,3,2,1,0:T(8,128)(2,1)S(1)} %slice_bitcast_fusion.28) | copy-start | bytes 196612
  64.4 2.5 %copy-start.8 = (bf16[1,1,8,32,128]{4,3,2,1,0:T(8,128)(2,1)}, bf16[1,1,8,32,128]{4,3,2,1,0:T(8,128)(2,1)S(1)}, u32[]{:S(2)}) copy-start(bf16[1,1,8,32,128]{4,3,2,1,0:T(8,128)(2,1)S(1)} %slice_bitcast_fusion.26) | copy-start | bytes 196612
  65.0 2.2 %copy-start.10 = (bf16[1,1,8,32,128]{4,3,2,1,0:T(8,128)(2,1)}, bf16[1,1,8,32,128]{4,3,2,1,0:T(8,128)(2,1)S(1)}, u32[]{:S(2)}) copy-start(bf16[1,1,8,32,128]{4,3,2,1,0:T(8,128)(2,1)S(1)} %slice_bitcast_fusion.27) | copy-start | bytes 196612
  65.5 2.2 %copy-start.9 = (bf16[1,1,8,32,128]{4,3,2,1,0:T(8,128)(2,1)}, bf16[1,1,8,32,128]{4,3,2,1,0:T(8,128)(2,1)S(1)}, u32[]{:S(2)}) copy-start(bf16[1,1,8,32,128]{4,3,2,1,0:T(8,128)(2,1)S(1)} %slice_bitcast_fusion.29) | copy-start | bytes 196612
  65.8 2.1 %copy-start.11 = (bf16[1,1,8,32,128]{4,3,2,1,0:T(8,128)(2,1)}, bf16[1,1,8,32,128]{4,3,2,1,0:T(8,128)(2,1)S(1)}, u32[]{:S(2)}) copy-start(bf16[1,1,8,32,128]{4,3,2,1,0:T(8,128)(2,1)S(1)} %slice_bitcast_fusion.30) | copy-start | bytes 196612
  68.2 1.1 slice-start.4
  68.2 1.9 %slice-start.3 = ((bf16[1,1,8,32,128]{4,3,2,1,0:T(8,128)(2,1)}), bf16[1,1,7,32,128]{4,3,2,1,0:T(8,128)(2,1)S(1)}, s32[]{:S(2)}) async-start(bf16[1,1,8,32,128]{4,3,2,1,0:T(8,128)(2,1)} %copy-done.10), calls=%async_computation.5 | async-start | bytes 114688 | tf_op jit(solution)/shard_map/slice | solution.py:16
  68.2 2.1 %slice-start.1 = ((bf16[1,1,8,32,128]{4,3,2,1,0:T(8,128)(2,1)}), bf16[1,1,7,32,128]{4,3,2,1,0:T(8,128)(2,1)S(1)}, s32[]{:S(2)}) async-start(bf16[1,1,8,32,128]{4,3,2,1,0:T(8,128)(2,1)} %copy-done.8), calls=%async_computation.3 | async-start | bytes 114688 | tf_op jit(solution)/shard_map/slice | solution.py:16
  68.5 2.1 %slice-start = ((bf16[1,1,8,32,128]{4,3,2,1,0:T(8,128)(2,1)}), bf16[1,1,7,32,128]{4,3,2,1,0:T(8,128)(2,1)S(1)}, s32[]{:S(2)}) async-start(bf16[1,1,8,32,128]{4,3,2,1,0:T(8,128)(2,1)} %copy-done.7), calls=%async_computation.2 | async-start | bytes 114688 | tf_op jit(solution)/shard_map/slice | solution.py:16
  68.5 2.4 %slice-start.2 = ((bf16[1,1,8,32,128]{4,3,2,1,0:T(8,128)(2,1)}), bf16[1,1,7,32,128]{4,3,2,1,0:T(8,128)(2,1)S(1)}, s32[]{:S(2)}) async-start(bf16[1,1,8,32,128]{4,3,2,1,0:T(8,128)(2,1)} %copy-done.9), calls=%async_computation.4 | async-start | bytes 114688 | tf_op jit(solution)/shard_map/slice | solution.py:16
  71.2 1.5 %copy-start.3 = (bf16[1,1,8,32,1,128]{5,3,2,4,1,0:T(8,128)(2,1)S(1)}, bf16[1,1,8,32,1,128]{5,3,2,4,1,0:T(8,128)(2,1)}, u32[]{:S(2)}) copy-start(bf16[1,1,8,32,1,128]{5,3,2,4,1,0:T(8,128)(2,1)} %fusion.37) | copy-start | bytes 196612
  71.2 1.5 %copy-start.4 = (bf16[1,1,8,32,1,128]{5,3,2,4,1,0:T(8,128)(2,1)S(1)}, bf16[1,1,8,32,1,128]{5,3,2,4,1,0:T(8,128)(2,1)}, u32[]{:S(2)}) copy-start(bf16[1,1,8,32,1,128]{5,3,2,4,1,0:T(8,128)(2,1)} %fusion.39) | copy-start | bytes 196612
  71.2 1.5 %copy-start.5 = (bf16[1,1,8,32,1,128]{5,3,2,4,1,0:T(8,128)(2,1)S(1)}, bf16[1,1,8,32,1,128]{5,3,2,4,1,0:T(8,128)(2,1)}, u32[]{:S(2)}) copy-start(bf16[1,1,8,32,1,128]{5,3,2,4,1,0:T(8,128)(2,1)} %fusion.36) | copy-start | bytes 196612
  71.2 1.5 %copy-start.6 = (bf16[1,1,8,32,1,128]{5,3,2,4,1,0:T(8,128)(2,1)S(1)}, bf16[1,1,8,32,1,128]{5,3,2,4,1,0:T(8,128)(2,1)}, u32[]{:S(2)}) copy-start(bf16[1,1,8,32,1,128]{5,3,2,4,1,0:T(8,128)(2,1)} %fusion.38) | copy-start | bytes 196612
  71.2 2.1 %copy-start.2 = (f32[1,1,8,32,1,128]{5,3,2,4,1,0:T(8,128)S(1)}, f32[1,1,8,32,1,128]{5,3,2,4,1,0:T(8,128)}, u32[]{:S(2)}) copy-start(f32[1,1,8,32,1,128]{5,3,2,4,1,0:T(8,128)} %fusion.22) | copy-start | bytes 393220
Sparse Core Ops, SparseCore 0:
  72.8 36.1 reduce-scatter.1
where the time goes:
time: 118 us; the launch traced here: 117 us
  waiting for transfers between devices  32.5 us (28%)
  starting transfers between devices  19.9 us (17%)
  local copies, waits for them, and re-layouts  19.7 us (17%)
  matrix products  14.7 us (12%)
  between operations  14.7 us (12%)
  blocking collectives  14.6 us (12%)
  other arithmetic  1.38 us (1%)
    reduce_scatter x1, waiting for transfers between devices, per_device(): lax.psum_scatter(partial_sum, 'chan', scatter_dimension=3, tiled=True)  32.4 us
    ppermute x2, starting transfers between devices, from_behind(): return lax.ppermute(block, axis, route)  19.8 us
    all_gather x1, blocking collectives, per_device(): full_cot = lax.all_gather(cotangent, 'chan', axis=3, tiled=True)  14.6 us
    reshape x1, local copies, waits for them, and re-layouts, per_device(): extended.reshape(count, planes_out + 1, 2, rows_out, 2, chans_in, cols_ou...  9.2 us
    dot_general x27, matrix products, transposed_phases(): jnp.einsum('bdhew,ce->bdhcw', picked, taps[row_tap, col_tap], preferred_e...  7.62 us
    dot_general x27, matrix products, per_device(): jnp.einsum('bdhcw,ce->bdhew', row_sets[row_tap], kernel[index], preferred...  7.08 us
    concatenate x2, local copies, waits for them, and re-layouts, per_device(): extended = jnp.concatenate([below, volume, jnp.zeros_like(below)], axis=1)  3.16 us
  transfers between devices with their start and end apart: 3, of which 1 were waited for; matrix products, arithmetic and copies ran while one was open for 28% of the time, Pallas kernels for 0%

commit v1 on v0

--- a/solution.py
+++ b/solution.py
@@ -44,12 +44,32 @@
     return jnp.stack([upper, lower], axis=3)
 
 
+def chan_shift(block, shift):
+    size = lax.axis_size("chan")
+    return lax.ppermute(block, "chan", [(i, (i + shift) % size) for i in range(size)])
+
+
+def from_next_slab(block, chan_offset):
+    slabs = lax.axis_size("space")
+    size = lax.axis_size("chan")
+    route = [
+        ((s + 1) * size + (c + chan_offset) % size, s * size + c)
+        for s in range(slabs - 1)
+        for c in range(size)
+    ]
+    return lax.ppermute(block, ("space", "chan"), route)
+
+
 def per_device(volume, kernel, cotangent):
     count, planes_in, rows_in, chans_in, cols_in = volume.shape
     planes_out = planes_in // 2
     rows_out = rows_in // 2
     cols_out = cols_in // 2
     chans_out = kernel.shape[2]
+    groups = lax.axis_size("chan")
+    share = chans_out // groups
+    me = lax.axis_index("chan")
+    kernel = jnp.roll(kernel, -me * share, axis=2)
     below = from_behind(volume[:, -1:], "space", 1)
     extended = jnp.concatenate([below, volume, jnp.zeros_like(below)], axis=1)
     extended = extended.reshape(count, planes_out + 1, 2, rows_out, 2, chans_in, cols_out, 2)
@@ -74,15 +94,17 @@
                     kernel[index],
                     preferred_element_type=jnp.float32,
                 )
-    response = lax.psum_scatter(partial_sum, "chan", scatter_dimension=3, tiled=True).astype(
-        jnp.bfloat16
-    )
-    full_cot = lax.all_gather(cotangent, "chan", axis=3, tiled=True)
+    total = partial_sum[:, :, :, :share]
+    for k in range(1, groups):
+        total = total + chan_shift(partial_sum[:, :, :, k * share:(k + 1) * share], k)
+    response = total.astype(jnp.bfloat16)
+    own = [cotangent] + [chan_shift(cotangent, -k) for k in range(1, groups)]
+    following = [from_next_slab(cotangent, k) for k in range(groups)]
+    full_cot = jnp.concatenate(own, axis=3)
+    next_cot = jnp.concatenate(following, axis=3)
     taps = kernel.reshape(3, 3, 3, chans_in, chans_out)
     even_planes = transposed_phases(full_cot, taps[1])
-    edge = transposed_phases(full_cot, taps[0])
-    from_above = from_behind(edge, "space", -1)
-    odd_planes = from_above + transposed_phases(full_cot, taps[2])
+    odd_planes = transposed_phases(next_cot, taps[0]) + transposed_phases(full_cot, taps[2])
     both = jnp.stack([even_planes, odd_planes], axis=2).astype(jnp.bfloat16)
     both = jnp.moveaxis(both, 6, 7)
     volume_grad = both.reshape(count, planes_in, rows_in, chans_in, cols_in)

time: 118 us -> 97.9 us (0.83)
  the two profiles are of different devices: /device:TPU:2 before, /device:TPU:512 now
where the time goes in v1:
time: 97.9 us; the launch traced here: 97.2 us
  starting transfers between devices  41 us (42%)
  waiting for transfers between devices  21.2 us (22%)
  local copies, waits for them, and re-layouts  19.1 us (20%)
  matrix products  11.2 us (11%)
  other arithmetic  3.23 us (3%)
  between operations  1.5 us (2%)
    ppermute x6, starting transfers between devices, chan_shift(): lax.ppermute(block, 'chan', [(i, (i + shift) % size) for i in range(size)])  19.2 us
    ppermute x4, starting transfers between devices, from_next_slab(): return lax.ppermute(block, ('space', 'chan'), route)  18.4 us
    ppermute x1, waiting for transfers between devices, from_behind(): return lax.ppermute(block, axis, route)  13.3 us
    reshape x1, local copies, waits for them, and re-layouts, per_device(): extended.reshape(count, planes_out + 1, 2, rows_out, 2, chans_in, cols_ou...  9.15 us
    dot_general x27, matrix products, per_device(): jnp.einsum('bdhcw,ce->bdhew', row_sets[row_tap], kernel[index], preferred...  6.89 us
    ppermute x4, waiting for transfers between devices, from_next_slab(): return lax.ppermute(block, ('space', 'chan'), route)  4.94 us
    dot_general x27, matrix products, transposed_phases(): jnp.einsum('bdhew,ce->bdhcw', picked, taps[row_tap, col_tap], preferred_e...  4.34 us
    ppermute x1, starting transfers between devices, from_behind(): return lax.ppermute(block, axis, route)  3.39 us
  transfers between devices with their start and end apart: 11, of which 3 were waited for; matrix products, arithmetic and copies ran while one was open for 12% of the time, Pallas kernels for 0%

profile of v1, /device:TPU:512, one launch (start us, length us, event | category | flops | bytes accessed | tf_op | source)
XLA Modules:
  0.0 97.2 jit_solution(15849721695086487280)
XLA Ops:
  0.6 6.7 %collective-permute-start.8 = (bf16[1,1,8,32,128]{4,3,2,1,0:T(8,128)(2,1)}, bf16[1,1,8,32,128]{4,3,2,1,0:T(8,128)(2,1)S(1)}, u32[]{:S(2)}, u32[]{:S(2)}) collective-permute-start(bf16[1,1,8,32,128]{4,3,2,1,0:T(8,128)(2,1)} %param.5), channel_id=1, source_target_pairs={{10,0},{12,2},{14,4},{8,6},{18,8},{20,10},{22,12},{16,14},{26,16},... | collective-permute-start | bytes 196616 | tf_op jit(solution)/shard_map/ppermute | solution.py:60
  7.3 6.0 %collective-permute-start.7 = (bf16[1,1,8,32,128]{4,3,2,1,0:T(8,128)(2,1)}, bf16[1,1,8,32,128]{4,3,2,1,0:T(8,128)(2,1)S(1)}, u32[]{:S(2)}, u32[]{:S(2)}) collective-permute-start(bf16[1,1,8,32,128]{4,3,2,1,0:T(8,128)(2,1)} %param.5), channel_id=1, source_target_pairs={{8,0},{10,2},{12,4},{14,6},{16,8},{18,10},{20,12},{22,14},{24,16},... | collective-permute-start | bytes 196616 | tf_op jit(solution)/shard_map/ppermute | solution.py:60
  13.4 2.7 %collective-permute-start.6 = (bf16[1,1,8,32,128]{4,3,2,1,0:T(8,128)(2,1)}, bf16[1,1,8,32,128]{4,3,2,1,0:T(8,128)(2,1)S(1)}, u32[]{:S(2)}, u32[]{:S(2)}) collective-permute-start(bf16[1,1,8,32,128]{4,3,2,1,0:T(8,128)(2,1)} %param.5), channel_id=1, source_target_pairs={{0,2},{2,4},{4,6},{6,0},{1,3},{3,5},{5,7},{7,1},{8,10},{10,12},{12... | collective-permute-start | bytes 196616 | tf_op jit(solution)/shard_map/ppermute | solution.py:49
  16.0 2.9 %collective-permute-start.5 = (bf16[1,1,8,32,128]{4,3,2,1,0:T(8,128)(2,1)}, bf16[1,1,8,32,128]{4,3,2,1,0:T(8,128)(2,1)S(1)}, u32[]{:S(2)}, u32[]{:S(2)}) collective-permute-start(bf16[1,1,8,32,128]{4,3,2,1,0:T(8,128)(2,1)} %param.5), channel_id=1, source_target_pairs={{0,4},{2,6},{4,0},{6,2},{1,5},{3,7},{5,1},{7,3},{8,12},{10,14},{12... | collective-permute-start | bytes 196616 | tf_op jit(solution)/shard_map/ppermute | solution.py:49
  19.0 4.0 %collective-permute-start.4 = (bf16[1,1,8,32,128]{4,3,2,1,0:T(8,128)(2,1)}, bf16[1,1,8,32,128]{4,3,2,1,0:T(8,128)(2,1)S(1)}, u32[]{:S(2)}, u32[]{:S(2)}) collective-permute-start(bf16[1,1,8,32,128]{4,3,2,1,0:T(8,128)(2,1)} %param.5), channel_id=1, source_target_pairs={{0,6},{2,0},{4,2},{6,4},{1,7},{3,1},{5,3},{7,5},{8,14},{10,8},{12,... | collective-permute-start | bytes 196616 | tf_op jit(solution)/shard_map/ppermute | solution.py:49
  23.1 1.2 %fusion.71 = bf16[27,32,128]{2,1,0:T(8,128)(2,1)S(1)} fusion(s32[]{:T(128)S(6)} %select_n.14, bf16[27,32,128]{2,1,0:T(8,128)(2,1)} %param.4), kind=kLoop, calls=%fused_computation.131 | loop fusion | flops 442368 | bytes 442372 | tf_op jit(solution)/shard_map/jit(_roll_dynamic)/concatenate | solution.py:72
  24.3 1.0 slice.338
  25.3 0.8 constant_dynamic-update-slice_fusion.3
  26.2 2.4 %collective-permute-start.10 = (bf16[1,1,8,32,128]{4,3,2,1,0:T(8,128)(2,1)}, bf16[1,1,8,32,128]{4,3,2,1,0:T(8,128)(2,1)S(1)}, u32[]{:S(2)}, u32[]{:S(2)}) collective-permute-start(bf16[1,1,8,32,128]{4,3,2,1,0:T(8,128)(2,1)} %param.5), channel_id=1, source_target_pairs={{14,0},{8,2},{10,4},{12,6},{22,8},{16,10},{18,12},{20,14},{30,16},... | collective-permute-start | bytes 196616 | tf_op jit(solution)/shard_map/ppermute | solution.py:60
  28.6 3.2 %collective-permute-start.9 = (bf16[1,1,8,32,128]{4,3,2,1,0:T(8,128)(2,1)}, bf16[1,1,8,32,128]{4,3,2,1,0:T(8,128)(2,1)S(1)}, u32[]{:S(2)}, u32[]{:S(2)}) collective-permute-start(bf16[1,1,8,32,128]{4,3,2,1,0:T(8,128)(2,1)} %param.5), channel_id=1, source_target_pairs={{12,0},{14,2},{8,4},{10,6},{20,8},{22,10},{16,12},{18,14},{28,16},... | collective-permute-start | bytes 196616 | tf_op jit(solution)/shard_map/ppermute | solution.py:60
  31.9 4.9 %collective-permute-done.9 = bf16[1,1,8,32,128]{4,3,2,1,0:T(8,128)(2,1)S(1)} collective-permute-done((bf16[1,1,8,32,128]{4,3,2,1,0:T(8,128)(2,1)}, bf16[1,1,8,32,128]{4,3,2,1,0:T(8,128)(2,1)S(1)}, u32[]{:S(2)}, u32[]{:S(2)}) %collective-permute-start.9) | collective-permute-done | bytes 65568 | tf_op jit(solution)/shard_map/ppermute | solution.py:60
  36.8 3.4 %collective-permute-start = (bf16[1,1,16,32,256]{4,3,2,1,0:T(8,128)(2,1)S(1)}, bf16[1,1,16,32,256]{4,3,2,1,0:T(8,128)(2,1)S(1)}, u32[]{:S(2)}, u32[]{:S(2)}) collective-permute-start(bf16[1,1,16,32,256]{4,3,2,1,0:T(8,128)(2,1)S(1)} %slice.338), channel_id=1, source_target_pairs={{0,8},{8,16},{16,24},{24,32},{32,40},{40,48},{48,56},{56,64},{64,7... | collective-permute-start | bytes 786440 | tf_op jit(solution)/shard_map/ppermute | solution.py:10
  45.6 13.3 %collective-permute-done = bf16[1,1,16,32,256]{4,3,2,1,0:T(8,128)(2,1)S(1)} collective-permute-done((bf16[1,1,16,32,256]{4,3,2,1,0:T(8,128)(2,1)S(1)}, bf16[1,1,16,32,256]{4,3,2,1,0:T(8,128)(2,1)S(1)}, u32[]{:S(2)}, u32[]{:S(2)}) %collective-permute-start) | collective-permute-done | bytes 262176 | tf_op jit(solution)/shard_map/ppermute | solution.py:10
  59.0 3.1 %copy.5 = bf16[1,4,16,32,256]{3,4,2,1,0:T(8,128)(2,1)} copy(bf16[1,4,16,32,256]{4,3,2,1,0:T(8,128)(2,1)S(1)} %maximum_maximum_fusion) | data formatting | bytes 2097152 | tf_op jit(solution)/shard_map/concatenate | solution.py:74
  62.1 9.2 %copy.6 = bf16[1,2,2,8,2,32,128,2]{6,5,3,4,2,1,7,0:T(8,128)(2,1)S(1)} copy(bf16[1,2,2,8,2,32,128,2]{5,7,6,4,3,2,1,0:T(2,128)(2,1)} %bitcast.614) | data formatting | bytes 2097152 | tf_op jit(solution)/shard_map/reshape | solution.py:75
  71.5 0.2 convolution_bitcast_fusion.6
  71.7 0.2 convolution_bitcast_fusion.7
  72.0 0.2 convolution_bitcast_fusion
  72.2 0.2 convolution_bitcast_fusion.1
  72.5 0.2 convolution_bitcast_fusion.3
  72.8 0.2 convolution_bitcast_fusion.4
  73.6 0.2 fusion.103
  73.9 0.3 convolution_add_fusion.14
  74.1 0.3 convolution_add_fusion.13
  74.4 0.2 convolution_add_fusion.12
  74.7 0.2 convolution_add_fusion.11
  74.9 0.2 convolution_add_fusion.10
  75.2 0.2 convolution_add_fusion.9
  75.4 0.2 convolution_add_fusion.8
  75.7 0.2 convolution_add_fusion.7
  76.0 0.3 convolution_add_fusion.6
  76.2 0.2 convolution_add_fusion.5
  76.5 0.2 convolution_add_fusion.4
  76.8 0.2 convolution_add_fusion.3
  77.0 0.2 convolution_add_fusion.2
  77.3 0.2 convolution_add_fusion.1
  77.8 0.2 convolution_bitcast_fusion.2
  78.0 0.2 convolution_bitcast_fusion.8
  78.3 0.3 fusion
  78.6 0.5 fusion.12
  79.1 0.8 fusion.147
  79.8 2.5 %collective-permute-start.1 = (f32[1,1,8,32,128]{4,3,2,1,0:T(8,128)}, f32[1,1,8,32,128]{4,3,2,1,0:T(8,128)S(1)}, u32[]{:S(2)}, u32[]{:S(2)}) collective-permute-start(f32[1,1,8,32,128]{4,3,2,1,0:T(8,128)} %get-tuple-element.6), channel_id=1, source_target_pairs={{0,2},{2,4},{4,6},{6,0},{1,3},{3,5},{5,7},{7,1},{8,10},{10,12},{12... | collective-permute-start | bytes 393224 | tf_op jit(solution)/shard_map/ppermute | solution.py:49
  82.4 5.1 %collective-permute-start.3 = (f32[1,1,8,32,128]{4,3,2,1,0:T(8,128)}, f32[1,1,8,32,128]{4,3,2,1,0:T(8,128)}, u32[]{:S(2)}, u32[]{:S(2)}) collective-permute-start(f32[1,1,8,32,128]{4,3,2,1,0:T(8,128)} %get-tuple-element.7), channel_id=1, source_target_pairs={{0,6},{2,0},{4,2},{6,4},{1,7},{3,1},{5,3},{7,5},{8,14},{10,8},{12,... | collective-permute-start | bytes 393224 | tf_op jit(solution)/shard_map/ppermute | solution.py:49
  87.5 1.9 %collective-permute-start.2 = (f32[1,1,8,32,128]{4,3,2,1,0:T(8,128)}, f32[1,1,8,32,128]{4,3,2,1,0:T(8,128)}, u32[]{:S(2)}, u32[]{:S(2)}) collective-permute-start(f32[1,1,8,32,128]{4,3,2,1,0:T(8,128)} %get-tuple-element.8), channel_id=1, source_target_pairs={{0,4},{2,6},{4,0},{6,2},{1,5},{3,7},{5,1},{7,3},{8,12},{10,14},{12... | collective-permute-start | bytes 393224 | tf_op jit(solution)/shard_map/ppermute | solution.py:49
  89.6 1.5 %copy.7 = bf16[1,1,2,8,2,32,128,2]{5,7,6,4,3,2,1,0:T(2,128)(2,1)S(1)} copy(bf16[1,1,2,8,2,32,128,2]{6,5,3,7,4,2,1,0:T(8,128)(2,1)S(1)} %maximum_bitcast_fusion) | data formatting | bytes 1048576 | tf_op jit(solution)/shard_map/transpose | solution.py:109
  91.1 1.5 %copy.8 = bf16[1,2,16,32,256]{4,3,2,1,0:T(8,128)(2,1)} copy(bf16[1,2,16,32,256]{3,4,2,1,0:T(8,128)(2,1)S(1)} %bitcast.615) | data formatting | bytes 1048576
  92.6 3.0 %collective-permute-done.2 = f32[1,1,8,32,128]{4,3,2,1,0:T(8,128)} collective-permute-done((f32[1,1,8,32,128]{4,3,2,1,0:T(8,128)}, f32[1,1,8,32,128]{4,3,2,1,0:T(8,128)}, u32[]{:S(2)}, u32[]{:S(2)}) %collective-permute-start.2) | collective-permute-done | bytes 131104 | tf_op jit(solution)/shard_map/ppermute | solution.py:49
  95.5 1.6 %fusion.85 = bf16[1,1,8,32,128]{4,3,2,1,0:T(8,128)(2,1)} fusion(f32[1,1,8,32,128]{4,3,2,1,0:T(8,128)} %collective-permute-done.3, f32[1,1,8,32,128]{4,3,2,1,0:T(8,128)} %collective-permute-done.2, f32[1,1,8,32,128]{4,3,2,1,0:T(8,128)S(1)} %collective-permute-done.1, f32[1,1,8,128,128]{4,3,2,1,0:T(8,128)S(1)} %fusion.12), kind=kLoop, calls=%fused_computation.147 | loop fusion | flops 131072 | bytes 589824 | tf_op jit(solution)/shard_map/convert_element_type | solution.py:100
  (96 shorter events, 6.5 us)
Async XLA Ops:
  0.6 28.0 %collective-permute-start.8 = (bf16[1,1,8,32,128]{4,3,2,1,0:T(8,128)(2,1)}, bf16[1,1,8,32,128]{4,3,2,1,0:T(8,128)(2,1)S(1)}, u32[]{:S(2)}, u32[]{:S(2)}) collective-permute-start(bf16[1,1,8,32,128]{4,3,2,1,0:T(8,128)(2,1)} %param.5), channel_id=1, source_target_pairs={{10,0},{12,2},{14,4},{8,6},{18,8},{20,10},{22,12},{16,14},{26,16},... | collective-permute-start | bytes 196616 | tf_op jit(solution)/shard_map/ppermute | solution.py:60
  7.3 18.8 %collective-permute-start.7 = (bf16[1,1,8,32,128]{4,3,2,1,0:T(8,128)(2,1)}, bf16[1,1,8,32,128]{4,3,2,1,0:T(8,128)(2,1)S(1)}, u32[]{:S(2)}, u32[]{:S(2)}) collective-permute-start(bf16[1,1,8,32,128]{4,3,2,1,0:T(8,128)(2,1)} %param.5), channel_id=1, source_target_pairs={{8,0},{10,2},{12,4},{14,6},{16,8},{18,10},{20,12},{22,14},{24,16},... | collective-permute-start | bytes 196616 | tf_op jit(solution)/shard_map/ppermute | solution.py:60
  13.4 27.6 %collective-permute-start.6 = (bf16[1,1,8,32,128]{4,3,2,1,0:T(8,128)(2,1)}, bf16[1,1,8,32,128]{4,3,2,1,0:T(8,128)(2,1)S(1)}, u32[]{:S(2)}, u32[]{:S(2)}) collective-permute-start(bf16[1,1,8,32,128]{4,3,2,1,0:T(8,128)(2,1)} %param.5), channel_id=1, source_target_pairs={{0,2},{2,4},{4,6},{6,0},{1,3},{3,5},{5,7},{7,1},{8,10},{10,12},{12... | collective-permute-start | bytes 196616 | tf_op jit(solution)/shard_map/ppermute | solution.py:49
  16.0 24.9 %collective-permute-start.5 = (bf16[1,1,8,32,128]{4,3,2,1,0:T(8,128)(2,1)}, bf16[1,1,8,32,128]{4,3,2,1,0:T(8,128)(2,1)S(1)}, u32[]{:S(2)}, u32[]{:S(2)}) collective-permute-start(bf16[1,1,8,32,128]{4,3,2,1,0:T(8,128)(2,1)} %param.5), channel_id=1, source_target_pairs={{0,4},{2,6},{4,0},{6,2},{1,5},{3,7},{5,1},{7,3},{8,12},{10,14},{12... | collective-permute-start | bytes 196616 | tf_op jit(solution)/shard_map/ppermute | solution.py:49
  19.0 21.9 %collective-permute-start.4 = (bf16[1,1,8,32,128]{4,3,2,1,0:T(8,128)(2,1)}, bf16[1,1,8,32,128]{4,3,2,1,0:T(8,128)(2,1)S(1)}, u32[]{:S(2)}, u32[]{:S(2)}) collective-permute-start(bf16[1,1,8,32,128]{4,3,2,1,0:T(8,128)(2,1)} %param.5), channel_id=1, source_target_pairs={{0,6},{2,0},{4,2},{6,4},{1,7},{3,1},{5,3},{7,5},{8,14},{10,8},{12,... | collective-permute-start | bytes 196616 | tf_op jit(solution)/shard_map/ppermute | solution.py:49
  26.2 14.1 %collective-permute-start.10 = (bf16[1,1,8,32,128]{4,3,2,1,0:T(8,128)(2,1)}, bf16[1,1,8,32,128]{4,3,2,1,0:T(8,128)(2,1)S(1)}, u32[]{:S(2)}, u32[]{:S(2)}) collective-permute-start(bf16[1,1,8,32,128]{4,3,2,1,0:T(8,128)(2,1)} %param.5), channel_id=1, source_target_pairs={{14,0},{8,2},{10,4},{12,6},{22,8},{16,10},{18,12},{20,14},{30,16},... | collective-permute-start | bytes 196616 | tf_op jit(solution)/shard_map/ppermute | solution.py:60
  28.6 8.2 %collective-permute-start.9 = (bf16[1,1,8,32,128]{4,3,2,1,0:T(8,128)(2,1)}, bf16[1,1,8,32,128]{4,3,2,1,0:T(8,128)(2,1)S(1)}, u32[]{:S(2)}, u32[]{:S(2)}) collective-permute-start(bf16[1,1,8,32,128]{4,3,2,1,0:T(8,128)(2,1)} %param.5), channel_id=1, source_target_pairs={{12,0},{14,2},{8,4},{10,6},{20,8},{22,10},{16,12},{18,14},{28,16},... | collective-permute-start | bytes 196616 | tf_op jit(solution)/shard_map/ppermute | solution.py:60
  36.8 22.1 %collective-permute-start = (bf16[1,1,16,32,256]{4,3,2,1,0:T(8,128)(2,1)S(1)}, bf16[1,1,16,32,256]{4,3,2,1,0:T(8,128)(2,1)S(1)}, u32[]{:S(2)}, u32[]{:S(2)}) collective-permute-start(bf16[1,1,16,32,256]{4,3,2,1,0:T(8,128)(2,1)S(1)} %slice.338), channel_id=1, source_target_pairs={{0,8},{8,16},{16,24},{24,32},{32,40},{40,48},{48,56},{56,64},{64,7... | collective-permute-start | bytes 786440 | tf_op jit(solution)/shard_map/ppermute | solution.py:10
  43.8 15.1 %copy-start = (bf16[1,2,16,32,256]{4,3,2,1,0:T(8,128)(2,1)S(1)}, bf16[1,2,16,32,256]{4,3,2,1,0:T(8,128)(2,1)}, u32[]{:S(2)}) copy-start(bf16[1,2,16,32,256]{4,3,2,1,0:T(8,128)(2,1)} %param.3) | copy-start | bytes 1572868
  71.5 2.7 %copy-start.1 = (bf16[1,1,8,32,128]{4,3,2,1,0:T(8,128)(2,1)}, bf16[1,1,8,32,128]{4,3,2,1,0:T(8,128)(2,1)S(1)}, u32[]{:S(2)}) copy-start(bf16[1,1,8,32,128]{4,3,2,1,0:T(8,128)(2,1)S(1)} %slice_bitcast_fusion.28) | copy-start | bytes 196612
  72.0 2.4 %copy-start.2 = (bf16[1,1,8,32,128]{4,3,2,1,0:T(8,128)(2,1)}, bf16[1,1,8,32,128]{4,3,2,1,0:T(8,128)(2,1)S(1)}, u32[]{:S(2)}) copy-start(bf16[1,1,8,32,128]{4,3,2,1,0:T(8,128)(2,1)S(1)} %slice_bitcast_fusion.26) | copy-start | bytes 196612
  72.5 2.1 %copy-start.4 = (bf16[1,1,8,32,128]{4,3,2,1,0:T(8,128)(2,1)}, bf16[1,1,8,32,128]{4,3,2,1,0:T(8,128)(2,1)S(1)}, u32[]{:S(2)}) copy-start(bf16[1,1,8,32,128]{4,3,2,1,0:T(8,128)(2,1)S(1)} %slice_bitcast_fusion.27) | copy-start | bytes 196612
  73.0 2.1 %copy-start.3 = (bf16[1,1,8,32,128]{4,3,2,1,0:T(8,128)(2,1)}, bf16[1,1,8,32,128]{4,3,2,1,0:T(8,128)(2,1)S(1)}, u32[]{:S(2)}) copy-start(bf16[1,1,8,32,128]{4,3,2,1,0:T(8,128)(2,1)S(1)} %slice_bitcast_fusion.29) | copy-start | bytes 196612
  73.3 2.1 %copy-start.5 = (bf16[1,1,8,32,128]{4,3,2,1,0:T(8,128)(2,1)}, bf16[1,1,8,32,128]{4,3,2,1,0:T(8,128)(2,1)S(1)}, u32[]{:S(2)}) copy-start(bf16[1,1,8,32,128]{4,3,2,1,0:T(8,128)(2,1)S(1)} %slice_bitcast_fusion.30) | copy-start | bytes 196612
  75.7 1.1 %slice-start.4 = ((bf16[1,1,8,32,128]{4,3,2,1,0:T(8,128)(2,1)}), bf16[1,1,7,32,128]{4,3,2,1,0:T(8,128)(2,1)S(1)}, s32[]{:S(2)}) async-start(bf16[1,1,8,32,128]{4,3,2,1,0:T(8,128)(2,1)} %copy-done.5), calls=%async_computation.4 | async-start | bytes 114688 | tf_op jit(solution)/shard_map/slice | solution.py:16
  75.7 1.8 %slice-start.3 = ((bf16[1,1,8,32,128]{4,3,2,1,0:T(8,128)(2,1)}), bf16[1,1,7,32,128]{4,3,2,1,0:T(8,128)(2,1)S(1)}, s32[]{:S(2)}) async-start(bf16[1,1,8,32,128]{4,3,2,1,0:T(8,128)(2,1)} %copy-done.4), calls=%async_computation.3 | async-start | bytes 114688 | tf_op jit(solution)/shard_map/slice | solution.py:16
  75.7 2.1 %slice-start.1 = ((bf16[1,1,8,32,128]{4,3,2,1,0:T(8,128)(2,1)}), bf16[1,1,7,32,128]{4,3,2,1,0:T(8,128)(2,1)S(1)}, s32[]{:S(2)}) async-start(bf16[1,1,8,32,128]{4,3,2,1,0:T(8,128)(2,1)} %copy-done.2), calls=%async_computation.1 | async-start | bytes 114688 | tf_op jit(solution)/shard_map/slice | solution.py:16
  76.0 2.1 %slice-start = ((bf16[1,1,8,32,128]{4,3,2,1,0:T(8,128)(2,1)}), bf16[1,1,7,32,128]{4,3,2,1,0:T(8,128)(2,1)S(1)}, s32[]{:S(2)}) async-start(bf16[1,1,8,32,128]{4,3,2,1,0:T(8,128)(2,1)} %copy-done.1), calls=%async_computation | async-start | bytes 114688 | tf_op jit(solution)/shard_map/slice | solution.py:16
  76.0 2.3 %slice-start.2 = ((bf16[1,1,8,32,128]{4,3,2,1,0:T(8,128)(2,1)}), bf16[1,1,7,32,128]{4,3,2,1,0:T(8,128)(2,1)S(1)}, s32[]{:S(2)}) async-start(bf16[1,1,8,32,128]{4,3,2,1,0:T(8,128)(2,1)} %copy-done.3), calls=%async_computation.2 | async-start | bytes 114688 | tf_op jit(solution)/shard_map/slice | solution.py:16
  79.8 12.7 %collective-permute-start.1 = (f32[1,1,8,32,128]{4,3,2,1,0:T(8,128)}, f32[1,1,8,32,128]{4,3,2,1,0:T(8,128)S(1)}, u32[]{:S(2)}, u32[]{:S(2)}) collective-permute-start(f32[1,1,8,32,128]{4,3,2,1,0:T(8,128)} %get-tuple-element.6), channel_id=1, source_target_pairs={{0,2},{2,4},{4,6},{6,0},{1,3},{3,5},{5,7},{7,1},{8,10},{10,12},{12... | collective-permute-start | bytes 393224 | tf_op jit(solution)/shard_map/ppermute | solution.py:49
  82.4 10.2 %collective-permute-start.3 = (f32[1,1,8,32,128]{4,3,2,1,0:T(8,128)}, f32[1,1,8,32,128]{4,3,2,1,0:T(8,128)}, u32[]{:S(2)}, u32[]{:S(2)}) collective-permute-start(f32[1,1,8,32,128]{4,3,2,1,0:T(8,128)} %get-tuple-element.7), channel_id=1, source_target_pairs={{0,6},{2,0},{4,2},{6,4},{1,7},{3,1},{5,3},{7,5},{8,14},{10,8},{12,... | collective-permute-start | bytes 393224 | tf_op jit(solution)/shard_map/ppermute | solution.py:49
  87.5 8.1 %collective-permute-start.2 = (f32[1,1,8,32,128]{4,3,2,1,0:T(8,128)}, f32[1,1,8,32,128]{4,3,2,1,0:T(8,128)}, u32[]{:S(2)}, u32[]{:S(2)}) collective-permute-start(f32[1,1,8,32,128]{4,3,2,1,0:T(8,128)} %get-tuple-element.8), channel_id=1, source_target_pairs={{0,4},{2,6},{4,0},{6,2},{1,5},{3,7},{5,1},{7,3},{8,12},{10,14},{12... | collective-permute-start | bytes 393224 | tf_op jit(solution)/shard_map/ppermute | solution.py:49

commit v2 on v1

--- a/solution.py
+++ b/solution.py
@@ -2,6 +2,8 @@
 import jax.numpy as jnp
 from jax import lax
 from jax.sharding import PartitionSpec as P
+from jax.experimental import pallas as pl
+from jax.experimental.pallas import tpu as pltpu
 
 
 def from_behind(block, axis, distance):
@@ -44,6 +46,51 @@
     return jnp.stack([upper, lower], axis=3)
 
 
+def forward_rows(halo_ref, vol_ref, sel_ref, kbig_ref, out_ref, picked_ref):
+    planes, rows, chans, cols = vol_ref.shape
+    rows_out = out_ref.shape[0]
+    cols_out = out_ref.shape[2]
+    sel = sel_ref[...]
+    for plane in range(planes + 1):
+        source = halo_ref[...] if plane == 0 else vol_ref[plane - 1]
+        flat = source.reshape(rows * chans, cols)
+        chosen = jnp.dot(flat, sel, preferred_element_type=jnp.float32)
+        picked_ref[plane] = chosen.astype(picked_ref.dtype).reshape(rows, chans, 3 * cols_out)
+    kbig = kbig_ref[...]
+    zero = jnp.zeros((chans, cols_out), picked_ref.dtype)
+    for i in range(rows_out):
+        pieces = []
+        for depth_tap in range(3):
+            for row_tap in range(3):
+                row = 2 * i + row_tap - 1
+                for col_tap in range(3):
+                    if row < 0:
+                        pieces.append(zero)
+                    else:
+                        pieces.append(picked_ref[depth_tap, row, :, col_tap * cols_out:(col_tap + 1) * cols_out])
+        stacked = jnp.concatenate(pieces, axis=0)
+        out_ref[i] = jnp.dot(kbig, stacked, preferred_element_type=jnp.float32)
+
+
+def forward_partial(halo, vol, kernel):
+    planes, rows, chans, cols = vol.shape
+    taps, _, chans_out = kernel.shape
+    rows_out, cols_out = rows // 2, cols // 2
+    w = jnp.arange(cols)[:, None]
+    k = jnp.arange(3 * cols_out)[None, :]
+    sel = (w == 2 * (k % cols_out) + k // cols_out - 1).astype(vol.dtype)
+    kbig = jnp.transpose(kernel, (2, 0, 1)).reshape(chans_out, taps * chans)
+    flops = 2 * (planes + 1) * rows * chans * cols * 3 * cols_out + 2 * rows_out * chans_out * taps * chans * cols_out
+    return pl.pallas_call(
+        forward_rows,
+        out_shape=jax.ShapeDtypeStruct((rows_out, chans_out, cols_out), jnp.float32),
+        in_specs=[pl.BlockSpec(memory_space=pltpu.VMEM)] * 4,
+        out_specs=pl.BlockSpec(memory_space=pltpu.VMEM),
+        scratch_shapes=[pltpu.VMEM((planes + 1, rows, chans, 3 * cols_out), vol.dtype)],
+        cost_estimate=pl.CostEstimate(flops=flops, bytes_accessed=2 * 4 * vol.size, transcendentals=0),
+    )(halo, vol, sel, kbig)
+
+
 def chan_shift(block, shift):
     size = lax.axis_size("chan")
     return lax.ppermute(block, "chan", [(i, (i + shift) % size) for i in range(size)])
@@ -71,29 +118,8 @@
     me = lax.axis_index("chan")
     kernel = jnp.roll(kernel, -me * share, axis=2)
     below = from_behind(volume[:, -1:], "space", 1)
-    extended = jnp.concatenate([below, volume, jnp.zeros_like(below)], axis=1)
-    extended = extended.reshape(count, planes_out + 1, 2, rows_out, 2, chans_in, cols_out, 2)
-    extended = jnp.moveaxis(extended, 7, 6)
-    column_sets = [
-        shift_front(extended[:, :, :, :, :, :, 1], 6),
-        extended[:, :, :, :, :, :, 0],
-        extended[:, :, :, :, :, :, 1],
-    ]
-    partial_sum = jnp.zeros((count, planes_out, rows_out, chans_out, cols_out), jnp.float32)
-    for col_tap in range(3):
-        columns = column_sets[col_tap]
-        depth_sets = [columns[:, :planes_out, 0], columns[:, :planes_out, 1], columns[:, 1:, 0]]
-        for depth_tap in range(3):
-            slab = depth_sets[depth_tap]
-            row_sets = [shift_front(slab[:, :, :, 1], 2), slab[:, :, :, 0], slab[:, :, :, 1]]
-            for row_tap in range(3):
-                index = 9 * depth_tap + 3 * row_tap + col_tap
-                partial_sum = partial_sum + jnp.einsum(
-                    "bdhcw,ce->bdhew",
-                    row_sets[row_tap],
-                    kernel[index],
-                    preferred_element_type=jnp.float32,
-                )
+    partial_sum = forward_partial(below[0, 0], volume[0], kernel)
+    partial_sum = partial_sum.reshape(count, planes_out, rows_out, chans_out, cols_out)
     total = partial_sum[:, :, :, :share]
     for k in range(1, groups):
         total = total + chan_shift(partial_sum[:, :, :, k * share:(k + 1) * share], k)

time: 97.9 us -> 77.5 us (0.79)
  local copies, waits for them, and re-layouts: 19.1 us -> 7.28 us
  matrix products: 11.2 us -> 4.39 us
  waiting for transfers between devices: 21.2 us -> 16.6 us
  Pallas kernels: 0 us -> 3.09 us
    reshape x1, local copies, waits for them, and re-layouts: 9.15 us -> 0.85 us  [forward_partial(): kbig = jnp.transpose(kernel, (2, 0, 1)).reshape(chans_out, taps * chans)]
    dot_general x27 -> x0, matrix products: 6.89 us -> none  [per_device(): jnp.einsum('bdhcw,ce->bdhew', row_sets[row_tap], kernel[index], preferred...]
    ppermute x4, waiting for transfers between devices: 4.94 us -> 1.68 us  [from_next_slab(): return lax.ppermute(block, ('space', 'chan'), route)]
    concatenate x2 -> x0, local copies, waits for them, and re-layouts: 3.16 us -> none  [per_device(): extended = jnp.concatenate([below, volume, jnp.zeros_like(below)], axis=1)]
    pallas_call x0 -> x1, Pallas kernels: none -> 3.09 us  [forward_partial(): pl.pallas_call(forward_rows, out_shape=jax.ShapeDtypeStruct((rows_out, ch...]
    ppermute x6, waiting for transfers between devices: 2.99 us -> 0.98 us  [chan_shift(): lax.ppermute(block, 'chan', [(i, (i + shift) % size) for i in range(size)])]
    ppermute x1, starting transfers between devices: 3.39 us -> 1.92 us  [from_behind(): return lax.ppermute(block, axis, route)]
    ppermute x6, starting transfers between devices: 19.2 us -> 20.6 us  [chan_shift(): lax.ppermute(block, 'chan', [(i, (i + shift) % size) for i in range(size)])]
  transfers between devices with their start and end apart: 11 -> 11, of which waited for: 3 -> 4; matrix products, arithmetic and copies ran while one was open for 12% -> 16% of each run, Pallas kernels for 0% -> 0%
where the time goes in v2:
time: 77.5 us; the launch traced here: 77 us
  starting transfers between devices  40.8 us (53%)
  waiting for transfers between devices  16.6 us (21%)
  local copies, waits for them, and re-layouts  7.28 us (9%)
  matrix products  4.39 us (6%)
  other arithmetic  3.75 us (5%)
  Pallas kernels  3.09 us (4%)
  between operations  1.07 us (1%)
    ppermute x6, starting transfers between devices, chan_shift(): lax.ppermute(block, 'chan', [(i, (i + shift) % size) for i in range(size)])  20.6 us
    ppermute x4, starting transfers between devices, from_next_slab(): return lax.ppermute(block, ('space', 'chan'), route)  18.3 us
    ppermute x1, waiting for transfers between devices, from_behind(): return lax.ppermute(block, axis, route)  13.9 us
    dot_general x27, matrix products, transposed_phases(): jnp.einsum('bdhew,ce->bdhcw', picked, taps[row_tap, col_tap], preferred_e...  4.39 us
    pallas_call x1, Pallas kernels, forward_partial(): pl.pallas_call(forward_rows, out_shape=jax.ShapeDtypeStruct((rows_out, ch...  3.09 us
    unnamed x11, local copies, waits for them, and re-layouts  2.28 us
    ppermute x1, starting transfers between devices, from_behind(): return lax.ppermute(block, axis, route)  1.92 us
    ppermute x4, waiting for transfers between devices, from_next_slab(): return lax.ppermute(block, ('space', 'chan'), route)  1.68 us
  transfers between devices with their start and end apart: 11, of which 4 were waited for; matrix products, arithmetic and copies ran while one was open for 16% of the time, Pallas kernels for 0%

profile of v2, /device:TPU:512, one launch (start us, length us, event | category | flops | bytes accessed | tf_op | source)
XLA Modules:
  0.0 77.0 jit_solution(9902949648571774770)
XLA Ops:
  0.6 6.0 %collective-permute-start.4 = (bf16[1,1,8,32,128]{4,3,2,1,0:T(8,128)(2,1)}, bf16[1,1,8,32,128]{4,3,2,1,0:T(8,128)(2,1)S(1)}, u32[]{:S(2)}, u32[]{:S(2)}) collective-permute-start(bf16[1,1,8,32,128]{4,3,2,1,0:T(8,128)(2,1)} %param.5), channel_id=1, source_target_pairs={{0,6},{2,0},{4,2},{6,4},{1,7},{3,1},{5,3},{7,5},{8,14},{10,8},{12,... | collective-permute-start | bytes 196616 | tf_op jit(solution)/shard_map/ppermute | solution.py:96
  6.6 1.9 %collective-permute-start.5 = (bf16[1,1,8,32,128]{4,3,2,1,0:T(8,128)(2,1)}, bf16[1,1,8,32,128]{4,3,2,1,0:T(8,128)(2,1)S(1)}, u32[]{:S(2)}, u32[]{:S(2)}) collective-permute-start(bf16[1,1,8,32,128]{4,3,2,1,0:T(8,128)(2,1)} %param.5), channel_id=1, source_target_pairs={{0,4},{2,6},{4,0},{6,2},{1,5},{3,7},{5,1},{7,3},{8,12},{10,14},{12... | collective-permute-start | bytes 196616 | tf_op jit(solution)/shard_map/ppermute | solution.py:96
  8.6 2.8 %collective-permute-start.6 = (bf16[1,1,8,32,128]{4,3,2,1,0:T(8,128)(2,1)}, bf16[1,1,8,32,128]{4,3,2,1,0:T(8,128)(2,1)S(1)}, u32[]{:S(2)}, u32[]{:S(2)}) collective-permute-start(bf16[1,1,8,32,128]{4,3,2,1,0:T(8,128)(2,1)} %param.5), channel_id=1, source_target_pairs={{0,2},{2,4},{4,6},{6,0},{1,3},{3,5},{5,7},{7,1},{8,10},{10,12},{12... | collective-permute-start | bytes 196616 | tf_op jit(solution)/shard_map/ppermute | solution.py:96
  11.4 6.9 %collective-permute-start.7 = (bf16[1,1,8,32,128]{4,3,2,1,0:T(8,128)(2,1)}, bf16[1,1,8,32,128]{4,3,2,1,0:T(8,128)(2,1)S(1)}, u32[]{:S(2)}, u32[]{:S(2)}) collective-permute-start(bf16[1,1,8,32,128]{4,3,2,1,0:T(8,128)(2,1)} %param.5), channel_id=1, source_target_pairs={{8,0},{10,2},{12,4},{14,6},{16,8},{18,10},{20,12},{22,14},{24,16},... | collective-permute-start | bytes 196616 | tf_op jit(solution)/shard_map/ppermute | solution.py:107
  18.2 3.1 %collective-permute-start.8 = (bf16[1,1,8,32,128]{4,3,2,1,0:T(8,128)(2,1)}, bf16[1,1,8,32,128]{4,3,2,1,0:T(8,128)(2,1)S(1)}, u32[]{:S(2)}, u32[]{:S(2)}) collective-permute-start(bf16[1,1,8,32,128]{4,3,2,1,0:T(8,128)(2,1)} %param.5), channel_id=1, source_target_pairs={{10,0},{12,2},{14,4},{8,6},{18,8},{20,10},{22,12},{16,14},{26,16},... | collective-permute-start | bytes 196616 | tf_op jit(solution)/shard_map/ppermute | solution.py:107
  21.4 1.2 %fusion.59 = bf16[27,32,128]{2,1,0:T(8,128)(2,1)S(1)} fusion(s32[]{:T(128)S(6)} %select_n.37, bf16[27,32,128]{2,1,0:T(8,128)(2,1)} %param.4), kind=kLoop, calls=%fused_computation.88 | loop fusion | flops 442368 | bytes 442372 | tf_op jit(solution)/shard_map/jit(_roll_dynamic)/concatenate | solution.py:119
  22.6 0.8 %copy.6.kbig_ref = bf16[128,864]{1,0:T(8,128)(2,1)} copy(bf16[128,864]{0,1:T(8,128)(2,1)S(1)} %bitcast.298) | data formatting | bytes 442368 | tf_op jit(solution)/shard_map/reshape | solution.py:82
  23.5 1.0 %slice.129 = bf16[1,1,16,32,256]{4,3,2,1,0:T(8,128)(2,1)S(1)} slice(bf16[1,2,16,32,256]{4,3,2,1,0:T(8,128)(2,1)} %param.3), slice={[0:1], [1:2], [0:16], [0:32], [0:256]} | slice | bytes 524288 | tf_op jit(solution)/shard_map/slice | solution.py:120
  24.4 0.7 fusion.14.sel_ref
  25.2 3.9 %collective-permute-start.9 = (bf16[1,1,8,32,128]{4,3,2,1,0:T(8,128)(2,1)S(1)}, bf16[1,1,8,32,128]{4,3,2,1,0:T(8,128)(2,1)S(1)}, u32[]{:S(2)}, u32[]{:S(2)}) collective-permute-start(bf16[1,1,8,32,128]{4,3,2,1,0:T(8,128)(2,1)S(1)} %copy-done), channel_id=1, source_target_pairs={{12,0},{14,2},{8,4},{10,6},{20,8},{22,10},{16,12},{18,14},{28,16},... | collective-permute-start | bytes 196616 | tf_op jit(solution)/shard_map/ppermute | solution.py:107
  29.1 4.5 %collective-permute-start.10 = (bf16[1,1,8,32,128]{4,3,2,1,0:T(8,128)(2,1)S(1)}, bf16[1,1,8,32,128]{4,3,2,1,0:T(8,128)(2,1)S(1)}, u32[]{:S(2)}, u32[]{:S(2)}) collective-permute-start(bf16[1,1,8,32,128]{4,3,2,1,0:T(8,128)(2,1)S(1)} %copy-done), channel_id=1, source_target_pairs={{14,0},{8,2},{10,4},{12,6},{22,8},{16,10},{18,12},{20,14},{30,16},... | collective-permute-start | bytes 196616 | tf_op jit(solution)/shard_map/ppermute | solution.py:107
  33.6 1.9 %collective-permute-start = (bf16[1,1,16,32,256]{4,3,2,1,0:T(8,128)(2,1)S(1)}, bf16[1,1,16,32,256]{4,3,2,1,0:T(8,128)(2,1)S(1)}, u32[]{:S(2)}, u32[]{:S(2)}) collective-permute-start(bf16[1,1,16,32,256]{4,3,2,1,0:T(8,128)(2,1)S(1)} %slice.129), channel_id=1, source_target_pairs={{0,8},{8,16},{16,24},{24,32},{32,40},{40,48},{48,56},{56,64},{64,7... | collective-permute-start | bytes 786440 | tf_op jit(solution)/shard_map/ppermute | solution.py:12
  35.9 0.2 fusion.47
  36.0 0.2 fusion.9
  36.3 1.7 %collective-permute-done.10 = bf16[1,1,8,32,128]{4,3,2,1,0:T(8,128)(2,1)S(1)} collective-permute-done((bf16[1,1,8,32,128]{4,3,2,1,0:T(8,128)(2,1)S(1)}, bf16[1,1,8,32,128]{4,3,2,1,0:T(8,128)(2,1)S(1)}, u32[]{:S(2)}, u32[]{:S(2)}) %collective-permute-start.10) | collective-permute-done | bytes 65568 | tf_op jit(solution)/shard_map/ppermute | solution.py:107
  38.3 0.2 fusion.23
  38.5 0.2 convolution_bitcast_fusion.1
  38.9 0.2 fusion.28
  39.1 0.2 fusion.43
  39.3 0.2 fusion.41
  39.4 0.2 convolution_bitcast_fusion
  39.6 0.2 convolution_add_fusion.12
  39.8 0.2 convolution_add_fusion.11
  40.0 0.2 fusion.10
  40.1 0.2 fusion.12
  40.3 0.2 fusion.11
  40.8 0.2 convolution_add_fusion.7
  40.9 0.2 convolution_add_fusion.6
  41.1 0.2 fusion.3
  41.3 0.2 fusion.5
  41.4 0.2 fusion.4
  41.6 0.2 convolution_add_fusion.2
  41.8 0.2 convolution_add_fusion.1
  42.0 0.2 fusion.2
  42.1 0.2 fusion.1
  42.4 0.2 fusion
  42.6 13.9 %collective-permute-done = bf16[1,1,16,32,256]{4,3,2,1,0:T(8,128)(2,1)S(1)} collective-permute-done((bf16[1,1,16,32,256]{4,3,2,1,0:T(8,128)(2,1)S(1)}, bf16[1,1,16,32,256]{4,3,2,1,0:T(8,128)(2,1)S(1)}, u32[]{:S(2)}, u32[]{:S(2)}) %collective-permute-start) | collective-permute-done | bytes 262176 | tf_op jit(solution)/shard_map/ppermute | solution.py:12
  56.5 0.7 copy-done.1
  57.2 3.1 %shard_map.50 = f32[8,128,128]{2,1,0:T(8,128)} custom-call(bf16[16,32,256]{2,1,0:T(8,128)(2,1)} %bitcast.329, bf16[2,16,32,256]{3,2,1,0:T(8,128)(2,1)} %bitcast.328, bf16[256,384]{1,0:T(8,128)(2,1)} %fusion.14.sel_ref, bf16[128,864]{1,0:T(8,128)(2,1)} %copy.6.kbig_ref), custom_call_target="tpu_custom_call" | custom-call | flops 528482304 | bytes 2097152 | tf_op jit(solution)/shard_map/pallas_call | solution.py:84
  60.3 1.1 %fusion.96 = (f32[1,1,8,32,128]{4,3,2,1,0:T(8,128)S(1)}, f32[1,1,8,32,128]{4,3,2,1,0:T(8,128)S(1)}, f32[1,1,8,32,128]{4,3,2,1,0:T(8,128)S(1)}) fusion(f32[1,1,8,128,128]{4,3,2,1,0:T(8,128)} %bitcast.299), kind=kLoop, calls=%fused_computation.168 | loop fusion | bytes 786432 | tf_op jit(solution)/shard_map/slice | solution.py:125
  61.4 2.4 %collective-permute-start.1 = (f32[1,1,8,32,128]{4,3,2,1,0:T(8,128)S(1)}, f32[1,1,8,32,128]{4,3,2,1,0:T(8,128)S(1)}, u32[]{:S(2)}, u32[]{:S(2)}) collective-permute-start(f32[1,1,8,32,128]{4,3,2,1,0:T(8,128)S(1)} %get-tuple-element.4), channel_id=1, source_target_pairs={{0,2},{2,4},{4,6},{6,0},{1,3},{3,5},{5,7},{7,1},{8,10},{10,12},{12... | collective-permute-start | bytes 393224 | tf_op jit(solution)/shard_map/ppermute | solution.py:96
  63.8 2.7 %collective-permute-start.2 = (f32[1,1,8,32,128]{4,3,2,1,0:T(8,128)S(1)}, f32[1,1,8,32,128]{4,3,2,1,0:T(8,128)S(1)}, u32[]{:S(2)}, u32[]{:S(2)}) collective-permute-start(f32[1,1,8,32,128]{4,3,2,1,0:T(8,128)S(1)} %get-tuple-element.6), channel_id=1, source_target_pairs={{0,4},{2,6},{4,0},{6,2},{1,5},{3,7},{5,1},{7,3},{8,12},{10,14},{12... | collective-permute-start | bytes 393224 | tf_op jit(solution)/shard_map/ppermute | solution.py:96
  66.4 4.8 %collective-permute-start.3 = (f32[1,1,8,32,128]{4,3,2,1,0:T(8,128)S(1)}, f32[1,1,8,32,128]{4,3,2,1,0:T(8,128)S(1)}, u32[]{:S(2)}, u32[]{:S(2)}) collective-permute-start(f32[1,1,8,32,128]{4,3,2,1,0:T(8,128)S(1)} %get-tuple-element.5), channel_id=1, source_target_pairs={{0,6},{2,0},{4,2},{6,4},{1,7},{3,1},{5,3},{7,5},{8,14},{10,8},{12,... | collective-permute-start | bytes 393224 | tf_op jit(solution)/shard_map/ppermute | solution.py:96
  71.4 1.5 %copy.7 = bf16[1,1,2,8,2,32,128,2]{5,7,6,4,3,2,1,0:T(2,128)(2,1)S(1)} copy(bf16[1,1,2,8,2,32,128,2]{6,5,3,7,4,2,1,0:T(8,128)(2,1)S(1)} %maximum_bitcast_fusion) | data formatting | bytes 1048576 | tf_op jit(solution)/shard_map/transpose | solution.py:135
  72.9 1.5 %copy.8 = bf16[1,2,16,32,256]{4,3,2,1,0:T(8,128)(2,1)} copy(bf16[1,2,16,32,256]{3,4,2,1,0:T(8,128)(2,1)S(1)} %bitcast.297) | data formatting | bytes 1048576
  74.4 0.2 collective-permute-done.2
  74.6 0.8 collective-permute-done.3
  75.4 1.6 %fusion.70 = bf16[1,1,8,32,128]{4,3,2,1,0:T(8,128)(2,1)} fusion(f32[1,1,8,32,128]{4,3,2,1,0:T(8,128)S(1)} %collective-permute-done.3, f32[1,1,8,32,128]{4,3,2,1,0:T(8,128)S(1)} %collective-permute-done.2, f32[1,1,8,32,128]{4,3,2,1,0:T(8,128)S(1)} %collective-permute-done.1, f32[1,1,8,128,128]{4,3,2,1,0:T(8,128)} %bitcast.300), kind=kLoop, calls=%fused_computation.101 | loop fusion | flops 131072 | bytes 589824 | tf_op jit(solution)/shard_map/convert_element_type | solution.py:126
  (36 shorter events, 1.6 us)
Async XLA Ops:
  0.6 24.5 %copy-start = (bf16[1,1,8,32,128]{4,3,2,1,0:T(8,128)(2,1)S(1)}, bf16[1,1,8,32,128]{4,3,2,1,0:T(8,128)(2,1)}, u32[]{:S(2)}) copy-start(bf16[1,1,8,32,128]{4,3,2,1,0:T(8,128)(2,1)} %param.5) | copy-start | bytes 196612
  0.6 24.5 %collective-permute-start.4 = (bf16[1,1,8,32,128]{4,3,2,1,0:T(8,128)(2,1)}, bf16[1,1,8,32,128]{4,3,2,1,0:T(8,128)(2,1)S(1)}, u32[]{:S(2)}, u32[]{:S(2)}) collective-permute-start(bf16[1,1,8,32,128]{4,3,2,1,0:T(8,128)(2,1)} %param.5), channel_id=1, source_target_pairs={{0,6},{2,0},{4,2},{6,4},{1,7},{3,1},{5,3},{7,5},{8,14},{10,8},{12,... | collective-permute-start | bytes 196616 | tf_op jit(solution)/shard_map/ppermute | solution.py:96
  6.6 22.5 %collective-permute-start.5 = (bf16[1,1,8,32,128]{4,3,2,1,0:T(8,128)(2,1)}, bf16[1,1,8,32,128]{4,3,2,1,0:T(8,128)(2,1)S(1)}, u32[]{:S(2)}, u32[]{:S(2)}) collective-permute-start(bf16[1,1,8,32,128]{4,3,2,1,0:T(8,128)(2,1)} %param.5), channel_id=1, source_target_pairs={{0,4},{2,6},{4,0},{6,2},{1,5},{3,7},{5,1},{7,3},{8,12},{10,14},{12... | collective-permute-start | bytes 196616 | tf_op jit(solution)/shard_map/ppermute | solution.py:96
  8.6 25.0 %collective-permute-start.6 = (bf16[1,1,8,32,128]{4,3,2,1,0:T(8,128)(2,1)}, bf16[1,1,8,32,128]{4,3,2,1,0:T(8,128)(2,1)S(1)}, u32[]{:S(2)}, u32[]{:S(2)}) collective-permute-start(bf16[1,1,8,32,128]{4,3,2,1,0:T(8,128)(2,1)} %param.5), channel_id=1, source_target_pairs={{0,2},{2,4},{4,6},{6,0},{1,3},{3,5},{5,7},{7,1},{8,10},{10,12},{12... | collective-permute-start | bytes 196616 | tf_op jit(solution)/shard_map/ppermute | solution.py:96
  11.4 24.9 %collective-permute-start.7 = (bf16[1,1,8,32,128]{4,3,2,1,0:T(8,128)(2,1)}, bf16[1,1,8,32,128]{4,3,2,1,0:T(8,128)(2,1)S(1)}, u32[]{:S(2)}, u32[]{:S(2)}) collective-permute-start(bf16[1,1,8,32,128]{4,3,2,1,0:T(8,128)(2,1)} %param.5), channel_id=1, source_target_pairs={{8,0},{10,2},{12,4},{14,6},{16,8},{18,10},{20,12},{22,14},{24,16},... | collective-permute-start | bytes 196616 | tf_op jit(solution)/shard_map/ppermute | solution.py:107
  18.2 18.0 %collective-permute-start.8 = (bf16[1,1,8,32,128]{4,3,2,1,0:T(8,128)(2,1)}, bf16[1,1,8,32,128]{4,3,2,1,0:T(8,128)(2,1)S(1)}, u32[]{:S(2)}, u32[]{:S(2)}) collective-permute-start(bf16[1,1,8,32,128]{4,3,2,1,0:T(8,128)(2,1)} %param.5), channel_id=1, source_target_pairs={{10,0},{12,2},{14,4},{8,6},{18,8},{20,10},{22,12},{16,14},{26,16},... | collective-permute-start | bytes 196616 | tf_op jit(solution)/shard_map/ppermute | solution.py:107
  25.2 11.1 %collective-permute-start.9 = (bf16[1,1,8,32,128]{4,3,2,1,0:T(8,128)(2,1)S(1)}, bf16[1,1,8,32,128]{4,3,2,1,0:T(8,128)(2,1)S(1)}, u32[]{:S(2)}, u32[]{:S(2)}) collective-permute-start(bf16[1,1,8,32,128]{4,3,2,1,0:T(8,128)(2,1)S(1)} %copy-done), channel_id=1, source_target_pairs={{12,0},{14,2},{8,4},{10,6},{20,8},{22,10},{16,12},{18,14},{28,16},... | collective-permute-start | bytes 196616 | tf_op jit(solution)/shard_map/ppermute | solution.py:107
  29.1 8.9 %collective-permute-start.10 = (bf16[1,1,8,32,128]{4,3,2,1,0:T(8,128)(2,1)S(1)}, bf16[1,1,8,32,128]{4,3,2,1,0:T(8,128)(2,1)S(1)}, u32[]{:S(2)}, u32[]{:S(2)}) collective-permute-start(bf16[1,1,8,32,128]{4,3,2,1,0:T(8,128)(2,1)S(1)} %copy-done), channel_id=1, source_target_pairs={{14,0},{8,2},{10,4},{12,6},{22,8},{16,10},{18,12},{20,14},{30,16},... | collective-permute-start | bytes 196616 | tf_op jit(solution)/shard_map/ppermute | solution.py:107
  33.6 22.9 %collective-permute-start = (bf16[1,1,16,32,256]{4,3,2,1,0:T(8,128)(2,1)S(1)}, bf16[1,1,16,32,256]{4,3,2,1,0:T(8,128)(2,1)S(1)}, u32[]{:S(2)}, u32[]{:S(2)}) collective-permute-start(bf16[1,1,16,32,256]{4,3,2,1,0:T(8,128)(2,1)S(1)} %slice.129), channel_id=1, source_target_pairs={{0,8},{8,16},{16,24},{24,32},{32,40},{40,48},{48,56},{56,64},{64,7... | collective-permute-start | bytes 786440 | tf_op jit(solution)/shard_map/ppermute | solution.py:12
  56.5 0.7 copy-start.1
  61.4 13.1 %collective-permute-start.1 = (f32[1,1,8,32,128]{4,3,2,1,0:T(8,128)S(1)}, f32[1,1,8,32,128]{4,3,2,1,0:T(8,128)S(1)}, u32[]{:S(2)}, u32[]{:S(2)}) collective-permute-start(f32[1,1,8,32,128]{4,3,2,1,0:T(8,128)S(1)} %get-tuple-element.4), channel_id=1, source_target_pairs={{0,2},{2,4},{4,6},{6,0},{1,3},{3,5},{5,7},{7,1},{8,10},{10,12},{12... | collective-permute-start | bytes 393224 | tf_op jit(solution)/shard_map/ppermute | solution.py:96
  63.8 10.9 %collective-permute-start.2 = (f32[1,1,8,32,128]{4,3,2,1,0:T(8,128)S(1)}, f32[1,1,8,32,128]{4,3,2,1,0:T(8,128)S(1)}, u32[]{:S(2)}, u32[]{:S(2)}) collective-permute-start(f32[1,1,8,32,128]{4,3,2,1,0:T(8,128)S(1)} %get-tuple-element.6), channel_id=1, source_target_pairs={{0,4},{2,6},{4,0},{6,2},{1,5},{3,7},{5,1},{7,3},{8,12},{10,14},{12... | collective-permute-start | bytes 393224 | tf_op jit(solution)/shard_map/ppermute | solution.py:96
  66.4 9.0 %collective-permute-start.3 = (f32[1,1,8,32,128]{4,3,2,1,0:T(8,128)S(1)}, f32[1,1,8,32,128]{4,3,2,1,0:T(8,128)S(1)}, u32[]{:S(2)}, u32[]{:S(2)}) collective-permute-start(f32[1,1,8,32,128]{4,3,2,1,0:T(8,128)S(1)} %get-tuple-element.5), channel_id=1, source_target_pairs={{0,6},{2,0},{4,2},{6,4},{1,7},{3,1},{5,3},{7,5},{8,14},{10,8},{12,... | collective-permute-start | bytes 393224 | tf_op jit(solution)/shard_map/ppermute | solution.py:96

commit v3 on v2

--- a/solution.py
+++ b/solution.py
@@ -96,17 +96,6 @@
     return lax.ppermute(block, "chan", [(i, (i + shift) % size) for i in range(size)])
 
 
-def from_next_slab(block, chan_offset):
-    slabs = lax.axis_size("space")
-    size = lax.axis_size("chan")
-    route = [
-        ((s + 1) * size + (c + chan_offset) % size, s * size + c)
-        for s in range(slabs - 1)
-        for c in range(size)
-    ]
-    return lax.ppermute(block, ("space", "chan"), route)
-
-
 def per_device(volume, kernel, cotangent):
     count, planes_in, rows_in, chans_in, cols_in = volume.shape
     planes_out = planes_in // 2
@@ -124,10 +113,11 @@
     for k in range(1, groups):
         total = total + chan_shift(partial_sum[:, :, :, k * share:(k + 1) * share], k)
     response = total.astype(jnp.bfloat16)
-    own = [cotangent] + [chan_shift(cotangent, -k) for k in range(1, groups)]
-    following = [from_next_slab(cotangent, k) for k in range(groups)]
-    full_cot = jnp.concatenate(own, axis=3)
-    next_cot = jnp.concatenate(following, axis=3)
+    pair = jnp.concatenate([cotangent, from_behind(cotangent, "space", -1)], axis=1)
+    pieces = [pair] + [chan_shift(pair, -k) for k in range(1, groups)]
+    both_cot = jnp.concatenate(pieces, axis=3)
+    full_cot = both_cot[:, :1]
+    next_cot = both_cot[:, 1:]
     taps = kernel.reshape(3, 3, 3, chans_in, chans_out)
     even_planes = transposed_phases(full_cot, taps[1])
     odd_planes = transposed_phases(next_cot, taps[0]) + transposed_phases(full_cot, taps[2])

time: 77.5 us -> 71.8 us (0.926)
  the two profiles are of different devices: /device:TPU:512 before, /device:TPU:384 now
where the time goes in v3:
time: 71.8 us; the launch traced here: 71.4 us
  starting transfers between devices  30.9 us (43%)
  waiting for transfers between devices  20.4 us (28%)
  local copies, waits for them, and re-layouts  7.9 us (11%)
  matrix products  4.37 us (6%)
  other arithmetic  3.78 us (5%)
  Pallas kernels  3.09 us (4%)
  between operations  0.98 us (1%)
    ppermute x6, waiting for transfers between devices, chan_shift(): lax.ppermute(block, 'chan', [(i, (i + shift) % size) for i in range(size)])  20.4 us
    ppermute x6, starting transfers between devices, chan_shift(): lax.ppermute(block, 'chan', [(i, (i + shift) % size) for i in range(size)])  20.3 us
    ppermute x2, starting transfers between devices, from_behind(): return lax.ppermute(block, axis, route)  10.6 us
    dot_general x27, matrix products, transposed_phases(): jnp.einsum('bdhew,ce->bdhcw', picked, taps[row_tap, col_tap], preferred_e...  4.37 us
    pallas_call x1, Pallas kernels, forward_partial(): pl.pallas_call(forward_rows, out_shape=jax.ShapeDtypeStruct((rows_out, ch...  3.09 us
    unnamed x4, local copies, waits for them, and re-layouts  3.05 us
    convert_element_type x1, other arithmetic, per_device(): response = total.astype(jnp.bfloat16)  1.57 us
    transpose x1, local copies, waits for them, and re-layouts, per_device(): both = jnp.moveaxis(both, 6, 7)  1.5 us
  transfers between devices with their start and end apart: 8, of which 3 were waited for; matrix products, arithmetic and copies ran while one was open for 18% of the time, Pallas kernels for 0%

profile of v3, /device:TPU:384, one launch (start us, length us, event | category | flops | bytes accessed | tf_op | source)
XLA Modules:
  0.0 71.4 jit_solution(17872340125055140819)
XLA Ops:
  0.6 8.7 %collective-permute-start.4 = (bf16[1,1,8,32,128]{4,3,2,1,0:T(8,128)(2,1)}, bf16[1,1,8,32,128]{4,3,2,1,0:T(8,128)(2,1)S(1)}, u32[]{:S(2)}, u32[]{:S(2)}) collective-permute-start(bf16[1,1,8,32,128]{4,3,2,1,0:T(8,128)(2,1)} %param.5), channel_id=1, source_target_pairs={{8,0},{16,8},{24,16},{32,24},{40,32},{48,40},{56,48},{64,56},{72,6... | collective-permute-start | bytes 196616 | tf_op jit(solution)/shard_map/ppermute | solution.py:12
  9.3 1.0 %slice.139 = bf16[1,1,16,32,256]{4,3,2,1,0:T(8,128)(2,1)S(1)} slice(bf16[1,2,16,32,256]{4,3,2,1,0:T(8,128)(2,1)} %param.3), slice={[0:1], [1:2], [0:16], [0:32], [0:256]} | slice | bytes 524288 | tf_op jit(solution)/shard_map/slice | solution.py:109
  10.3 1.9 %collective-permute-start = (bf16[1,1,16,32,256]{4,3,2,1,0:T(8,128)(2,1)S(1)}, bf16[1,1,16,32,256]{4,3,2,1,0:T(8,128)(2,1)S(1)}, u32[]{:S(2)}, u32[]{:S(2)}) collective-permute-start(bf16[1,1,16,32,256]{4,3,2,1,0:T(8,128)(2,1)S(1)} %slice.139), channel_id=1, source_target_pairs={{0,8},{8,16},{16,24},{24,32},{32,40},{40,48},{48,56},{56,64},{64,7... | collective-permute-start | bytes 786440 | tf_op jit(solution)/shard_map/ppermute | solution.py:12
  12.2 0.8 %constant_dynamic-update-slice_fusion.1 = bf16[1,2,8,32,128]{4,3,2,1,0:T(8,128)(2,1)S(1)} fusion(bf16[1,1,8,32,128]{4,3,2,1,0:T(8,128)(2,1)} %param.5), kind=kLoop, calls=%fused_computation.123 | loop fusion | bytes 131072
  13.1 1.1 %fusion.47 = bf16[27,32,128]{2,1,0:T(8,128)(2,1)S(1)} fusion(s32[]{:T(128)S(6)} %select_n.37, bf16[27,32,128]{2,1,0:T(8,128)(2,1)} %param.4), kind=kLoop, calls=%fused_computation.79 | loop fusion | flops 442368 | bytes 442372 | tf_op jit(solution)/shard_map/jit(_roll_dynamic)/concatenate | solution.py:108
  14.3 0.8 %copy.6.kbig_ref = bf16[128,864]{1,0:T(8,128)(2,1)} copy(bf16[128,864]{0,1:T(8,128)(2,1)S(1)} %bitcast.288) | data formatting | bytes 442368 | tf_op jit(solution)/shard_map/reshape | solution.py:82
  15.1 2.8 %collective-permute-start.7 = (bf16[1,2,8,32,128]{4,3,2,1,0:T(8,128)(2,1)S(1)}, bf16[1,2,8,32,128]{4,3,2,1,0:T(8,128)(2,1)S(1)}, u32[]{:S(2)}, u32[]{:S(2)}) collective-permute-start(bf16[1,2,8,32,128]{4,3,2,1,0:T(8,128)(2,1)S(1)} %constant_dynamic-update-slice_fusion), channel_id=1, source_target_pairs={{0,2},{2,4},{4,6},{6,0},{1,3},{3,5},{5,7},{7,1},{8,10},{10,12},{12... | collective-permute-start | bytes 393224 | tf_op jit(solution)/shard_map/ppermute | solution.py:96
  17.9 2.9 %collective-permute-start.6 = (bf16[1,2,8,32,128]{4,3,2,1,0:T(8,128)(2,1)S(1)}, bf16[1,2,8,32,128]{4,3,2,1,0:T(8,128)(2,1)S(1)}, u32[]{:S(2)}, u32[]{:S(2)}) collective-permute-start(bf16[1,2,8,32,128]{4,3,2,1,0:T(8,128)(2,1)S(1)} %constant_dynamic-update-slice_fusion), channel_id=1, source_target_pairs={{0,4},{2,6},{4,0},{6,2},{1,5},{3,7},{5,1},{7,3},{8,12},{10,14},{12... | collective-permute-start | bytes 393224 | tf_op jit(solution)/shard_map/ppermute | solution.py:96
  20.9 4.0 %collective-permute-start.5 = (bf16[1,2,8,32,128]{4,3,2,1,0:T(8,128)(2,1)S(1)}, bf16[1,2,8,32,128]{4,3,2,1,0:T(8,128)(2,1)S(1)}, u32[]{:S(2)}, u32[]{:S(2)}) collective-permute-start(bf16[1,2,8,32,128]{4,3,2,1,0:T(8,128)(2,1)S(1)} %constant_dynamic-update-slice_fusion), channel_id=1, source_target_pairs={{0,6},{2,0},{4,2},{6,4},{1,7},{3,1},{5,3},{7,5},{8,14},{10,8},{12,... | collective-permute-start | bytes 393224 | tf_op jit(solution)/shard_map/ppermute | solution.py:96
  24.9 0.7 %fusion.14.sel_ref = bf16[256,384]{1,0:T(8,128)(2,1)} fusion(s32[384]{0:T(512)S(1)} %fusion.64), kind=kLoop, calls=%fused_computation.38 | loop fusion | flops 196608 | bytes 198144 | tf_op jit(solution)/shard_map/convert_element_type | solution.py:81
  25.6 10.5 %collective-permute-done.7 = bf16[1,2,8,32,128]{4,3,2,1,0:T(8,128)(2,1)S(1)} collective-permute-done((bf16[1,2,8,32,128]{4,3,2,1,0:T(8,128)(2,1)S(1)}, bf16[1,2,8,32,128]{4,3,2,1,0:T(8,128)(2,1)S(1)}, u32[]{:S(2)}, u32[]{:S(2)}) %collective-permute-start.7) | collective-permute-done | bytes 131104 | tf_op jit(solution)/shard_map/ppermute | solution.py:96
  36.1 5.5 %collective-permute-done.6 = bf16[1,2,8,32,128]{4,3,2,1,0:T(8,128)(2,1)S(1)} collective-permute-done((bf16[1,2,8,32,128]{4,3,2,1,0:T(8,128)(2,1)S(1)}, bf16[1,2,8,32,128]{4,3,2,1,0:T(8,128)(2,1)S(1)}, u32[]{:S(2)}, u32[]{:S(2)}) %collective-permute-start.6) | collective-permute-done | bytes 131104 | tf_op jit(solution)/shard_map/ppermute | solution.py:96
  41.7 0.2 fusion.9
  41.8 0.2 convolution_bitcast_fusion
  42.0 0.2 fusion.29
  42.2 0.2 fusion.32
  42.3 0.2 convolution_bitcast_fusion.1
  42.5 0.2 fusion.19
  42.7 0.2 pad_slice_fusion
  43.0 0.2 fusion.26
  43.2 0.2 fusion.84
  43.6 0.2 fusion.38
  43.8 0.2 fusion.4
  43.9 0.2 fusion.1
  44.1 0.2 fusion.11
  44.4 0.2 convolution_add_fusion.7
  44.6 0.2 convolution_add_fusion.12
  44.8 0.2 convolution_add_fusion.2
  45.0 0.2 fusion.22
  45.1 0.2 convolution_add_fusion.6
  45.3 0.2 fusion.5
  45.5 0.2 fusion.3
  45.6 0.2 convolution_add_fusion.1
  45.8 0.2 fusion
  46.0 0.2 convolution_add_fusion.11
  46.1 0.2 fusion.10
  46.3 0.2 fusion.12
  46.6 0.2 fusion.2
  46.9 0.7 copy-done
  47.6 3.1 %shard_map.50 = f32[8,128,128]{2,1,0:T(8,128)} custom-call(bf16[16,32,256]{2,1,0:T(8,128)(2,1)} %bitcast.319, bf16[2,16,32,256]{3,2,1,0:T(8,128)(2,1)} %bitcast.318, bf16[256,384]{1,0:T(8,128)(2,1)} %fusion.14.sel_ref, bf16[128,864]{1,0:T(8,128)(2,1)} %copy.6.kbig_ref), custom_call_target="tpu_custom_call" | custom-call | flops 528482304 | bytes 2097152 | tf_op jit(solution)/shard_map/pallas_call | solution.py:84
  50.6 1.1 %fusion.86 = (f32[1,1,8,32,128]{4,3,2,1,0:T(8,128)S(1)}, f32[1,1,8,32,128]{4,3,2,1,0:T(8,128)S(1)}, f32[1,1,8,32,128]{4,3,2,1,0:T(8,128)S(1)}) fusion(f32[1,1,8,128,128]{4,3,2,1,0:T(8,128)} %bitcast.289), kind=kLoop, calls=%fused_computation.155 | loop fusion | bytes 786432 | tf_op jit(solution)/shard_map/slice | solution.py:114
  51.7 5.2 %collective-permute-start.1 = (f32[1,1,8,32,128]{4,3,2,1,0:T(8,128)S(1)}, f32[1,1,8,32,128]{4,3,2,1,0:T(8,128)S(1)}, u32[]{:S(2)}, u32[]{:S(2)}) collective-permute-start(f32[1,1,8,32,128]{4,3,2,1,0:T(8,128)S(1)} %get-tuple-element.8), channel_id=1, source_target_pairs={{0,2},{2,4},{4,6},{6,0},{1,3},{3,5},{5,7},{7,1},{8,10},{10,12},{12... | collective-permute-start | bytes 393224 | tf_op jit(solution)/shard_map/ppermute | solution.py:96
  56.9 2.4 %collective-permute-start.3 = (f32[1,1,8,32,128]{4,3,2,1,0:T(8,128)S(1)}, f32[1,1,8,32,128]{4,3,2,1,0:T(8,128)S(1)}, u32[]{:S(2)}, u32[]{:S(2)}) collective-permute-start(f32[1,1,8,32,128]{4,3,2,1,0:T(8,128)S(1)} %get-tuple-element.9), channel_id=1, source_target_pairs={{0,6},{2,0},{4,2},{6,4},{1,7},{3,1},{5,3},{7,5},{8,14},{10,8},{12,... | collective-permute-start | bytes 393224 | tf_op jit(solution)/shard_map/ppermute | solution.py:96
  59.4 2.9 %collective-permute-start.2 = (f32[1,1,8,32,128]{4,3,2,1,0:T(8,128)S(1)}, f32[1,1,8,32,128]{4,3,2,1,0:T(8,128)S(1)}, u32[]{:S(2)}, u32[]{:S(2)}) collective-permute-start(f32[1,1,8,32,128]{4,3,2,1,0:T(8,128)S(1)} %get-tuple-element.10), channel_id=1, source_target_pairs={{0,4},{2,6},{4,0},{6,2},{1,5},{3,7},{5,1},{7,3},{8,12},{10,14},{12... | collective-permute-start | bytes 393224 | tf_op jit(solution)/shard_map/ppermute | solution.py:96
  62.4 1.5 %copy.7 = bf16[1,1,2,8,2,32,128,2]{5,7,6,4,3,2,1,0:T(2,128)(2,1)S(1)} copy(bf16[1,1,2,8,2,32,128,2]{6,5,3,7,4,2,1,0:T(8,128)(2,1)S(1)} %maximum_bitcast_fusion) | data formatting | bytes 1048576 | tf_op jit(solution)/shard_map/transpose | solution.py:125
  63.9 1.5 %copy.8 = bf16[1,2,16,32,256]{4,3,2,1,0:T(8,128)(2,1)} copy(bf16[1,2,16,32,256]{3,4,2,1,0:T(8,128)(2,1)S(1)} %bitcast.287) | data formatting | bytes 1048576
  65.4 4.4 %collective-permute-done.2 = f32[1,1,8,32,128]{4,3,2,1,0:T(8,128)S(1)} collective-permute-done((f32[1,1,8,32,128]{4,3,2,1,0:T(8,128)S(1)}, f32[1,1,8,32,128]{4,3,2,1,0:T(8,128)S(1)}, u32[]{:S(2)}, u32[]{:S(2)}) %collective-permute-start.2) | collective-permute-done | bytes 131104 | tf_op jit(solution)/shard_map/ppermute | solution.py:96
  69.8 1.6 %fusion.58 = bf16[1,1,8,32,128]{4,3,2,1,0:T(8,128)(2,1)} fusion(f32[1,1,8,32,128]{4,3,2,1,0:T(8,128)S(1)} %collective-permute-done.3, f32[1,1,8,32,128]{4,3,2,1,0:T(8,128)S(1)} %collective-permute-done.2, f32[1,1,8,32,128]{4,3,2,1,0:T(8,128)S(1)} %collective-permute-done.1, f32[1,1,8,128,128]{4,3,2,1,0:T(8,128)} %bitcast.290), kind=kLoop, calls=%fused_computation.92 | loop fusion | flops 131072 | bytes 589824 | tf_op jit(solution)/shard_map/convert_element_type | solution.py:115
  (22 shorter events, 0.9 us)
Async XLA Ops:
  0.6 14.5 %collective-permute-start.4 = (bf16[1,1,8,32,128]{4,3,2,1,0:T(8,128)(2,1)}, bf16[1,1,8,32,128]{4,3,2,1,0:T(8,128)(2,1)S(1)}, u32[]{:S(2)}, u32[]{:S(2)}) collective-permute-start(bf16[1,1,8,32,128]{4,3,2,1,0:T(8,128)(2,1)} %param.5), channel_id=1, source_target_pairs={{8,0},{16,8},{24,16},{32,24},{40,32},{48,40},{56,48},{64,56},{72,6... | collective-permute-start | bytes 196616 | tf_op jit(solution)/shard_map/ppermute | solution.py:12
  10.3 36.5 %collective-permute-start = (bf16[1,1,16,32,256]{4,3,2,1,0:T(8,128)(2,1)S(1)}, bf16[1,1,16,32,256]{4,3,2,1,0:T(8,128)(2,1)S(1)}, u32[]{:S(2)}, u32[]{:S(2)}) collective-permute-start(bf16[1,1,16,32,256]{4,3,2,1,0:T(8,128)(2,1)S(1)} %slice.139), channel_id=1, source_target_pairs={{0,8},{8,16},{16,24},{24,32},{32,40},{40,48},{48,56},{56,64},{64,7... | collective-permute-start | bytes 786440 | tf_op jit(solution)/shard_map/ppermute | solution.py:12
  15.1 21.0 %collective-permute-start.7 = (bf16[1,2,8,32,128]{4,3,2,1,0:T(8,128)(2,1)S(1)}, bf16[1,2,8,32,128]{4,3,2,1,0:T(8,128)(2,1)S(1)}, u32[]{:S(2)}, u32[]{:S(2)}) collective-permute-start(bf16[1,2,8,32,128]{4,3,2,1,0:T(8,128)(2,1)S(1)} %constant_dynamic-update-slice_fusion), channel_id=1, source_target_pairs={{0,2},{2,4},{4,6},{6,0},{1,3},{3,5},{5,7},{7,1},{8,10},{10,12},{12... | collective-permute-start | bytes 393224 | tf_op jit(solution)/shard_map/ppermute | solution.py:96
  17.9 23.7 %collective-permute-start.6 = (bf16[1,2,8,32,128]{4,3,2,1,0:T(8,128)(2,1)S(1)}, bf16[1,2,8,32,128]{4,3,2,1,0:T(8,128)(2,1)S(1)}, u32[]{:S(2)}, u32[]{:S(2)}) collective-permute-start(bf16[1,2,8,32,128]{4,3,2,1,0:T(8,128)(2,1)S(1)} %constant_dynamic-update-slice_fusion), channel_id=1, source_target_pairs={{0,4},{2,6},{4,0},{6,2},{1,5},{3,7},{5,1},{7,3},{8,12},{10,14},{12... | collective-permute-start | bytes 393224 | tf_op jit(solution)/shard_map/ppermute | solution.py:96
  20.9 20.7 %collective-permute-start.5 = (bf16[1,2,8,32,128]{4,3,2,1,0:T(8,128)(2,1)S(1)}, bf16[1,2,8,32,128]{4,3,2,1,0:T(8,128)(2,1)S(1)}, u32[]{:S(2)}, u32[]{:S(2)}) collective-permute-start(bf16[1,2,8,32,128]{4,3,2,1,0:T(8,128)(2,1)S(1)} %constant_dynamic-update-slice_fusion), channel_id=1, source_target_pairs={{0,6},{2,0},{4,2},{6,4},{1,7},{3,1},{5,3},{7,5},{8,14},{10,8},{12,... | collective-permute-start | bytes 393224 | tf_op jit(solution)/shard_map/ppermute | solution.py:96
  46.8 0.7 copy-start
  51.7 13.7 %collective-permute-start.1 = (f32[1,1,8,32,128]{4,3,2,1,0:T(8,128)S(1)}, f32[1,1,8,32,128]{4,3,2,1,0:T(8,128)S(1)}, u32[]{:S(2)}, u32[]{:S(2)}) collective-permute-start(f32[1,1,8,32,128]{4,3,2,1,0:T(8,128)S(1)} %get-tuple-element.8), channel_id=1, source_target_pairs={{0,2},{2,4},{4,6},{6,0},{1,3},{3,5},{5,7},{7,1},{8,10},{10,12},{12... | collective-permute-start | bytes 393224 | tf_op jit(solution)/shard_map/ppermute | solution.py:96
  56.9 8.5 %collective-permute-start.3 = (f32[1,1,8,32,128]{4,3,2,1,0:T(8,128)S(1)}, f32[1,1,8,32,128]{4,3,2,1,0:T(8,128)S(1)}, u32[]{:S(2)}, u32[]{:S(2)}) collective-permute-start(f32[1,1,8,32,128]{4,3,2,1,0:T(8,128)S(1)} %get-tuple-element.9), channel_id=1, source_target_pairs={{0,6},{2,0},{4,2},{6,4},{1,7},{3,1},{5,3},{7,5},{8,14},{10,8},{12,... | collective-permute-start | bytes 393224 | tf_op jit(solution)/shard_map/ppermute | solution.py:96
  59.4 10.4 %collective-permute-start.2 = (f32[1,1,8,32,128]{4,3,2,1,0:T(8,128)S(1)}, f32[1,1,8,32,128]{4,3,2,1,0:T(8,128)S(1)}, u32[]{:S(2)}, u32[]{:S(2)}) collective-permute-start(f32[1,1,8,32,128]{4,3,2,1,0:T(8,128)S(1)} %get-tuple-element.10), channel_id=1, source_target_pairs={{0,4},{2,6},{4,0},{6,2},{1,5},{3,7},{5,1},{7,3},{8,12},{10,14},{12... | collective-permute-start | bytes 393224 | tf_op jit(solution)/shard_map/ppermute | solution.py:96

commit v4 on v3

--- a/solution.py
+++ b/solution.py
@@ -109,11 +109,12 @@
     below = from_behind(volume[:, -1:], "space", 1)
     partial_sum = forward_partial(below[0, 0], volume[0], kernel)
     partial_sum = partial_sum.reshape(count, planes_out, rows_out, chans_out, cols_out)
+    pair = jnp.concatenate([cotangent, from_behind(cotangent, "space", -1)], axis=1)
+    partial_sum, pair = lax.optimization_barrier((partial_sum, pair))
     total = partial_sum[:, :, :, :share]
     for k in range(1, groups):
         total = total + chan_shift(partial_sum[:, :, :, k * share:(k + 1) * share], k)
     response = total.astype(jnp.bfloat16)
-    pair = jnp.concatenate([cotangent, from_behind(cotangent, "space", -1)], axis=1)
     pieces = [pair] + [chan_shift(pair, -k) for k in range(1, groups)]
     both_cot = jnp.concatenate(pieces, axis=3)
     full_cot = both_cot[:, :1]

time: 71.8 us -> 69.5 us (0.968)
  the two profiles are of different devices: /device:TPU:384 before, /device:TPU:768 now
where the time goes in v4:
time: 69.5 us; the launch traced here: 69.1 us
  starting transfers between devices  30.9 us (44%)
  waiting for transfers between devices  18.7 us (27%)
  local copies, waits for them, and re-layouts  7.14 us (10%)
  matrix products  4.4 us (6%)
  other arithmetic  3.76 us (5%)
  Pallas kernels  3.09 us (4%)
  between operations  1.03 us (1%)
    ppermute x6, starting transfers between devices, chan_shift(): lax.ppermute(block, 'chan', [(i, (i + shift) % size) for i in range(size)])  19.3 us
    ppermute x2, waiting for transfers between devices, from_behind(): return lax.ppermute(block, axis, route)  18.7 us
    ppermute x2, starting transfers between devices, from_behind(): return lax.ppermute(block, axis, route)  11.6 us
    dot_general x27, matrix products, transposed_phases(): jnp.einsum('bdhew,ce->bdhcw', picked, taps[row_tap, col_tap], preferred_e...  4.4 us
    pallas_call x1, Pallas kernels, forward_partial(): pl.pallas_call(forward_rows, out_shape=jax.ShapeDtypeStruct((rows_out, ch...  3.09 us
    unnamed x8, local copies, waits for them, and re-layouts  2.26 us
    convert_element_type x1, other arithmetic, per_device(): response = total.astype(jnp.bfloat16)  1.58 us
    transpose x1, local copies, waits for them, and re-layouts, per_device(): both = jnp.moveaxis(both, 6, 7)  1.5 us
  transfers between devices with their start and end apart: 8, of which 1 were waited for; matrix products, arithmetic and copies ran while one was open for 19% of the time, Pallas kernels for 0%

profile of v4, /device:TPU:768, one launch (start us, length us, event | category | flops | bytes accessed | tf_op | source)
XLA Modules:
  0.0 69.1 jit_solution(4128768474189053606)
XLA Ops:
  0.6 9.7 %collective-permute-start.1 = (bf16[1,1,8,32,128]{4,3,2,1,0:T(8,128)(2,1)}, bf16[1,1,8,32,128]{4,3,2,1,0:T(8,128)(2,1)S(1)}, u32[]{:S(2)}, u32[]{:S(2)}) collective-permute-start(bf16[1,1,8,32,128]{4,3,2,1,0:T(8,128)(2,1)} %param.5), channel_id=1, source_target_pairs={{8,0},{16,8},{24,16},{32,24},{40,32},{48,40},{56,48},{64,56},{72,6... | collective-permute-start | bytes 196616 | tf_op jit(solution)/shard_map/ppermute | solution.py:12
  10.4 1.0 %slice.139 = bf16[1,1,16,32,256]{4,3,2,1,0:T(8,128)(2,1)S(1)} slice(bf16[1,2,16,32,256]{4,3,2,1,0:T(8,128)(2,1)} %param.3), slice={[0:1], [1:2], [0:16], [0:32], [0:256]} | slice | bytes 524288 | tf_op jit(solution)/shard_map/slice | solution.py:109
  11.3 1.9 %collective-permute-start = (bf16[1,1,16,32,256]{4,3,2,1,0:T(8,128)(2,1)S(1)}, bf16[1,1,16,32,256]{4,3,2,1,0:T(8,128)(2,1)S(1)}, u32[]{:S(2)}, u32[]{:S(2)}) collective-permute-start(bf16[1,1,16,32,256]{4,3,2,1,0:T(8,128)(2,1)S(1)} %slice.139), channel_id=1, source_target_pairs={{0,8},{8,16},{16,24},{24,32},{32,40},{40,48},{48,56},{56,64},{64,7... | collective-permute-start | bytes 786440 | tf_op jit(solution)/shard_map/ppermute | solution.py:12
  13.3 1.2 %fusion.41 = bf16[27,32,128]{2,1,0:T(8,128)(2,1)S(1)} fusion(s32[]{:T(128)S(6)} %select_n.37, bf16[27,32,128]{2,1,0:T(8,128)(2,1)} %param.4), kind=kLoop, calls=%fused_computation.72 | loop fusion | flops 442368 | bytes 442372 | tf_op jit(solution)/shard_map/jit(_roll_dynamic)/concatenate | solution.py:108
  14.5 0.7 %fusion.14.sel_ref = bf16[256,384]{1,0:T(8,128)(2,1)} fusion(s32[384]{0:T(512)S(1)} %fusion.61), kind=kLoop, calls=%fused_computation.37 | loop fusion | flops 196608 | bytes 198144 | tf_op jit(solution)/shard_map/convert_element_type | solution.py:81
  15.2 0.8 %copy.6.kbig_ref = bf16[128,864]{1,0:T(8,128)(2,1)} copy(bf16[128,864]{0,1:T(8,128)(2,1)S(1)} %bitcast.288) | data formatting | bytes 442368 | tf_op jit(solution)/shard_map/reshape | solution.py:82
  16.1 18.7 %collective-permute-done = bf16[1,1,16,32,256]{4,3,2,1,0:T(8,128)(2,1)S(1)} collective-permute-done((bf16[1,1,16,32,256]{4,3,2,1,0:T(8,128)(2,1)S(1)}, bf16[1,1,16,32,256]{4,3,2,1,0:T(8,128)(2,1)S(1)}, u32[]{:S(2)}, u32[]{:S(2)}) %collective-permute-start) | collective-permute-done | bytes 262176 | tf_op jit(solution)/shard_map/ppermute | solution.py:12
  34.8 0.7 %copy-done.1 = bf16[1,1,16,32,256]{4,3,2,1,0:T(8,128)(2,1)} copy-done((bf16[1,1,16,32,256]{4,3,2,1,0:T(8,128)(2,1)}, bf16[1,1,16,32,256]{4,3,2,1,0:T(8,128)(2,1)S(1)}, u32[]{:S(2)}) %copy-start.1) | copy-done | bytes 262168
  35.5 3.1 %shard_map.50 = f32[8,128,128]{2,1,0:T(8,128)} custom-call(bf16[16,32,256]{2,1,0:T(8,128)(2,1)} %bitcast.319, bf16[2,16,32,256]{3,2,1,0:T(8,128)(2,1)} %bitcast.318, bf16[256,384]{1,0:T(8,128)(2,1)} %fusion.14.sel_ref, bf16[128,864]{1,0:T(8,128)(2,1)} %copy.6.kbig_ref), custom_call_target="tpu_custom_call" | custom-call | flops 528482304 | bytes 2097152 | tf_op jit(solution)/shard_map/pallas_call | solution.py:84
  38.5 1.9 %collective-permute-start.7 = (bf16[1,2,8,32,128]{4,3,2,1,0:T(8,128)(2,1)S(1)}, bf16[1,2,8,32,128]{4,3,2,1,0:T(8,128)(2,1)S(1)}, u32[]{:S(2)}, u32[]{:S(2)}) collective-permute-start(bf16[1,2,8,32,128]{4,3,2,1,0:T(8,128)(2,1)S(1)} %pad_maximum_fusion), channel_id=1, source_target_pairs={{0,2},{2,4},{4,6},{6,0},{1,3},{3,5},{5,7},{7,1},{8,10},{10,12},{12... | collective-permute-start | bytes 393224 | tf_op jit(solution)/shard_map/ppermute | solution.py:96
  40.5 2.9 %collective-permute-start.6 = (bf16[1,2,8,32,128]{4,3,2,1,0:T(8,128)(2,1)S(1)}, bf16[1,2,8,32,128]{4,3,2,1,0:T(8,128)(2,1)S(1)}, u32[]{:S(2)}, u32[]{:S(2)}) collective-permute-start(bf16[1,2,8,32,128]{4,3,2,1,0:T(8,128)(2,1)S(1)} %pad_maximum_fusion), channel_id=1, source_target_pairs={{0,4},{2,6},{4,0},{6,2},{1,5},{3,7},{5,1},{7,3},{8,12},{10,14},{12... | collective-permute-start | bytes 393224 | tf_op jit(solution)/shard_map/ppermute | solution.py:96
  43.4 4.8 %collective-permute-start.5 = (bf16[1,2,8,32,128]{4,3,2,1,0:T(8,128)(2,1)S(1)}, bf16[1,2,8,32,128]{4,3,2,1,0:T(8,128)(2,1)S(1)}, u32[]{:S(2)}, u32[]{:S(2)}) collective-permute-start(bf16[1,2,8,32,128]{4,3,2,1,0:T(8,128)(2,1)S(1)} %pad_maximum_fusion), channel_id=1, source_target_pairs={{0,6},{2,0},{4,2},{6,4},{1,7},{3,1},{5,3},{7,5},{8,14},{10,8},{12,... | collective-permute-start | bytes 393224 | tf_op jit(solution)/shard_map/ppermute | solution.py:96
  48.2 1.1 %fusion.83 = (f32[1,1,8,32,128]{4,3,2,1,0:T(8,128)S(1)}, f32[1,1,8,32,128]{4,3,2,1,0:T(8,128)S(1)}, f32[1,1,8,32,128]{4,3,2,1,0:T(8,128)S(1)}) fusion(f32[1,1,8,128,128]{4,3,2,1,0:T(8,128)} %bitcast.289), kind=kLoop, calls=%fused_computation.154 | loop fusion | bytes 786432 | tf_op jit(solution)/shard_map/slice | solution.py:116
  49.3 2.4 %collective-permute-start.2 = (f32[1,1,8,32,128]{4,3,2,1,0:T(8,128)S(1)}, f32[1,1,8,32,128]{4,3,2,1,0:T(8,128)S(1)}, u32[]{:S(2)}, u32[]{:S(2)}) collective-permute-start(f32[1,1,8,32,128]{4,3,2,1,0:T(8,128)S(1)} %get-tuple-element.12), channel_id=1, source_target_pairs={{0,2},{2,4},{4,6},{6,0},{1,3},{3,5},{5,7},{7,1},{8,10},{10,12},{12... | collective-permute-start | bytes 393224 | tf_op jit(solution)/shard_map/ppermute | solution.py:96
  51.7 5.3 %collective-permute-start.4 = (f32[1,1,8,32,128]{4,3,2,1,0:T(8,128)S(1)}, f32[1,1,8,32,128]{4,3,2,1,0:T(8,128)S(1)}, u32[]{:S(2)}, u32[]{:S(2)}) collective-permute-start(f32[1,1,8,32,128]{4,3,2,1,0:T(8,128)S(1)} %get-tuple-element.13), channel_id=1, source_target_pairs={{0,6},{2,0},{4,2},{6,4},{1,7},{3,1},{5,3},{7,5},{8,14},{10,8},{12,... | collective-permute-start | bytes 393224 | tf_op jit(solution)/shard_map/ppermute | solution.py:96
  57.0 2.0 %collective-permute-start.3 = (f32[1,1,8,32,128]{4,3,2,1,0:T(8,128)S(1)}, f32[1,1,8,32,128]{4,3,2,1,0:T(8,128)S(1)}, u32[]{:S(2)}, u32[]{:S(2)}) collective-permute-start(f32[1,1,8,32,128]{4,3,2,1,0:T(8,128)S(1)} %get-tuple-element.14), channel_id=1, source_target_pairs={{0,4},{2,6},{4,0},{6,2},{1,5},{3,7},{5,1},{7,3},{8,12},{10,14},{12... | collective-permute-start | bytes 393224 | tf_op jit(solution)/shard_map/ppermute | solution.py:96
  59.1 0.2 convolution_bitcast_fusion
  59.3 0.2 fusion.53
  59.4 0.2 fusion.52
  59.6 0.2 fusion.47
  59.8 0.2 fusion.46
  59.9 0.2 convolution_bitcast_fusion.1
  60.1 0.2 fusion.9
  60.3 0.2 fusion.55
  60.4 0.2 fusion.54
  60.7 0.2 pad_slice_fusion
  60.9 0.1 fusion.22
  61.0 0.2 fusion.24
  61.2 0.2 fusion.81
  61.4 0.2 fusion.11
  61.6 0.2 fusion.4
  61.7 0.2 fusion.1
  61.9 0.2 fusion.16
  62.1 0.2 convolution_add_fusion.7
  62.2 0.2 convolution_add_fusion.12
  62.4 0.2 convolution_add_fusion.2
  62.6 0.2 convolution_add_fusion.6
  62.8 0.2 fusion.5
  62.9 0.2 fusion.3
  63.1 0.2 fusion.12
  63.3 0.2 convolution_add_fusion.1
  63.4 0.2 fusion
  63.6 0.2 fusion.2
  63.8 0.2 convolution_add_fusion.11
  63.9 0.2 fusion.10
  64.5 1.5 %copy.7 = bf16[1,1,2,8,2,32,128,2]{5,7,6,4,3,2,1,0:T(2,128)(2,1)S(1)} copy(bf16[1,1,2,8,2,32,128,2]{6,5,3,7,4,2,1,0:T(8,128)(2,1)S(1)} %maximum_bitcast_fusion) | data formatting | bytes 1048576 | tf_op jit(solution)/shard_map/transpose | solution.py:126
  66.0 1.5 %copy.8 = bf16[1,2,16,32,256]{4,3,2,1,0:T(8,128)(2,1)} copy(bf16[1,2,16,32,256]{3,4,2,1,0:T(8,128)(2,1)S(1)} %bitcast.287) | data formatting | bytes 1048576
  67.5 1.6 %add_convert_fusion = bf16[1,1,8,32,128]{4,3,2,1,0:T(8,128)(2,1)} fusion(f32[1,1,8,32,128]{4,3,2,1,0:T(8,128)S(1)} %collective-permute-done.4, f32[1,1,8,32,128]{4,3,2,1,0:T(8,128)S(1)} %collective-permute-done.3, f32[1,1,8,32,128]{4,3,2,1,0:T(8,128)S(1)} %collective-permute-done.2, f32[1,1,8,128,128]{4,3,2,1,0:T(8,128)} %bitcast.290), kind=kLoop, calls=%fused_computation.87 | loop fusion | flops 131072 | bytes 589824 | tf_op jit(solution)/shard_map/convert_element_type | solution.py:117
  (26 shorter events, 0.5 us)
Async XLA Ops:
  0.6 15.4 %copy-start = (bf16[1,1,8,32,128]{4,3,2,1,0:T(8,128)(2,1)S(1)}, bf16[1,1,8,32,128]{4,3,2,1,0:T(8,128)(2,1)}, u32[]{:S(2)}) copy-start(bf16[1,1,8,32,128]{4,3,2,1,0:T(8,128)(2,1)} %param.5) | copy-start | bytes 196612
  0.6 15.4 %collective-permute-start.1 = (bf16[1,1,8,32,128]{4,3,2,1,0:T(8,128)(2,1)}, bf16[1,1,8,32,128]{4,3,2,1,0:T(8,128)(2,1)S(1)}, u32[]{:S(2)}, u32[]{:S(2)}) collective-permute-start(bf16[1,1,8,32,128]{4,3,2,1,0:T(8,128)(2,1)} %param.5), channel_id=1, source_target_pairs={{8,0},{16,8},{24,16},{32,24},{40,32},{48,40},{56,48},{64,56},{72,6... | collective-permute-start | bytes 196616 | tf_op jit(solution)/shard_map/ppermute | solution.py:12
  11.3 23.4 %collective-permute-start = (bf16[1,1,16,32,256]{4,3,2,1,0:T(8,128)(2,1)S(1)}, bf16[1,1,16,32,256]{4,3,2,1,0:T(8,128)(2,1)S(1)}, u32[]{:S(2)}, u32[]{:S(2)}) collective-permute-start(bf16[1,1,16,32,256]{4,3,2,1,0:T(8,128)(2,1)S(1)} %slice.139), channel_id=1, source_target_pairs={{0,8},{8,16},{16,24},{24,32},{32,40},{40,48},{48,56},{56,64},{64,7... | collective-permute-start | bytes 786440 | tf_op jit(solution)/shard_map/ppermute | solution.py:12
  34.8 0.7 %copy-start.1 = (bf16[1,1,16,32,256]{4,3,2,1,0:T(8,128)(2,1)}, bf16[1,1,16,32,256]{4,3,2,1,0:T(8,128)(2,1)S(1)}, u32[]{:S(2)}) copy-start(bf16[1,1,16,32,256]{4,3,2,1,0:T(8,128)(2,1)S(1)} %collective-permute-done) | copy-start | bytes 786436
  38.5 20.5 %collective-permute-start.7 = (bf16[1,2,8,32,128]{4,3,2,1,0:T(8,128)(2,1)S(1)}, bf16[1,2,8,32,128]{4,3,2,1,0:T(8,128)(2,1)S(1)}, u32[]{:S(2)}, u32[]{:S(2)}) collective-permute-start(bf16[1,2,8,32,128]{4,3,2,1,0:T(8,128)(2,1)S(1)} %pad_maximum_fusion), channel_id=1, source_target_pairs={{0,2},{2,4},{4,6},{6,0},{1,3},{3,5},{5,7},{7,1},{8,10},{10,12},{12... | collective-permute-start | bytes 393224 | tf_op jit(solution)/shard_map/ppermute | solution.py:96
  40.5 18.6 %collective-permute-start.6 = (bf16[1,2,8,32,128]{4,3,2,1,0:T(8,128)(2,1)S(1)}, bf16[1,2,8,32,128]{4,3,2,1,0:T(8,128)(2,1)S(1)}, u32[]{:S(2)}, u32[]{:S(2)}) collective-permute-start(bf16[1,2,8,32,128]{4,3,2,1,0:T(8,128)(2,1)S(1)} %pad_maximum_fusion), channel_id=1, source_target_pairs={{0,4},{2,6},{4,0},{6,2},{1,5},{3,7},{5,1},{7,3},{8,12},{10,14},{12... | collective-permute-start | bytes 393224 | tf_op jit(solution)/shard_map/ppermute | solution.py:96
  43.4 13.6 %collective-permute-start.5 = (bf16[1,2,8,32,128]{4,3,2,1,0:T(8,128)(2,1)S(1)}, bf16[1,2,8,32,128]{4,3,2,1,0:T(8,128)(2,1)S(1)}, u32[]{:S(2)}, u32[]{:S(2)}) collective-permute-start(bf16[1,2,8,32,128]{4,3,2,1,0:T(8,128)(2,1)S(1)} %pad_maximum_fusion), channel_id=1, source_target_pairs={{0,6},{2,0},{4,2},{6,4},{1,7},{3,1},{5,3},{7,5},{8,14},{10,8},{12,... | collective-permute-start | bytes 393224 | tf_op jit(solution)/shard_map/ppermute | solution.py:96
  49.3 18.2 %collective-permute-start.2 = (f32[1,1,8,32,128]{4,3,2,1,0:T(8,128)S(1)}, f32[1,1,8,32,128]{4,3,2,1,0:T(8,128)S(1)}, u32[]{:S(2)}, u32[]{:S(2)}) collective-permute-start(f32[1,1,8,32,128]{4,3,2,1,0:T(8,128)S(1)} %get-tuple-element.12), channel_id=1, source_target_pairs={{0,2},{2,4},{4,6},{6,0},{1,3},{3,5},{5,7},{7,1},{8,10},{10,12},{12... | collective-permute-start | bytes 393224 | tf_op jit(solution)/shard_map/ppermute | solution.py:96
  51.7 15.8 %collective-permute-start.4 = (f32[1,1,8,32,128]{4,3,2,1,0:T(8,128)S(1)}, f32[1,1,8,32,128]{4,3,2,1,0:T(8,128)S(1)}, u32[]{:S(2)}, u32[]{:S(2)}) collective-permute-start(f32[1,1,8,32,128]{4,3,2,1,0:T(8,128)S(1)} %get-tuple-element.13), channel_id=1, source_target_pairs={{0,6},{2,0},{4,2},{6,4},{1,7},{3,1},{5,3},{7,5},{8,14},{10,8},{12,... | collective-permute-start | bytes 393224 | tf_op jit(solution)/shard_map/ppermute | solution.py:96
  57.0 10.5 %collective-permute-start.3 = (f32[1,1,8,32,128]{4,3,2,1,0:T(8,128)S(1)}, f32[1,1,8,32,128]{4,3,2,1,0:T(8,128)S(1)}, u32[]{:S(2)}, u32[]{:S(2)}) collective-permute-start(f32[1,1,8,32,128]{4,3,2,1,0:T(8,128)S(1)} %get-tuple-element.14), channel_id=1, source_target_pairs={{0,4},{2,6},{4,0},{6,2},{1,5},{3,7},{5,1},{7,3},{8,12},{10,14},{12... | collective-permute-start | bytes 393224 | tf_op jit(solution)/shard_map/ppermute | solution.py:96

commit v5 on v4

--- a/solution.py
+++ b/solution.py
@@ -91,6 +91,52 @@
     )(halo, vol, sel, kbig)
 
 
+def backward_rows(cot_ref, k_ref, tsel_ref, out_ref, up_ref):
+    planes, rows_out, chans_out, cols_out = cot_ref.shape
+    rows = out_ref.shape[1]
+    cols = out_ref.shape[3]
+    tsel = tsel_ref[...]
+    for plane in range(planes):
+        flat = cot_ref[plane].reshape(rows_out * chans_out, cols_out)
+        spread = jnp.dot(flat, tsel, preferred_element_type=jnp.float32)
+        up_ref[plane] = spread.astype(up_ref.dtype).reshape(rows_out, chans_out, 3 * cols)
+    for depth in range(2):
+        sources = [(1, 0)] if depth == 0 else [(2, 0), (0, 1)]
+        for row in range(rows):
+            weights, values = [], []
+            for depth_tap, plane in sources:
+                for row_tap in range(3):
+                    if (row + 1 - row_tap) % 2:
+                        continue
+                    i = (row + 1 - row_tap) // 2
+                    if not 0 <= i < rows_out:
+                        continue
+                    for col_tap in range(3):
+                        weights.append(k_ref[9 * depth_tap + 3 * row_tap + col_tap])
+                        values.append(up_ref[plane, i, :, col_tap * cols:(col_tap + 1) * cols])
+            lhs = jnp.concatenate(weights, axis=1)
+            rhs = jnp.concatenate(values, axis=0)
+            out_ref[depth, row] = jnp.dot(lhs, rhs, preferred_element_type=jnp.float32).astype(out_ref.dtype)
+
+
+def backward_grad(cot, kernel):
+    planes, rows_out, chans_out, cols_out = cot.shape
+    taps, chans, _ = kernel.shape
+    rows, cols = 2 * rows_out, 2 * cols_out
+    j = jnp.arange(cols_out)[:, None]
+    k = jnp.arange(3 * cols)[None, :]
+    tsel = (k % cols == 2 * j + k // cols - 1).astype(cot.dtype)
+    flops = 2 * planes * rows_out * chans_out * cols_out * 3 * cols + 2 * 2 * rows * chans * 9 * chans_out * cols
+    return pl.pallas_call(
+        backward_rows,
+        out_shape=jax.ShapeDtypeStruct((2, rows, chans, cols), cot.dtype),
+        in_specs=[pl.BlockSpec(memory_space=pltpu.VMEM)] * 3,
+        out_specs=pl.BlockSpec(memory_space=pltpu.VMEM),
+        scratch_shapes=[pltpu.VMEM((planes, rows_out, chans_out, 3 * cols), cot.dtype)],
+        cost_estimate=pl.CostEstimate(flops=flops, bytes_accessed=2 * cot.size + 2 * 2 * rows * chans * cols, transcendentals=0),
+    )(cot, kernel, tsel)
+
+
 def chan_shift(block, shift):
     size = lax.axis_size("chan")
     return lax.ppermute(block, "chan", [(i, (i + shift) % size) for i in range(size)])
@@ -117,14 +163,7 @@
     response = total.astype(jnp.bfloat16)
     pieces = [pair] + [chan_shift(pair, -k) for k in range(1, groups)]
     both_cot = jnp.concatenate(pieces, axis=3)
-    full_cot = both_cot[:, :1]
-    next_cot = both_cot[:, 1:]
-    taps = kernel.reshape(3, 3, 3, chans_in, chans_out)
-    even_planes = transposed_phases(full_cot, taps[1])
-    odd_planes = transposed_phases(next_cot, taps[0]) + transposed_phases(full_cot, taps[2])
-    both = jnp.stack([even_planes, odd_planes], axis=2).astype(jnp.bfloat16)
-    both = jnp.moveaxis(both, 6, 7)
-    volume_grad = both.reshape(count, planes_in, rows_in, chans_in, cols_in)
+    volume_grad = backward_grad(both_cot[0], kernel).reshape(count, planes_in, rows_in, chans_in, cols_in)
     return (response, volume_grad)
 
 

time: 69.5 us -> 59.7 us (0.86)
  the two profiles are of different devices: /device:TPU:768 before, /device:TPU:560 now
where the time goes in v5:
time: 59.7 us; the launch traced here: 59.3 us
  starting transfers between devices  33.3 us (56%)
  waiting for transfers between devices  9.16 us (15%)
  Pallas kernels  8.3 us (14%)
  other arithmetic  4.17 us (7%)
  local copies, waits for them, and re-layouts  3.62 us (6%)
  between operations  0.77 us (1%)
    ppermute x6, starting transfers between devices, chan_shift(): lax.ppermute(block, 'chan', [(i, (i + shift) % size) for i in range(size)])  19.3 us
    ppermute x2, starting transfers between devices, from_behind(): return lax.ppermute(block, axis, route)  14 us
    ppermute x2, waiting for transfers between devices, from_behind(): return lax.ppermute(block, axis, route)  6.4 us
    pallas_call x1, Pallas kernels, backward_grad(): pl.pallas_call(backward_rows, out_shape=jax.ShapeDtypeStruct((2, rows, ch...  5.2 us
    pallas_call x1, Pallas kernels, forward_partial(): pl.pallas_call(forward_rows, out_shape=jax.ShapeDtypeStruct((rows_out, ch...  3.09 us
    ppermute x6, waiting for transfers between devices, chan_shift(): lax.ppermute(block, 'chan', [(i, (i + shift) % size) for i in range(size)])  2.76 us
    convert_element_type x1, other arithmetic, per_device(): response = total.astype(jnp.bfloat16)  1.58 us
  transfers between devices with their start and end apart: 8, of which 2 were waited for; matrix products, arithmetic and copies ran while one was open for 8% of the time, Pallas kernels for 9%

profile of v5, /device:TPU:560, one launch (start us, length us, event | category | flops | bytes accessed | tf_op | source)
XLA Modules:
  0.0 59.3 jit_solution(98046447709889100)
XLA Ops:
  0.6 0.0 copy-start.2
  0.6 1.0 %slice.15 = bf16[1,1,16,32,256]{4,3,2,1,0:T(8,128)(2,1)S(1)} slice(bf16[1,2,16,32,256]{4,3,2,1,0:T(8,128)(2,1)} %param.3), slice={[0:1], [1:2], [0:16], [0:32], [0:256]} | slice | bytes 524288 | tf_op jit(solution)/shard_map/slice | solution.py:155
  1.6 3.4 %collective-permute-start = (bf16[1,1,16,32,256]{4,3,2,1,0:T(8,128)(2,1)S(1)}, bf16[1,1,16,32,256]{4,3,2,1,0:T(8,128)(2,1)S(1)}, u32[]{:S(2)}, u32[]{:S(2)}) collective-permute-start(bf16[1,1,16,32,256]{4,3,2,1,0:T(8,128)(2,1)S(1)} %slice.15), channel_id=1, source_target_pairs={{0,8},{8,16},{16,24},{24,32},{32,40},{40,48},{48,56},{56,64},{64,7... | collective-permute-start | bytes 786440 | tf_op jit(solution)/shard_map/ppermute | solution.py:12
  5.1 0.0 copy-done.2
  5.1 10.6 %collective-permute-start.1 = (bf16[1,1,8,32,128]{4,3,2,1,0:T(8,128)(2,1)S(1)}, bf16[1,1,8,32,128]{4,3,2,1,0:T(8,128)(2,1)S(1)}, u32[]{:S(2)}, u32[]{:S(2)}) collective-permute-start(bf16[1,1,8,32,128]{4,3,2,1,0:T(8,128)(2,1)S(1)} %copy-done.2), channel_id=1, source_target_pairs={{8,0},{16,8},{24,16},{32,24},{40,32},{48,40},{56,48},{64,56},{72,6... | collective-permute-start | bytes 196616 | tf_op jit(solution)/shard_map/ppermute | solution.py:12
  15.7 0.0 copy-start.1
  15.7 0.8 %fusion.tsel_ref = bf16[128,768]{1,0:T(8,128)(2,1)} fusion(s32[768]{0:T(1024)S(1)} %get-tuple-element.9, s32[128]{0:T(128)S(1)} %iota_multiply_fusion, s32[768]{0:T(1024)S(1)} %get-tuple-element.10), kind=kLoop, calls=%fused_computation.5 | loop fusion | flops 393216 | bytes 203264 | tf_op jit(solution)/shard_map/convert_element_type | solution.py:128
  16.5 0.7 %fusion.1.sel_ref = bf16[256,384]{1,0:T(8,128)(2,1)} fusion(s32[384]{0:T(512)S(1)} %fusion.13), kind=kLoop, calls=%fused_computation.6 | loop fusion | flops 196608 | bytes 198144 | tf_op jit(solution)/shard_map/convert_element_type | solution.py:81
  17.2 0.0 copy-done.1
  17.2 0.2 fusion.2.k_ref
  17.4 0.0 copy-start
  17.4 0.8 %copy.5.kbig_ref = bf16[128,864]{1,0:T(8,128)(2,1)} copy(bf16[128,864]{0,1:T(8,128)(2,1)S(1)} %bitcast.9) | data formatting | bytes 442368 | tf_op jit(solution)/shard_map/reshape | solution.py:82
  18.3 0.0 copy-done
  18.3 0.0 collective-permute-done.1
  18.3 6.4 %collective-permute-done = bf16[1,1,16,32,256]{4,3,2,1,0:T(8,128)(2,1)S(1)} collective-permute-done((bf16[1,1,16,32,256]{4,3,2,1,0:T(8,128)(2,1)S(1)}, bf16[1,1,16,32,256]{4,3,2,1,0:T(8,128)(2,1)S(1)}, u32[]{:S(2)}, u32[]{:S(2)}) %collective-permute-start) | collective-permute-done | bytes 262176 | tf_op jit(solution)/shard_map/ppermute | solution.py:12
  24.7 0.0 copy-start.3
  24.7 0.7 %copy-done.3 = bf16[1,1,16,32,256]{4,3,2,1,0:T(8,128)(2,1)} copy-done((bf16[1,1,16,32,256]{4,3,2,1,0:T(8,128)(2,1)}, bf16[1,1,16,32,256]{4,3,2,1,0:T(8,128)(2,1)S(1)}, u32[]{:S(2)}) %copy-start.3) | copy-done | bytes 262168
  25.4 3.1 %shard_map.50 = f32[8,128,128]{2,1,0:T(8,128)} custom-call(bf16[16,32,256]{2,1,0:T(8,128)(2,1)} %bitcast.13, bf16[2,16,32,256]{3,2,1,0:T(8,128)(2,1)} %bitcast.12, bf16[256,384]{1,0:T(8,128)(2,1)} %fusion.1.sel_ref, bf16[128,864]{1,0:T(8,128)(2,1)} %copy.5.kbig_ref), custom_call_target="tpu_custom_call" | custom-call | flops 528482304 | bytes 2097152 | tf_op jit(solution)/shard_map/pallas_call | solution.py:84
  28.5 3.8 %collective-permute-start.7 = (bf16[1,2,8,32,128]{4,3,2,1,0:T(8,128)(2,1)S(1)}, bf16[1,2,8,32,128]{4,3,2,1,0:T(8,128)(2,1)S(1)}, u32[]{:S(2)}, u32[]{:S(2)}) collective-permute-start(bf16[1,2,8,32,128]{4,3,2,1,0:T(8,128)(2,1)S(1)} %pad_maximum_fusion), channel_id=1, source_target_pairs={{0,2},{2,4},{4,6},{6,0},{1,3},{3,5},{5,7},{7,1},{8,10},{10,12},{12... | collective-permute-start | bytes 393224 | tf_op jit(solution)/shard_map/ppermute | solution.py:142
  32.3 3.2 %collective-permute-start.6 = (bf16[1,2,8,32,128]{4,3,2,1,0:T(8,128)(2,1)S(1)}, bf16[1,2,8,32,128]{4,3,2,1,0:T(8,128)(2,1)S(1)}, u32[]{:S(2)}, u32[]{:S(2)}) collective-permute-start(bf16[1,2,8,32,128]{4,3,2,1,0:T(8,128)(2,1)S(1)} %pad_maximum_fusion), channel_id=1, source_target_pairs={{0,4},{2,6},{4,0},{6,2},{1,5},{3,7},{5,1},{7,3},{8,12},{10,14},{12... | collective-permute-start | bytes 393224 | tf_op jit(solution)/shard_map/ppermute | solution.py:142
  35.5 1.9 %collective-permute-start.5 = (bf16[1,2,8,32,128]{4,3,2,1,0:T(8,128)(2,1)S(1)}, bf16[1,2,8,32,128]{4,3,2,1,0:T(8,128)(2,1)S(1)}, u32[]{:S(2)}, u32[]{:S(2)}) collective-permute-start(bf16[1,2,8,32,128]{4,3,2,1,0:T(8,128)(2,1)S(1)} %pad_maximum_fusion), channel_id=1, source_target_pairs={{0,6},{2,0},{4,2},{6,4},{1,7},{3,1},{5,3},{7,5},{8,14},{10,8},{12,... | collective-permute-start | bytes 393224 | tf_op jit(solution)/shard_map/ppermute | solution.py:142
  37.5 1.1 %fusion.18 = (f32[1,1,8,32,128]{4,3,2,1,0:T(8,128)S(1)}, f32[1,1,8,32,128]{4,3,2,1,0:T(8,128)S(1)}, f32[1,1,8,32,128]{4,3,2,1,0:T(8,128)S(1)}) fusion(f32[1,1,8,128,128]{4,3,2,1,0:T(8,128)} %bitcast.10), kind=kLoop, calls=%fused_computation.35 | loop fusion | bytes 786432 | tf_op jit(solution)/shard_map/slice | solution.py:162
  38.5 4.1 %collective-permute-start.4 = (f32[1,1,8,32,128]{4,3,2,1,0:T(8,128)S(1)}, f32[1,1,8,32,128]{4,3,2,1,0:T(8,128)S(1)}, u32[]{:S(2)}, u32[]{:S(2)}) collective-permute-start(f32[1,1,8,32,128]{4,3,2,1,0:T(8,128)S(1)} %get-tuple-element.7), channel_id=1, source_target_pairs={{0,6},{2,0},{4,2},{6,4},{1,7},{3,1},{5,3},{7,5},{8,14},{10,8},{12,... | collective-permute-start | bytes 393224 | tf_op jit(solution)/shard_map/ppermute | solution.py:142
  42.6 4.1 %collective-permute-start.3 = (f32[1,1,8,32,128]{4,3,2,1,0:T(8,128)S(1)}, f32[1,1,8,32,128]{4,3,2,1,0:T(8,128)S(1)}, u32[]{:S(2)}, u32[]{:S(2)}) collective-permute-start(f32[1,1,8,32,128]{4,3,2,1,0:T(8,128)S(1)} %get-tuple-element.8), channel_id=1, source_target_pairs={{0,4},{2,6},{4,0},{6,2},{1,5},{3,7},{5,1},{7,3},{8,12},{10,14},{12... | collective-permute-start | bytes 393224 | tf_op jit(solution)/shard_map/ppermute | solution.py:142
  46.8 0.0 collective-permute-done.7
  46.8 2.1 %collective-permute-start.2 = (f32[1,1,8,32,128]{4,3,2,1,0:T(8,128)S(1)}, f32[1,1,8,32,128]{4,3,2,1,0:T(8,128)S(1)}, u32[]{:S(2)}, u32[]{:S(2)}) collective-permute-start(f32[1,1,8,32,128]{4,3,2,1,0:T(8,128)S(1)} %get-tuple-element.6), channel_id=1, source_target_pairs={{0,2},{2,4},{4,6},{6,0},{1,3},{3,5},{5,7},{7,1},{8,10},{10,12},{12... | collective-permute-start | bytes 393224 | tf_op jit(solution)/shard_map/ppermute | solution.py:142
  48.9 2.7 %collective-permute-done.6 = bf16[1,2,8,32,128]{4,3,2,1,0:T(8,128)(2,1)S(1)} collective-permute-done((bf16[1,2,8,32,128]{4,3,2,1,0:T(8,128)(2,1)S(1)}, bf16[1,2,8,32,128]{4,3,2,1,0:T(8,128)(2,1)S(1)}, u32[]{:S(2)}, u32[]{:S(2)}) %collective-permute-start.6) | collective-permute-done | bytes 131104 | tf_op jit(solution)/shard_map/ppermute | solution.py:142
  51.7 0.0 collective-permute-done.5
  51.7 0.8 %maximum_bitcast_fusion.cot_ref = bf16[2,8,128,128]{3,2,1,0:T(8,128)(2,1)} fusion(bf16[1,2,8,32,128]{4,3,2,1,0:T(8,128)(2,1)S(1)} %collective-permute-done.7, bf16[1,2,8,32,128]{4,3,2,1,0:T(8,128)(2,1)S(1)} %collective-permute-done.6, bf16[1,2,8,32,128]{4,3,2,1,0:T(8,128)(2,1)S(1)} %collective-permute-done.5, bf16[1,2,8,32,128]{4,3,2,1,0:T(8,128)(2,1)S(1)} %pad_maximum_fusion), kind=kLoop, calls=%fused_computation | loop fusion | flops 2097152 | bytes 1048576 | tf_op jit(solution)/shard_map/squeeze | solution.py:166
  52.5 5.2 %shard_map.51 = bf16[2,16,32,256]{3,2,1,0:T(8,128)(2,1)} custom-call(bf16[2,8,128,128]{3,2,1,0:T(8,128)(2,1)} %maximum_bitcast_fusion.cot_ref, bf16[27,32,128]{2,1,0:T(8,128)(2,1)} %copy-done, bf16[128,768]{1,0:T(8,128)(2,1)} %fusion.tsel_ref), custom_call_target="tpu_custom_call" | custom-call | flops 1006632960 | bytes 1048576 | tf_op jit(solution)/shard_map/pallas_call | solution.py:130
  57.7 0.0 collective-permute-done.4
  57.7 0.0 collective-permute-done.3
  57.7 0.0 collective-permute-done.2
  57.7 1.6 %add_convert_fusion = bf16[1,1,8,32,128]{4,3,2,1,0:T(8,128)(2,1)} fusion(f32[1,1,8,32,128]{4,3,2,1,0:T(8,128)S(1)} %collective-permute-done.4, f32[1,1,8,32,128]{4,3,2,1,0:T(8,128)S(1)} %collective-permute-done.3, f32[1,1,8,32,128]{4,3,2,1,0:T(8,128)S(1)} %collective-permute-done.2, f32[1,1,8,128,128]{4,3,2,1,0:T(8,128)} %bitcast.11), kind=kLoop, calls=%fused_computation.9 | loop fusion | flops 131072 | bytes 589824 | tf_op jit(solution)/shard_map/convert_element_type | solution.py:163
  (4 shorter events, 0.0 us)
Async XLA Ops:
  0.6 4.4 %copy-start.2 = (bf16[1,1,8,32,128]{4,3,2,1,0:T(8,128)(2,1)S(1)}, bf16[1,1,8,32,128]{4,3,2,1,0:T(8,128)(2,1)}, u32[]{:S(2)}) copy-start(bf16[1,1,8,32,128]{4,3,2,1,0:T(8,128)(2,1)} %param.5) | copy-start | bytes 196612
  1.6 23.0 %collective-permute-start = (bf16[1,1,16,32,256]{4,3,2,1,0:T(8,128)(2,1)S(1)}, bf16[1,1,16,32,256]{4,3,2,1,0:T(8,128)(2,1)S(1)}, u32[]{:S(2)}, u32[]{:S(2)}) collective-permute-start(bf16[1,1,16,32,256]{4,3,2,1,0:T(8,128)(2,1)S(1)} %slice.15), channel_id=1, source_target_pairs={{0,8},{8,16},{16,24},{24,32},{32,40},{40,48},{48,56},{56,64},{64,7... | collective-permute-start | bytes 786440 | tf_op jit(solution)/shard_map/ppermute | solution.py:12
  5.1 13.2 %collective-permute-start.1 = (bf16[1,1,8,32,128]{4,3,2,1,0:T(8,128)(2,1)S(1)}, bf16[1,1,8,32,128]{4,3,2,1,0:T(8,128)(2,1)S(1)}, u32[]{:S(2)}, u32[]{:S(2)}) collective-permute-start(bf16[1,1,8,32,128]{4,3,2,1,0:T(8,128)(2,1)S(1)} %copy-done.2), channel_id=1, source_target_pairs={{8,0},{16,8},{24,16},{32,24},{40,32},{48,40},{56,48},{64,56},{72,6... | collective-permute-start | bytes 196616 | tf_op jit(solution)/shard_map/ppermute | solution.py:12
  15.7 1.5 %copy-start.1 = (bf16[27,32,128]{2,1,0:T(8,128)(2,1)S(1)}, bf16[27,32,128]{2,1,0:T(8,128)(2,1)}, u32[]{:S(2)}) copy-start(bf16[27,32,128]{2,1,0:T(8,128)(2,1)} %param.4) | copy-start | bytes 663556
  17.4 0.8 %copy-start = (bf16[27,32,128]{2,1,0:T(8,128)(2,1)}, bf16[27,32,128]{2,1,0:T(8,128)(2,1)S(1)}, u32[]{:S(2)}) copy-start(bf16[27,32,128]{2,1,0:T(8,128)(2,1)S(1)} %fusion.2.k_ref) | copy-start | bytes 663556
  24.7 0.7 %copy-start.3 = (bf16[1,1,16,32,256]{4,3,2,1,0:T(8,128)(2,1)}, bf16[1,1,16,32,256]{4,3,2,1,0:T(8,128)(2,1)S(1)}, u32[]{:S(2)}) copy-start(bf16[1,1,16,32,256]{4,3,2,1,0:T(8,128)(2,1)S(1)} %collective-permute-done) | copy-start | bytes 786436
  28.5 18.3 %collective-permute-start.7 = (bf16[1,2,8,32,128]{4,3,2,1,0:T(8,128)(2,1)S(1)}, bf16[1,2,8,32,128]{4,3,2,1,0:T(8,128)(2,1)S(1)}, u32[]{:S(2)}, u32[]{:S(2)}) collective-permute-start(bf16[1,2,8,32,128]{4,3,2,1,0:T(8,128)(2,1)S(1)} %pad_maximum_fusion), channel_id=1, source_target_pairs={{0,2},{2,4},{4,6},{6,0},{1,3},{3,5},{5,7},{7,1},{8,10},{10,12},{12... | collective-permute-start | bytes 393224 | tf_op jit(solution)/shard_map/ppermute | solution.py:142
  32.3 19.3 %collective-permute-start.6 = (bf16[1,2,8,32,128]{4,3,2,1,0:T(8,128)(2,1)S(1)}, bf16[1,2,8,32,128]{4,3,2,1,0:T(8,128)(2,1)S(1)}, u32[]{:S(2)}, u32[]{:S(2)}) collective-permute-start(bf16[1,2,8,32,128]{4,3,2,1,0:T(8,128)(2,1)S(1)} %pad_maximum_fusion), channel_id=1, source_target_pairs={{0,4},{2,6},{4,0},{6,2},{1,5},{3,7},{5,1},{7,3},{8,12},{10,14},{12... | collective-permute-start | bytes 393224 | tf_op jit(solution)/shard_map/ppermute | solution.py:142
  35.5 16.1 %collective-permute-start.5 = (bf16[1,2,8,32,128]{4,3,2,1,0:T(8,128)(2,1)S(1)}, bf16[1,2,8,32,128]{4,3,2,1,0:T(8,128)(2,1)S(1)}, u32[]{:S(2)}, u32[]{:S(2)}) collective-permute-start(bf16[1,2,8,32,128]{4,3,2,1,0:T(8,128)(2,1)S(1)} %pad_maximum_fusion), channel_id=1, source_target_pairs={{0,6},{2,0},{4,2},{6,4},{1,7},{3,1},{5,3},{7,5},{8,14},{10,8},{12,... | collective-permute-start | bytes 393224 | tf_op jit(solution)/shard_map/ppermute | solution.py:142
  38.5 19.2 %collective-permute-start.4 = (f32[1,1,8,32,128]{4,3,2,1,0:T(8,128)S(1)}, f32[1,1,8,32,128]{4,3,2,1,0:T(8,128)S(1)}, u32[]{:S(2)}, u32[]{:S(2)}) collective-permute-start(f32[1,1,8,32,128]{4,3,2,1,0:T(8,128)S(1)} %get-tuple-element.7), channel_id=1, source_target_pairs={{0,6},{2,0},{4,2},{6,4},{1,7},{3,1},{5,3},{7,5},{8,14},{10,8},{12,... | collective-permute-start | bytes 393224 | tf_op jit(solution)/shard_map/ppermute | solution.py:142
  42.6 15.1 %collective-permute-start.3 = (f32[1,1,8,32,128]{4,3,2,1,0:T(8,128)S(1)}, f32[1,1,8,32,128]{4,3,2,1,0:T(8,128)S(1)}, u32[]{:S(2)}, u32[]{:S(2)}) collective-permute-start(f32[1,1,8,32,128]{4,3,2,1,0:T(8,128)S(1)} %get-tuple-element.8), channel_id=1, source_target_pairs={{0,4},{2,6},{4,0},{6,2},{1,5},{3,7},{5,1},{7,3},{8,12},{10,14},{12... | collective-permute-start | bytes 393224 | tf_op jit(solution)/shard_map/ppermute | solution.py:142
  46.8 11.0 %collective-permute-start.2 = (f32[1,1,8,32,128]{4,3,2,1,0:T(8,128)S(1)}, f32[1,1,8,32,128]{4,3,2,1,0:T(8,128)S(1)}, u32[]{:S(2)}, u32[]{:S(2)}) collective-permute-start(f32[1,1,8,32,128]{4,3,2,1,0:T(8,128)S(1)} %get-tuple-element.6), channel_id=1, source_target_pairs={{0,2},{2,4},{4,6},{6,0},{1,3},{3,5},{5,7},{7,1},{8,10},{10,12},{12... | collective-permute-start | bytes 393224 | tf_op jit(solution)/shard_map/ppermute | solution.py:142

commit v6 on v5

--- a/solution.py
+++ b/solution.py
@@ -46,11 +46,20 @@
     return jnp.stack([upper, lower], axis=3)
 
 
-def forward_rows(halo_ref, vol_ref, sel_ref, kbig_ref, out_ref, picked_ref):
+def spread_matrix(rows, cols, transposed):
+    blocks = []
+    for tap in range(3):
+        narrow = lax.broadcasted_iota(jnp.int32, (rows, cols), 1 if not transposed else 0)
+        wide = lax.broadcasted_iota(jnp.int32, (rows, cols), 0 if not transposed else 1)
+        blocks.append(jnp.where(wide == 2 * narrow + tap - 1, 1.0, 0.0).astype(jnp.bfloat16))
+    return jnp.concatenate(blocks, axis=1)
+
+
+def forward_rows(halo_ref, vol_ref, kbig_ref, *refs):
+    out_refs, picked_ref = refs[:-1], refs[-1]
     planes, rows, chans, cols = vol_ref.shape
-    rows_out = out_ref.shape[0]
-    cols_out = out_ref.shape[2]
-    sel = sel_ref[...]
+    rows_out, share, cols_out = out_refs[0].shape
+    sel = spread_matrix(cols, cols_out, False)
     for plane in range(planes + 1):
         source = halo_ref[...] if plane == 0 else vol_ref[plane - 1]
         flat = source.reshape(rows * chans, cols)
@@ -69,37 +78,39 @@
                     else:
                         pieces.append(picked_ref[depth_tap, row, :, col_tap * cols_out:(col_tap + 1) * cols_out])
         stacked = jnp.concatenate(pieces, axis=0)
-        out_ref[i] = jnp.dot(kbig, stacked, preferred_element_type=jnp.float32)
+        result = jnp.dot(kbig, stacked, preferred_element_type=jnp.float32)
+        for k, out_ref in enumerate(out_refs):
+            out_ref[i] = result[k * share:(k + 1) * share]
 
 
-def forward_partial(halo, vol, kernel):
+def forward_partial(halo, vol, kernel, groups):
     planes, rows, chans, cols = vol.shape
     taps, _, chans_out = kernel.shape
     rows_out, cols_out = rows // 2, cols // 2
-    w = jnp.arange(cols)[:, None]
-    k = jnp.arange(3 * cols_out)[None, :]
-    sel = (w == 2 * (k % cols_out) + k // cols_out - 1).astype(vol.dtype)
+    share = chans_out // groups
     kbig = jnp.transpose(kernel, (2, 0, 1)).reshape(chans_out, taps * chans)
     flops = 2 * (planes + 1) * rows * chans * cols * 3 * cols_out + 2 * rows_out * chans_out * taps * chans * cols_out
     return pl.pallas_call(
         forward_rows,
-        out_shape=jax.ShapeDtypeStruct((rows_out, chans_out, cols_out), jnp.float32),
-        in_specs=[pl.BlockSpec(memory_space=pltpu.VMEM)] * 4,
-        out_specs=pl.BlockSpec(memory_space=pltpu.VMEM),
+        out_shape=[jax.ShapeDtypeStruct((rows_out, share, cols_out), jnp.float32)] * groups,
+        in_specs=[pl.BlockSpec(memory_space=pltpu.VMEM)] * 3,
+        out_specs=[pl.BlockSpec(memory_space=pltpu.VMEM)] * groups,
         scratch_shapes=[pltpu.VMEM((planes + 1, rows, chans, 3 * cols_out), vol.dtype)],
         cost_estimate=pl.CostEstimate(flops=flops, bytes_accessed=2 * 4 * vol.size, transcendentals=0),
-    )(halo, vol, sel, kbig)
+    )(halo, vol, kbig)
 
 
-def backward_rows(cot_ref, k_ref, tsel_ref, out_ref, up_ref):
-    planes, rows_out, chans_out, cols_out = cot_ref.shape
+def backward_rows(*refs):
+    groups = (len(refs) - 3)
+    cot_refs, k_ref, out_ref, up_ref = refs[:groups], refs[groups], refs[groups + 1], refs[groups + 2]
+    planes, rows_out, share, cols_out = cot_refs[0].shape
     rows = out_ref.shape[1]
     cols = out_ref.shape[3]
-    tsel = tsel_ref[...]
-    for plane in range(planes):
-        flat = cot_ref[plane].reshape(rows_out * chans_out, cols_out)
+    tsel = spread_matrix(cols_out, cols, True)
+    for k, cot_ref in enumerate(cot_refs):
+        flat = cot_ref[...].reshape(planes * rows_out * share, cols_out)
         spread = jnp.dot(flat, tsel, preferred_element_type=jnp.float32)
-        up_ref[plane] = spread.astype(up_ref.dtype).reshape(rows_out, chans_out, 3 * cols)
+        up_ref[:, :, k * share:(k + 1) * share, :] = spread.astype(up_ref.dtype).reshape(planes, rows_out, share, 3 * cols)
     for depth in range(2):
         sources = [(1, 0)] if depth == 0 else [(2, 0), (0, 1)]
         for row in range(rows):
@@ -119,22 +130,20 @@
             out_ref[depth, row] = jnp.dot(lhs, rhs, preferred_element_type=jnp.float32).astype(out_ref.dtype)
 
 
-def backward_grad(cot, kernel):
-    planes, rows_out, chans_out, cols_out = cot.shape
+def backward_grad(pieces, kernel):
+    planes, rows_out, share, cols_out = pieces[0].shape
+    chans_out = share * len(pieces)
     taps, chans, _ = kernel.shape
     rows, cols = 2 * rows_out, 2 * cols_out
-    j = jnp.arange(cols_out)[:, None]
-    k = jnp.arange(3 * cols)[None, :]
-    tsel = (k % cols == 2 * j + k // cols - 1).astype(cot.dtype)
     flops = 2 * planes * rows_out * chans_out * cols_out * 3 * cols + 2 * 2 * rows * chans * 9 * chans_out * cols
     return pl.pallas_call(
         backward_rows,
-        out_shape=jax.ShapeDtypeStruct((2, rows, chans, cols), cot.dtype),
-        in_specs=[pl.BlockSpec(memory_space=pltpu.VMEM)] * 3,
+        out_shape=jax.ShapeDtypeStruct((2, rows, chans, cols), kernel.dtype),
+        in_specs=[pl.BlockSpec(memory_space=pltpu.VMEM)] * (len(pieces) + 1),
         out_specs=pl.BlockSpec(memory_space=pltpu.VMEM),
-        scratch_shapes=[pltpu.VMEM((planes, rows_out, chans_out, 3 * cols), cot.dtype)],
-        cost_estimate=pl.CostEstimate(flops=flops, bytes_accessed=2 * cot.size + 2 * 2 * rows * chans * cols, transcendentals=0),
-    )(cot, kernel, tsel)
+        scratch_shapes=[pltpu.VMEM((planes, rows_out, chans_out, 3 * cols), kernel.dtype)],
+        cost_estimate=pl.CostEstimate(flops=flops, bytes_accessed=2 * planes * rows_out * chans_out * cols_out + 2 * 2 * rows * chans * cols, transcendentals=0),
+    )(*pieces, kernel)
 
 
 def chan_shift(block, shift):
@@ -153,17 +162,15 @@
     me = lax.axis_index("chan")
     kernel = jnp.roll(kernel, -me * share, axis=2)
     below = from_behind(volume[:, -1:], "space", 1)
-    partial_sum = forward_partial(below[0, 0], volume[0], kernel)
-    partial_sum = partial_sum.reshape(count, planes_out, rows_out, chans_out, cols_out)
+    chunks = forward_partial(below[0, 0], volume[0], kernel, groups)
     pair = jnp.concatenate([cotangent, from_behind(cotangent, "space", -1)], axis=1)
-    partial_sum, pair = lax.optimization_barrier((partial_sum, pair))
-    total = partial_sum[:, :, :, :share]
+    chunks, pair = lax.optimization_barrier((chunks, pair))
+    total = chunks[0]
     for k in range(1, groups):
-        total = total + chan_shift(partial_sum[:, :, :, k * share:(k + 1) * share], k)
-    response = total.astype(jnp.bfloat16)
-    pieces = [pair] + [chan_shift(pair, -k) for k in range(1, groups)]
-    both_cot = jnp.concatenate(pieces, axis=3)
-    volume_grad = backward_grad(both_cot[0], kernel).reshape(count, planes_in, rows_in, chans_in, cols_in)
+        total = total + chan_shift(chunks[k], k)
+    response = total.astype(jnp.bfloat16).reshape(count, planes_out, rows_out, share, cols_out)
+    pieces = [pair[0]] + [chan_shift(pair[0], -k) for k in range(1, groups)]
+    volume_grad = backward_grad(pieces, kernel).reshape(count, planes_in, rows_in, chans_in, cols_in)
     return (response, volume_grad)
 
 

time: 59.7 us -> 58.4 us (0.978)
  the two profiles are of different devices: /device:TPU:560 before, /device:TPU:512 now
where the time goes in v6:
time: 58.4 us; the launch traced here: 58 us
  starting transfers between devices  32.5 us (56%)
  waiting for transfers between devices  12.1 us (21%)
  Pallas kernels  7.83 us (13%)
  local copies, waits for them, and re-layouts  3.84 us (7%)
  other arithmetic  0.91 us (2%)
  between operations  0.84 us (1%)
    ppermute x6, starting transfers between devices, chan_shift(): lax.ppermute(block, 'chan', [(i, (i + shift) % size) for i in range(size)])  18.5 us
    ppermute x2, starting transfers between devices, from_behind(): return lax.ppermute(block, axis, route)  14 us
    ppermute x2, waiting for transfers between devices, from_behind(): return lax.ppermute(block, axis, route)  9.96 us
    pallas_call x1, Pallas kernels, backward_grad(): pl.pallas_call(backward_rows, out_shape=jax.ShapeDtypeStruct((2, rows, ch...  4.81 us
    pallas_call x1, Pallas kernels, forward_partial(): pl.pallas_call(forward_rows, out_shape=[jax.ShapeDtypeStruct((rows_out, s...  3.01 us
    ppermute x6, waiting for transfers between devices, chan_shift(): lax.ppermute(block, 'chan', [(i, (i + shift) % size) for i in range(size)])  2.11 us
    unnamed x18, local copies, waits for them, and re-layouts  2 us
  transfers between devices with their start and end apart: 8, of which 3 were waited for; matrix products, arithmetic and copies ran while one was open for 2% of the time, Pallas kernels for 8%

profile of v6, /device:TPU:512, one launch (start us, length us, event | category | flops | bytes accessed | tf_op | source)
XLA Modules:
  0.0 58.0 jit_solution(4749486394931390656)
XLA Ops:
  0.6 0.0 copy-start.4
  0.6 0.0 copy-start.1
  0.6 1.0 %slice.3 = bf16[1,1,16,32,256]{4,3,2,1,0:T(8,128)(2,1)S(1)} slice(bf16[1,2,16,32,256]{4,3,2,1,0:T(8,128)(2,1)} %param.3), slice={[0:1], [1:2], [0:16], [0:32], [0:256]} | slice | bytes 524288 | tf_op jit(solution)/shard_map/slice | solution.py:164
  1.7 3.4 %collective-permute-start = (bf16[1,1,16,32,256]{4,3,2,1,0:T(8,128)(2,1)S(1)}, bf16[1,1,16,32,256]{4,3,2,1,0:T(8,128)(2,1)S(1)}, u32[]{:S(2)}, u32[]{:S(2)}) collective-permute-start(bf16[1,1,16,32,256]{4,3,2,1,0:T(8,128)(2,1)S(1)} %slice.3), channel_id=1, source_target_pairs={{0,8},{8,16},{16,24},{24,32},{32,40},{40,48},{48,56},{56,64},{64,7... | collective-permute-start | bytes 786440 | tf_op jit(solution)/shard_map/ppermute | solution.py:12
  5.1 0.0 copy-done.4
  5.1 10.6 %collective-permute-start.1 = (bf16[1,1,8,32,128]{4,3,2,1,0:T(8,128)(2,1)S(1)}, bf16[1,1,8,32,128]{4,3,2,1,0:T(8,128)(2,1)S(1)}, u32[]{:S(2)}, u32[]{:S(2)}) collective-permute-start(bf16[1,1,8,32,128]{4,3,2,1,0:T(8,128)(2,1)S(1)} %copy-done.4), channel_id=1, source_target_pairs={{8,0},{16,8},{24,16},{32,24},{40,32},{48,40},{56,48},{64,56},{72,6... | collective-permute-start | bytes 196616 | tf_op jit(solution)/shard_map/ppermute | solution.py:12
  15.7 0.0 copy-done.1
  15.7 0.2 fusion.refs_4_
  15.9 0.0 copy-start
  15.9 0.8 %copy.5.kbig_ref = bf16[128,864]{1,0:T(8,128)(2,1)} copy(bf16[128,864]{0,1:T(8,128)(2,1)S(1)} %bitcast.9) | data formatting | bytes 442368 | tf_op jit(solution)/shard_map/reshape | solution.py:91
  16.8 0.0 copy-done
  16.8 0.8 %collective-permute-done.1 = bf16[1,1,8,32,128]{4,3,2,1,0:T(8,128)(2,1)S(1)} collective-permute-done((bf16[1,1,8,32,128]{4,3,2,1,0:T(8,128)(2,1)S(1)}, bf16[1,1,8,32,128]{4,3,2,1,0:T(8,128)(2,1)S(1)}, u32[]{:S(2)}, u32[]{:S(2)}) %collective-permute-start.1) | collective-permute-done | bytes 65568 | tf_op jit(solution)/shard_map/ppermute | solution.py:12
  17.6 0.0 copy-start.2
  17.6 9.2 %collective-permute-done = bf16[1,1,16,32,256]{4,3,2,1,0:T(8,128)(2,1)S(1)} collective-permute-done((bf16[1,1,16,32,256]{4,3,2,1,0:T(8,128)(2,1)S(1)}, bf16[1,1,16,32,256]{4,3,2,1,0:T(8,128)(2,1)S(1)}, u32[]{:S(2)}, u32[]{:S(2)}) %collective-permute-start) | collective-permute-done | bytes 262176 | tf_op jit(solution)/shard_map/ppermute | solution.py:12
  26.8 0.0 copy-start.5
  26.8 0.7 %copy-done.5 = bf16[1,1,16,32,256]{4,3,2,1,0:T(8,128)(2,1)} copy-done((bf16[1,1,16,32,256]{4,3,2,1,0:T(8,128)(2,1)}, bf16[1,1,16,32,256]{4,3,2,1,0:T(8,128)(2,1)S(1)}, u32[]{:S(2)}) %copy-start.5) | copy-done | bytes 262168
  27.5 3.0 %shard_map.50 = (f32[8,32,128]{2,1,0:T(8,128)}, f32[8,32,128]{2,1,0:T(8,128)}, f32[8,32,128]{2,1,0:T(8,128)}, f32[8,32,128]{2,1,0:T(8,128)}) custom-call(bf16[16,32,256]{2,1,0:T(8,128)(2,1)} %bitcast.15, bf16[2,16,32,256]{3,2,1,0:T(8,128)(2,1)} %bitcast.10, bf16[128,864]{1,0:T(8,128)(2,1)} %copy.5.kbig_ref), custom_call_target="tpu_custom_call" | custom-call | flops 528482304 | bytes 2097152 | tf_op jit(solution)/shard_map/pallas_call | solution.py:93
  30.5 0.0 copy-start.3
  30.5 3.9 %collective-permute-start.5 = (bf16[2,8,32,128]{3,2,1,0:T(8,128)(2,1)S(1)}, bf16[2,8,32,128]{3,2,1,0:T(8,128)(2,1)S(1)}, u32[]{:S(2)}, u32[]{:S(2)}) collective-permute-start(bf16[2,8,32,128]{3,2,1,0:T(8,128)(2,1)S(1)} %bitcast.11), channel_id=1, source_target_pairs={{0,6},{2,0},{4,2},{6,4},{1,7},{3,1},{5,3},{7,5},{8,14},{10,8},{12,... | collective-permute-start | bytes 393224 | tf_op jit(solution)/shard_map/ppermute | solution.py:151
  34.4 2.3 %collective-permute-start.6 = (bf16[2,8,32,128]{3,2,1,0:T(8,128)(2,1)S(1)}, bf16[2,8,32,128]{3,2,1,0:T(8,128)(2,1)S(1)}, u32[]{:S(2)}, u32[]{:S(2)}) collective-permute-start(bf16[2,8,32,128]{3,2,1,0:T(8,128)(2,1)S(1)} %bitcast.12), channel_id=1, source_target_pairs={{0,4},{2,6},{4,0},{6,2},{1,5},{3,7},{5,1},{7,3},{8,12},{10,14},{12... | collective-permute-start | bytes 393224 | tf_op jit(solution)/shard_map/ppermute | solution.py:151
  36.7 0.0 copy-done.2
  36.7 3.9 %collective-permute-start.7 = (bf16[2,8,32,128]{3,2,1,0:T(8,128)(2,1)S(1)}, bf16[2,8,32,128]{3,2,1,0:T(8,128)(2,1)S(1)}, u32[]{:S(2)}, u32[]{:S(2)}) collective-permute-start(bf16[2,8,32,128]{3,2,1,0:T(8,128)(2,1)S(1)} %bitcast.13), channel_id=1, source_target_pairs={{0,2},{2,4},{4,6},{6,0},{1,3},{3,5},{5,7},{7,1},{8,10},{10,12},{12... | collective-permute-start | bytes 393224 | tf_op jit(solution)/shard_map/ppermute | solution.py:151
  40.6 3.7 %collective-permute-start.4 = (f32[8,32,128]{2,1,0:T(8,128)}, f32[8,32,128]{2,1,0:T(8,128)S(1)}, u32[]{:S(2)}, u32[]{:S(2)}) collective-permute-start(f32[8,32,128]{2,1,0:T(8,128)} %get-tuple-element.18), channel_id=1, source_target_pairs={{0,6},{2,0},{4,2},{6,4},{1,7},{3,1},{5,3},{7,5},{8,14},{10,8},{12,... | collective-permute-start | bytes 393224 | tf_op jit(solution)/shard_map/ppermute | solution.py:151
  44.3 2.7 %collective-permute-start.3 = (f32[8,32,128]{2,1,0:T(8,128)}, f32[8,32,128]{2,1,0:T(8,128)S(1)}, u32[]{:S(2)}, u32[]{:S(2)}) collective-permute-start(f32[8,32,128]{2,1,0:T(8,128)} %get-tuple-element.17), channel_id=1, source_target_pairs={{0,4},{2,6},{4,0},{6,2},{1,5},{3,7},{5,1},{7,3},{8,12},{10,14},{12... | collective-permute-start | bytes 393224 | tf_op jit(solution)/shard_map/ppermute | solution.py:151
  47.0 0.0 collective-permute-done.5.refs_1_
  47.0 0.0 copy-start.6
  47.0 2.1 %collective-permute-start.2 = (f32[8,32,128]{2,1,0:T(8,128)}, f32[8,32,128]{2,1,0:T(8,128)S(1)}, u32[]{:S(2)}, u32[]{:S(2)}) collective-permute-start(f32[8,32,128]{2,1,0:T(8,128)} %get-tuple-element.16), channel_id=1, source_target_pairs={{0,2},{2,4},{4,6},{6,0},{1,3},{3,5},{5,7},{7,1},{8,10},{10,12},{12... | collective-permute-start | bytes 393224 | tf_op jit(solution)/shard_map/ppermute | solution.py:151
  49.1 0.0 collective-permute-done.6.refs_2_
  49.1 0.0 copy-start.7
  49.1 0.0 collective-permute-done.7.refs_3_
  49.1 0.0 copy-done.6
  49.1 0.6 %copy-done.7 = bf16[2,8,32,128]{3,2,1,0:T(8,128)(2,1)} copy-done((bf16[2,8,32,128]{3,2,1,0:T(8,128)(2,1)}, bf16[2,8,32,128]{3,2,1,0:T(8,128)(2,1)S(1)}, u32[]{:S(2)}) %copy-start.7) | copy-done | bytes 131096
  49.8 0.0 copy-start.8
  49.8 0.7 %copy-done.8 = bf16[2,8,32,128]{3,2,1,0:T(8,128)(2,1)} copy-done((bf16[2,8,32,128]{3,2,1,0:T(8,128)(2,1)}, bf16[2,8,32,128]{3,2,1,0:T(8,128)(2,1)S(1)}, u32[]{:S(2)}) %copy-start.8) | copy-done | bytes 131096
  50.4 4.8 %shard_map.51 = bf16[2,16,32,256]{3,2,1,0:T(8,128)(2,1)} custom-call(bf16[2,8,32,128]{3,2,1,0:T(8,128)(2,1)} %bitcast.14, bf16[2,8,32,128]{3,2,1,0:T(8,128)(2,1)} %copy-done.6, bf16[2,8,32,128]{3,2,1,0:T(8,128)(2,1)} %copy-done.7, bf16[2,8,32,128]{3,2,1,0:T(8,128)(2,1)} %copy-done.8, bf16[27,32,128]{2,1,0:T(8,128)(2,1)} %copy-done), custom_call_target="tpu_custom_call" | custom-call | flops 1006632960 | bytes 1048576 | tf_op jit(solution)/shard_map/pallas_call | solution.py:139
  55.2 0.0 collective-permute-done.4
  55.2 2.1 %collective-permute-done.3 = f32[8,32,128]{2,1,0:T(8,128)S(1)} collective-permute-done((f32[8,32,128]{2,1,0:T(8,128)}, f32[8,32,128]{2,1,0:T(8,128)S(1)}, u32[]{:S(2)}, u32[]{:S(2)}) %collective-permute-start.3) | collective-permute-done | bytes 131104 | tf_op jit(solution)/shard_map/ppermute | solution.py:151
  57.3 0.0 collective-permute-done.2
  57.3 0.0 copy-done.3
  57.3 0.7 %fusion.1 = bf16[1,1,8,32,128]{4,3,2,1,0:T(8,128)(2,1)} fusion(f32[8,32,128]{2,1,0:T(8,128)S(1)} %collective-permute-done.4, f32[8,32,128]{2,1,0:T(8,128)S(1)} %collective-permute-done.3, f32[8,32,128]{2,1,0:T(8,128)S(1)} %copy-done.3, f32[8,32,128]{2,1,0:T(8,128)S(1)} %collective-permute-done.2), kind=kLoop, calls=%fused_computation.5 | loop fusion | flops 131072 | bytes 589824 | tf_op jit(solution)/shard_map/reshape | solution.py:171
  (1 shorter events, 0.0 us)
Async XLA Ops:
  0.6 4.5 %copy-start.4 = (bf16[1,1,8,32,128]{4,3,2,1,0:T(8,128)(2,1)S(1)}, bf16[1,1,8,32,128]{4,3,2,1,0:T(8,128)(2,1)}, u32[]{:S(2)}) copy-start(bf16[1,1,8,32,128]{4,3,2,1,0:T(8,128)(2,1)} %param.5) | copy-start | bytes 196612
  0.6 15.0 %copy-start.1 = (bf16[27,32,128]{2,1,0:T(8,128)(2,1)S(1)}, bf16[27,32,128]{2,1,0:T(8,128)(2,1)}, u32[]{:S(2)}) copy-start(bf16[27,32,128]{2,1,0:T(8,128)(2,1)} %param.4) | copy-start | bytes 663556
  1.7 25.1 %collective-permute-start = (bf16[1,1,16,32,256]{4,3,2,1,0:T(8,128)(2,1)S(1)}, bf16[1,1,16,32,256]{4,3,2,1,0:T(8,128)(2,1)S(1)}, u32[]{:S(2)}, u32[]{:S(2)}) collective-permute-start(bf16[1,1,16,32,256]{4,3,2,1,0:T(8,128)(2,1)S(1)} %slice.3), channel_id=1, source_target_pairs={{0,8},{8,16},{16,24},{24,32},{32,40},{40,48},{48,56},{56,64},{64,7... | collective-permute-start | bytes 786440 | tf_op jit(solution)/shard_map/ppermute | solution.py:12
  5.1 12.5 %collective-permute-start.1 = (bf16[1,1,8,32,128]{4,3,2,1,0:T(8,128)(2,1)S(1)}, bf16[1,1,8,32,128]{4,3,2,1,0:T(8,128)(2,1)S(1)}, u32[]{:S(2)}, u32[]{:S(2)}) collective-permute-start(bf16[1,1,8,32,128]{4,3,2,1,0:T(8,128)(2,1)S(1)} %copy-done.4), channel_id=1, source_target_pairs={{8,0},{16,8},{24,16},{32,24},{40,32},{48,40},{56,48},{64,56},{72,6... | collective-permute-start | bytes 196616 | tf_op jit(solution)/shard_map/ppermute | solution.py:12
  15.9 0.8 %copy-start = (bf16[27,32,128]{2,1,0:T(8,128)(2,1)}, bf16[27,32,128]{2,1,0:T(8,128)(2,1)S(1)}, u32[]{:S(2)}) copy-start(bf16[27,32,128]{2,1,0:T(8,128)(2,1)S(1)} %fusion.refs_4_) | copy-start | bytes 663556
  17.6 19.1 %copy-start.2 = (bf16[1,2,8,32,128]{4,3,2,1,0:T(8,128)(2,1)}, bf16[1,2,8,32,128]{4,3,2,1,0:T(8,128)(2,1)S(1)}, u32[]{:S(2)}) copy-start(bf16[1,2,8,32,128]{4,3,2,1,0:T(8,128)(2,1)S(1)} %pad_maximum_fusion) | copy-start | bytes 393220
  26.8 0.7 %copy-start.5 = (bf16[1,1,16,32,256]{4,3,2,1,0:T(8,128)(2,1)}, bf16[1,1,16,32,256]{4,3,2,1,0:T(8,128)(2,1)S(1)}, u32[]{:S(2)}) copy-start(bf16[1,1,16,32,256]{4,3,2,1,0:T(8,128)(2,1)S(1)} %collective-permute-done) | copy-start | bytes 786436
  30.5 26.9 %copy-start.3 = (f32[8,32,128]{2,1,0:T(8,128)S(1)}, f32[8,32,128]{2,1,0:T(8,128)}, u32[]{:S(2)}) copy-start(f32[8,32,128]{2,1,0:T(8,128)} %get-tuple-element.15) | copy-start | bytes 393220
  30.5 16.5 %collective-permute-start.5 = (bf16[2,8,32,128]{3,2,1,0:T(8,128)(2,1)S(1)}, bf16[2,8,32,128]{3,2,1,0:T(8,128)(2,1)S(1)}, u32[]{:S(2)}, u32[]{:S(2)}) collective-permute-start(bf16[2,8,32,128]{3,2,1,0:T(8,128)(2,1)S(1)} %bitcast.11), channel_id=1, source_target_pairs={{0,6},{2,0},{4,2},{6,4},{1,7},{3,1},{5,3},{7,5},{8,14},{10,8},{12,... | collective-permute-start | bytes 393224 | tf_op jit(solution)/shard_map/ppermute | solution.py:151
  34.4 14.7 %collective-permute-start.6 = (bf16[2,8,32,128]{3,2,1,0:T(8,128)(2,1)S(1)}, bf16[2,8,32,128]{3,2,1,0:T(8,128)(2,1)S(1)}, u32[]{:S(2)}, u32[]{:S(2)}) collective-permute-start(bf16[2,8,32,128]{3,2,1,0:T(8,128)(2,1)S(1)} %bitcast.12), channel_id=1, source_target_pairs={{0,4},{2,6},{4,0},{6,2},{1,5},{3,7},{5,1},{7,3},{8,12},{10,14},{12... | collective-permute-start | bytes 393224 | tf_op jit(solution)/shard_map/ppermute | solution.py:151
  36.7 12.5 %collective-permute-start.7 = (bf16[2,8,32,128]{3,2,1,0:T(8,128)(2,1)S(1)}, bf16[2,8,32,128]{3,2,1,0:T(8,128)(2,1)S(1)}, u32[]{:S(2)}, u32[]{:S(2)}) collective-permute-start(bf16[2,8,32,128]{3,2,1,0:T(8,128)(2,1)S(1)} %bitcast.13), channel_id=1, source_target_pairs={{0,2},{2,4},{4,6},{6,0},{1,3},{3,5},{5,7},{7,1},{8,10},{10,12},{12... | collective-permute-start | bytes 393224 | tf_op jit(solution)/shard_map/ppermute | solution.py:151
  40.6 14.6 %collective-permute-start.4 = (f32[8,32,128]{2,1,0:T(8,128)}, f32[8,32,128]{2,1,0:T(8,128)S(1)}, u32[]{:S(2)}, u32[]{:S(2)}) collective-permute-start(f32[8,32,128]{2,1,0:T(8,128)} %get-tuple-element.18), channel_id=1, source_target_pairs={{0,6},{2,0},{4,2},{6,4},{1,7},{3,1},{5,3},{7,5},{8,14},{10,8},{12,... | collective-permute-start | bytes 393224 | tf_op jit(solution)/shard_map/ppermute | solution.py:151
  44.3 13.0 %collective-permute-start.3 = (f32[8,32,128]{2,1,0:T(8,128)}, f32[8,32,128]{2,1,0:T(8,128)S(1)}, u32[]{:S(2)}, u32[]{:S(2)}) collective-permute-start(f32[8,32,128]{2,1,0:T(8,128)} %get-tuple-element.17), channel_id=1, source_target_pairs={{0,4},{2,6},{4,0},{6,2},{1,5},{3,7},{5,1},{7,3},{8,12},{10,14},{12... | collective-permute-start | bytes 393224 | tf_op jit(solution)/shard_map/ppermute | solution.py:151
  47.0 2.1 %copy-start.6 = (bf16[2,8,32,128]{3,2,1,0:T(8,128)(2,1)}, bf16[2,8,32,128]{3,2,1,0:T(8,128)(2,1)S(1)}, u32[]{:S(2)}) copy-start(bf16[2,8,32,128]{3,2,1,0:T(8,128)(2,1)S(1)} %collective-permute-done.5.refs_1_) | copy-start | bytes 393220
  47.0 10.3 %collective-permute-start.2 = (f32[8,32,128]{2,1,0:T(8,128)}, f32[8,32,128]{2,1,0:T(8,128)S(1)}, u32[]{:S(2)}, u32[]{:S(2)}) collective-permute-start(f32[8,32,128]{2,1,0:T(8,128)} %get-tuple-element.16), channel_id=1, source_target_pairs={{0,2},{2,4},{4,6},{6,0},{1,3},{3,5},{5,7},{7,1},{8,10},{10,12},{12... | collective-permute-start | bytes 393224 | tf_op jit(solution)/shard_map/ppermute | solution.py:151
  49.1 0.6 %copy-start.7 = (bf16[2,8,32,128]{3,2,1,0:T(8,128)(2,1)}, bf16[2,8,32,128]{3,2,1,0:T(8,128)(2,1)S(1)}, u32[]{:S(2)}) copy-start(bf16[2,8,32,128]{3,2,1,0:T(8,128)(2,1)S(1)} %collective-permute-done.6.refs_2_) | copy-start | bytes 393220
  49.8 0.7 %copy-start.8 = (bf16[2,8,32,128]{3,2,1,0:T(8,128)(2,1)}, bf16[2,8,32,128]{3,2,1,0:T(8,128)(2,1)S(1)}, u32[]{:S(2)}) copy-start(bf16[2,8,32,128]{3,2,1,0:T(8,128)(2,1)S(1)} %collective-permute-done.7.refs_3_) | copy-start | bytes 393220

commit v7 on v6

--- a/solution.py
+++ b/solution.py
@@ -55,10 +55,13 @@
     return jnp.concatenate(blocks, axis=1)
 
 
-def forward_rows(halo_ref, vol_ref, kbig_ref, *refs):
-    out_refs, picked_ref = refs[:-1], refs[-1]
+def forward_rows(halo_ref, vol_ref, kbig_ref, pair_ref, own_ref, *refs):
+    sent_refs, picked_ref = refs[:-1], refs[-1]
     planes, rows, chans, cols = vol_ref.shape
-    rows_out, share, cols_out = out_refs[0].shape
+    rows_out, share, cols_out = own_ref.shape
+    carried = pair_ref[...].astype(jnp.float32)
+    for sent_ref in sent_refs:
+        sent_ref[1:] = carried
     sel = spread_matrix(cols, cols_out, False)
     for plane in range(planes + 1):
         source = halo_ref[...] if plane == 0 else vol_ref[plane - 1]
@@ -79,38 +82,49 @@
                         pieces.append(picked_ref[depth_tap, row, :, col_tap * cols_out:(col_tap + 1) * cols_out])
         stacked = jnp.concatenate(pieces, axis=0)
         result = jnp.dot(kbig, stacked, preferred_element_type=jnp.float32)
-        for k, out_ref in enumerate(out_refs):
-            out_ref[i] = result[k * share:(k + 1) * share]
-
-
-def forward_partial(halo, vol, kernel, groups):
+        own_ref[i] = result[:share]
+        for k, sent_ref in enumerate(sent_refs, start=1):
+            sent_ref[0, i] = result[k * share:(k + 1) * share]
+
+
+def forward_partial(halo, vol, kernel, pair, groups):
     planes, rows, chans, cols = vol.shape
     taps, _, chans_out = kernel.shape
     rows_out, cols_out = rows // 2, cols // 2
     share = chans_out // groups
     kbig = jnp.transpose(kernel, (2, 0, 1)).reshape(chans_out, taps * chans)
     flops = 2 * (planes + 1) * rows * chans * cols * 3 * cols_out + 2 * rows_out * chans_out * taps * chans * cols_out
+    sent = jax.ShapeDtypeStruct((1 + pair.shape[0], rows_out, share, cols_out), jnp.float32)
     return pl.pallas_call(
         forward_rows,
-        out_shape=[jax.ShapeDtypeStruct((rows_out, share, cols_out), jnp.float32)] * groups,
-        in_specs=[pl.BlockSpec(memory_space=pltpu.VMEM)] * 3,
+        out_shape=[jax.ShapeDtypeStruct((rows_out, share, cols_out), jnp.float32)] + [sent] * (groups - 1),
+        in_specs=[pl.BlockSpec(memory_space=pltpu.VMEM)] * 4,
         out_specs=[pl.BlockSpec(memory_space=pltpu.VMEM)] * groups,
         scratch_shapes=[pltpu.VMEM((planes + 1, rows, chans, 3 * cols_out), vol.dtype)],
         cost_estimate=pl.CostEstimate(flops=flops, bytes_accessed=2 * 4 * vol.size, transcendentals=0),
-    )(halo, vol, kbig)
-
-
-def backward_rows(*refs):
-    groups = (len(refs) - 3)
-    cot_refs, k_ref, out_ref, up_ref = refs[:groups], refs[groups], refs[groups + 1], refs[groups + 2]
-    planes, rows_out, share, cols_out = cot_refs[0].shape
+    )(halo, vol, kbig, pair)
+
+
+def backward_rows(pair_ref, *refs):
+    groups = len(refs) - 4
+    recv_refs = refs[:groups - 1]
+    own_ref, k_ref, out_ref, resp_ref, up_ref = refs[groups - 1:]
+    planes, rows_out, share, cols_out = pair_ref.shape
     rows = out_ref.shape[1]
     cols = out_ref.shape[3]
+    total = own_ref[...]
+    for recv_ref in recv_refs:
+        total = total + recv_ref[0]
+    resp_ref[...] = total.astype(resp_ref.dtype)
     tsel = spread_matrix(cols_out, cols, True)
-    for k, cot_ref in enumerate(cot_refs):
-        flat = cot_ref[...].reshape(planes * rows_out * share, cols_out)
+    for q in range(groups):
+        if q == 0:
+            piece = pair_ref[...]
+        else:
+            piece = recv_refs[groups - q - 1][1:].astype(up_ref.dtype)
+        flat = piece.reshape(planes * rows_out * share, cols_out)
         spread = jnp.dot(flat, tsel, preferred_element_type=jnp.float32)
-        up_ref[:, :, k * share:(k + 1) * share, :] = spread.astype(up_ref.dtype).reshape(planes, rows_out, share, 3 * cols)
+        up_ref[:, :, q * share:(q + 1) * share, :] = spread.astype(up_ref.dtype).reshape(planes, rows_out, share, 3 * cols)
     for depth in range(2):
         sources = [(1, 0)] if depth == 0 else [(2, 0), (0, 1)]
         for row in range(rows):
@@ -130,20 +144,24 @@
             out_ref[depth, row] = jnp.dot(lhs, rhs, preferred_element_type=jnp.float32).astype(out_ref.dtype)
 
 
-def backward_grad(pieces, kernel):
-    planes, rows_out, share, cols_out = pieces[0].shape
-    chans_out = share * len(pieces)
+def backward_grad(pair, received, own, kernel):
+    planes, rows_out, share, cols_out = pair.shape
+    groups = len(received) + 1
+    chans_out = share * groups
     taps, chans, _ = kernel.shape
     rows, cols = 2 * rows_out, 2 * cols_out
     flops = 2 * planes * rows_out * chans_out * cols_out * 3 * cols + 2 * 2 * rows * chans * 9 * chans_out * cols
     return pl.pallas_call(
         backward_rows,
-        out_shape=jax.ShapeDtypeStruct((2, rows, chans, cols), kernel.dtype),
-        in_specs=[pl.BlockSpec(memory_space=pltpu.VMEM)] * (len(pieces) + 1),
-        out_specs=pl.BlockSpec(memory_space=pltpu.VMEM),
+        out_shape=[
+            jax.ShapeDtypeStruct((2, rows, chans, cols), kernel.dtype),
+            jax.ShapeDtypeStruct(own.shape, kernel.dtype),
+        ],
+        in_specs=[pl.BlockSpec(memory_space=pltpu.VMEM)] * (groups + 2),
+        out_specs=[pl.BlockSpec(memory_space=pltpu.VMEM)] * 2,
         scratch_shapes=[pltpu.VMEM((planes, rows_out, chans_out, 3 * cols), kernel.dtype)],
         cost_estimate=pl.CostEstimate(flops=flops, bytes_accessed=2 * planes * rows_out * chans_out * cols_out + 2 * 2 * rows * chans * cols, transcendentals=0),
-    )(*pieces, kernel)
+    )(pair, *received, own, kernel)
 
 
 def chan_shift(block, shift):
@@ -162,15 +180,12 @@
     me = lax.axis_index("chan")
     kernel = jnp.roll(kernel, -me * share, axis=2)
     below = from_behind(volume[:, -1:], "space", 1)
-    chunks = forward_partial(below[0, 0], volume[0], kernel, groups)
-    pair = jnp.concatenate([cotangent, from_behind(cotangent, "space", -1)], axis=1)
-    chunks, pair = lax.optimization_barrier((chunks, pair))
-    total = chunks[0]
-    for k in range(1, groups):
-        total = total + chan_shift(chunks[k], k)
-    response = total.astype(jnp.bfloat16).reshape(count, planes_out, rows_out, share, cols_out)
-    pieces = [pair[0]] + [chan_shift(pair[0], -k) for k in range(1, groups)]
-    volume_grad = backward_grad(pieces, kernel).reshape(count, planes_in, rows_in, chans_in, cols_in)
+    pair = jnp.concatenate([cotangent, from_behind(cotangent, "space", -1)], axis=1)[0]
+    own, *sent = forward_partial(below[0, 0], volume[0], kernel, pair, groups)
+    received = [chan_shift(block, k) for k, block in enumerate(sent, start=1)]
+    volume_grad, response = backward_grad(pair, received, own, kernel)
+    response = response.reshape(count, planes_out, rows_out, share, cols_out)
+    volume_grad = volume_grad.reshape(count, planes_in, rows_in, chans_in, cols_in)
     return (response, volume_grad)
 
 

time: 58.4 us -> 74 us (1.27)
  the two profiles are of different devices: /device:TPU:512 before, /device:TPU:529 now
where the time goes in v7:
time: 74 us; the launch traced here: 73.7 us
  waiting for transfers between devices  36.3 us (49%)
  starting transfers between devices  24.1 us (33%)
  Pallas kernels  8.3 us (11%)
  local copies, waits for them, and re-layouts  3.32 us (4%)
  other arithmetic  0.88 us (1%)
  between operations  0.75 us (1%)
    ppermute x3, waiting for transfers between devices, chan_shift(): lax.ppermute(block, 'chan', [(i, (i + shift) % size) for i in range(size)])  31.2 us
    ppermute x2, starting transfers between devices, from_behind(): return lax.ppermute(block, axis, route)  13.4 us
    ppermute x3, starting transfers between devices, chan_shift(): lax.ppermute(block, 'chan', [(i, (i + shift) % size) for i in range(size)])  10.7 us
    ppermute x2, waiting for transfers between devices, from_behind(): return lax.ppermute(block, axis, route)  5.15 us
    pallas_call x1, Pallas kernels, backward_grad(): pl.pallas_call(backward_rows, out_shape=[jax.ShapeDtypeStruct((2, rows, c...  4.99 us
    pallas_call x1, Pallas kernels, forward_partial(): pl.pallas_call(forward_rows, out_shape=[jax.ShapeDtypeStruct((rows_out, s...  3.31 us
  transfers between devices with their start and end apart: 5, of which 5 were waited for; matrix products, arithmetic and copies ran while one was open for 2% of the time, Pallas kernels for 0%

profile of v7, /device:TPU:529, one launch (start us, length us, event | category | flops | bytes accessed | tf_op | source)
XLA Modules:
  0.0 73.7 jit_solution(17654568894667267042)
XLA Ops:
  0.6 0.0 copy-start.2
  0.6 0.0 copy-start.1
  0.6 1.0 %slice.3 = bf16[1,1,16,32,256]{4,3,2,1,0:T(8,128)(2,1)S(1)} slice(bf16[1,2,16,32,256]{4,3,2,1,0:T(8,128)(2,1)} %param.3), slice={[0:1], [1:2], [0:16], [0:32], [0:256]} | slice | bytes 524288 | tf_op jit(solution)/shard_map/slice | solution.py:182
  1.7 3.1 %collective-permute-start.1 = (bf16[1,1,16,32,256]{4,3,2,1,0:T(8,128)(2,1)S(1)}, bf16[1,1,16,32,256]{4,3,2,1,0:T(8,128)(2,1)S(1)}, u32[]{:S(2)}, u32[]{:S(2)}) collective-permute-start(bf16[1,1,16,32,256]{4,3,2,1,0:T(8,128)(2,1)S(1)} %slice.3), channel_id=1, source_target_pairs={{0,8},{8,16},{16,24},{24,32},{32,40},{40,48},{48,56},{56,64},{64,7... | collective-permute-start | bytes 786440 | tf_op jit(solution)/shard_map/ppermute | solution.py:12
  4.8 0.0 copy-done.2
  4.8 10.3 %collective-permute-start = (bf16[1,1,8,32,128]{4,3,2,1,0:T(8,128)(2,1)S(1)}, bf16[1,1,8,32,128]{4,3,2,1,0:T(8,128)(2,1)S(1)}, u32[]{:S(2)}, u32[]{:S(2)}) collective-permute-start(bf16[1,1,8,32,128]{4,3,2,1,0:T(8,128)(2,1)S(1)} %copy-done.2), channel_id=1, source_target_pairs={{8,0},{16,8},{24,16},{32,24},{40,32},{48,40},{56,48},{64,56},{72,6... | collective-permute-start | bytes 196616 | tf_op jit(solution)/shard_map/ppermute | solution.py:12
  15.1 0.0 copy-done.1
  15.1 0.2 fusion.refs_4_
  15.4 0.0 copy-start
  15.4 0.8 %copy.5.kbig_ref = bf16[128,864]{1,0:T(8,128)(2,1)} copy(bf16[128,864]{0,1:T(8,128)(2,1)S(1)} %bitcast.9) | data formatting | bytes 442368 | tf_op jit(solution)/shard_map/reshape | solution.py:95
  16.2 0.0 copy-done
  16.2 0.2 collective-permute-done
  16.4 0.7 maximum_bitcast_fusion.pair_ref
  17.1 5.0 %collective-permute-done.1 = bf16[1,1,16,32,256]{4,3,2,1,0:T(8,128)(2,1)S(1)} collective-permute-done((bf16[1,1,16,32,256]{4,3,2,1,0:T(8,128)(2,1)S(1)}, bf16[1,1,16,32,256]{4,3,2,1,0:T(8,128)(2,1)S(1)}, u32[]{:S(2)}, u32[]{:S(2)}) %collective-permute-start.1) | collective-permute-done | bytes 262176 | tf_op jit(solution)/shard_map/ppermute | solution.py:12
  22.0 0.0 copy-start.6
  22.0 0.7 copy-done.6
  22.7 3.3 %shard_map.50 = (f32[8,32,128]{2,1,0:T(8,128)}, f32[3,8,32,128]{3,2,1,0:T(8,128)}, f32[3,8,32,128]{3,2,1,0:T(8,128)}, f32[3,8,32,128]{3,2,1,0:T(8,128)}) custom-call(bf16[16,32,256]{2,1,0:T(8,128)(2,1)} %bitcast.11, bf16[2,16,32,256]{3,2,1,0:T(8,128)(2,1)} %bitcast.10, bf16[128,864]{1,0:T(8,128)(2,1)} %copy.5.kbig_ref, ...), custom_call_target="tpu_custom_call" | custom-call | flops 528482304 | bytes 2097152 | tf_op jit(solution)/shard_map/pallas_call | solution.py:98
  26.0 4.8 %collective-permute-start.2 = (f32[3,8,32,128]{3,2,1,0:T(8,128)}, f32[3,8,32,128]{3,2,1,0:T(8,128)S(1)}, u32[]{:S(2)}, u32[]{:S(2)}) collective-permute-start(f32[3,8,32,128]{3,2,1,0:T(8,128)} %get-tuple-element.8), channel_id=1, source_target_pairs={{0,2},{2,4},{4,6},{6,0},{1,3},{3,5},{5,7},{7,1},{8,10},{10,12},{12... | collective-permute-start | bytes 1179656 | tf_op jit(solution)/shard_map/ppermute | solution.py:169
  30.9 3.9 %collective-permute-start.3 = (f32[3,8,32,128]{3,2,1,0:T(8,128)}, f32[3,8,32,128]{3,2,1,0:T(8,128)S(1)}, u32[]{:S(2)}, u32[]{:S(2)}) collective-permute-start(f32[3,8,32,128]{3,2,1,0:T(8,128)} %get-tuple-element.9), channel_id=1, source_target_pairs={{0,4},{2,6},{4,0},{6,2},{1,5},{3,7},{5,1},{7,3},{8,12},{10,14},{12... | collective-permute-start | bytes 1179656 | tf_op jit(solution)/shard_map/ppermute | solution.py:169
  34.8 1.9 %collective-permute-start.4 = (f32[3,8,32,128]{3,2,1,0:T(8,128)}, f32[3,8,32,128]{3,2,1,0:T(8,128)S(1)}, u32[]{:S(2)}, u32[]{:S(2)}) collective-permute-start(f32[3,8,32,128]{3,2,1,0:T(8,128)} %get-tuple-element.10), channel_id=1, source_target_pairs={{0,6},{2,0},{4,2},{6,4},{1,7},{3,1},{5,3},{7,5},{8,14},{10,8},{12,... | collective-permute-start | bytes 1179656 | tf_op jit(solution)/shard_map/ppermute | solution.py:169
  36.7 1.1 %collective-permute-done.2.refs_0_ = f32[3,8,32,128]{3,2,1,0:T(8,128)S(1)} collective-permute-done((f32[3,8,32,128]{3,2,1,0:T(8,128)}, f32[3,8,32,128]{3,2,1,0:T(8,128)S(1)}, u32[]{:S(2)}, u32[]{:S(2)}) %collective-permute-start.2) | collective-permute-done | bytes 393248 | tf_op jit(solution)/shard_map/ppermute | solution.py:169
  37.8 0.0 copy-start.3
  37.8 23.7 %collective-permute-done.3.refs_1_ = f32[3,8,32,128]{3,2,1,0:T(8,128)S(1)} collective-permute-done((f32[3,8,32,128]{3,2,1,0:T(8,128)}, f32[3,8,32,128]{3,2,1,0:T(8,128)S(1)}, u32[]{:S(2)}, u32[]{:S(2)}) %collective-permute-start.3) | collective-permute-done | bytes 393248 | tf_op jit(solution)/shard_map/ppermute | solution.py:169
  61.5 0.0 copy-start.4
  61.5 6.4 %collective-permute-done.4.refs_2_ = f32[3,8,32,128]{3,2,1,0:T(8,128)S(1)} collective-permute-done((f32[3,8,32,128]{3,2,1,0:T(8,128)}, f32[3,8,32,128]{3,2,1,0:T(8,128)S(1)}, u32[]{:S(2)}, u32[]{:S(2)}) %collective-permute-start.4) | collective-permute-done | bytes 393248 | tf_op jit(solution)/shard_map/ppermute | solution.py:169
  67.9 0.0 copy-start.5
  67.9 0.0 copy-done.3
  67.9 0.0 copy-done.4
  67.9 0.7 %copy-done.5 = f32[3,8,32,128]{3,2,1,0:T(8,128)} copy-done((f32[3,8,32,128]{3,2,1,0:T(8,128)}, f32[3,8,32,128]{3,2,1,0:T(8,128)S(1)}, u32[]{:S(2)}) %copy-start.5) | copy-done | bytes 393240
  68.7 5.0 %shard_map.51 = (bf16[2,16,32,256]{3,2,1,0:T(8,128)(2,1)}, bf16[8,32,128]{2,1,0:T(8,128)(2,1)}) custom-call(bf16[2,8,32,128]{3,2,1,0:T(8,128)(2,1)} %maximum_bitcast_fusion.pair_ref, f32[3,8,32,128]{3,2,1,0:T(8,128)} %copy-done.3, f32[3,8,32,128]{3,2,1,0:T(8,128)} %copy-done.4, f32[3,8,32,128]{3,2,1,0:T(8,128)} %copy-done.5, ...), custom_call_target="tpu_custom_call" | custom-call | flops 1006632960 | bytes 1048576 | tf_op jit(solution)/shard_map/pallas_call | solution.py:154
Async XLA Ops:
  0.6 4.2 %copy-start.2 = (bf16[1,1,8,32,128]{4,3,2,1,0:T(8,128)(2,1)S(1)}, bf16[1,1,8,32,128]{4,3,2,1,0:T(8,128)(2,1)}, u32[]{:S(2)}) copy-start(bf16[1,1,8,32,128]{4,3,2,1,0:T(8,128)(2,1)} %param.5) | copy-start | bytes 196612
  0.6 14.5 %copy-start.1 = (bf16[27,32,128]{2,1,0:T(8,128)(2,1)S(1)}, bf16[27,32,128]{2,1,0:T(8,128)(2,1)}, u32[]{:S(2)}) copy-start(bf16[27,32,128]{2,1,0:T(8,128)(2,1)} %param.4) | copy-start | bytes 663556
  1.7 20.4 %collective-permute-start.1 = (bf16[1,1,16,32,256]{4,3,2,1,0:T(8,128)(2,1)S(1)}, bf16[1,1,16,32,256]{4,3,2,1,0:T(8,128)(2,1)S(1)}, u32[]{:S(2)}, u32[]{:S(2)}) collective-permute-start(bf16[1,1,16,32,256]{4,3,2,1,0:T(8,128)(2,1)S(1)} %slice.3), channel_id=1, source_target_pairs={{0,8},{8,16},{16,24},{24,32},{32,40},{40,48},{48,56},{56,64},{64,7... | collective-permute-start | bytes 786440 | tf_op jit(solution)/shard_map/ppermute | solution.py:12
  4.8 11.6 %collective-permute-start = (bf16[1,1,8,32,128]{4,3,2,1,0:T(8,128)(2,1)S(1)}, bf16[1,1,8,32,128]{4,3,2,1,0:T(8,128)(2,1)S(1)}, u32[]{:S(2)}, u32[]{:S(2)}) collective-permute-start(bf16[1,1,8,32,128]{4,3,2,1,0:T(8,128)(2,1)S(1)} %copy-done.2), channel_id=1, source_target_pairs={{8,0},{16,8},{24,16},{32,24},{40,32},{48,40},{56,48},{64,56},{72,6... | collective-permute-start | bytes 196616 | tf_op jit(solution)/shard_map/ppermute | solution.py:12
  15.4 0.9 %copy-start = (bf16[27,32,128]{2,1,0:T(8,128)(2,1)}, bf16[27,32,128]{2,1,0:T(8,128)(2,1)S(1)}, u32[]{:S(2)}) copy-start(bf16[27,32,128]{2,1,0:T(8,128)(2,1)S(1)} %fusion.refs_4_) | copy-start | bytes 663556
  22.0 0.7 copy-start.6
  26.0 11.8 %collective-permute-start.2 = (f32[3,8,32,128]{3,2,1,0:T(8,128)}, f32[3,8,32,128]{3,2,1,0:T(8,128)S(1)}, u32[]{:S(2)}, u32[]{:S(2)}) collective-permute-start(f32[3,8,32,128]{3,2,1,0:T(8,128)} %get-tuple-element.8), channel_id=1, source_target_pairs={{0,2},{2,4},{4,6},{6,0},{1,3},{3,5},{5,7},{7,1},{8,10},{10,12},{12... | collective-permute-start | bytes 1179656 | tf_op jit(solution)/shard_map/ppermute | solution.py:169
  30.9 30.7 %collective-permute-start.3 = (f32[3,8,32,128]{3,2,1,0:T(8,128)}, f32[3,8,32,128]{3,2,1,0:T(8,128)S(1)}, u32[]{:S(2)}, u32[]{:S(2)}) collective-permute-start(f32[3,8,32,128]{3,2,1,0:T(8,128)} %get-tuple-element.9), channel_id=1, source_target_pairs={{0,4},{2,6},{4,0},{6,2},{1,5},{3,7},{5,1},{7,3},{8,12},{10,14},{12... | collective-permute-start | bytes 1179656 | tf_op jit(solution)/shard_map/ppermute | solution.py:169
  34.8 33.1 %collective-permute-start.4 = (f32[3,8,32,128]{3,2,1,0:T(8,128)}, f32[3,8,32,128]{3,2,1,0:T(8,128)S(1)}, u32[]{:S(2)}, u32[]{:S(2)}) collective-permute-start(f32[3,8,32,128]{3,2,1,0:T(8,128)} %get-tuple-element.10), channel_id=1, source_target_pairs={{0,6},{2,0},{4,2},{6,4},{1,7},{3,1},{5,3},{7,5},{8,14},{10,8},{12,... | collective-permute-start | bytes 1179656 | tf_op jit(solution)/shard_map/ppermute | solution.py:169
  37.8 30.1 %copy-start.3 = (f32[3,8,32,128]{3,2,1,0:T(8,128)}, f32[3,8,32,128]{3,2,1,0:T(8,128)S(1)}, u32[]{:S(2)}) copy-start(f32[3,8,32,128]{3,2,1,0:T(8,128)S(1)} %collective-permute-done.2.refs_0_) | copy-start | bytes 1179652
  61.5 6.4 %copy-start.4 = (f32[3,8,32,128]{3,2,1,0:T(8,128)}, f32[3,8,32,128]{3,2,1,0:T(8,128)S(1)}, u32[]{:S(2)}) copy-start(f32[3,8,32,128]{3,2,1,0:T(8,128)S(1)} %collective-permute-done.3.refs_1_) | copy-start | bytes 1179652
  67.9 0.7 %copy-start.5 = (f32[3,8,32,128]{3,2,1,0:T(8,128)}, f32[3,8,32,128]{3,2,1,0:T(8,128)S(1)}, u32[]{:S(2)}) copy-start(f32[3,8,32,128]{3,2,1,0:T(8,128)S(1)} %collective-permute-done.4.refs_2_) | copy-start | bytes 1179652

commit v8 on v6

--- a/solution.py
+++ b/solution.py
@@ -101,16 +101,20 @@
 
 
 def backward_rows(*refs):
-    groups = (len(refs) - 3)
-    cot_refs, k_ref, out_ref, up_ref = refs[:groups], refs[groups], refs[groups + 1], refs[groups + 2]
-    planes, rows_out, share, cols_out = cot_refs[0].shape
+    groups = len(refs) - 4
+    cot_refs, next_ref, k_ref, out_ref, up_ref = refs[:groups], refs[groups], refs[groups + 1], refs[groups + 2], refs[groups + 3]
+    rows_out, share, cols_out = cot_refs[0].shape
+    chans_out = next_ref.shape[1]
     rows = out_ref.shape[1]
     cols = out_ref.shape[3]
     tsel = spread_matrix(cols_out, cols, True)
     for k, cot_ref in enumerate(cot_refs):
-        flat = cot_ref[...].reshape(planes * rows_out * share, cols_out)
+        flat = cot_ref[...].reshape(rows_out * share, cols_out)
         spread = jnp.dot(flat, tsel, preferred_element_type=jnp.float32)
-        up_ref[:, :, k * share:(k + 1) * share, :] = spread.astype(up_ref.dtype).reshape(planes, rows_out, share, 3 * cols)
+        up_ref[0, :, k * share:(k + 1) * share, :] = spread.astype(up_ref.dtype).reshape(rows_out, share, 3 * cols)
+    flat = next_ref[...].reshape(rows_out * chans_out, cols_out)
+    spread = jnp.dot(flat, tsel, preferred_element_type=jnp.float32)
+    up_ref[1] = spread.astype(up_ref.dtype).reshape(rows_out, chans_out, 3 * cols)
     for depth in range(2):
         sources = [(1, 0)] if depth == 0 else [(2, 0), (0, 1)]
         for row in range(rows):
@@ -130,8 +134,9 @@
             out_ref[depth, row] = jnp.dot(lhs, rhs, preferred_element_type=jnp.float32).astype(out_ref.dtype)
 
 
-def backward_grad(pieces, kernel):
-    planes, rows_out, share, cols_out = pieces[0].shape
+def backward_grad(pieces, following, kernel):
+    planes = 2
+    rows_out, share, cols_out = pieces[0].shape
     chans_out = share * len(pieces)
     taps, chans, _ = kernel.shape
     rows, cols = 2 * rows_out, 2 * cols_out
@@ -139,11 +144,11 @@
     return pl.pallas_call(
         backward_rows,
         out_shape=jax.ShapeDtypeStruct((2, rows, chans, cols), kernel.dtype),
-        in_specs=[pl.BlockSpec(memory_space=pltpu.VMEM)] * (len(pieces) + 1),
+        in_specs=[pl.BlockSpec(memory_space=pltpu.VMEM)] * (len(pieces) + 2),
         out_specs=pl.BlockSpec(memory_space=pltpu.VMEM),
         scratch_shapes=[pltpu.VMEM((planes, rows_out, chans_out, 3 * cols), kernel.dtype)],
         cost_estimate=pl.CostEstimate(flops=flops, bytes_accessed=2 * planes * rows_out * chans_out * cols_out + 2 * 2 * rows * chans * cols, transcendentals=0),
-    )(*pieces, kernel)
+    )(*pieces, following, kernel)
 
 
 def chan_shift(block, shift):
@@ -161,16 +166,17 @@
     share = chans_out // groups
     me = lax.axis_index("chan")
     kernel = jnp.roll(kernel, -me * share, axis=2)
+    own = cotangent[0, 0]
+    pieces = [own] + [chan_shift(own, -k) for k in range(1, groups)]
     below = from_behind(volume[:, -1:], "space", 1)
+    pieces, below = lax.optimization_barrier((pieces, below))
     chunks = forward_partial(below[0, 0], volume[0], kernel, groups)
-    pair = jnp.concatenate([cotangent, from_behind(cotangent, "space", -1)], axis=1)
-    chunks, pair = lax.optimization_barrier((chunks, pair))
     total = chunks[0]
     for k in range(1, groups):
         total = total + chan_shift(chunks[k], k)
     response = total.astype(jnp.bfloat16).reshape(count, planes_out, rows_out, share, cols_out)
-    pieces = [pair[0]] + [chan_shift(pair[0], -k) for k in range(1, groups)]
-    volume_grad = backward_grad(pieces, kernel).reshape(count, planes_in, rows_in, chans_in, cols_in)
+    following = from_behind(jnp.concatenate(pieces, axis=1), "space", -1)
+    volume_grad = backward_grad(pieces, following, kernel).reshape(count, planes_in, rows_in, chans_in, cols_in)
     return (response, volume_grad)
 
 

time: 58.4 us -> 68.8 us (1.18)
  the two profiles are of different devices: /device:TPU:512 before, /device:TPU:782 now
where the time goes in v8:
time: 68.8 us; the launch traced here: 68.4 us
  starting transfers between devices  29.8 us (43%)
  waiting for transfers between devices  25.5 us (37%)
  Pallas kernels  8.13 us (12%)
  local copies, waits for them, and re-layouts  3.3 us (5%)
  other arithmetic  0.91 us (1%)
  between operations  0.82 us (1%)
    ppermute x2, waiting for transfers between devices, from_behind(): return lax.ppermute(block, axis, route)  20.7 us
    ppermute x6, starting transfers between devices, chan_shift(): lax.ppermute(block, 'chan', [(i, (i + shift) % size) for i in range(size)])  19.9 us
    ppermute x2, starting transfers between devices, from_behind(): return lax.ppermute(block, axis, route)  9.91 us
    pallas_call x1, Pallas kernels, backward_grad(): pl.pallas_call(backward_rows, out_shape=jax.ShapeDtypeStruct((2, rows, ch...  5.1 us
    ppermute x6, waiting for transfers between devices, chan_shift(): lax.ppermute(block, 'chan', [(i, (i + shift) % size) for i in range(size)])  4.81 us
    pallas_call x1, Pallas kernels, forward_partial(): pl.pallas_call(forward_rows, out_shape=[jax.ShapeDtypeStruct((rows_out, s...  3.02 us
    unnamed x18, local copies, waits for them, and re-layouts  1.45 us
  transfers between devices with their start and end apart: 8, of which 5 were waited for; matrix products, arithmetic and copies ran while one was open for 3% of the time, Pallas kernels for 0%

profile of v8, /device:TPU:782, one launch (start us, length us, event | category | flops | bytes accessed | tf_op | source)
XLA Modules:
  0.0 68.4 jit_solution(4555963156621625466)
XLA Ops:
  0.6 0.0 copy-start.3
  0.6 0.0 copy-start.1
  0.7 1.0 %slice.3 = bf16[1,1,16,32,256]{4,3,2,1,0:T(8,128)(2,1)S(1)} slice(bf16[1,2,16,32,256]{4,3,2,1,0:T(8,128)(2,1)} %param.3), slice={[0:1], [1:2], [0:16], [0:32], [0:256]} | slice | bytes 524288 | tf_op jit(solution)/shard_map/slice | solution.py:171
  1.7 8.0 %collective-permute-start.3 = (bf16[1,1,16,32,256]{4,3,2,1,0:T(8,128)(2,1)S(1)}, bf16[1,1,16,32,256]{4,3,2,1,0:T(8,128)(2,1)S(1)}, u32[]{:S(2)}, u32[]{:S(2)}) collective-permute-start(bf16[1,1,16,32,256]{4,3,2,1,0:T(8,128)(2,1)S(1)} %slice.3), channel_id=1, source_target_pairs={{0,8},{8,16},{16,24},{24,32},{32,40},{40,48},{48,56},{56,64},{64,7... | collective-permute-start | bytes 786440 | tf_op jit(solution)/shard_map/ppermute | solution.py:12
  9.7 0.0 copy-done.3
  9.7 2.7 %collective-permute-start.2 = (bf16[8,32,128]{2,1,0:T(8,128)(2,1)S(1)}, bf16[8,32,128]{2,1,0:T(8,128)(2,1)S(1)}, u32[]{:S(2)}, u32[]{:S(2)}) collective-permute-start(bf16[8,32,128]{2,1,0:T(8,128)(2,1)S(1)} %bitcast.12), channel_id=1, source_target_pairs={{0,2},{2,4},{4,6},{6,0},{1,3},{3,5},{5,7},{7,1},{8,10},{10,12},{12... | collective-permute-start | bytes 196616 | tf_op jit(solution)/shard_map/ppermute | solution.py:156
  12.4 2.9 %collective-permute-start.1 = (bf16[8,32,128]{2,1,0:T(8,128)(2,1)S(1)}, bf16[8,32,128]{2,1,0:T(8,128)(2,1)S(1)}, u32[]{:S(2)}, u32[]{:S(2)}) collective-permute-start(bf16[8,32,128]{2,1,0:T(8,128)(2,1)S(1)} %bitcast.13), channel_id=1, source_target_pairs={{0,4},{2,6},{4,0},{6,2},{1,5},{3,7},{5,1},{7,3},{8,12},{10,14},{12... | collective-permute-start | bytes 196616 | tf_op jit(solution)/shard_map/ppermute | solution.py:156
  15.3 4.0 %collective-permute-start = (bf16[8,32,128]{2,1,0:T(8,128)(2,1)S(1)}, bf16[8,32,128]{2,1,0:T(8,128)(2,1)S(1)}, u32[]{:S(2)}, u32[]{:S(2)}) collective-permute-start(bf16[8,32,128]{2,1,0:T(8,128)(2,1)S(1)} %bitcast.14), channel_id=1, source_target_pairs={{0,6},{2,0},{4,2},{6,4},{1,7},{3,1},{5,3},{7,5},{8,14},{10,8},{12,... | collective-permute-start | bytes 196616 | tf_op jit(solution)/shard_map/ppermute | solution.py:156
  19.4 0.0 copy-done.1
  19.4 0.2 fusion.refs_5_
  19.6 0.0 copy-start
  19.6 0.8 %copy.5.kbig_ref = bf16[128,864]{1,0:T(8,128)(2,1)} copy(bf16[128,864]{0,1:T(8,128)(2,1)S(1)} %bitcast.9) | data formatting | bytes 442368 | tf_op jit(solution)/shard_map/reshape | solution.py:91
  20.5 0.0 copy-done
  20.5 0.0 collective-permute-done.2.refs_3_
  20.5 0.0 copy-start.4
  20.5 0.1 collective-permute-done.1.refs_2_
  20.5 0.0 copy-start.5
  20.6 1.5 %collective-permute-done.refs_1_ = bf16[8,32,128]{2,1,0:T(8,128)(2,1)S(1)} collective-permute-done((bf16[8,32,128]{2,1,0:T(8,128)(2,1)S(1)}, bf16[8,32,128]{2,1,0:T(8,128)(2,1)S(1)}, u32[]{:S(2)}, u32[]{:S(2)}) %collective-permute-start) | collective-permute-done | bytes 65568 | tf_op jit(solution)/shard_map/ppermute | solution.py:156
  22.0 0.0 copy-start.6
  22.0 0.0 collective-permute-done.3
  22.0 0.0 copy-start.7
  22.0 0.7 %copy-done.7 = bf16[1,1,16,32,256]{4,3,2,1,0:T(8,128)(2,1)} copy-done((bf16[1,1,16,32,256]{4,3,2,1,0:T(8,128)(2,1)}, bf16[1,1,16,32,256]{4,3,2,1,0:T(8,128)(2,1)S(1)}, u32[]{:S(2)}) %copy-start.7) | copy-done | bytes 262168
  22.8 3.0 %shard_map.50 = (f32[8,32,128]{2,1,0:T(8,128)}, f32[8,32,128]{2,1,0:T(8,128)}, f32[8,32,128]{2,1,0:T(8,128)}, f32[8,32,128]{2,1,0:T(8,128)}) custom-call(bf16[16,32,256]{2,1,0:T(8,128)(2,1)} %bitcast.16, bf16[2,16,32,256]{3,2,1,0:T(8,128)(2,1)} %bitcast.10, bf16[128,864]{1,0:T(8,128)(2,1)} %copy.5.kbig_ref), custom_call_target="tpu_custom_call" | custom-call | flops 528482304 | bytes 2097152 | tf_op jit(solution)/shard_map/pallas_call | solution.py:93
  25.8 3.9 %collective-permute-start.4 = (f32[8,32,128]{2,1,0:T(8,128)}, f32[8,32,128]{2,1,0:T(8,128)S(1)}, u32[]{:S(2)}, u32[]{:S(2)}) collective-permute-start(f32[8,32,128]{2,1,0:T(8,128)} %get-tuple-element.13), channel_id=1, source_target_pairs={{0,2},{2,4},{4,6},{6,0},{1,3},{3,5},{5,7},{7,1},{8,10},{10,12},{12... | collective-permute-start | bytes 393224 | tf_op jit(solution)/shard_map/ppermute | solution.py:156
  29.7 3.8 %collective-permute-start.5 = (f32[8,32,128]{2,1,0:T(8,128)}, f32[8,32,128]{2,1,0:T(8,128)S(1)}, u32[]{:S(2)}, u32[]{:S(2)}) collective-permute-start(f32[8,32,128]{2,1,0:T(8,128)} %get-tuple-element.14), channel_id=1, source_target_pairs={{0,4},{2,6},{4,0},{6,2},{1,5},{3,7},{5,1},{7,3},{8,12},{10,14},{12... | collective-permute-start | bytes 393224 | tf_op jit(solution)/shard_map/ppermute | solution.py:156
  33.5 0.0 copy-start.2
  33.5 2.5 %collective-permute-start.6 = (f32[8,32,128]{2,1,0:T(8,128)}, f32[8,32,128]{2,1,0:T(8,128)S(1)}, u32[]{:S(2)}, u32[]{:S(2)}) collective-permute-start(f32[8,32,128]{2,1,0:T(8,128)} %get-tuple-element.15), channel_id=1, source_target_pairs={{0,6},{2,0},{4,2},{6,4},{1,7},{3,1},{5,3},{7,5},{8,14},{10,8},{12,... | collective-permute-start | bytes 393224 | tf_op jit(solution)/shard_map/ppermute | solution.py:156
  36.1 0.0 copy-done.4
  36.1 0.0 copy-done.5
  36.1 0.0 copy-done.6
  36.1 1.9 %collective-permute-start.7 = (bf16[8,128,128]{2,1,0:T(8,128)(2,1)S(1)}, bf16[8,128,128]{2,1,0:T(8,128)(2,1)S(1)}, u32[]{:S(2)}, u32[]{:S(2)}) collective-permute-start(bf16[8,128,128]{2,1,0:T(8,128)(2,1)S(1)} %pad_maximum_fusion), channel_id=1, source_target_pairs={{8,0},{16,8},{24,16},{32,24},{40,32},{48,40},{56,48},{64,56},{72,6... | collective-permute-start | bytes 786440 | tf_op jit(solution)/shard_map/ppermute | solution.py:12
  38.0 0.0 collective-permute-done.4
  38.0 2.1 %collective-permute-done.5 = f32[8,32,128]{2,1,0:T(8,128)S(1)} collective-permute-done((f32[8,32,128]{2,1,0:T(8,128)}, f32[8,32,128]{2,1,0:T(8,128)S(1)}, u32[]{:S(2)}, u32[]{:S(2)}) %collective-permute-start.5) | collective-permute-done | bytes 131104 | tf_op jit(solution)/shard_map/ppermute | solution.py:156
  40.1 1.2 %collective-permute-done.6 = f32[8,32,128]{2,1,0:T(8,128)S(1)} collective-permute-done((f32[8,32,128]{2,1,0:T(8,128)}, f32[8,32,128]{2,1,0:T(8,128)S(1)}, u32[]{:S(2)}, u32[]{:S(2)}) %collective-permute-start.6) | collective-permute-done | bytes 131104 | tf_op jit(solution)/shard_map/ppermute | solution.py:156
  41.3 0.0 copy-done.2
  41.3 0.7 fusion.1
  42.0 20.7 %collective-permute-done.7.refs_4_ = bf16[8,128,128]{2,1,0:T(8,128)(2,1)S(1)} collective-permute-done((bf16[8,128,128]{2,1,0:T(8,128)(2,1)S(1)}, bf16[8,128,128]{2,1,0:T(8,128)(2,1)S(1)}, u32[]{:S(2)}, u32[]{:S(2)}) %collective-permute-start.7) | collective-permute-done | bytes 262176 | tf_op jit(solution)/shard_map/ppermute | solution.py:12
  62.6 0.0 copy-start.8
  62.6 0.7 %copy-done.8 = bf16[8,128,128]{2,1,0:T(8,128)(2,1)} copy-done((bf16[8,128,128]{2,1,0:T(8,128)(2,1)}, bf16[8,128,128]{2,1,0:T(8,128)(2,1)S(1)}, u32[]{:S(2)}) %copy-start.8) | copy-done | bytes 262168
  63.3 5.1 %shard_map.51 = bf16[2,16,32,256]{3,2,1,0:T(8,128)(2,1)} custom-call(bf16[8,32,128]{2,1,0:T(8,128)(2,1)} %bitcast.11, bf16[8,32,128]{2,1,0:T(8,128)(2,1)} %copy-done.6, bf16[8,32,128]{2,1,0:T(8,128)(2,1)} %copy-done.5, bf16[8,32,128]{2,1,0:T(8,128)(2,1)} %copy-done.4, bf16[8,128,128]{2,1,0:T(8,128)(2,1)} %copy-done.8, bf16[27,32,128]{2,1,0:T(8,128)(2,1)} %copy-done), custom_call_target="tpu_custom_call" | custom-call | flops 1006632960 | bytes 1048576 | tf_op jit(solution)/shard_map/pallas_call | solution.py:144
  (1 shorter events, 0.0 us)
Async XLA Ops:
  0.6 9.0 %copy-start.3 = (bf16[1,1,8,32,128]{4,3,2,1,0:T(8,128)(2,1)S(1)}, bf16[1,1,8,32,128]{4,3,2,1,0:T(8,128)(2,1)}, u32[]{:S(2)}) copy-start(bf16[1,1,8,32,128]{4,3,2,1,0:T(8,128)(2,1)} %param.5) | copy-start | bytes 196612
  0.6 18.8 %copy-start.1 = (bf16[27,32,128]{2,1,0:T(8,128)(2,1)S(1)}, bf16[27,32,128]{2,1,0:T(8,128)(2,1)}, u32[]{:S(2)}) copy-start(bf16[27,32,128]{2,1,0:T(8,128)(2,1)} %param.4) | copy-start | bytes 663556
  1.7 20.4 %collective-permute-start.3 = (bf16[1,1,16,32,256]{4,3,2,1,0:T(8,128)(2,1)S(1)}, bf16[1,1,16,32,256]{4,3,2,1,0:T(8,128)(2,1)S(1)}, u32[]{:S(2)}, u32[]{:S(2)}) collective-permute-start(bf16[1,1,16,32,256]{4,3,2,1,0:T(8,128)(2,1)S(1)} %slice.3), channel_id=1, source_target_pairs={{0,8},{8,16},{16,24},{24,32},{32,40},{40,48},{48,56},{56,64},{64,7... | collective-permute-start | bytes 786440 | tf_op jit(solution)/shard_map/ppermute | solution.py:12
  9.7 10.8 %collective-permute-start.2 = (bf16[8,32,128]{2,1,0:T(8,128)(2,1)S(1)}, bf16[8,32,128]{2,1,0:T(8,128)(2,1)S(1)}, u32[]{:S(2)}, u32[]{:S(2)}) collective-permute-start(bf16[8,32,128]{2,1,0:T(8,128)(2,1)S(1)} %bitcast.12), channel_id=1, source_target_pairs={{0,2},{2,4},{4,6},{6,0},{1,3},{3,5},{5,7},{7,1},{8,10},{10,12},{12... | collective-permute-start | bytes 196616 | tf_op jit(solution)/shard_map/ppermute | solution.py:156
  12.4 8.2 %collective-permute-start.1 = (bf16[8,32,128]{2,1,0:T(8,128)(2,1)S(1)}, bf16[8,32,128]{2,1,0:T(8,128)(2,1)S(1)}, u32[]{:S(2)}, u32[]{:S(2)}) collective-permute-start(bf16[8,32,128]{2,1,0:T(8,128)(2,1)S(1)} %bitcast.13), channel_id=1, source_target_pairs={{0,4},{2,6},{4,0},{6,2},{1,5},{3,7},{5,1},{7,3},{8,12},{10,14},{12... | collective-permute-start | bytes 196616 | tf_op jit(solution)/shard_map/ppermute | solution.py:156
  15.3 6.7 %collective-permute-start = (bf16[8,32,128]{2,1,0:T(8,128)(2,1)S(1)}, bf16[8,32,128]{2,1,0:T(8,128)(2,1)S(1)}, u32[]{:S(2)}, u32[]{:S(2)}) collective-permute-start(bf16[8,32,128]{2,1,0:T(8,128)(2,1)S(1)} %bitcast.14), channel_id=1, source_target_pairs={{0,6},{2,0},{4,2},{6,4},{1,7},{3,1},{5,3},{7,5},{8,14},{10,8},{12,... | collective-permute-start | bytes 196616 | tf_op jit(solution)/shard_map/ppermute | solution.py:156
  19.6 0.8 %copy-start = (bf16[27,32,128]{2,1,0:T(8,128)(2,1)}, bf16[27,32,128]{2,1,0:T(8,128)(2,1)S(1)}, u32[]{:S(2)}) copy-start(bf16[27,32,128]{2,1,0:T(8,128)(2,1)S(1)} %fusion.refs_5_) | copy-start | bytes 663556
  20.5 15.6 %copy-start.4 = (bf16[8,32,128]{2,1,0:T(8,128)(2,1)}, bf16[8,32,128]{2,1,0:T(8,128)(2,1)S(1)}, u32[]{:S(2)}) copy-start(bf16[8,32,128]{2,1,0:T(8,128)(2,1)S(1)} %collective-permute-done.2.refs_3_) | copy-start | bytes 196612
  20.5 15.5 %copy-start.5 = (bf16[8,32,128]{2,1,0:T(8,128)(2,1)}, bf16[8,32,128]{2,1,0:T(8,128)(2,1)S(1)}, u32[]{:S(2)}) copy-start(bf16[8,32,128]{2,1,0:T(8,128)(2,1)S(1)} %collective-permute-done.1.refs_2_) | copy-start | bytes 196612
  22.0 14.0 %copy-start.6 = (bf16[8,32,128]{2,1,0:T(8,128)(2,1)}, bf16[8,32,128]{2,1,0:T(8,128)(2,1)S(1)}, u32[]{:S(2)}) copy-start(bf16[8,32,128]{2,1,0:T(8,128)(2,1)S(1)} %collective-permute-done.refs_1_) | copy-start | bytes 196612
  22.0 0.7 %copy-start.7 = (bf16[1,1,16,32,256]{4,3,2,1,0:T(8,128)(2,1)}, bf16[1,1,16,32,256]{4,3,2,1,0:T(8,128)(2,1)S(1)}, u32[]{:S(2)}) copy-start(bf16[1,1,16,32,256]{4,3,2,1,0:T(8,128)(2,1)S(1)} %collective-permute-done.3) | copy-start | bytes 786436
  25.8 12.3 %collective-permute-start.4 = (f32[8,32,128]{2,1,0:T(8,128)}, f32[8,32,128]{2,1,0:T(8,128)S(1)}, u32[]{:S(2)}, u32[]{:S(2)}) collective-permute-start(f32[8,32,128]{2,1,0:T(8,128)} %get-tuple-element.13), channel_id=1, source_target_pairs={{0,2},{2,4},{4,6},{6,0},{1,3},{3,5},{5,7},{7,1},{8,10},{10,12},{12... | collective-permute-start | bytes 393224 | tf_op jit(solution)/shard_map/ppermute | solution.py:156
  29.7 10.4 %collective-permute-start.5 = (f32[8,32,128]{2,1,0:T(8,128)}, f32[8,32,128]{2,1,0:T(8,128)S(1)}, u32[]{:S(2)}, u32[]{:S(2)}) collective-permute-start(f32[8,32,128]{2,1,0:T(8,128)} %get-tuple-element.14), channel_id=1, source_target_pairs={{0,4},{2,6},{4,0},{6,2},{1,5},{3,7},{5,1},{7,3},{8,12},{10,14},{12... | collective-permute-start | bytes 393224 | tf_op jit(solution)/shard_map/ppermute | solution.py:156
  33.5 7.8 %copy-start.2 = (f32[8,32,128]{2,1,0:T(8,128)S(1)}, f32[8,32,128]{2,1,0:T(8,128)}, u32[]{:S(2)}) copy-start(f32[8,32,128]{2,1,0:T(8,128)} %get-tuple-element.12) | copy-start | bytes 393220
  33.5 7.7 %collective-permute-start.6 = (f32[8,32,128]{2,1,0:T(8,128)}, f32[8,32,128]{2,1,0:T(8,128)S(1)}, u32[]{:S(2)}, u32[]{:S(2)}) collective-permute-start(f32[8,32,128]{2,1,0:T(8,128)} %get-tuple-element.15), channel_id=1, source_target_pairs={{0,6},{2,0},{4,2},{6,4},{1,7},{3,1},{5,3},{7,5},{8,14},{10,8},{12,... | collective-permute-start | bytes 393224 | tf_op jit(solution)/shard_map/ppermute | solution.py:156
  36.1 26.5 %collective-permute-start.7 = (bf16[8,128,128]{2,1,0:T(8,128)(2,1)S(1)}, bf16[8,128,128]{2,1,0:T(8,128)(2,1)S(1)}, u32[]{:S(2)}, u32[]{:S(2)}) collective-permute-start(bf16[8,128,128]{2,1,0:T(8,128)(2,1)S(1)} %pad_maximum_fusion), channel_id=1, source_target_pairs={{8,0},{16,8},{24,16},{32,24},{40,32},{48,40},{56,48},{64,56},{72,6... | collective-permute-start | bytes 786440 | tf_op jit(solution)/shard_map/ppermute | solution.py:12
  62.6 0.7 %copy-start.8 = (bf16[8,128,128]{2,1,0:T(8,128)(2,1)}, bf16[8,128,128]{2,1,0:T(8,128)(2,1)S(1)}, u32[]{:S(2)}) copy-start(bf16[8,128,128]{2,1,0:T(8,128)(2,1)S(1)} %collective-permute-done.7.refs_4_) | copy-start | bytes 786436

commit v9 on v6

--- a/solution.py
+++ b/solution.py
@@ -101,16 +101,19 @@
 
 
 def backward_rows(*refs):
-    groups = (len(refs) - 3)
-    cot_refs, k_ref, out_ref, up_ref = refs[:groups], refs[groups], refs[groups + 1], refs[groups + 2]
-    planes, rows_out, share, cols_out = cot_refs[0].shape
+    count = len(refs) - 3
+    cot_refs, k_ref, out_ref, up_ref = refs[:count], refs[count], refs[count + 1], refs[count + 2]
+    planes = 2
+    groups = count // planes
+    rows_out, share, cols_out = cot_refs[0].shape
     rows = out_ref.shape[1]
     cols = out_ref.shape[3]
     tsel = spread_matrix(cols_out, cols, True)
-    for k, cot_ref in enumerate(cot_refs):
-        flat = cot_ref[...].reshape(planes * rows_out * share, cols_out)
+    for n, cot_ref in enumerate(cot_refs):
+        plane, k = divmod(n, groups)
+        flat = cot_ref[...].reshape(rows_out * share, cols_out)
         spread = jnp.dot(flat, tsel, preferred_element_type=jnp.float32)
-        up_ref[:, :, k * share:(k + 1) * share, :] = spread.astype(up_ref.dtype).reshape(planes, rows_out, share, 3 * cols)
+        up_ref[plane, :, k * share:(k + 1) * share, :] = spread.astype(up_ref.dtype).reshape(rows_out, share, 3 * cols)
     for depth in range(2):
         sources = [(1, 0)] if depth == 0 else [(2, 0), (0, 1)]
         for row in range(rows):
@@ -131,8 +134,9 @@
 
 
 def backward_grad(pieces, kernel):
-    planes, rows_out, share, cols_out = pieces[0].shape
-    chans_out = share * len(pieces)
+    planes = 2
+    rows_out, share, cols_out = pieces[0].shape
+    chans_out = share * len(pieces) // planes
     taps, chans, _ = kernel.shape
     rows, cols = 2 * rows_out, 2 * cols_out
     flops = 2 * planes * rows_out * chans_out * cols_out * 3 * cols + 2 * 2 * rows * chans * 9 * chans_out * cols
@@ -161,15 +165,18 @@
     share = chans_out // groups
     me = lax.axis_index("chan")
     kernel = jnp.roll(kernel, -me * share, axis=2)
+    own = cotangent[0, 0]
+    own_pieces = [own] + [chan_shift(own, -k) for k in range(1, groups)]
+    following = from_behind(cotangent, "space", -1)[0, 0]
     below = from_behind(volume[:, -1:], "space", 1)
+    own_pieces, below = lax.optimization_barrier((own_pieces, below))
     chunks = forward_partial(below[0, 0], volume[0], kernel, groups)
-    pair = jnp.concatenate([cotangent, from_behind(cotangent, "space", -1)], axis=1)
-    chunks, pair = lax.optimization_barrier((chunks, pair))
+    chunks, following = lax.optimization_barrier((chunks, following))
     total = chunks[0]
     for k in range(1, groups):
         total = total + chan_shift(chunks[k], k)
     response = total.astype(jnp.bfloat16).reshape(count, planes_out, rows_out, share, cols_out)
-    pieces = [pair[0]] + [chan_shift(pair[0], -k) for k in range(1, groups)]
+    pieces = own_pieces + [following] + [chan_shift(following, -k) for k in range(1, groups)]
     volume_grad = backward_grad(pieces, kernel).reshape(count, planes_in, rows_in, chans_in, cols_in)
     return (response, volume_grad)
 

time: 58.4 us -> 63.8 us (1.092)
  the two profiles are of different devices: /device:TPU:512 before, /device:TPU:384 now
where the time goes in v9:
time: 63.8 us; the launch traced here: 63.3 us
  starting transfers between devices  44.2 us (69%)
  Pallas kernels  8.22 us (13%)
  waiting for transfers between devices  5.32 us (8%)
  local copies, waits for them, and re-layouts  3.82 us (6%)
  other arithmetic  0.89 us (1%)
  between operations  0.89 us (1%)
    ppermute x9, starting transfers between devices, chan_shift(): lax.ppermute(block, 'chan', [(i, (i + shift) % size) for i in range(size)])  31.4 us
    ppermute x2, starting transfers between devices, from_behind(): return lax.ppermute(block, axis, route)  12.8 us
    ppermute x9, waiting for transfers between devices, chan_shift(): lax.ppermute(block, 'chan', [(i, (i + shift) % size) for i in range(size)])  5.32 us
    pallas_call x1, Pallas kernels, backward_grad(): pl.pallas_call(backward_rows, out_shape=jax.ShapeDtypeStruct((2, rows, ch...  5.2 us
    pallas_call x1, Pallas kernels, forward_partial(): pl.pallas_call(forward_rows, out_shape=[jax.ShapeDtypeStruct((rows_out, s...  3.03 us
    unnamed x24, local copies, waits for them, and re-layouts  1.96 us
  transfers between devices with their start and end apart: 11, of which 3 were waited for; matrix products, arithmetic and copies ran while one was open for 2% of the time, Pallas kernels for 13%

profile of v9, /device:TPU:384, one launch (start us, length us, event | category | flops | bytes accessed | tf_op | source)
XLA Modules:
  0.0 63.3 jit_solution(12842190220374626802)
XLA Ops:
  0.6 0.0 copy-start.4
  0.6 0.0 copy-start.1
  0.7 1.0 %slice.3 = bf16[1,1,16,32,256]{4,3,2,1,0:T(8,128)(2,1)S(1)} slice(bf16[1,2,16,32,256]{4,3,2,1,0:T(8,128)(2,1)} %param.3), slice={[0:1], [1:2], [0:16], [0:32], [0:256]} | slice | bytes 524288 | tf_op jit(solution)/shard_map/slice | solution.py:171
  1.7 3.4 %collective-permute-start.3 = (bf16[1,1,16,32,256]{4,3,2,1,0:T(8,128)(2,1)S(1)}, bf16[1,1,16,32,256]{4,3,2,1,0:T(8,128)(2,1)S(1)}, u32[]{:S(2)}, u32[]{:S(2)}) collective-permute-start(bf16[1,1,16,32,256]{4,3,2,1,0:T(8,128)(2,1)S(1)} %slice.3), channel_id=1, source_target_pairs={{0,8},{8,16},{16,24},{24,32},{32,40},{40,48},{48,56},{56,64},{64,7... | collective-permute-start | bytes 786440 | tf_op jit(solution)/shard_map/ppermute | solution.py:12
  5.1 0.0 copy-done.4
  5.1 5.9 %collective-permute-start = (bf16[8,32,128]{2,1,0:T(8,128)(2,1)S(1)}, bf16[8,32,128]{2,1,0:T(8,128)(2,1)S(1)}, u32[]{:S(2)}, u32[]{:S(2)}) collective-permute-start(bf16[8,32,128]{2,1,0:T(8,128)(2,1)S(1)} %bitcast.14), channel_id=1, source_target_pairs={{0,6},{2,0},{4,2},{6,4},{1,7},{3,1},{5,3},{7,5},{8,14},{10,8},{12,... | collective-permute-start | bytes 196616 | tf_op jit(solution)/shard_map/ppermute | solution.py:155
  10.9 1.9 %collective-permute-start.1 = (bf16[8,32,128]{2,1,0:T(8,128)(2,1)S(1)}, bf16[8,32,128]{2,1,0:T(8,128)(2,1)S(1)}, u32[]{:S(2)}, u32[]{:S(2)}) collective-permute-start(bf16[8,32,128]{2,1,0:T(8,128)(2,1)S(1)} %bitcast.15), channel_id=1, source_target_pairs={{0,4},{2,6},{4,0},{6,2},{1,5},{3,7},{5,1},{7,3},{8,12},{10,14},{12... | collective-permute-start | bytes 196616 | tf_op jit(solution)/shard_map/ppermute | solution.py:155
  12.9 2.8 %collective-permute-start.2 = (bf16[8,32,128]{2,1,0:T(8,128)(2,1)S(1)}, bf16[8,32,128]{2,1,0:T(8,128)(2,1)S(1)}, u32[]{:S(2)}, u32[]{:S(2)}) collective-permute-start(bf16[8,32,128]{2,1,0:T(8,128)(2,1)S(1)} %bitcast.16), channel_id=1, source_target_pairs={{0,2},{2,4},{4,6},{6,0},{1,3},{3,5},{5,7},{7,1},{8,10},{10,12},{12... | collective-permute-start | bytes 196616 | tf_op jit(solution)/shard_map/ppermute | solution.py:155
  15.7 9.4 %collective-permute-start.4 = (bf16[1,1,8,32,128]{4,3,2,1,0:T(8,128)(2,1)S(1)}, bf16[1,1,8,32,128]{4,3,2,1,0:T(8,128)(2,1)S(1)}, u32[]{:S(2)}, u32[]{:S(2)}) collective-permute-start(bf16[1,1,8,32,128]{4,3,2,1,0:T(8,128)(2,1)S(1)} %copy-done.4), channel_id=1, source_target_pairs={{8,0},{16,8},{24,16},{32,24},{40,32},{48,40},{56,48},{64,56},{72,6... | collective-permute-start | bytes 196616 | tf_op jit(solution)/shard_map/ppermute | solution.py:12
  25.1 0.0 copy-done.1
  25.1 0.2 fusion.refs_8_
  25.3 0.0 copy-start
  25.3 0.8 %copy.5.kbig_ref = bf16[128,864]{1,0:T(8,128)(2,1)} copy(bf16[128,864]{0,1:T(8,128)(2,1)S(1)} %bitcast.10) | data formatting | bytes 442368 | tf_op jit(solution)/shard_map/reshape | solution.py:91
  26.2 0.0 copy-done
  26.2 1.5 %collective-permute-done.refs_1_ = bf16[8,32,128]{2,1,0:T(8,128)(2,1)S(1)} collective-permute-done((bf16[8,32,128]{2,1,0:T(8,128)(2,1)S(1)}, bf16[8,32,128]{2,1,0:T(8,128)(2,1)S(1)}, u32[]{:S(2)}, u32[]{:S(2)}) %collective-permute-start) | collective-permute-done | bytes 65568 | tf_op jit(solution)/shard_map/ppermute | solution.py:155
  27.7 2.5 %collective-permute-done.1.refs_2_ = bf16[8,32,128]{2,1,0:T(8,128)(2,1)S(1)} collective-permute-done((bf16[8,32,128]{2,1,0:T(8,128)(2,1)S(1)}, bf16[8,32,128]{2,1,0:T(8,128)(2,1)S(1)}, u32[]{:S(2)}, u32[]{:S(2)}) %collective-permute-start.1) | collective-permute-done | bytes 65568 | tf_op jit(solution)/shard_map/ppermute | solution.py:155
  30.2 0.0 collective-permute-done.2.refs_3_
  30.2 0.0 collective-permute-done.3
  30.2 0.0 copy-start.3
  30.2 0.7 %copy-done.3 = bf16[1,1,16,32,256]{4,3,2,1,0:T(8,128)(2,1)} copy-done((bf16[1,1,16,32,256]{4,3,2,1,0:T(8,128)(2,1)}, bf16[1,1,16,32,256]{4,3,2,1,0:T(8,128)(2,1)S(1)}, u32[]{:S(2)}) %copy-start.3) | copy-done | bytes 262168
  31.0 3.0 %shard_map.50 = (f32[8,32,128]{2,1,0:T(8,128)}, f32[8,32,128]{2,1,0:T(8,128)}, f32[8,32,128]{2,1,0:T(8,128)}, f32[8,32,128]{2,1,0:T(8,128)}) custom-call(bf16[16,32,256]{2,1,0:T(8,128)(2,1)} %bitcast.12, bf16[2,16,32,256]{3,2,1,0:T(8,128)(2,1)} %bitcast.11, bf16[128,864]{1,0:T(8,128)(2,1)} %copy.5.kbig_ref), custom_call_target="tpu_custom_call" | custom-call | flops 528482304 | bytes 2097152 | tf_op jit(solution)/shard_map/pallas_call | solution.py:93
  34.0 0.0 copy-done.5
  34.0 0.0 copy-done.6
  34.0 0.0 copy-done.7
  34.0 0.0 collective-permute-done.4
  34.0 0.0 copy-start.8
  34.0 0.0 copy-start.2
  34.0 6.3 %collective-permute-start.8 = (bf16[8,32,128]{2,1,0:T(8,128)(2,1)S(1)}, bf16[8,32,128]{2,1,0:T(8,128)(2,1)S(1)}, u32[]{:S(2)}, u32[]{:S(2)}) collective-permute-start(bf16[8,32,128]{2,1,0:T(8,128)(2,1)S(1)} %bitcast.17), channel_id=1, source_target_pairs={{0,6},{2,0},{4,2},{6,4},{1,7},{3,1},{5,3},{7,5},{8,14},{10,8},{12,... | collective-permute-start | bytes 196616 | tf_op jit(solution)/shard_map/ppermute | solution.py:155
  40.4 2.1 %collective-permute-start.9 = (bf16[8,32,128]{2,1,0:T(8,128)(2,1)S(1)}, bf16[8,32,128]{2,1,0:T(8,128)(2,1)S(1)}, u32[]{:S(2)}, u32[]{:S(2)}) collective-permute-start(bf16[8,32,128]{2,1,0:T(8,128)(2,1)S(1)} %bitcast.18), channel_id=1, source_target_pairs={{0,4},{2,6},{4,0},{6,2},{1,5},{3,7},{5,1},{7,3},{8,12},{10,14},{12... | collective-permute-start | bytes 196616 | tf_op jit(solution)/shard_map/ppermute | solution.py:155
  42.5 3.9 %collective-permute-start.10 = (bf16[8,32,128]{2,1,0:T(8,128)(2,1)S(1)}, bf16[8,32,128]{2,1,0:T(8,128)(2,1)S(1)}, u32[]{:S(2)}, u32[]{:S(2)}) collective-permute-start(bf16[8,32,128]{2,1,0:T(8,128)(2,1)S(1)} %bitcast.19), channel_id=1, source_target_pairs={{0,2},{2,4},{4,6},{6,0},{1,3},{3,5},{5,7},{7,1},{8,10},{10,12},{12... | collective-permute-start | bytes 196616 | tf_op jit(solution)/shard_map/ppermute | solution.py:155
  46.4 3.7 %collective-permute-start.7 = (f32[8,32,128]{2,1,0:T(8,128)}, f32[8,32,128]{2,1,0:T(8,128)S(1)}, u32[]{:S(2)}, u32[]{:S(2)}) collective-permute-start(f32[8,32,128]{2,1,0:T(8,128)} %get-tuple-element.24), channel_id=1, source_target_pairs={{0,6},{2,0},{4,2},{6,4},{1,7},{3,1},{5,3},{7,5},{8,14},{10,8},{12,... | collective-permute-start | bytes 393224 | tf_op jit(solution)/shard_map/ppermute | solution.py:155
  50.1 2.9 %collective-permute-start.6 = (f32[8,32,128]{2,1,0:T(8,128)}, f32[8,32,128]{2,1,0:T(8,128)S(1)}, u32[]{:S(2)}, u32[]{:S(2)}) collective-permute-start(f32[8,32,128]{2,1,0:T(8,128)} %get-tuple-element.23), channel_id=1, source_target_pairs={{0,4},{2,6},{4,0},{6,2},{1,5},{3,7},{5,1},{7,3},{8,12},{10,14},{12... | collective-permute-start | bytes 393224 | tf_op jit(solution)/shard_map/ppermute | solution.py:155
  53.0 0.0 collective-permute-done.8.refs_5_
  53.0 0.0 copy-start.9
  53.0 1.9 %collective-permute-start.5 = (f32[8,32,128]{2,1,0:T(8,128)}, f32[8,32,128]{2,1,0:T(8,128)S(1)}, u32[]{:S(2)}, u32[]{:S(2)}) collective-permute-start(f32[8,32,128]{2,1,0:T(8,128)} %get-tuple-element.22), channel_id=1, source_target_pairs={{0,2},{2,4},{4,6},{6,0},{1,3},{3,5},{5,7},{7,1},{8,10},{10,12},{12... | collective-permute-start | bytes 393224 | tf_op jit(solution)/shard_map/ppermute | solution.py:155
  54.9 0.0 collective-permute-done.9.refs_6_
  55.0 0.0 copy-start.10
  55.0 0.0 collective-permute-done.10.refs_7_
  55.0 0.0 copy-done.8
  55.0 0.0 copy-done.9
  55.0 0.6 copy-done.10
  55.6 0.6 copy-done.11
  56.2 5.2 %shard_map.51 = bf16[2,16,32,256]{3,2,1,0:T(8,128)(2,1)} custom-call(bf16[8,32,128]{2,1,0:T(8,128)(2,1)} %bitcast.13, bf16[8,32,128]{2,1,0:T(8,128)(2,1)} %copy-done.5, bf16[8,32,128]{2,1,0:T(8,128)(2,1)} %copy-done.6, bf16[8,32,128]{2,1,0:T(8,128)(2,1)} %copy-done.7, bf16[8,32,128]{2,1,0:T(8,128)(2,1)} %bitcast.20, bf16[8,32,128]{2,1,0:T(8,128)(2,1)} %copy-done.9, ...), custom_call_target="tpu_custom_call" | custom-call | flops 1006632960 | bytes 1048576 | tf_op jit(solution)/shard_map/pallas_call | solution.py:143
  61.4 0.0 collective-permute-done.7
  61.4 1.2 %collective-permute-done.6 = f32[8,32,128]{2,1,0:T(8,128)S(1)} collective-permute-done((f32[8,32,128]{2,1,0:T(8,128)}, f32[8,32,128]{2,1,0:T(8,128)S(1)}, u32[]{:S(2)}, u32[]{:S(2)}) %collective-permute-start.6) | collective-permute-done | bytes 131104 | tf_op jit(solution)/shard_map/ppermute | solution.py:155
  62.6 0.0 collective-permute-done.5
  62.6 0.0 copy-done.2
  62.6 0.7 %fusion.1 = bf16[1,1,8,32,128]{4,3,2,1,0:T(8,128)(2,1)} fusion(f32[8,32,128]{2,1,0:T(8,128)S(1)} %collective-permute-done.7, f32[8,32,128]{2,1,0:T(8,128)S(1)} %collective-permute-done.6, f32[8,32,128]{2,1,0:T(8,128)S(1)} %copy-done.2, f32[8,32,128]{2,1,0:T(8,128)S(1)} %collective-permute-done.5), kind=kLoop, calls=%fused_computation.4 | loop fusion | flops 131072 | bytes 589824 | tf_op jit(solution)/shard_map/reshape | solution.py:178
  (4 shorter events, 0.0 us)
Async XLA Ops:
  0.6 4.4 %copy-start.4 = (bf16[1,1,8,32,128]{4,3,2,1,0:T(8,128)(2,1)S(1)}, bf16[1,1,8,32,128]{4,3,2,1,0:T(8,128)(2,1)}, u32[]{:S(2)}) copy-start(bf16[1,1,8,32,128]{4,3,2,1,0:T(8,128)(2,1)} %param.5) | copy-start | bytes 196612
  0.6 24.4 %copy-start.1 = (bf16[27,32,128]{2,1,0:T(8,128)(2,1)S(1)}, bf16[27,32,128]{2,1,0:T(8,128)(2,1)}, u32[]{:S(2)}) copy-start(bf16[27,32,128]{2,1,0:T(8,128)(2,1)} %param.4) | copy-start | bytes 663556
  1.7 28.6 %collective-permute-start.3 = (bf16[1,1,16,32,256]{4,3,2,1,0:T(8,128)(2,1)S(1)}, bf16[1,1,16,32,256]{4,3,2,1,0:T(8,128)(2,1)S(1)}, u32[]{:S(2)}, u32[]{:S(2)}) collective-permute-start(bf16[1,1,16,32,256]{4,3,2,1,0:T(8,128)(2,1)S(1)} %slice.3), channel_id=1, source_target_pairs={{0,8},{8,16},{16,24},{24,32},{32,40},{40,48},{48,56},{56,64},{64,7... | collective-permute-start | bytes 786440 | tf_op jit(solution)/shard_map/ppermute | solution.py:12
  5.1 22.6 %collective-permute-start = (bf16[8,32,128]{2,1,0:T(8,128)(2,1)S(1)}, bf16[8,32,128]{2,1,0:T(8,128)(2,1)S(1)}, u32[]{:S(2)}, u32[]{:S(2)}) collective-permute-start(bf16[8,32,128]{2,1,0:T(8,128)(2,1)S(1)} %bitcast.14), channel_id=1, source_target_pairs={{0,6},{2,0},{4,2},{6,4},{1,7},{3,1},{5,3},{7,5},{8,14},{10,8},{12,... | collective-permute-start | bytes 196616 | tf_op jit(solution)/shard_map/ppermute | solution.py:155
  10.9 19.3 %collective-permute-start.1 = (bf16[8,32,128]{2,1,0:T(8,128)(2,1)S(1)}, bf16[8,32,128]{2,1,0:T(8,128)(2,1)S(1)}, u32[]{:S(2)}, u32[]{:S(2)}) collective-permute-start(bf16[8,32,128]{2,1,0:T(8,128)(2,1)S(1)} %bitcast.15), channel_id=1, source_target_pairs={{0,4},{2,6},{4,0},{6,2},{1,5},{3,7},{5,1},{7,3},{8,12},{10,14},{12... | collective-permute-start | bytes 196616 | tf_op jit(solution)/shard_map/ppermute | solution.py:155
  12.9 17.4 %collective-permute-start.2 = (bf16[8,32,128]{2,1,0:T(8,128)(2,1)S(1)}, bf16[8,32,128]{2,1,0:T(8,128)(2,1)S(1)}, u32[]{:S(2)}, u32[]{:S(2)}) collective-permute-start(bf16[8,32,128]{2,1,0:T(8,128)(2,1)S(1)} %bitcast.16), channel_id=1, source_target_pairs={{0,2},{2,4},{4,6},{6,0},{1,3},{3,5},{5,7},{7,1},{8,10},{10,12},{12... | collective-permute-start | bytes 196616 | tf_op jit(solution)/shard_map/ppermute | solution.py:155
  15.7 18.3 %collective-permute-start.4 = (bf16[1,1,8,32,128]{4,3,2,1,0:T(8,128)(2,1)S(1)}, bf16[1,1,8,32,128]{4,3,2,1,0:T(8,128)(2,1)S(1)}, u32[]{:S(2)}, u32[]{:S(2)}) collective-permute-start(bf16[1,1,8,32,128]{4,3,2,1,0:T(8,128)(2,1)S(1)} %copy-done.4), channel_id=1, source_target_pairs={{8,0},{16,8},{24,16},{32,24},{40,32},{48,40},{56,48},{64,56},{72,6... | collective-permute-start | bytes 196616 | tf_op jit(solution)/shard_map/ppermute | solution.py:12
  25.3 0.9 %copy-start = (bf16[27,32,128]{2,1,0:T(8,128)(2,1)}, bf16[27,32,128]{2,1,0:T(8,128)(2,1)S(1)}, u32[]{:S(2)}) copy-start(bf16[27,32,128]{2,1,0:T(8,128)(2,1)S(1)} %fusion.refs_8_) | copy-start | bytes 663556
  27.7 6.3 %copy-start.5 = (bf16[8,32,128]{2,1,0:T(8,128)(2,1)}, bf16[8,32,128]{2,1,0:T(8,128)(2,1)S(1)}, u32[]{:S(2)}) copy-start(bf16[8,32,128]{2,1,0:T(8,128)(2,1)S(1)} %collective-permute-done.refs_1_) | copy-start | bytes 196612
  30.2 3.8 %copy-start.6 = (bf16[8,32,128]{2,1,0:T(8,128)(2,1)}, bf16[8,32,128]{2,1,0:T(8,128)(2,1)S(1)}, u32[]{:S(2)}) copy-start(bf16[8,32,128]{2,1,0:T(8,128)(2,1)S(1)} %collective-permute-done.1.refs_2_) | copy-start | bytes 196612
  30.2 3.8 %copy-start.7 = (bf16[8,32,128]{2,1,0:T(8,128)(2,1)}, bf16[8,32,128]{2,1,0:T(8,128)(2,1)S(1)}, u32[]{:S(2)}) copy-start(bf16[8,32,128]{2,1,0:T(8,128)(2,1)S(1)} %collective-permute-done.2.refs_3_) | copy-start | bytes 196612
  30.2 0.7 %copy-start.3 = (bf16[1,1,16,32,256]{4,3,2,1,0:T(8,128)(2,1)}, bf16[1,1,16,32,256]{4,3,2,1,0:T(8,128)(2,1)S(1)}, u32[]{:S(2)}) copy-start(bf16[1,1,16,32,256]{4,3,2,1,0:T(8,128)(2,1)S(1)} %collective-permute-done.3) | copy-start | bytes 786436
  34.0 21.0 %copy-start.8 = (bf16[1,1,8,32,128]{4,3,2,1,0:T(8,128)(2,1)}, bf16[1,1,8,32,128]{4,3,2,1,0:T(8,128)(2,1)S(1)}, u32[]{:S(2)}) copy-start(bf16[1,1,8,32,128]{4,3,2,1,0:T(8,128)(2,1)S(1)} %collective-permute-done.4) | copy-start | bytes 196612
  34.0 28.6 %copy-start.2 = (f32[8,32,128]{2,1,0:T(8,128)S(1)}, f32[8,32,128]{2,1,0:T(8,128)}, u32[]{:S(2)}) copy-start(f32[8,32,128]{2,1,0:T(8,128)} %get-tuple-element.21) | copy-start | bytes 393220
  34.0 19.0 %collective-permute-start.8 = (bf16[8,32,128]{2,1,0:T(8,128)(2,1)S(1)}, bf16[8,32,128]{2,1,0:T(8,128)(2,1)S(1)}, u32[]{:S(2)}, u32[]{:S(2)}) collective-permute-start(bf16[8,32,128]{2,1,0:T(8,128)(2,1)S(1)} %bitcast.17), channel_id=1, source_target_pairs={{0,6},{2,0},{4,2},{6,4},{1,7},{3,1},{5,3},{7,5},{8,14},{10,8},{12,... | collective-permute-start | bytes 196616 | tf_op jit(solution)/shard_map/ppermute | solution.py:155
  40.4 14.6 %collective-permute-start.9 = (bf16[8,32,128]{2,1,0:T(8,128)(2,1)S(1)}, bf16[8,32,128]{2,1,0:T(8,128)(2,1)S(1)}, u32[]{:S(2)}, u32[]{:S(2)}) collective-permute-start(bf16[8,32,128]{2,1,0:T(8,128)(2,1)S(1)} %bitcast.18), channel_id=1, source_target_pairs={{0,4},{2,6},{4,0},{6,2},{1,5},{3,7},{5,1},{7,3},{8,12},{10,14},{12... | collective-permute-start | bytes 196616 | tf_op jit(solution)/shard_map/ppermute | solution.py:155
  42.5 12.5 %collective-permute-start.10 = (bf16[8,32,128]{2,1,0:T(8,128)(2,1)S(1)}, bf16[8,32,128]{2,1,0:T(8,128)(2,1)S(1)}, u32[]{:S(2)}, u32[]{:S(2)}) collective-permute-start(bf16[8,32,128]{2,1,0:T(8,128)(2,1)S(1)} %bitcast.19), channel_id=1, source_target_pairs={{0,2},{2,4},{4,6},{6,0},{1,3},{3,5},{5,7},{7,1},{8,10},{10,12},{12... | collective-permute-start | bytes 196616 | tf_op jit(solution)/shard_map/ppermute | solution.py:155
  46.4 15.0 %collective-permute-start.7 = (f32[8,32,128]{2,1,0:T(8,128)}, f32[8,32,128]{2,1,0:T(8,128)S(1)}, u32[]{:S(2)}, u32[]{:S(2)}) collective-permute-start(f32[8,32,128]{2,1,0:T(8,128)} %get-tuple-element.24), channel_id=1, source_target_pairs={{0,6},{2,0},{4,2},{6,4},{1,7},{3,1},{5,3},{7,5},{8,14},{10,8},{12,... | collective-permute-start | bytes 393224 | tf_op jit(solution)/shard_map/ppermute | solution.py:155
  50.1 12.5 %collective-permute-start.6 = (f32[8,32,128]{2,1,0:T(8,128)}, f32[8,32,128]{2,1,0:T(8,128)S(1)}, u32[]{:S(2)}, u32[]{:S(2)}) collective-permute-start(f32[8,32,128]{2,1,0:T(8,128)} %get-tuple-element.23), channel_id=1, source_target_pairs={{0,4},{2,6},{4,0},{6,2},{1,5},{3,7},{5,1},{7,3},{8,12},{10,14},{12... | collective-permute-start | bytes 393224 | tf_op jit(solution)/shard_map/ppermute | solution.py:155
  53.0 2.0 %copy-start.9 = (bf16[8,32,128]{2,1,0:T(8,128)(2,1)}, bf16[8,32,128]{2,1,0:T(8,128)(2,1)S(1)}, u32[]{:S(2)}) copy-start(bf16[8,32,128]{2,1,0:T(8,128)(2,1)S(1)} %collective-permute-done.8.refs_5_) | copy-start | bytes 196612
  53.0 9.6 %collective-permute-start.5 = (f32[8,32,128]{2,1,0:T(8,128)}, f32[8,32,128]{2,1,0:T(8,128)S(1)}, u32[]{:S(2)}, u32[]{:S(2)}) collective-permute-start(f32[8,32,128]{2,1,0:T(8,128)} %get-tuple-element.22), channel_id=1, source_target_pairs={{0,2},{2,4},{4,6},{6,0},{1,3},{3,5},{5,7},{7,1},{8,10},{10,12},{12... | collective-permute-start | bytes 393224 | tf_op jit(solution)/shard_map/ppermute | solution.py:155
  55.0 0.6 copy-start.10
  55.6 0.6 copy-start.11

commit v10 on v6

--- a/solution.py
+++ b/solution.py
@@ -55,32 +55,46 @@
     return jnp.concatenate(blocks, axis=1)
 
 
-def forward_rows(halo_ref, vol_ref, kbig_ref, *refs):
-    out_refs, picked_ref = refs[:-1], refs[-1]
-    planes, rows, chans, cols = vol_ref.shape
-    rows_out, share, cols_out = out_refs[0].shape
+def forward_taps(source_refs, kbig_ref, acc_ref, out_refs, picked_ref, first_tap):
+    planes = len(source_refs)
+    rows, chans, cols = source_refs[0].shape
+    rows_out, cols_out = rows // 2, cols // 2
+    share = out_refs[0].shape[1]
     sel = spread_matrix(cols, cols_out, False)
-    for plane in range(planes + 1):
-        source = halo_ref[...] if plane == 0 else vol_ref[plane - 1]
-        flat = source.reshape(rows * chans, cols)
+    for plane, source_ref in enumerate(source_refs):
+        flat = source_ref[...].reshape(rows * chans, cols)
         chosen = jnp.dot(flat, sel, preferred_element_type=jnp.float32)
         picked_ref[plane] = chosen.astype(picked_ref.dtype).reshape(rows, chans, 3 * cols_out)
-    kbig = kbig_ref[...]
+    kpart = kbig_ref[:, first_tap * 9 * chans:(first_tap + planes) * 9 * chans]
     zero = jnp.zeros((chans, cols_out), picked_ref.dtype)
     for i in range(rows_out):
         pieces = []
-        for depth_tap in range(3):
+        for plane in range(planes):
             for row_tap in range(3):
                 row = 2 * i + row_tap - 1
                 for col_tap in range(3):
                     if row < 0:
                         pieces.append(zero)
                     else:
-                        pieces.append(picked_ref[depth_tap, row, :, col_tap * cols_out:(col_tap + 1) * cols_out])
+                        pieces.append(picked_ref[plane, row, :, col_tap * cols_out:(col_tap + 1) * cols_out])
         stacked = jnp.concatenate(pieces, axis=0)
-        result = jnp.dot(kbig, stacked, preferred_element_type=jnp.float32)
-        for k, out_ref in enumerate(out_refs):
-            out_ref[i] = result[k * share:(k + 1) * share]
+        result = jnp.dot(kpart, stacked, preferred_element_type=jnp.float32)
+        if acc_ref is not None:
+            result = acc_ref[i] + result
+        if len(out_refs) == 1 and share == result.shape[0]:
+            out_refs[0][i] = result
+        else:
+            for k, out_ref in enumerate(out_refs):
+                out_ref[i] = result[k * share:(k + 1) * share]
+
+
+def forward_local_rows(vol_ref, kbig_ref, acc_ref, picked_ref):
+    forward_taps([vol_ref.at[0], vol_ref.at[1]], kbig_ref, None, [acc_ref], picked_ref, 1)
+
+
+def forward_halo_rows(halo_ref, acc_ref, kbig_ref, *refs):
+    out_refs, picked_ref = refs[:-1], refs[-1]
+    forward_taps([halo_ref], kbig_ref, acc_ref, list(out_refs), picked_ref, 0)
 
 
 def forward_partial(halo, vol, kernel, groups):
@@ -89,15 +103,24 @@
     rows_out, cols_out = rows // 2, cols // 2
     share = chans_out // groups
     kbig = jnp.transpose(kernel, (2, 0, 1)).reshape(chans_out, taps * chans)
-    flops = 2 * (planes + 1) * rows * chans * cols * 3 * cols_out + 2 * rows_out * chans_out * taps * chans * cols_out
+    vmem = pl.BlockSpec(memory_space=pltpu.VMEM)
+    per_plane = 2 * rows * chans * cols * 3 * cols_out + 2 * rows_out * chans_out * 9 * chans * cols_out
+    acc = pl.pallas_call(
+        forward_local_rows,
+        out_shape=jax.ShapeDtypeStruct((rows_out, chans_out, cols_out), jnp.float32),
+        in_specs=[vmem] * 2,
+        out_specs=vmem,
+        scratch_shapes=[pltpu.VMEM((planes, rows, chans, 3 * cols_out), vol.dtype)],
+        cost_estimate=pl.CostEstimate(flops=planes * per_plane, bytes_accessed=2 * vol.size + 4 * rows_out * chans_out * cols_out, transcendentals=0),
+    )(vol, kbig)
     return pl.pallas_call(
-        forward_rows,
+        forward_halo_rows,
         out_shape=[jax.ShapeDtypeStruct((rows_out, share, cols_out), jnp.float32)] * groups,
-        in_specs=[pl.BlockSpec(memory_space=pltpu.VMEM)] * 3,
-        out_specs=[pl.BlockSpec(memory_space=pltpu.VMEM)] * groups,
-        scratch_shapes=[pltpu.VMEM((planes + 1, rows, chans, 3 * cols_out), vol.dtype)],
-        cost_estimate=pl.CostEstimate(flops=flops, bytes_accessed=2 * 4 * vol.size, transcendentals=0),
-    )(halo, vol, kbig)
+        in_specs=[vmem] * 3,
+        out_specs=[vmem] * groups,
+        scratch_shapes=[pltpu.VMEM((1, rows, chans, 3 * cols_out), vol.dtype)],
+        cost_estimate=pl.CostEstimate(flops=per_plane, bytes_accessed=2 * halo.size + 8 * rows_out * chans_out * cols_out, transcendentals=0),
+    )(halo, acc, kbig)
 
 
 def backward_rows(*refs):

time: 58.4 us -> 57.9 us (level)
  waiting for transfers between devices: 12.1 us -> 9.38 us
  Pallas kernels: 7.83 us -> 10 us
    ppermute x2, waiting for transfers between devices: 9.96 us -> 7.26 us  [from_behind(): return lax.ppermute(block, axis, route)]
    pallas_call x1 -> x2, Pallas kernels: 3.01 us -> 5.21 us  [the longest x1 2.7 us: forward_partial(): pl.pallas_call(forward_local_rows, out_shape=jax.ShapeDtypeStruct((rows_o...]
  transfers between devices with their start and end apart: 8 -> 8, of which waited for: 3 -> 2; matrix products, arithmetic and copies ran while one was open for 2% -> 2% of each run, Pallas kernels for 8% -> 13%
where the time goes in v10:
time: 57.9 us; the launch traced here: 57.5 us
  starting transfers between devices  32.5 us (56%)
  Pallas kernels  10 us (17%)
  waiting for transfers between devices  9.38 us (16%)
  local copies, waits for them, and re-layouts  3.82 us (7%)
  other arithmetic  0.91 us (2%)
  between operations  0.84 us (1%)
    ppermute x6, starting transfers between devices, chan_shift(): lax.ppermute(block, 'chan', [(i, (i + shift) % size) for i in range(size)])  18.5 us
    ppermute x2, starting transfers between devices, from_behind(): return lax.ppermute(block, axis, route)  14 us
    ppermute x2, waiting for transfers between devices, from_behind(): return lax.ppermute(block, axis, route)  7.26 us
    pallas_call x1, Pallas kernels, backward_grad(): pl.pallas_call(backward_rows, out_shape=jax.ShapeDtypeStruct((2, rows, ch...  4.82 us
    pallas_call x1, Pallas kernels, forward_partial(): pl.pallas_call(forward_local_rows, out_shape=jax.ShapeDtypeStruct((rows_o...  2.7 us
    pallas_call x1, Pallas kernels, forward_partial(): pl.pallas_call(forward_halo_rows, out_shape=[jax.ShapeDtypeStruct((rows_o...  2.51 us
    ppermute x6, waiting for transfers between devices, chan_shift(): lax.ppermute(block, 'chan', [(i, (i + shift) % size) for i in range(size)])  2.12 us
    unnamed x18, local copies, waits for them, and re-layouts  1.98 us
  transfers between devices with their start and end apart: 8, of which 2 were waited for; matrix products, arithmetic and copies ran while one was open for 2% of the time, Pallas kernels for 13%

profile of v10, /device:TPU:512, one launch (start us, length us, event | category | flops | bytes accessed | tf_op | source)
XLA Modules:
  0.0 57.5 jit_solution(4346666961360679804)
XLA Ops:
  0.6 0.0 copy-start.5
  0.6 0.0 copy-start.2
  0.6 1.0 %slice.3 = bf16[1,1,16,32,256]{4,3,2,1,0:T(8,128)(2,1)S(1)} slice(bf16[1,2,16,32,256]{4,3,2,1,0:T(8,128)(2,1)} %param.3), slice={[0:1], [1:2], [0:16], [0:32], [0:256]} | slice | bytes 524288 | tf_op jit(solution)/shard_map/slice | solution.py:187
  1.7 3.4 %collective-permute-start = (bf16[1,1,16,32,256]{4,3,2,1,0:T(8,128)(2,1)S(1)}, bf16[1,1,16,32,256]{4,3,2,1,0:T(8,128)(2,1)S(1)}, u32[]{:S(2)}, u32[]{:S(2)}) collective-permute-start(bf16[1,1,16,32,256]{4,3,2,1,0:T(8,128)(2,1)S(1)} %slice.3), channel_id=1, source_target_pairs={{0,8},{8,16},{16,24},{24,32},{32,40},{40,48},{48,56},{56,64},{64,7... | collective-permute-start | bytes 786440 | tf_op jit(solution)/shard_map/ppermute | solution.py:12
  5.1 0.0 copy-done.5
  5.1 10.6 %collective-permute-start.1 = (bf16[1,1,8,32,128]{4,3,2,1,0:T(8,128)(2,1)S(1)}, bf16[1,1,8,32,128]{4,3,2,1,0:T(8,128)(2,1)S(1)}, u32[]{:S(2)}, u32[]{:S(2)}) collective-permute-start(bf16[1,1,8,32,128]{4,3,2,1,0:T(8,128)(2,1)S(1)} %copy-done.5), channel_id=1, source_target_pairs={{8,0},{16,8},{24,16},{32,24},{40,32},{48,40},{56,48},{64,56},{72,6... | collective-permute-start | bytes 196616 | tf_op jit(solution)/shard_map/ppermute | solution.py:12
  15.7 0.0 copy-done.2
  15.7 0.2 fusion.refs_4_
  15.9 0.0 copy-start
  15.9 0.8 %copy.5.kbig_ref = bf16[128,864]{1,0:T(8,128)(2,1)} copy(bf16[128,864]{0,1:T(8,128)(2,1)S(1)} %bitcast.9) | data formatting | bytes 442368 | tf_op jit(solution)/shard_map/reshape | solution.py:105
  16.8 0.0 copy-done
  16.8 2.7 %shard_map.50.acc_ref = f32[8,128,128]{2,1,0:T(8,128)} custom-call(bf16[2,16,32,256]{3,2,1,0:T(8,128)(2,1)} %bitcast.11, bf16[128,864]{1,0:T(8,128)(2,1)} %copy.5.kbig_ref), custom_call_target="tpu_custom_call" | custom-call | flops 352321536 | bytes 1048576 | tf_op jit(solution)/shard_map/pallas_call | solution.py:108
  19.5 0.0 collective-permute-done.1
  19.5 0.0 copy-start.3
  19.5 7.3 %collective-permute-done = bf16[1,1,16,32,256]{4,3,2,1,0:T(8,128)(2,1)S(1)} collective-permute-done((bf16[1,1,16,32,256]{4,3,2,1,0:T(8,128)(2,1)S(1)}, bf16[1,1,16,32,256]{4,3,2,1,0:T(8,128)(2,1)S(1)}, u32[]{:S(2)}, u32[]{:S(2)}) %collective-permute-start) | collective-permute-done | bytes 262176 | tf_op jit(solution)/shard_map/ppermute | solution.py:12
  26.8 0.0 copy-start.1
  26.8 0.7 %copy-done.1 = bf16[1,1,16,32,256]{4,3,2,1,0:T(8,128)(2,1)} copy-done((bf16[1,1,16,32,256]{4,3,2,1,0:T(8,128)(2,1)}, bf16[1,1,16,32,256]{4,3,2,1,0:T(8,128)(2,1)S(1)}, u32[]{:S(2)}) %copy-start.1) | copy-done | bytes 262168
  27.4 2.5 %shard_map.51 = (f32[8,32,128]{2,1,0:T(8,128)}, f32[8,32,128]{2,1,0:T(8,128)}, f32[8,32,128]{2,1,0:T(8,128)}, f32[8,32,128]{2,1,0:T(8,128)}) custom-call(bf16[16,32,256]{2,1,0:T(8,128)(2,1)} %bitcast.10, f32[8,128,128]{2,1,0:T(8,128)} %shard_map.50.acc_ref, bf16[128,864]{1,0:T(8,128)(2,1)} %copy.5.kbig_ref), custom_call_target="tpu_custom_call" | custom-call | flops 176160768 | bytes 1310720 | tf_op jit(solution)/shard_map/pallas_call | solution.py:116
  30.0 0.0 copy-start.4
  30.0 3.9 %collective-permute-start.5 = (bf16[2,8,32,128]{3,2,1,0:T(8,128)(2,1)S(1)}, bf16[2,8,32,128]{3,2,1,0:T(8,128)(2,1)S(1)}, u32[]{:S(2)}, u32[]{:S(2)}) collective-permute-start(bf16[2,8,32,128]{3,2,1,0:T(8,128)(2,1)S(1)} %bitcast.12), channel_id=1, source_target_pairs={{0,6},{2,0},{4,2},{6,4},{1,7},{3,1},{5,3},{7,5},{8,14},{10,8},{12,... | collective-permute-start | bytes 393224 | tf_op jit(solution)/shard_map/ppermute | solution.py:174
  33.9 2.3 %collective-permute-start.6 = (bf16[2,8,32,128]{3,2,1,0:T(8,128)(2,1)S(1)}, bf16[2,8,32,128]{3,2,1,0:T(8,128)(2,1)S(1)}, u32[]{:S(2)}, u32[]{:S(2)}) collective-permute-start(bf16[2,8,32,128]{3,2,1,0:T(8,128)(2,1)S(1)} %bitcast.13), channel_id=1, source_target_pairs={{0,4},{2,6},{4,0},{6,2},{1,5},{3,7},{5,1},{7,3},{8,12},{10,14},{12... | collective-permute-start | bytes 393224 | tf_op jit(solution)/shard_map/ppermute | solution.py:174
  36.1 0.0 copy-done.3
  36.2 3.9 %collective-permute-start.7 = (bf16[2,8,32,128]{3,2,1,0:T(8,128)(2,1)S(1)}, bf16[2,8,32,128]{3,2,1,0:T(8,128)(2,1)S(1)}, u32[]{:S(2)}, u32[]{:S(2)}) collective-permute-start(bf16[2,8,32,128]{3,2,1,0:T(8,128)(2,1)S(1)} %bitcast.14), channel_id=1, source_target_pairs={{0,2},{2,4},{4,6},{6,0},{1,3},{3,5},{5,7},{7,1},{8,10},{10,12},{12... | collective-permute-start | bytes 393224 | tf_op jit(solution)/shard_map/ppermute | solution.py:174
  40.1 3.7 %collective-permute-start.4 = (f32[8,32,128]{2,1,0:T(8,128)}, f32[8,32,128]{2,1,0:T(8,128)S(1)}, u32[]{:S(2)}, u32[]{:S(2)}) collective-permute-start(f32[8,32,128]{2,1,0:T(8,128)} %get-tuple-element.18), channel_id=1, source_target_pairs={{0,6},{2,0},{4,2},{6,4},{1,7},{3,1},{5,3},{7,5},{8,14},{10,8},{12,... | collective-permute-start | bytes 393224 | tf_op jit(solution)/shard_map/ppermute | solution.py:174
  43.8 2.7 %collective-permute-start.3 = (f32[8,32,128]{2,1,0:T(8,128)}, f32[8,32,128]{2,1,0:T(8,128)S(1)}, u32[]{:S(2)}, u32[]{:S(2)}) collective-permute-start(f32[8,32,128]{2,1,0:T(8,128)} %get-tuple-element.17), channel_id=1, source_target_pairs={{0,4},{2,6},{4,0},{6,2},{1,5},{3,7},{5,1},{7,3},{8,12},{10,14},{12... | collective-permute-start | bytes 393224 | tf_op jit(solution)/shard_map/ppermute | solution.py:174
  46.5 0.0 collective-permute-done.5.refs_1_
  46.5 0.0 copy-start.6
  46.5 2.1 %collective-permute-start.2 = (f32[8,32,128]{2,1,0:T(8,128)}, f32[8,32,128]{2,1,0:T(8,128)S(1)}, u32[]{:S(2)}, u32[]{:S(2)}) collective-permute-start(f32[8,32,128]{2,1,0:T(8,128)} %get-tuple-element.16), channel_id=1, source_target_pairs={{0,2},{2,4},{4,6},{6,0},{1,3},{3,5},{5,7},{7,1},{8,10},{10,12},{12... | collective-permute-start | bytes 393224 | tf_op jit(solution)/shard_map/ppermute | solution.py:174
  48.6 0.0 collective-permute-done.6.refs_2_
  48.6 0.0 copy-start.7
  48.6 0.0 collective-permute-done.7.refs_3_
  48.6 0.0 copy-done.6
  48.6 0.6 %copy-done.7 = bf16[2,8,32,128]{3,2,1,0:T(8,128)(2,1)} copy-done((bf16[2,8,32,128]{3,2,1,0:T(8,128)(2,1)}, bf16[2,8,32,128]{3,2,1,0:T(8,128)(2,1)S(1)}, u32[]{:S(2)}) %copy-start.7) | copy-done | bytes 131096
  49.2 0.0 copy-start.8
  49.2 0.6 %copy-done.8 = bf16[2,8,32,128]{3,2,1,0:T(8,128)(2,1)} copy-done((bf16[2,8,32,128]{3,2,1,0:T(8,128)(2,1)}, bf16[2,8,32,128]{3,2,1,0:T(8,128)(2,1)S(1)}, u32[]{:S(2)}) %copy-start.8) | copy-done | bytes 131096
  49.9 4.8 %shard_map.52 = bf16[2,16,32,256]{3,2,1,0:T(8,128)(2,1)} custom-call(bf16[2,8,32,128]{3,2,1,0:T(8,128)(2,1)} %bitcast.15, bf16[2,8,32,128]{3,2,1,0:T(8,128)(2,1)} %copy-done.6, bf16[2,8,32,128]{3,2,1,0:T(8,128)(2,1)} %copy-done.7, bf16[2,8,32,128]{3,2,1,0:T(8,128)(2,1)} %copy-done.8, bf16[27,32,128]{2,1,0:T(8,128)(2,1)} %copy-done), custom_call_target="tpu_custom_call" | custom-call | flops 1006632960 | bytes 1048576 | tf_op jit(solution)/shard_map/pallas_call | solution.py:162
  54.7 0.0 collective-permute-done.4
  54.7 2.1 %collective-permute-done.3 = f32[8,32,128]{2,1,0:T(8,128)S(1)} collective-permute-done((f32[8,32,128]{2,1,0:T(8,128)}, f32[8,32,128]{2,1,0:T(8,128)S(1)}, u32[]{:S(2)}, u32[]{:S(2)}) %collective-permute-start.3) | collective-permute-done | bytes 131104 | tf_op jit(solution)/shard_map/ppermute | solution.py:174
  56.8 0.0 collective-permute-done.2
  56.8 0.0 copy-done.4
  56.8 0.7 %fusion.1 = bf16[1,1,8,32,128]{4,3,2,1,0:T(8,128)(2,1)} fusion(f32[8,32,128]{2,1,0:T(8,128)S(1)} %collective-permute-done.4, f32[8,32,128]{2,1,0:T(8,128)S(1)} %collective-permute-done.3, f32[8,32,128]{2,1,0:T(8,128)S(1)} %copy-done.4, f32[8,32,128]{2,1,0:T(8,128)S(1)} %collective-permute-done.2), kind=kLoop, calls=%fused_computation.5 | loop fusion | flops 131072 | bytes 589824 | tf_op jit(solution)/shard_map/reshape | solution.py:194
  (1 shorter events, 0.0 us)
Async XLA Ops:
  0.6 4.5 %copy-start.5 = (bf16[1,1,8,32,128]{4,3,2,1,0:T(8,128)(2,1)S(1)}, bf16[1,1,8,32,128]{4,3,2,1,0:T(8,128)(2,1)}, u32[]{:S(2)}) copy-start(bf16[1,1,8,32,128]{4,3,2,1,0:T(8,128)(2,1)} %param.5) | copy-start | bytes 196612
  0.6 15.0 %copy-start.2 = (bf16[27,32,128]{2,1,0:T(8,128)(2,1)S(1)}, bf16[27,32,128]{2,1,0:T(8,128)(2,1)}, u32[]{:S(2)}) copy-start(bf16[27,32,128]{2,1,0:T(8,128)(2,1)} %param.4) | copy-start | bytes 663556
  1.7 25.1 %collective-permute-start = (bf16[1,1,16,32,256]{4,3,2,1,0:T(8,128)(2,1)S(1)}, bf16[1,1,16,32,256]{4,3,2,1,0:T(8,128)(2,1)S(1)}, u32[]{:S(2)}, u32[]{:S(2)}) collective-permute-start(bf16[1,1,16,32,256]{4,3,2,1,0:T(8,128)(2,1)S(1)} %slice.3), channel_id=1, source_target_pairs={{0,8},{8,16},{16,24},{24,32},{32,40},{40,48},{48,56},{56,64},{64,7... | collective-permute-start | bytes 786440 | tf_op jit(solution)/shard_map/ppermute | solution.py:12
  5.1 14.4 %collective-permute-start.1 = (bf16[1,1,8,32,128]{4,3,2,1,0:T(8,128)(2,1)S(1)}, bf16[1,1,8,32,128]{4,3,2,1,0:T(8,128)(2,1)S(1)}, u32[]{:S(2)}, u32[]{:S(2)}) collective-permute-start(bf16[1,1,8,32,128]{4,3,2,1,0:T(8,128)(2,1)S(1)} %copy-done.5), channel_id=1, source_target_pairs={{8,0},{16,8},{24,16},{32,24},{40,32},{48,40},{56,48},{64,56},{72,6... | collective-permute-start | bytes 196616 | tf_op jit(solution)/shard_map/ppermute | solution.py:12
  15.9 0.8 %copy-start = (bf16[27,32,128]{2,1,0:T(8,128)(2,1)}, bf16[27,32,128]{2,1,0:T(8,128)(2,1)S(1)}, u32[]{:S(2)}) copy-start(bf16[27,32,128]{2,1,0:T(8,128)(2,1)S(1)} %fusion.refs_4_) | copy-start | bytes 663556
  19.5 16.7 %copy-start.3 = (bf16[1,2,8,32,128]{4,3,2,1,0:T(8,128)(2,1)}, bf16[1,2,8,32,128]{4,3,2,1,0:T(8,128)(2,1)S(1)}, u32[]{:S(2)}) copy-start(bf16[1,2,8,32,128]{4,3,2,1,0:T(8,128)(2,1)S(1)} %pad_maximum_fusion) | copy-start | bytes 393220
  26.8 0.7 %copy-start.1 = (bf16[1,1,16,32,256]{4,3,2,1,0:T(8,128)(2,1)}, bf16[1,1,16,32,256]{4,3,2,1,0:T(8,128)(2,1)S(1)}, u32[]{:S(2)}) copy-start(bf16[1,1,16,32,256]{4,3,2,1,0:T(8,128)(2,1)S(1)} %collective-permute-done) | copy-start | bytes 786436
  30.0 26.9 %copy-start.4 = (f32[8,32,128]{2,1,0:T(8,128)S(1)}, f32[8,32,128]{2,1,0:T(8,128)}, u32[]{:S(2)}) copy-start(f32[8,32,128]{2,1,0:T(8,128)} %get-tuple-element.15) | copy-start | bytes 393220
  30.0 16.5 %collective-permute-start.5 = (bf16[2,8,32,128]{3,2,1,0:T(8,128)(2,1)S(1)}, bf16[2,8,32,128]{3,2,1,0:T(8,128)(2,1)S(1)}, u32[]{:S(2)}, u32[]{:S(2)}) collective-permute-start(bf16[2,8,32,128]{3,2,1,0:T(8,128)(2,1)S(1)} %bitcast.12), channel_id=1, source_target_pairs={{0,6},{2,0},{4,2},{6,4},{1,7},{3,1},{5,3},{7,5},{8,14},{10,8},{12,... | collective-permute-start | bytes 393224 | tf_op jit(solution)/shard_map/ppermute | solution.py:174
  33.9 14.7 %collective-permute-start.6 = (bf16[2,8,32,128]{3,2,1,0:T(8,128)(2,1)S(1)}, bf16[2,8,32,128]{3,2,1,0:T(8,128)(2,1)S(1)}, u32[]{:S(2)}, u32[]{:S(2)}) collective-permute-start(bf16[2,8,32,128]{3,2,1,0:T(8,128)(2,1)S(1)} %bitcast.13), channel_id=1, source_target_pairs={{0,4},{2,6},{4,0},{6,2},{1,5},{3,7},{5,1},{7,3},{8,12},{10,14},{12... | collective-permute-start | bytes 393224 | tf_op jit(solution)/shard_map/ppermute | solution.py:174
  36.2 12.5 %collective-permute-start.7 = (bf16[2,8,32,128]{3,2,1,0:T(8,128)(2,1)S(1)}, bf16[2,8,32,128]{3,2,1,0:T(8,128)(2,1)S(1)}, u32[]{:S(2)}, u32[]{:S(2)}) collective-permute-start(bf16[2,8,32,128]{3,2,1,0:T(8,128)(2,1)S(1)} %bitcast.14), channel_id=1, source_target_pairs={{0,2},{2,4},{4,6},{6,0},{1,3},{3,5},{5,7},{7,1},{8,10},{10,12},{12... | collective-permute-start | bytes 393224 | tf_op jit(solution)/shard_map/ppermute | solution.py:174
  40.1 14.6 %collective-permute-start.4 = (f32[8,32,128]{2,1,0:T(8,128)}, f32[8,32,128]{2,1,0:T(8,128)S(1)}, u32[]{:S(2)}, u32[]{:S(2)}) collective-permute-start(f32[8,32,128]{2,1,0:T(8,128)} %get-tuple-element.18), channel_id=1, source_target_pairs={{0,6},{2,0},{4,2},{6,4},{1,7},{3,1},{5,3},{7,5},{8,14},{10,8},{12,... | collective-permute-start | bytes 393224 | tf_op jit(solution)/shard_map/ppermute | solution.py:174
  43.8 13.0 %collective-permute-start.3 = (f32[8,32,128]{2,1,0:T(8,128)}, f32[8,32,128]{2,1,0:T(8,128)S(1)}, u32[]{:S(2)}, u32[]{:S(2)}) collective-permute-start(f32[8,32,128]{2,1,0:T(8,128)} %get-tuple-element.17), channel_id=1, source_target_pairs={{0,4},{2,6},{4,0},{6,2},{1,5},{3,7},{5,1},{7,3},{8,12},{10,14},{12... | collective-permute-start | bytes 393224 | tf_op jit(solution)/shard_map/ppermute | solution.py:174
  46.5 2.1 %copy-start.6 = (bf16[2,8,32,128]{3,2,1,0:T(8,128)(2,1)}, bf16[2,8,32,128]{3,2,1,0:T(8,128)(2,1)S(1)}, u32[]{:S(2)}) copy-start(bf16[2,8,32,128]{3,2,1,0:T(8,128)(2,1)S(1)} %collective-permute-done.5.refs_1_) | copy-start | bytes 393220
  46.5 10.3 %collective-permute-start.2 = (f32[8,32,128]{2,1,0:T(8,128)}, f32[8,32,128]{2,1,0:T(8,128)S(1)}, u32[]{:S(2)}, u32[]{:S(2)}) collective-permute-start(f32[8,32,128]{2,1,0:T(8,128)} %get-tuple-element.16), channel_id=1, source_target_pairs={{0,2},{2,4},{4,6},{6,0},{1,3},{3,5},{5,7},{7,1},{8,10},{10,12},{12... | collective-permute-start | bytes 393224 | tf_op jit(solution)/shard_map/ppermute | solution.py:174
  48.6 0.6 %copy-start.7 = (bf16[2,8,32,128]{3,2,1,0:T(8,128)(2,1)}, bf16[2,8,32,128]{3,2,1,0:T(8,128)(2,1)S(1)}, u32[]{:S(2)}) copy-start(bf16[2,8,32,128]{3,2,1,0:T(8,128)(2,1)S(1)} %collective-permute-done.6.refs_2_) | copy-start | bytes 393220
  49.2 0.7 %copy-start.8 = (bf16[2,8,32,128]{3,2,1,0:T(8,128)(2,1)}, bf16[2,8,32,128]{3,2,1,0:T(8,128)(2,1)S(1)}, u32[]{:S(2)}) copy-start(bf16[2,8,32,128]{3,2,1,0:T(8,128)(2,1)S(1)} %collective-permute-done.7.refs_3_) | copy-start | bytes 393220

commit v11 on v10

--- a/solution.py
+++ b/solution.py
@@ -84,8 +84,10 @@
         if len(out_refs) == 1 and share == result.shape[0]:
             out_refs[0][i] = result
         else:
-            for k, out_ref in enumerate(out_refs):
-                out_ref[i] = result[k * share:(k + 1) * share]
+            out_refs[0][i] = result[:share]
+            out_refs[1][i] = result[2 * share:3 * share]
+            out_refs[2][0, i] = result[share:2 * share]
+            out_refs[2][1, i] = result[3 * share:]
 
 
 def forward_local_rows(vol_ref, kbig_ref, acc_ref, picked_ref):
@@ -113,11 +115,12 @@
         scratch_shapes=[pltpu.VMEM((planes, rows, chans, 3 * cols_out), vol.dtype)],
         cost_estimate=pl.CostEstimate(flops=planes * per_plane, bytes_accessed=2 * vol.size + 4 * rows_out * chans_out * cols_out, transcendentals=0),
     )(vol, kbig)
+    block = jax.ShapeDtypeStruct((rows_out, share, cols_out), jnp.float32)
     return pl.pallas_call(
         forward_halo_rows,
-        out_shape=[jax.ShapeDtypeStruct((rows_out, share, cols_out), jnp.float32)] * groups,
+        out_shape=[block, block, jax.ShapeDtypeStruct((2, rows_out, share, cols_out), jnp.float32)],
         in_specs=[vmem] * 3,
-        out_specs=[vmem] * groups,
+        out_specs=[vmem] * 3,
         scratch_shapes=[pltpu.VMEM((1, rows, chans, 3 * cols_out), vol.dtype)],
         cost_estimate=pl.CostEstimate(flops=per_plane, bytes_accessed=2 * halo.size + 8 * rows_out * chans_out * cols_out, transcendentals=0),
     )(halo, acc, kbig)
@@ -169,9 +172,9 @@
     )(*pieces, kernel)
 
 
-def chan_shift(block, shift):
+def chan_swap(block, mask):
     size = lax.axis_size("chan")
-    return lax.ppermute(block, "chan", [(i, (i + shift) % size) for i in range(size)])
+    return lax.ppermute(block, "chan", [(i, i ^ mask) for i in range(size)])
 
 
 def per_device(volume, kernel, cotangent):
@@ -183,16 +186,20 @@
     groups = lax.axis_size("chan")
     share = chans_out // groups
     me = lax.axis_index("chan")
-    kernel = jnp.roll(kernel, -me * share, axis=2)
+    kernel = jnp.concatenate(
+        [lax.dynamic_slice_in_dim(kernel, (me ^ k) * share, share, axis=2) for k in range(groups)], axis=2
+    )
     below = from_behind(volume[:, -1:], "space", 1)
-    chunks = forward_partial(below[0, 0], volume[0], kernel, groups)
-    pair = jnp.concatenate([cotangent, from_behind(cotangent, "space", -1)], axis=1)
-    chunks, pair = lax.optimization_barrier((chunks, pair))
-    total = chunks[0]
-    for k in range(1, groups):
-        total = total + chan_shift(chunks[k], k)
+    own_block, far_block, sent = forward_partial(below[0, 0], volume[0], kernel, groups)
+    pair = jnp.concatenate([cotangent, from_behind(cotangent, "space", -1)], axis=1)[0]
+    (own_block, far_block, sent), pair = lax.optimization_barrier(((own_block, far_block, sent), pair))
+    near = chan_swap(sent, 1)
+    across = chan_swap(pair, 2)
+    far_sum = far_block + near[1]
+    total = (own_block + near[0]) + chan_swap(far_sum, 2)
     response = total.astype(jnp.bfloat16).reshape(count, planes_out, rows_out, share, cols_out)
-    pieces = [pair[0]] + [chan_shift(pair[0], -k) for k in range(1, groups)]
+    other = chan_swap(jnp.stack([pair, across]), 1)
+    pieces = [pair, other[0], across, other[1]]
     volume_grad = backward_grad(pieces, kernel).reshape(count, planes_in, rows_in, chans_in, cols_in)
     return (response, volume_grad)
 

time: 57.9 us -> 60.5 us (1.045)
  waiting for transfers between devices: 9.38 us -> 19.9 us
  starting transfers between devices: 32.5 us -> 24.2 us
    ppermute x6 -> x4, waiting for transfers between devices: 2.12 us -> 13.1 us  [chan_swap(): return lax.ppermute(block, 'chan', [(i, i ^ mask) for i in range(size)])]
    ppermute x6 -> x4, starting transfers between devices: 18.5 us -> 10.2 us  [chan_swap(): return lax.ppermute(block, 'chan', [(i, i ^ mask) for i in range(size)])]
    squeeze x0 -> x1, local copies, waits for them, and re-layouts: none -> 0.71 us  [per_device(): pieces = [pair, other[0], across, other[1]]]
    unnamed x18 -> x16, local copies, waits for them, and re-layouts: 1.98 us -> 1.34 us
  transfers between devices with their start and end apart: 8 -> 6, of which waited for: 2 -> 5; matrix products, arithmetic and copies ran while one was open for 2% -> 4% of each run, Pallas kernels for 13% -> 4%
where the time goes in v11:
time: 60.5 us; the launch traced here: 60.2 us
  starting transfers between devices  24.2 us (40%)
  waiting for transfers between devices  19.9 us (33%)
  Pallas kernels  10 us (17%)
  local copies, waits for them, and re-layouts  4.23 us (7%)
  other arithmetic  1.02 us (2%)
  between operations  0.79 us (1%)
    ppermute x2, starting transfers between devices, from_behind(): return lax.ppermute(block, axis, route)  14 us
    ppermute x4, waiting for transfers between devices, chan_swap(): return lax.ppermute(block, 'chan', [(i, i ^ mask) for i in range(size)])  13.1 us
    ppermute x4, starting transfers between devices, chan_swap(): return lax.ppermute(block, 'chan', [(i, i ^ mask) for i in range(size)])  10.2 us
    ppermute x2, waiting for transfers between devices, from_behind(): return lax.ppermute(block, axis, route)  6.84 us
    pallas_call x1, Pallas kernels, backward_grad(): pl.pallas_call(backward_rows, out_shape=jax.ShapeDtypeStruct((2, rows, ch...  4.82 us
    pallas_call x1, Pallas kernels, forward_partial(): pl.pallas_call(forward_local_rows, out_shape=jax.ShapeDtypeStruct((rows_o...  2.71 us
    pallas_call x1, Pallas kernels, forward_partial(): pl.pallas_call(forward_halo_rows, out_shape=[block, block, jax.ShapeDtype...  2.49 us
    unnamed x16, local copies, waits for them, and re-layouts  1.34 us
  transfers between devices with their start and end apart: 6, of which 5 were waited for; matrix products, arithmetic and copies ran while one was open for 4% of the time, Pallas kernels for 4%

profile of v11, /device:TPU:512, one launch (start us, length us, event | category | flops | bytes accessed | tf_op | source)
XLA Modules:
  0.0 60.2 jit_solution(6927933329854014919)
XLA Ops:
  0.6 0.0 copy-start.7
  0.6 0.0 copy-start
  0.6 1.0 %slice.15 = bf16[1,1,16,32,256]{4,3,2,1,0:T(8,128)(2,1)S(1)} slice(bf16[1,2,16,32,256]{4,3,2,1,0:T(8,128)(2,1)} %param.3), slice={[0:1], [1:2], [0:16], [0:32], [0:256]} | slice | bytes 524288 | tf_op jit(solution)/shard_map/slice | solution.py:192
  1.7 3.4 %collective-permute-start = (bf16[1,1,16,32,256]{4,3,2,1,0:T(8,128)(2,1)S(1)}, bf16[1,1,16,32,256]{4,3,2,1,0:T(8,128)(2,1)S(1)}, u32[]{:S(2)}, u32[]{:S(2)}) collective-permute-start(bf16[1,1,16,32,256]{4,3,2,1,0:T(8,128)(2,1)S(1)} %slice.15), channel_id=1, source_target_pairs={{0,8},{8,16},{16,24},{24,32},{32,40},{40,48},{48,56},{56,64},{64,7... | collective-permute-start | bytes 786440 | tf_op jit(solution)/shard_map/ppermute | solution.py:12
  5.1 0.0 copy-done.7
  5.1 10.6 %collective-permute-start.1 = (bf16[1,1,8,32,128]{4,3,2,1,0:T(8,128)(2,1)S(1)}, bf16[1,1,8,32,128]{4,3,2,1,0:T(8,128)(2,1)S(1)}, u32[]{:S(2)}, u32[]{:S(2)}) collective-permute-start(bf16[1,1,8,32,128]{4,3,2,1,0:T(8,128)(2,1)S(1)} %copy-done.7), channel_id=1, source_target_pairs={{8,0},{16,8},{24,16},{32,24},{40,32},{48,40},{56,48},{64,56},{72,6... | collective-permute-start | bytes 196616 | tf_op jit(solution)/shard_map/ppermute | solution.py:12
  15.7 0.0 copy-done
  15.7 0.3 constant_dynamic-slice_fusion.3
  16.0 0.3 pad_maximum_fusion.1.refs_4_
  16.3 0.0 copy-start.1
  16.3 0.9 %copy.5.kbig_ref = bf16[128,864]{1,0:T(8,128)(2,1)} copy(bf16[128,864]{0,1:T(8,128)(2,1)S(1)} %bitcast.30) | data formatting | bytes 442368 | tf_op jit(solution)/shard_map/reshape | solution.py:107
  17.2 0.0 copy-done.1
  17.2 2.7 %shard_map.50.acc_ref = f32[8,128,128]{2,1,0:T(8,128)} custom-call(bf16[2,16,32,256]{3,2,1,0:T(8,128)(2,1)} %bitcast.33, bf16[128,864]{1,0:T(8,128)(2,1)} %copy.5.kbig_ref), custom_call_target="tpu_custom_call" | custom-call | flops 352321536 | bytes 1048576 | tf_op jit(solution)/shard_map/pallas_call | solution.py:110
  19.9 0.0 collective-permute-done.1
  19.9 0.0 copy-start.2
  19.9 6.8 %collective-permute-done = bf16[1,1,16,32,256]{4,3,2,1,0:T(8,128)(2,1)S(1)} collective-permute-done((bf16[1,1,16,32,256]{4,3,2,1,0:T(8,128)(2,1)S(1)}, bf16[1,1,16,32,256]{4,3,2,1,0:T(8,128)(2,1)S(1)}, u32[]{:S(2)}, u32[]{:S(2)}) %collective-permute-start) | collective-permute-done | bytes 262176 | tf_op jit(solution)/shard_map/ppermute | solution.py:12
  26.8 0.0 copy-start.3
  26.8 0.7 %copy-done.3 = bf16[1,1,16,32,256]{4,3,2,1,0:T(8,128)(2,1)} copy-done((bf16[1,1,16,32,256]{4,3,2,1,0:T(8,128)(2,1)}, bf16[1,1,16,32,256]{4,3,2,1,0:T(8,128)(2,1)S(1)}, u32[]{:S(2)}) %copy-start.3) | copy-done | bytes 262168
  27.5 2.5 %shard_map.51 = (f32[8,32,128]{2,1,0:T(8,128)}, f32[8,32,128]{2,1,0:T(8,128)}, f32[2,8,32,128]{3,2,1,0:T(8,128)}) custom-call(bf16[16,32,256]{2,1,0:T(8,128)(2,1)} %bitcast.32, f32[8,128,128]{2,1,0:T(8,128)} %shard_map.50.acc_ref, bf16[128,864]{1,0:T(8,128)(2,1)} %copy.5.kbig_ref), custom_call_target="tpu_custom_call" | custom-call | flops 176160768 | bytes 1310720 | tf_op jit(solution)/shard_map/pallas_call | solution.py:119
  29.9 4.1 %collective-permute-start.4 = (bf16[2,8,32,128]{3,2,1,0:T(8,128)(2,1)S(1)}, bf16[2,8,32,128]{3,2,1,0:T(8,128)(2,1)S(1)}, u32[]{:S(2)}, u32[]{:S(2)}) collective-permute-start(bf16[2,8,32,128]{3,2,1,0:T(8,128)(2,1)S(1)} %maximum_bitcast_fusion.refs_0_), channel_id=1, source_target_pairs={{0,4},{2,6},{4,0},{6,2},{1,5},{3,7},{5,1},{7,3},{8,12},{10,14},{12... | collective-permute-start | bytes 393224 | tf_op jit(solution)/shard_map/ppermute | solution.py:177
  34.1 2.1 %collective-permute-start.2 = (f32[2,8,32,128]{3,2,1,0:T(8,128)}, f32[2,8,32,128]{3,2,1,0:T(8,128)S(1)}, u32[]{:S(2)}, u32[]{:S(2)}) collective-permute-start(f32[2,8,32,128]{3,2,1,0:T(8,128)} %get-tuple-element.13), channel_id=1, source_target_pairs={{0,2},{2,0},{4,6},{6,4},{1,3},{3,1},{5,7},{7,5},{8,10},{10,8},{12,... | collective-permute-start | bytes 786440 | tf_op jit(solution)/shard_map/ppermute | solution.py:177
  36.2 2.0 %collective-permute-done.4.refs_2_ = bf16[2,8,32,128]{3,2,1,0:T(8,128)(2,1)S(1)} collective-permute-done((bf16[2,8,32,128]{3,2,1,0:T(8,128)(2,1)S(1)}, bf16[2,8,32,128]{3,2,1,0:T(8,128)(2,1)S(1)}, u32[]{:S(2)}, u32[]{:S(2)}) %collective-permute-start.4) | collective-permute-done | bytes 131104 | tf_op jit(solution)/shard_map/ppermute | solution.py:177
  38.2 0.0 copy-start.6
  38.2 0.0 copy-done.2
  38.2 0.0 copy-start.5
  38.2 0.6 %copy-done.6 = bf16[2,8,32,128]{3,2,1,0:T(8,128)(2,1)} copy-done((bf16[2,8,32,128]{3,2,1,0:T(8,128)(2,1)}, bf16[2,8,32,128]{3,2,1,0:T(8,128)(2,1)S(1)}, u32[]{:S(2)}) %copy-start.6) | copy-done | bytes 131096
  38.8 1.9 %collective-permute-start.5 = (bf16[2,2,8,32,128]{4,3,2,1,0:T(8,128)(2,1)S(1)}, bf16[2,2,8,32,128]{4,3,2,1,0:T(8,128)(2,1)S(1)}, u32[]{:S(2)}, u32[]{:S(2)}) collective-permute-start(bf16[2,2,8,32,128]{4,3,2,1,0:T(8,128)(2,1)S(1)} %pad_maximum_fusion), channel_id=1, source_target_pairs={{0,2},{2,0},{4,6},{6,4},{1,3},{3,1},{5,7},{7,5},{8,10},{10,8},{12,... | collective-permute-start | bytes 786440 | tf_op jit(solution)/shard_map/ppermute | solution.py:177
  40.7 4.6 %collective-permute-done.2 = f32[2,8,32,128]{3,2,1,0:T(8,128)S(1)} collective-permute-done((f32[2,8,32,128]{3,2,1,0:T(8,128)}, f32[2,8,32,128]{3,2,1,0:T(8,128)S(1)}, u32[]{:S(2)}, u32[]{:S(2)}) %collective-permute-start.2) | collective-permute-done | bytes 262176 | tf_op jit(solution)/shard_map/ppermute | solution.py:177
  45.4 0.0 copy-done.5
  45.4 0.0 copy-start.4
  45.4 2.1 %collective-permute-start.3 = (f32[8,32,128]{2,1,0:T(8,128)S(1)}, f32[8,32,128]{2,1,0:T(8,128)S(1)}, u32[]{:S(2)}, u32[]{:S(2)}) collective-permute-start(f32[8,32,128]{2,1,0:T(8,128)S(1)} %fusion), channel_id=1, source_target_pairs={{0,4},{2,6},{4,0},{6,2},{1,5},{3,7},{5,1},{7,3},{8,12},{10,14},{12... | collective-permute-start | bytes 393224 | tf_op jit(solution)/shard_map/ppermute | solution.py:177
  47.5 2.3 %collective-permute-done.5 = bf16[2,2,8,32,128]{4,3,2,1,0:T(8,128)(2,1)S(1)} collective-permute-done((bf16[2,2,8,32,128]{4,3,2,1,0:T(8,128)(2,1)S(1)}, bf16[2,2,8,32,128]{4,3,2,1,0:T(8,128)(2,1)S(1)}, u32[]{:S(2)}, u32[]{:S(2)}) %collective-permute-start.5) | collective-permute-done | bytes 262176 | tf_op jit(solution)/shard_map/ppermute | solution.py:177
  49.7 0.7 %slice_bitcast_fusion = (bf16[2,8,32,128]{3,2,1,0:T(8,128)(2,1)}, bf16[2,8,32,128]{3,2,1,0:T(8,128)(2,1)}) fusion(bf16[2,2,8,32,128]{4,3,2,1,0:T(8,128)(2,1)S(1)} %collective-permute-done.5), kind=kLoop, calls=%fused_computation.2 | loop fusion | bytes 524288 | tf_op jit(solution)/shard_map/squeeze | solution.py:202
  50.4 4.3 %collective-permute-done.3 = f32[8,32,128]{2,1,0:T(8,128)S(1)} collective-permute-done((f32[8,32,128]{2,1,0:T(8,128)S(1)}, f32[8,32,128]{2,1,0:T(8,128)S(1)}, u32[]{:S(2)}, u32[]{:S(2)}) %collective-permute-start.3) | collective-permute-done | bytes 131104 | tf_op jit(solution)/shard_map/ppermute | solution.py:177
  54.7 0.0 copy-done.4
  54.7 0.7 %fusion.4 = bf16[1,1,8,32,128]{4,3,2,1,0:T(8,128)(2,1)} fusion(f32[8,32,128]{2,1,0:T(8,128)S(1)} %collective-permute-done.3, f32[8,32,128]{2,1,0:T(8,128)S(1)} %copy-done.4, f32[2,8,32,128]{3,2,1,0:T(8,128)S(1)} %collective-permute-done.2), kind=kLoop, calls=%fused_computation.11 | loop fusion | flops 98304 | bytes 458752 | tf_op jit(solution)/shard_map/reshape | solution.py:200
  55.4 4.8 %shard_map.52 = bf16[2,16,32,256]{3,2,1,0:T(8,128)(2,1)} custom-call(bf16[2,8,32,128]{3,2,1,0:T(8,128)(2,1)} %copy-done.2, bf16[2,8,32,128]{3,2,1,0:T(8,128)(2,1)} %get-tuple-element.17.refs_1_, bf16[2,8,32,128]{3,2,1,0:T(8,128)(2,1)} %copy-done.6, bf16[2,8,32,128]{3,2,1,0:T(8,128)(2,1)} %get-tuple-element.16.refs_3_, bf16[27,32,128]{2,1,0:T(8,128)(2,1)} %copy-done.1), custom_call_target="tpu_custom_call" | custom-call | flops 1006632960 | bytes 1048576 | tf_op jit(solution)/shard_map/pallas_call | solution.py:165
  (3 shorter events, 0.1 us)
Async XLA Ops:
  0.6 4.5 %copy-start.7 = (bf16[1,1,8,32,128]{4,3,2,1,0:T(8,128)(2,1)S(1)}, bf16[1,1,8,32,128]{4,3,2,1,0:T(8,128)(2,1)}, u32[]{:S(2)}) copy-start(bf16[1,1,8,32,128]{4,3,2,1,0:T(8,128)(2,1)} %param.5) | copy-start | bytes 196612
  0.6 15.0 %copy-start = (bf16[27,32,128]{2,1,0:T(8,128)(2,1)S(1)}, bf16[27,32,128]{2,1,0:T(8,128)(2,1)}, u32[]{:S(2)}) copy-start(bf16[27,32,128]{2,1,0:T(8,128)(2,1)} %param.4) | copy-start | bytes 663556
  1.7 25.1 %collective-permute-start = (bf16[1,1,16,32,256]{4,3,2,1,0:T(8,128)(2,1)S(1)}, bf16[1,1,16,32,256]{4,3,2,1,0:T(8,128)(2,1)S(1)}, u32[]{:S(2)}, u32[]{:S(2)}) collective-permute-start(bf16[1,1,16,32,256]{4,3,2,1,0:T(8,128)(2,1)S(1)} %slice.15), channel_id=1, source_target_pairs={{0,8},{8,16},{16,24},{24,32},{32,40},{40,48},{48,56},{56,64},{64,7... | collective-permute-start | bytes 786440 | tf_op jit(solution)/shard_map/ppermute | solution.py:12
  5.1 14.8 %collective-permute-start.1 = (bf16[1,1,8,32,128]{4,3,2,1,0:T(8,128)(2,1)S(1)}, bf16[1,1,8,32,128]{4,3,2,1,0:T(8,128)(2,1)S(1)}, u32[]{:S(2)}, u32[]{:S(2)}) collective-permute-start(bf16[1,1,8,32,128]{4,3,2,1,0:T(8,128)(2,1)S(1)} %copy-done.7), channel_id=1, source_target_pairs={{8,0},{16,8},{24,16},{32,24},{40,32},{48,40},{56,48},{64,56},{72,6... | collective-permute-start | bytes 196616 | tf_op jit(solution)/shard_map/ppermute | solution.py:12
  16.3 0.9 %copy-start.1 = (bf16[27,32,128]{2,1,0:T(8,128)(2,1)}, bf16[27,32,128]{2,1,0:T(8,128)(2,1)S(1)}, u32[]{:S(2)}) copy-start(bf16[27,32,128]{2,1,0:T(8,128)(2,1)S(1)} %pad_maximum_fusion.1.refs_4_) | copy-start | bytes 663556
  19.9 18.3 %copy-start.2 = (bf16[2,8,32,128]{3,2,1,0:T(8,128)(2,1)}, bf16[2,8,32,128]{3,2,1,0:T(8,128)(2,1)S(1)}, u32[]{:S(2)}) copy-start(bf16[2,8,32,128]{3,2,1,0:T(8,128)(2,1)S(1)} %maximum_bitcast_fusion.refs_0_) | copy-start | bytes 393220
  26.8 0.7 %copy-start.3 = (bf16[1,1,16,32,256]{4,3,2,1,0:T(8,128)(2,1)}, bf16[1,1,16,32,256]{4,3,2,1,0:T(8,128)(2,1)S(1)}, u32[]{:S(2)}) copy-start(bf16[1,1,16,32,256]{4,3,2,1,0:T(8,128)(2,1)S(1)} %collective-permute-done) | copy-start | bytes 786436
  29.9 8.2 %collective-permute-start.4 = (bf16[2,8,32,128]{3,2,1,0:T(8,128)(2,1)S(1)}, bf16[2,8,32,128]{3,2,1,0:T(8,128)(2,1)S(1)}, u32[]{:S(2)}, u32[]{:S(2)}) collective-permute-start(bf16[2,8,32,128]{3,2,1,0:T(8,128)(2,1)S(1)} %maximum_bitcast_fusion.refs_0_), channel_id=1, source_target_pairs={{0,4},{2,6},{4,0},{6,2},{1,5},{3,7},{5,1},{7,3},{8,12},{10,14},{12... | collective-permute-start | bytes 393224 | tf_op jit(solution)/shard_map/ppermute | solution.py:177
  34.1 11.3 %collective-permute-start.2 = (f32[2,8,32,128]{3,2,1,0:T(8,128)}, f32[2,8,32,128]{3,2,1,0:T(8,128)S(1)}, u32[]{:S(2)}, u32[]{:S(2)}) collective-permute-start(f32[2,8,32,128]{3,2,1,0:T(8,128)} %get-tuple-element.13), channel_id=1, source_target_pairs={{0,2},{2,0},{4,6},{6,4},{1,3},{3,1},{5,7},{7,5},{8,10},{10,8},{12,... | collective-permute-start | bytes 786440 | tf_op jit(solution)/shard_map/ppermute | solution.py:177
  38.2 0.7 %copy-start.6 = (bf16[2,8,32,128]{3,2,1,0:T(8,128)(2,1)}, bf16[2,8,32,128]{3,2,1,0:T(8,128)(2,1)S(1)}, u32[]{:S(2)}) copy-start(bf16[2,8,32,128]{3,2,1,0:T(8,128)(2,1)S(1)} %collective-permute-done.4.refs_2_) | copy-start | bytes 393220
  38.2 7.2 %copy-start.5 = (f32[8,32,128]{2,1,0:T(8,128)S(1)}, f32[8,32,128]{2,1,0:T(8,128)}, u32[]{:S(2)}) copy-start(f32[8,32,128]{2,1,0:T(8,128)} %get-tuple-element.14) | copy-start | bytes 393220
  38.8 10.9 %collective-permute-start.5 = (bf16[2,2,8,32,128]{4,3,2,1,0:T(8,128)(2,1)S(1)}, bf16[2,2,8,32,128]{4,3,2,1,0:T(8,128)(2,1)S(1)}, u32[]{:S(2)}, u32[]{:S(2)}) collective-permute-start(bf16[2,2,8,32,128]{4,3,2,1,0:T(8,128)(2,1)S(1)} %pad_maximum_fusion), channel_id=1, source_target_pairs={{0,2},{2,0},{4,6},{6,4},{1,3},{3,1},{5,7},{7,5},{8,10},{10,8},{12,... | collective-permute-start | bytes 786440 | tf_op jit(solution)/shard_map/ppermute | solution.py:177
  45.4 9.3 %copy-start.4 = (f32[8,32,128]{2,1,0:T(8,128)S(1)}, f32[8,32,128]{2,1,0:T(8,128)}, u32[]{:S(2)}) copy-start(f32[8,32,128]{2,1,0:T(8,128)} %get-tuple-element.12) | copy-start | bytes 393220
  45.4 9.3 %collective-permute-start.3 = (f32[8,32,128]{2,1,0:T(8,128)S(1)}, f32[8,32,128]{2,1,0:T(8,128)S(1)}, u32[]{:S(2)}, u32[]{:S(2)}) collective-permute-start(f32[8,32,128]{2,1,0:T(8,128)S(1)} %fusion), channel_id=1, source_target_pairs={{0,4},{2,6},{4,0},{6,2},{1,5},{3,7},{5,1},{7,3},{8,12},{10,14},{12... | collective-permute-start | bytes 393224 | tf_op jit(solution)/shard_map/ppermute | solution.py:177

commit v12 on v11

--- a/solution.py
+++ b/solution.py
@@ -196,9 +196,10 @@
     near = chan_swap(sent, 1)
     across = chan_swap(pair, 2)
     far_sum = far_block + near[1]
+    other = chan_swap(jnp.stack([pair, across]), 1)
+    other, far_sum = lax.optimization_barrier((other, far_sum))
     total = (own_block + near[0]) + chan_swap(far_sum, 2)
     response = total.astype(jnp.bfloat16).reshape(count, planes_out, rows_out, share, cols_out)
-    other = chan_swap(jnp.stack([pair, across]), 1)
     pieces = [pair, other[0], across, other[1]]
     volume_grad = backward_grad(pieces, kernel).reshape(count, planes_in, rows_in, chans_in, cols_in)
     return (response, volume_grad)

time: 60.5 us -> 58.7 us (0.970)
  waiting for transfers between devices: 19.9 us -> 16.4 us
  starting transfers between devices: 24.2 us -> 25.9 us
    ppermute x4, waiting for transfers between devices: 13.1 us -> 9.53 us  [chan_swap(): return lax.ppermute(block, 'chan', [(i, i ^ mask) for i in range(size)])]
    ppermute x4, starting transfers between devices: 10.2 us -> 12 us  [chan_swap(): return lax.ppermute(block, 'chan', [(i, i ^ mask) for i in range(size)])]
  transfers between devices with their start and end apart: 6 -> 6, of which waited for: 5 -> 4; matrix products, arithmetic and copies ran while one was open for 4% -> 4% of each run, Pallas kernels for 4% -> 13%
where the time goes in v12:
time: 58.7 us; the launch traced here: 58.4 us
  starting transfers between devices  25.9 us (44%)
  waiting for transfers between devices  16.4 us (28%)
  Pallas kernels  10 us (17%)
  local copies, waits for them, and re-layouts  4.23 us (7%)
  other arithmetic  1.02 us (2%)
  between operations  0.78 us (1%)
    ppermute x2, starting transfers between devices, from_behind(): return lax.ppermute(block, axis, route)  14 us
    ppermute x4, starting transfers between devices, chan_swap(): return lax.ppermute(block, 'chan', [(i, i ^ mask) for i in range(size)])  12 us
    ppermute x4, waiting for transfers between devices, chan_swap(): return lax.ppermute(block, 'chan', [(i, i ^ mask) for i in range(size)])  9.53 us
    ppermute x2, waiting for transfers between devices, from_behind(): return lax.ppermute(block, axis, route)  6.84 us
    pallas_call x1, Pallas kernels, backward_grad(): pl.pallas_call(backward_rows, out_shape=jax.ShapeDtypeStruct((2, rows, ch...  4.84 us
    pallas_call x1, Pallas kernels, forward_partial(): pl.pallas_call(forward_local_rows, out_shape=jax.ShapeDtypeStruct((rows_o...  2.71 us
    pallas_call x1, Pallas kernels, forward_partial(): pl.pallas_call(forward_halo_rows, out_shape=[block, block, jax.ShapeDtype...  2.48 us
    unnamed x16, local copies, waits for them, and re-layouts  1.34 us
  transfers between devices with their start and end apart: 6, of which 4 were waited for; matrix products, arithmetic and copies ran while one was open for 4% of the time, Pallas kernels for 13%

profile of v12, /device:TPU:512, one launch (start us, length us, event | category | flops | bytes accessed | tf_op | source)
XLA Modules:
  0.0 58.4 jit_solution(2331094006571772348)
XLA Ops:
  0.6 0.0 copy-start.7
  0.6 0.0 copy-start
  0.6 1.0 %slice.15 = bf16[1,1,16,32,256]{4,3,2,1,0:T(8,128)(2,1)S(1)} slice(bf16[1,2,16,32,256]{4,3,2,1,0:T(8,128)(2,1)} %param.3), slice={[0:1], [1:2], [0:16], [0:32], [0:256]} | slice | bytes 524288 | tf_op jit(solution)/shard_map/slice | solution.py:192
  1.7 3.4 %collective-permute-start = (bf16[1,1,16,32,256]{4,3,2,1,0:T(8,128)(2,1)S(1)}, bf16[1,1,16,32,256]{4,3,2,1,0:T(8,128)(2,1)S(1)}, u32[]{:S(2)}, u32[]{:S(2)}) collective-permute-start(bf16[1,1,16,32,256]{4,3,2,1,0:T(8,128)(2,1)S(1)} %slice.15), channel_id=1, source_target_pairs={{0,8},{8,16},{16,24},{24,32},{32,40},{40,48},{48,56},{56,64},{64,7... | collective-permute-start | bytes 786440 | tf_op jit(solution)/shard_map/ppermute | solution.py:12
  5.1 0.0 copy-done.7
  5.1 10.6 %collective-permute-start.1 = (bf16[1,1,8,32,128]{4,3,2,1,0:T(8,128)(2,1)S(1)}, bf16[1,1,8,32,128]{4,3,2,1,0:T(8,128)(2,1)S(1)}, u32[]{:S(2)}, u32[]{:S(2)}) collective-permute-start(bf16[1,1,8,32,128]{4,3,2,1,0:T(8,128)(2,1)S(1)} %copy-done.7), channel_id=1, source_target_pairs={{8,0},{16,8},{24,16},{32,24},{40,32},{48,40},{56,48},{64,56},{72,6... | collective-permute-start | bytes 196616 | tf_op jit(solution)/shard_map/ppermute | solution.py:12
  15.7 0.0 copy-done
  15.7 0.3 constant_dynamic-slice_fusion.3
  16.0 0.3 pad_maximum_fusion.1.refs_4_
  16.3 0.0 copy-start.1
  16.3 0.9 %copy.5.kbig_ref = bf16[128,864]{1,0:T(8,128)(2,1)} copy(bf16[128,864]{0,1:T(8,128)(2,1)S(1)} %bitcast.30) | data formatting | bytes 442368 | tf_op jit(solution)/shard_map/reshape | solution.py:107
  17.2 0.0 copy-done.1
  17.2 2.7 %shard_map.50.acc_ref = f32[8,128,128]{2,1,0:T(8,128)} custom-call(bf16[2,16,32,256]{3,2,1,0:T(8,128)(2,1)} %bitcast.33, bf16[128,864]{1,0:T(8,128)(2,1)} %copy.5.kbig_ref), custom_call_target="tpu_custom_call" | custom-call | flops 352321536 | bytes 1048576 | tf_op jit(solution)/shard_map/pallas_call | solution.py:110
  19.9 0.0 collective-permute-done.1
  19.9 0.0 copy-start.2
  19.9 6.8 %collective-permute-done = bf16[1,1,16,32,256]{4,3,2,1,0:T(8,128)(2,1)S(1)} collective-permute-done((bf16[1,1,16,32,256]{4,3,2,1,0:T(8,128)(2,1)S(1)}, bf16[1,1,16,32,256]{4,3,2,1,0:T(8,128)(2,1)S(1)}, u32[]{:S(2)}, u32[]{:S(2)}) %collective-permute-start) | collective-permute-done | bytes 262176 | tf_op jit(solution)/shard_map/ppermute | solution.py:12
  26.8 0.0 copy-start.3
  26.8 0.7 %copy-done.3 = bf16[1,1,16,32,256]{4,3,2,1,0:T(8,128)(2,1)} copy-done((bf16[1,1,16,32,256]{4,3,2,1,0:T(8,128)(2,1)}, bf16[1,1,16,32,256]{4,3,2,1,0:T(8,128)(2,1)S(1)}, u32[]{:S(2)}) %copy-start.3) | copy-done | bytes 262168
  27.5 2.5 %shard_map.51 = (f32[8,32,128]{2,1,0:T(8,128)}, f32[8,32,128]{2,1,0:T(8,128)}, f32[2,8,32,128]{3,2,1,0:T(8,128)}) custom-call(bf16[16,32,256]{2,1,0:T(8,128)(2,1)} %bitcast.32, f32[8,128,128]{2,1,0:T(8,128)} %shard_map.50.acc_ref, bf16[128,864]{1,0:T(8,128)(2,1)} %copy.5.kbig_ref), custom_call_target="tpu_custom_call" | custom-call | flops 176160768 | bytes 1310720 | tf_op jit(solution)/shard_map/pallas_call | solution.py:119
  29.9 4.1 %collective-permute-start.3 = (bf16[2,8,32,128]{3,2,1,0:T(8,128)(2,1)S(1)}, bf16[2,8,32,128]{3,2,1,0:T(8,128)(2,1)S(1)}, u32[]{:S(2)}, u32[]{:S(2)}) collective-permute-start(bf16[2,8,32,128]{3,2,1,0:T(8,128)(2,1)S(1)} %maximum_bitcast_fusion.refs_0_), channel_id=1, source_target_pairs={{0,4},{2,6},{4,0},{6,2},{1,5},{3,7},{5,1},{7,3},{8,12},{10,14},{12... | collective-permute-start | bytes 393224 | tf_op jit(solution)/shard_map/ppermute | solution.py:177
  34.0 2.1 %collective-permute-start.2 = (f32[2,8,32,128]{3,2,1,0:T(8,128)}, f32[2,8,32,128]{3,2,1,0:T(8,128)S(1)}, u32[]{:S(2)}, u32[]{:S(2)}) collective-permute-start(f32[2,8,32,128]{3,2,1,0:T(8,128)} %get-tuple-element.15), channel_id=1, source_target_pairs={{0,2},{2,0},{4,6},{6,4},{1,3},{3,1},{5,7},{7,5},{8,10},{10,8},{12,... | collective-permute-start | bytes 786440 | tf_op jit(solution)/shard_map/ppermute | solution.py:177
  36.2 2.0 %collective-permute-done.3.refs_2_ = bf16[2,8,32,128]{3,2,1,0:T(8,128)(2,1)S(1)} collective-permute-done((bf16[2,8,32,128]{3,2,1,0:T(8,128)(2,1)S(1)}, bf16[2,8,32,128]{3,2,1,0:T(8,128)(2,1)S(1)}, u32[]{:S(2)}, u32[]{:S(2)}) %collective-permute-start.3) | collective-permute-done | bytes 131104 | tf_op jit(solution)/shard_map/ppermute | solution.py:177
  38.2 0.0 copy-start.6
  38.2 0.0 copy-done.2
  38.2 0.0 copy-start.5
  38.2 0.6 %copy-done.6 = bf16[2,8,32,128]{3,2,1,0:T(8,128)(2,1)} copy-done((bf16[2,8,32,128]{3,2,1,0:T(8,128)(2,1)}, bf16[2,8,32,128]{3,2,1,0:T(8,128)(2,1)S(1)}, u32[]{:S(2)}) %copy-start.6) | copy-done | bytes 131096
  38.8 1.9 %collective-permute-start.4 = (bf16[2,2,8,32,128]{4,3,2,1,0:T(8,128)(2,1)S(1)}, bf16[2,2,8,32,128]{4,3,2,1,0:T(8,128)(2,1)S(1)}, u32[]{:S(2)}, u32[]{:S(2)}) collective-permute-start(bf16[2,2,8,32,128]{4,3,2,1,0:T(8,128)(2,1)S(1)} %pad_maximum_fusion), channel_id=1, source_target_pairs={{0,2},{2,0},{4,6},{6,4},{1,3},{3,1},{5,7},{7,5},{8,10},{10,8},{12,... | collective-permute-start | bytes 786440 | tf_op jit(solution)/shard_map/ppermute | solution.py:177
  40.7 4.6 %collective-permute-done.2 = f32[2,8,32,128]{3,2,1,0:T(8,128)S(1)} collective-permute-done((f32[2,8,32,128]{3,2,1,0:T(8,128)}, f32[2,8,32,128]{3,2,1,0:T(8,128)S(1)}, u32[]{:S(2)}, u32[]{:S(2)}) %collective-permute-start.2) | collective-permute-done | bytes 262176 | tf_op jit(solution)/shard_map/ppermute | solution.py:177
  45.4 0.0 copy-done.5
  45.4 2.9 %collective-permute-done.4 = bf16[2,2,8,32,128]{4,3,2,1,0:T(8,128)(2,1)S(1)} collective-permute-done((bf16[2,2,8,32,128]{4,3,2,1,0:T(8,128)(2,1)S(1)}, bf16[2,2,8,32,128]{4,3,2,1,0:T(8,128)(2,1)S(1)}, u32[]{:S(2)}, u32[]{:S(2)}) %collective-permute-start.4) | collective-permute-done | bytes 262176 | tf_op jit(solution)/shard_map/ppermute | solution.py:177
  48.3 3.8 %collective-permute-start.5 = (f32[8,32,128]{2,1,0:T(8,128)S(1)}, f32[8,32,128]{2,1,0:T(8,128)S(1)}, u32[]{:S(2)}, u32[]{:S(2)}) collective-permute-start(f32[8,32,128]{2,1,0:T(8,128)S(1)} %fusion), channel_id=1, source_target_pairs={{0,4},{2,6},{4,0},{6,2},{1,5},{3,7},{5,1},{7,3},{8,12},{10,14},{12... | collective-permute-start | bytes 393224 | tf_op jit(solution)/shard_map/ppermute | solution.py:177
  52.1 0.7 %slice_bitcast_fusion.2 = (bf16[2,8,32,128]{3,2,1,0:T(8,128)(2,1)}, bf16[2,8,32,128]{3,2,1,0:T(8,128)(2,1)}) fusion(bf16[2,2,8,32,128]{4,3,2,1,0:T(8,128)(2,1)S(1)} %collective-permute-done.4), kind=kLoop, calls=%fused_computation.9 | loop fusion | bytes 524288 | tf_op jit(solution)/shard_map/squeeze | solution.py:203
  52.8 0.0 copy-start.4
  52.8 4.8 %shard_map.52 = bf16[2,16,32,256]{3,2,1,0:T(8,128)(2,1)} custom-call(bf16[2,8,32,128]{3,2,1,0:T(8,128)(2,1)} %copy-done.2, bf16[2,8,32,128]{3,2,1,0:T(8,128)(2,1)} %get-tuple-element.21.refs_1_, bf16[2,8,32,128]{3,2,1,0:T(8,128)(2,1)} %copy-done.6, bf16[2,8,32,128]{3,2,1,0:T(8,128)(2,1)} %get-tuple-element.20.refs_3_, bf16[27,32,128]{2,1,0:T(8,128)(2,1)} %copy-done.1), custom_call_target="tpu_custom_call" | custom-call | flops 1006632960 | bytes 1048576 | tf_op jit(solution)/shard_map/pallas_call | solution.py:165
  57.7 0.0 collective-permute-done.5
  57.7 0.0 copy-done.4
  57.7 0.7 %fusion.4 = bf16[1,1,8,32,128]{4,3,2,1,0:T(8,128)(2,1)} fusion(f32[8,32,128]{2,1,0:T(8,128)S(1)} %collective-permute-done.5, f32[8,32,128]{2,1,0:T(8,128)S(1)} %copy-done.4, f32[2,8,32,128]{3,2,1,0:T(8,128)S(1)} %collective-permute-done.2), kind=kLoop, calls=%fused_computation.11 | loop fusion | flops 98304 | bytes 458752 | tf_op jit(solution)/shard_map/reshape | solution.py:202
  (3 shorter events, 0.1 us)
Async XLA Ops:
  0.6 4.5 %copy-start.7 = (bf16[1,1,8,32,128]{4,3,2,1,0:T(8,128)(2,1)S(1)}, bf16[1,1,8,32,128]{4,3,2,1,0:T(8,128)(2,1)}, u32[]{:S(2)}) copy-start(bf16[1,1,8,32,128]{4,3,2,1,0:T(8,128)(2,1)} %param.5) | copy-start | bytes 196612
  0.6 15.0 %copy-start = (bf16[27,32,128]{2,1,0:T(8,128)(2,1)S(1)}, bf16[27,32,128]{2,1,0:T(8,128)(2,1)}, u32[]{:S(2)}) copy-start(bf16[27,32,128]{2,1,0:T(8,128)(2,1)} %param.4) | copy-start | bytes 663556
  1.7 25.1 %collective-permute-start = (bf16[1,1,16,32,256]{4,3,2,1,0:T(8,128)(2,1)S(1)}, bf16[1,1,16,32,256]{4,3,2,1,0:T(8,128)(2,1)S(1)}, u32[]{:S(2)}, u32[]{:S(2)}) collective-permute-start(bf16[1,1,16,32,256]{4,3,2,1,0:T(8,128)(2,1)S(1)} %slice.15), channel_id=1, source_target_pairs={{0,8},{8,16},{16,24},{24,32},{32,40},{40,48},{48,56},{56,64},{64,7... | collective-permute-start | bytes 786440 | tf_op jit(solution)/shard_map/ppermute | solution.py:12
  5.1 14.8 %collective-permute-start.1 = (bf16[1,1,8,32,128]{4,3,2,1,0:T(8,128)(2,1)S(1)}, bf16[1,1,8,32,128]{4,3,2,1,0:T(8,128)(2,1)S(1)}, u32[]{:S(2)}, u32[]{:S(2)}) collective-permute-start(bf16[1,1,8,32,128]{4,3,2,1,0:T(8,128)(2,1)S(1)} %copy-done.7), channel_id=1, source_target_pairs={{8,0},{16,8},{24,16},{32,24},{40,32},{48,40},{56,48},{64,56},{72,6... | collective-permute-start | bytes 196616 | tf_op jit(solution)/shard_map/ppermute | solution.py:12
  16.3 0.9 %copy-start.1 = (bf16[27,32,128]{2,1,0:T(8,128)(2,1)}, bf16[27,32,128]{2,1,0:T(8,128)(2,1)S(1)}, u32[]{:S(2)}) copy-start(bf16[27,32,128]{2,1,0:T(8,128)(2,1)S(1)} %pad_maximum_fusion.1.refs_4_) | copy-start | bytes 663556
  19.9 18.2 %copy-start.2 = (bf16[2,8,32,128]{3,2,1,0:T(8,128)(2,1)}, bf16[2,8,32,128]{3,2,1,0:T(8,128)(2,1)S(1)}, u32[]{:S(2)}) copy-start(bf16[2,8,32,128]{3,2,1,0:T(8,128)(2,1)S(1)} %maximum_bitcast_fusion.refs_0_) | copy-start | bytes 393220
  26.8 0.7 %copy-start.3 = (bf16[1,1,16,32,256]{4,3,2,1,0:T(8,128)(2,1)}, bf16[1,1,16,32,256]{4,3,2,1,0:T(8,128)(2,1)S(1)}, u32[]{:S(2)}) copy-start(bf16[1,1,16,32,256]{4,3,2,1,0:T(8,128)(2,1)S(1)} %collective-permute-done) | copy-start | bytes 786436
  29.9 8.2 %collective-permute-start.3 = (bf16[2,8,32,128]{3,2,1,0:T(8,128)(2,1)S(1)}, bf16[2,8,32,128]{3,2,1,0:T(8,128)(2,1)S(1)}, u32[]{:S(2)}, u32[]{:S(2)}) collective-permute-start(bf16[2,8,32,128]{3,2,1,0:T(8,128)(2,1)S(1)} %maximum_bitcast_fusion.refs_0_), channel_id=1, source_target_pairs={{0,4},{2,6},{4,0},{6,2},{1,5},{3,7},{5,1},{7,3},{8,12},{10,14},{12... | collective-permute-start | bytes 393224 | tf_op jit(solution)/shard_map/ppermute | solution.py:177
  34.0 11.3 %collective-permute-start.2 = (f32[2,8,32,128]{3,2,1,0:T(8,128)}, f32[2,8,32,128]{3,2,1,0:T(8,128)S(1)}, u32[]{:S(2)}, u32[]{:S(2)}) collective-permute-start(f32[2,8,32,128]{3,2,1,0:T(8,128)} %get-tuple-element.15), channel_id=1, source_target_pairs={{0,2},{2,0},{4,6},{6,4},{1,3},{3,1},{5,7},{7,5},{8,10},{10,8},{12,... | collective-permute-start | bytes 786440 | tf_op jit(solution)/shard_map/ppermute | solution.py:177
  38.2 0.7 %copy-start.6 = (bf16[2,8,32,128]{3,2,1,0:T(8,128)(2,1)}, bf16[2,8,32,128]{3,2,1,0:T(8,128)(2,1)S(1)}, u32[]{:S(2)}) copy-start(bf16[2,8,32,128]{3,2,1,0:T(8,128)(2,1)S(1)} %collective-permute-done.3.refs_2_) | copy-start | bytes 393220
  38.2 7.2 %copy-start.5 = (f32[8,32,128]{2,1,0:T(8,128)S(1)}, f32[8,32,128]{2,1,0:T(8,128)}, u32[]{:S(2)}) copy-start(f32[8,32,128]{2,1,0:T(8,128)} %get-tuple-element.17) | copy-start | bytes 393220
  38.8 9.5 %collective-permute-start.4 = (bf16[2,2,8,32,128]{4,3,2,1,0:T(8,128)(2,1)S(1)}, bf16[2,2,8,32,128]{4,3,2,1,0:T(8,128)(2,1)S(1)}, u32[]{:S(2)}, u32[]{:S(2)}) collective-permute-start(bf16[2,2,8,32,128]{4,3,2,1,0:T(8,128)(2,1)S(1)} %pad_maximum_fusion), channel_id=1, source_target_pairs={{0,2},{2,0},{4,6},{6,4},{1,3},{3,1},{5,7},{7,5},{8,10},{10,8},{12,... | collective-permute-start | bytes 786440 | tf_op jit(solution)/shard_map/ppermute | solution.py:177
  48.3 9.4 %collective-permute-start.5 = (f32[8,32,128]{2,1,0:T(8,128)S(1)}, f32[8,32,128]{2,1,0:T(8,128)S(1)}, u32[]{:S(2)}, u32[]{:S(2)}) collective-permute-start(f32[8,32,128]{2,1,0:T(8,128)S(1)} %fusion), channel_id=1, source_target_pairs={{0,4},{2,6},{4,0},{6,2},{1,5},{3,7},{5,1},{7,3},{8,12},{10,14},{12... | collective-permute-start | bytes 393224 | tf_op jit(solution)/shard_map/ppermute | solution.py:177
  52.8 4.9 %copy-start.4 = (f32[8,32,128]{2,1,0:T(8,128)S(1)}, f32[8,32,128]{2,1,0:T(8,128)}, u32[]{:S(2)}) copy-start(f32[8,32,128]{2,1,0:T(8,128)} %get-tuple-element.14) | copy-start | bytes 393220

commit v13 on v10

--- a/solution.py
+++ b/solution.py
@@ -185,14 +185,14 @@
     me = lax.axis_index("chan")
     kernel = jnp.roll(kernel, -me * share, axis=2)
     below = from_behind(volume[:, -1:], "space", 1)
+    pair = jnp.concatenate([cotangent, from_behind(cotangent, "space", -1)], axis=1)
+    pieces = [pair[0]] + [chan_shift(pair[0], -k) for k in range(1, groups)]
+    pieces, below = lax.optimization_barrier((pieces, below))
     chunks = forward_partial(below[0, 0], volume[0], kernel, groups)
-    pair = jnp.concatenate([cotangent, from_behind(cotangent, "space", -1)], axis=1)
-    chunks, pair = lax.optimization_barrier((chunks, pair))
     total = chunks[0]
     for k in range(1, groups):
         total = total + chan_shift(chunks[k], k)
     response = total.astype(jnp.bfloat16).reshape(count, planes_out, rows_out, share, cols_out)
-    pieces = [pair[0]] + [chan_shift(pair[0], -k) for k in range(1, groups)]
     volume_grad = backward_grad(pieces, kernel).reshape(count, planes_in, rows_in, chans_in, cols_in)
     return (response, volume_grad)
 

time: 57.9 us -> 63.2 us (1.092)
  the two profiles are of different devices: /device:TPU:512 before, /device:TPU:401 now
where the time goes in v13:
time: 63.2 us; the launch traced here: 62.8 us
  starting transfers between devices  25.7 us (41%)
  waiting for transfers between devices  22.8 us (36%)
  Pallas kernels  10 us (16%)
  local copies, waits for them, and re-layouts  2.59 us (4%)
  other arithmetic  0.91 us (1%)
  between operations  0.81 us (1%)
    ppermute x6, waiting for transfers between devices, chan_shift(): lax.ppermute(block, 'chan', [(i, (i + shift) % size) for i in range(size)])  22.8 us
    ppermute x6, starting transfers between devices, chan_shift(): lax.ppermute(block, 'chan', [(i, (i + shift) % size) for i in range(size)])  16.1 us
    ppermute x2, starting transfers between devices, from_behind(): return lax.ppermute(block, axis, route)  9.55 us
    pallas_call x1, Pallas kernels, backward_grad(): pl.pallas_call(backward_rows, out_shape=jax.ShapeDtypeStruct((2, rows, ch...  4.82 us
    pallas_call x1, Pallas kernels, forward_partial(): pl.pallas_call(forward_local_rows, out_shape=jax.ShapeDtypeStruct((rows_o...  2.71 us
    pallas_call x1, Pallas kernels, forward_partial(): pl.pallas_call(forward_halo_rows, out_shape=[jax.ShapeDtypeStruct((rows_o...  2.5 us
  transfers between devices with their start and end apart: 8, of which 4 were waited for; matrix products, arithmetic and copies ran while one was open for 3% of the time, Pallas kernels for 12%

profile of v13, /device:TPU:401, one launch (start us, length us, event | category | flops | bytes accessed | tf_op | source)
XLA Modules:
  0.0 62.8 jit_solution(7554105145809935445)
XLA Ops:
  0.6 7.5 %collective-permute-start = (bf16[1,1,8,32,128]{4,3,2,1,0:T(8,128)(2,1)}, bf16[1,1,8,32,128]{4,3,2,1,0:T(8,128)(2,1)S(1)}, u32[]{:S(2)}, u32[]{:S(2)}) collective-permute-start(bf16[1,1,8,32,128]{4,3,2,1,0:T(8,128)(2,1)} %param.5), channel_id=1, source_target_pairs={{8,0},{16,8},{24,16},{32,24},{40,32},{48,40},{56,48},{64,56},{72,6... | collective-permute-start | bytes 196616 | tf_op jit(solution)/shard_map/ppermute | solution.py:12
  8.1 0.0 copy-start.5
  8.1 1.0 %slice.3 = bf16[1,1,16,32,256]{4,3,2,1,0:T(8,128)(2,1)S(1)} slice(bf16[1,2,16,32,256]{4,3,2,1,0:T(8,128)(2,1)} %param.3), slice={[0:1], [1:2], [0:16], [0:32], [0:256]} | slice | bytes 524288 | tf_op jit(solution)/shard_map/slice | solution.py:187
  9.1 0.0 copy-start.2
  9.2 2.1 %collective-permute-start.4 = (bf16[1,1,16,32,256]{4,3,2,1,0:T(8,128)(2,1)S(1)}, bf16[1,1,16,32,256]{4,3,2,1,0:T(8,128)(2,1)S(1)}, u32[]{:S(2)}, u32[]{:S(2)}) collective-permute-start(bf16[1,1,16,32,256]{4,3,2,1,0:T(8,128)(2,1)S(1)} %slice.3), channel_id=1, source_target_pairs={{0,8},{8,16},{16,24},{24,32},{32,40},{40,48},{48,56},{56,64},{64,7... | collective-permute-start | bytes 786440 | tf_op jit(solution)/shard_map/ppermute | solution.py:12
  11.2 0.0 collective-permute-done
  11.3 0.0 copy-done.5
  11.3 0.0 copy-start.3
  11.3 2.4 %collective-permute-start.3 = (bf16[2,8,32,128]{3,2,1,0:T(8,128)(2,1)S(1)}, bf16[2,8,32,128]{3,2,1,0:T(8,128)(2,1)S(1)}, u32[]{:S(2)}, u32[]{:S(2)}) collective-permute-start(bf16[2,8,32,128]{3,2,1,0:T(8,128)(2,1)S(1)} %maximum_bitcast_fusion.refs_0_), channel_id=1, source_target_pairs={{0,2},{2,4},{4,6},{6,0},{1,3},{3,5},{5,7},{7,1},{8,10},{10,12},{12... | collective-permute-start | bytes 393224 | tf_op jit(solution)/shard_map/ppermute | solution.py:174
  13.7 4.4 %collective-permute-start.2 = (bf16[2,8,32,128]{3,2,1,0:T(8,128)(2,1)S(1)}, bf16[2,8,32,128]{3,2,1,0:T(8,128)(2,1)S(1)}, u32[]{:S(2)}, u32[]{:S(2)}) collective-permute-start(bf16[2,8,32,128]{3,2,1,0:T(8,128)(2,1)S(1)} %maximum_bitcast_fusion.refs_0_), channel_id=1, source_target_pairs={{0,4},{2,6},{4,0},{6,2},{1,5},{3,7},{5,1},{7,3},{8,12},{10,14},{12... | collective-permute-start | bytes 393224 | tf_op jit(solution)/shard_map/ppermute | solution.py:174
  18.2 1.9 %collective-permute-start.1 = (bf16[2,8,32,128]{3,2,1,0:T(8,128)(2,1)S(1)}, bf16[2,8,32,128]{3,2,1,0:T(8,128)(2,1)S(1)}, u32[]{:S(2)}, u32[]{:S(2)}) collective-permute-start(bf16[2,8,32,128]{3,2,1,0:T(8,128)(2,1)S(1)} %maximum_bitcast_fusion.refs_0_), channel_id=1, source_target_pairs={{0,6},{2,0},{4,2},{6,4},{1,7},{3,1},{5,3},{7,5},{8,14},{10,8},{12,... | collective-permute-start | bytes 393224 | tf_op jit(solution)/shard_map/ppermute | solution.py:174
  20.1 0.0 copy-done.2
  20.1 0.2 fusion.refs_4_
  20.3 0.0 copy-done.3
  20.3 0.0 copy-start
  20.4 0.8 %copy.5.kbig_ref = bf16[128,864]{1,0:T(8,128)(2,1)} copy(bf16[128,864]{0,1:T(8,128)(2,1)S(1)} %bitcast.10) | data formatting | bytes 442368 | tf_op jit(solution)/shard_map/reshape | solution.py:105
  21.2 0.0 copy-done
  21.2 2.7 %shard_map.50.acc_ref = f32[8,128,128]{2,1,0:T(8,128)} custom-call(bf16[2,16,32,256]{3,2,1,0:T(8,128)(2,1)} %bitcast.12, bf16[128,864]{1,0:T(8,128)(2,1)} %copy.5.kbig_ref), custom_call_target="tpu_custom_call" | custom-call | flops 352321536 | bytes 1048576 | tf_op jit(solution)/shard_map/pallas_call | solution.py:108
  23.9 0.0 collective-permute-done.3.refs_3_
  23.9 0.0 copy-start.6
  23.9 15.6 %collective-permute-done.2.refs_2_ = bf16[2,8,32,128]{3,2,1,0:T(8,128)(2,1)S(1)} collective-permute-done((bf16[2,8,32,128]{3,2,1,0:T(8,128)(2,1)S(1)}, bf16[2,8,32,128]{3,2,1,0:T(8,128)(2,1)S(1)}, u32[]{:S(2)}, u32[]{:S(2)}) %collective-permute-start.2) | collective-permute-done | bytes 131104 | tf_op jit(solution)/shard_map/ppermute | solution.py:174
  39.6 0.0 copy-start.7
  39.6 3.3 %collective-permute-done.1.refs_1_ = bf16[2,8,32,128]{3,2,1,0:T(8,128)(2,1)S(1)} collective-permute-done((bf16[2,8,32,128]{3,2,1,0:T(8,128)(2,1)S(1)}, bf16[2,8,32,128]{3,2,1,0:T(8,128)(2,1)S(1)}, u32[]{:S(2)}, u32[]{:S(2)}) %collective-permute-start.1) | collective-permute-done | bytes 131104 | tf_op jit(solution)/shard_map/ppermute | solution.py:174
  42.9 0.0 copy-start.8
  42.9 0.0 collective-permute-done.4
  42.9 0.0 copy-start.1
  42.9 0.7 %copy-done.1 = bf16[1,1,16,32,256]{4,3,2,1,0:T(8,128)(2,1)} copy-done((bf16[1,1,16,32,256]{4,3,2,1,0:T(8,128)(2,1)}, bf16[1,1,16,32,256]{4,3,2,1,0:T(8,128)(2,1)S(1)}, u32[]{:S(2)}) %copy-start.1) | copy-done | bytes 262168
  43.6 2.5 %shard_map.51 = (f32[8,32,128]{2,1,0:T(8,128)}, f32[8,32,128]{2,1,0:T(8,128)}, f32[8,32,128]{2,1,0:T(8,128)}, f32[8,32,128]{2,1,0:T(8,128)}) custom-call(bf16[16,32,256]{2,1,0:T(8,128)(2,1)} %bitcast.11, f32[8,128,128]{2,1,0:T(8,128)} %shard_map.50.acc_ref, bf16[128,864]{1,0:T(8,128)(2,1)} %copy.5.kbig_ref), custom_call_target="tpu_custom_call" | custom-call | flops 176160768 | bytes 1310720 | tf_op jit(solution)/shard_map/pallas_call | solution.py:116
  46.1 0.0 copy-done.6
  46.1 0.0 copy-done.7
  46.1 0.0 copy-done.8
  46.1 1.9 %collective-permute-start.5 = (f32[8,32,128]{2,1,0:T(8,128)}, f32[8,32,128]{2,1,0:T(8,128)S(1)}, u32[]{:S(2)}, u32[]{:S(2)}) collective-permute-start(f32[8,32,128]{2,1,0:T(8,128)} %get-tuple-element.13), channel_id=1, source_target_pairs={{0,2},{2,4},{4,6},{6,0},{1,3},{3,5},{5,7},{7,1},{8,10},{10,12},{12... | collective-permute-start | bytes 393224 | tf_op jit(solution)/shard_map/ppermute | solution.py:174
  48.0 2.4 %collective-permute-start.6 = (f32[8,32,128]{2,1,0:T(8,128)}, f32[8,32,128]{2,1,0:T(8,128)S(1)}, u32[]{:S(2)}, u32[]{:S(2)}) collective-permute-start(f32[8,32,128]{2,1,0:T(8,128)} %get-tuple-element.14), channel_id=1, source_target_pairs={{0,4},{2,6},{4,0},{6,2},{1,5},{3,7},{5,1},{7,3},{8,12},{10,14},{12... | collective-permute-start | bytes 393224 | tf_op jit(solution)/shard_map/ppermute | solution.py:174
  50.4 0.0 copy-start.4
  50.4 3.1 %collective-permute-start.7 = (f32[8,32,128]{2,1,0:T(8,128)}, f32[8,32,128]{2,1,0:T(8,128)S(1)}, u32[]{:S(2)}, u32[]{:S(2)}) collective-permute-start(f32[8,32,128]{2,1,0:T(8,128)} %get-tuple-element.15), channel_id=1, source_target_pairs={{0,6},{2,0},{4,2},{6,4},{1,7},{3,1},{5,3},{7,5},{8,14},{10,8},{12,... | collective-permute-start | bytes 393224 | tf_op jit(solution)/shard_map/ppermute | solution.py:174
  53.5 4.8 %shard_map.52 = bf16[2,16,32,256]{3,2,1,0:T(8,128)(2,1)} custom-call(bf16[2,8,32,128]{3,2,1,0:T(8,128)(2,1)} %copy-done.3, bf16[2,8,32,128]{3,2,1,0:T(8,128)(2,1)} %copy-done.8, bf16[2,8,32,128]{3,2,1,0:T(8,128)(2,1)} %copy-done.7, bf16[2,8,32,128]{3,2,1,0:T(8,128)(2,1)} %copy-done.6, bf16[27,32,128]{2,1,0:T(8,128)(2,1)} %copy-done), custom_call_target="tpu_custom_call" | custom-call | flops 1006632960 | bytes 1048576 | tf_op jit(solution)/shard_map/pallas_call | solution.py:162
  58.3 0.0 collective-permute-done.5
  58.3 1.0 %collective-permute-done.6 = f32[8,32,128]{2,1,0:T(8,128)S(1)} collective-permute-done((f32[8,32,128]{2,1,0:T(8,128)}, f32[8,32,128]{2,1,0:T(8,128)S(1)}, u32[]{:S(2)}, u32[]{:S(2)}) %collective-permute-start.6) | collective-permute-done | bytes 131104 | tf_op jit(solution)/shard_map/ppermute | solution.py:174
  59.3 2.8 %collective-permute-done.7 = f32[8,32,128]{2,1,0:T(8,128)S(1)} collective-permute-done((f32[8,32,128]{2,1,0:T(8,128)}, f32[8,32,128]{2,1,0:T(8,128)S(1)}, u32[]{:S(2)}, u32[]{:S(2)}) %collective-permute-start.7) | collective-permute-done | bytes 131104 | tf_op jit(solution)/shard_map/ppermute | solution.py:174
  62.1 0.0 copy-done.4
  62.1 0.7 %fusion.1 = bf16[1,1,8,32,128]{4,3,2,1,0:T(8,128)(2,1)} fusion(f32[8,32,128]{2,1,0:T(8,128)S(1)} %collective-permute-done.7, f32[8,32,128]{2,1,0:T(8,128)S(1)} %collective-permute-done.6, f32[8,32,128]{2,1,0:T(8,128)S(1)} %copy-done.4, f32[8,32,128]{2,1,0:T(8,128)S(1)} %collective-permute-done.5), kind=kLoop, calls=%fused_computation.5 | loop fusion | flops 131072 | bytes 589824 | tf_op jit(solution)/shard_map/reshape | solution.py:195
  (1 shorter events, 0.0 us)
Async XLA Ops:
  0.6 10.6 %collective-permute-start = (bf16[1,1,8,32,128]{4,3,2,1,0:T(8,128)(2,1)}, bf16[1,1,8,32,128]{4,3,2,1,0:T(8,128)(2,1)S(1)}, u32[]{:S(2)}, u32[]{:S(2)}) collective-permute-start(bf16[1,1,8,32,128]{4,3,2,1,0:T(8,128)(2,1)} %param.5), channel_id=1, source_target_pairs={{8,0},{16,8},{24,16},{32,24},{40,32},{48,40},{56,48},{64,56},{72,6... | collective-permute-start | bytes 196616 | tf_op jit(solution)/shard_map/ppermute | solution.py:12
  8.1 3.1 %copy-start.5 = (bf16[1,1,8,32,128]{4,3,2,1,0:T(8,128)(2,1)S(1)}, bf16[1,1,8,32,128]{4,3,2,1,0:T(8,128)(2,1)}, u32[]{:S(2)}) copy-start(bf16[1,1,8,32,128]{4,3,2,1,0:T(8,128)(2,1)} %param.5) | copy-start | bytes 196612
  9.1 11.0 %copy-start.2 = (bf16[27,32,128]{2,1,0:T(8,128)(2,1)S(1)}, bf16[27,32,128]{2,1,0:T(8,128)(2,1)}, u32[]{:S(2)}) copy-start(bf16[27,32,128]{2,1,0:T(8,128)(2,1)} %param.4) | copy-start | bytes 663556
  9.2 33.7 %collective-permute-start.4 = (bf16[1,1,16,32,256]{4,3,2,1,0:T(8,128)(2,1)S(1)}, bf16[1,1,16,32,256]{4,3,2,1,0:T(8,128)(2,1)S(1)}, u32[]{:S(2)}, u32[]{:S(2)}) collective-permute-start(bf16[1,1,16,32,256]{4,3,2,1,0:T(8,128)(2,1)S(1)} %slice.3), channel_id=1, source_target_pairs={{0,8},{8,16},{16,24},{24,32},{32,40},{40,48},{48,56},{56,64},{64,7... | collective-permute-start | bytes 786440 | tf_op jit(solution)/shard_map/ppermute | solution.py:12
  11.3 9.0 %copy-start.3 = (bf16[2,8,32,128]{3,2,1,0:T(8,128)(2,1)}, bf16[2,8,32,128]{3,2,1,0:T(8,128)(2,1)S(1)}, u32[]{:S(2)}) copy-start(bf16[2,8,32,128]{3,2,1,0:T(8,128)(2,1)S(1)} %maximum_bitcast_fusion.refs_0_) | copy-start | bytes 393220
  11.3 12.6 %collective-permute-start.3 = (bf16[2,8,32,128]{3,2,1,0:T(8,128)(2,1)S(1)}, bf16[2,8,32,128]{3,2,1,0:T(8,128)(2,1)S(1)}, u32[]{:S(2)}, u32[]{:S(2)}) collective-permute-start(bf16[2,8,32,128]{3,2,1,0:T(8,128)(2,1)S(1)} %maximum_bitcast_fusion.refs_0_), channel_id=1, source_target_pairs={{0,2},{2,4},{4,6},{6,0},{1,3},{3,5},{5,7},{7,1},{8,10},{10,12},{12... | collective-permute-start | bytes 393224 | tf_op jit(solution)/shard_map/ppermute | solution.py:174
  13.7 25.8 %collective-permute-start.2 = (bf16[2,8,32,128]{3,2,1,0:T(8,128)(2,1)S(1)}, bf16[2,8,32,128]{3,2,1,0:T(8,128)(2,1)S(1)}, u32[]{:S(2)}, u32[]{:S(2)}) collective-permute-start(bf16[2,8,32,128]{3,2,1,0:T(8,128)(2,1)S(1)} %maximum_bitcast_fusion.refs_0_), channel_id=1, source_target_pairs={{0,4},{2,6},{4,0},{6,2},{1,5},{3,7},{5,1},{7,3},{8,12},{10,14},{12... | collective-permute-start | bytes 393224 | tf_op jit(solution)/shard_map/ppermute | solution.py:174
  18.2 24.7 %collective-permute-start.1 = (bf16[2,8,32,128]{3,2,1,0:T(8,128)(2,1)S(1)}, bf16[2,8,32,128]{3,2,1,0:T(8,128)(2,1)S(1)}, u32[]{:S(2)}, u32[]{:S(2)}) collective-permute-start(bf16[2,8,32,128]{3,2,1,0:T(8,128)(2,1)S(1)} %maximum_bitcast_fusion.refs_0_), channel_id=1, source_target_pairs={{0,6},{2,0},{4,2},{6,4},{1,7},{3,1},{5,3},{7,5},{8,14},{10,8},{12,... | collective-permute-start | bytes 393224 | tf_op jit(solution)/shard_map/ppermute | solution.py:174
  20.3 0.8 %copy-start = (bf16[27,32,128]{2,1,0:T(8,128)(2,1)}, bf16[27,32,128]{2,1,0:T(8,128)(2,1)S(1)}, u32[]{:S(2)}) copy-start(bf16[27,32,128]{2,1,0:T(8,128)(2,1)S(1)} %fusion.refs_4_) | copy-start | bytes 663556
  23.9 22.2 %copy-start.6 = (bf16[2,8,32,128]{3,2,1,0:T(8,128)(2,1)}, bf16[2,8,32,128]{3,2,1,0:T(8,128)(2,1)S(1)}, u32[]{:S(2)}) copy-start(bf16[2,8,32,128]{3,2,1,0:T(8,128)(2,1)S(1)} %collective-permute-done.3.refs_3_) | copy-start | bytes 393220
  39.6 6.5 %copy-start.7 = (bf16[2,8,32,128]{3,2,1,0:T(8,128)(2,1)}, bf16[2,8,32,128]{3,2,1,0:T(8,128)(2,1)S(1)}, u32[]{:S(2)}) copy-start(bf16[2,8,32,128]{3,2,1,0:T(8,128)(2,1)S(1)} %collective-permute-done.2.refs_2_) | copy-start | bytes 393220
  42.9 3.2 %copy-start.8 = (bf16[2,8,32,128]{3,2,1,0:T(8,128)(2,1)}, bf16[2,8,32,128]{3,2,1,0:T(8,128)(2,1)S(1)}, u32[]{:S(2)}) copy-start(bf16[2,8,32,128]{3,2,1,0:T(8,128)(2,1)S(1)} %collective-permute-done.1.refs_1_) | copy-start | bytes 393220
  42.9 0.7 %copy-start.1 = (bf16[1,1,16,32,256]{4,3,2,1,0:T(8,128)(2,1)}, bf16[1,1,16,32,256]{4,3,2,1,0:T(8,128)(2,1)S(1)}, u32[]{:S(2)}) copy-start(bf16[1,1,16,32,256]{4,3,2,1,0:T(8,128)(2,1)S(1)} %collective-permute-done.4) | copy-start | bytes 786436
  46.1 12.2 %collective-permute-start.5 = (f32[8,32,128]{2,1,0:T(8,128)}, f32[8,32,128]{2,1,0:T(8,128)S(1)}, u32[]{:S(2)}, u32[]{:S(2)}) collective-permute-start(f32[8,32,128]{2,1,0:T(8,128)} %get-tuple-element.13), channel_id=1, source_target_pairs={{0,2},{2,4},{4,6},{6,0},{1,3},{3,5},{5,7},{7,1},{8,10},{10,12},{12... | collective-permute-start | bytes 393224 | tf_op jit(solution)/shard_map/ppermute | solution.py:174
  48.0 11.3 %collective-permute-start.6 = (f32[8,32,128]{2,1,0:T(8,128)}, f32[8,32,128]{2,1,0:T(8,128)S(1)}, u32[]{:S(2)}, u32[]{:S(2)}) collective-permute-start(f32[8,32,128]{2,1,0:T(8,128)} %get-tuple-element.14), channel_id=1, source_target_pairs={{0,4},{2,6},{4,0},{6,2},{1,5},{3,7},{5,1},{7,3},{8,12},{10,14},{12... | collective-permute-start | bytes 393224 | tf_op jit(solution)/shard_map/ppermute | solution.py:174
  50.4 11.7 %copy-start.4 = (f32[8,32,128]{2,1,0:T(8,128)S(1)}, f32[8,32,128]{2,1,0:T(8,128)}, u32[]{:S(2)}) copy-start(f32[8,32,128]{2,1,0:T(8,128)} %get-tuple-element.12) | copy-start | bytes 393220
  50.4 11.7 %collective-permute-start.7 = (f32[8,32,128]{2,1,0:T(8,128)}, f32[8,32,128]{2,1,0:T(8,128)S(1)}, u32[]{:S(2)}, u32[]{:S(2)}) collective-permute-start(f32[8,32,128]{2,1,0:T(8,128)} %get-tuple-element.15), channel_id=1, source_target_pairs={{0,6},{2,0},{4,2},{6,4},{1,7},{3,1},{5,3},{7,5},{8,14},{10,8},{12,... | collective-permute-start | bytes 393224 | tf_op jit(solution)/shard_map/ppermute | solution.py:174

commit v14 on v10

--- a/solution.py
+++ b/solution.py
@@ -55,7 +55,7 @@
     return jnp.concatenate(blocks, axis=1)
 
 
-def forward_taps(source_refs, kbig_ref, acc_ref, out_refs, picked_ref, first_tap):
+def forward_taps(source_refs, kbig_ref, acc_ref, out_refs, picked_ref):
     planes = len(source_refs)
     rows, chans, cols = source_refs[0].shape
     rows_out, cols_out = rows // 2, cols // 2
@@ -65,7 +65,7 @@
         flat = source_ref[...].reshape(rows * chans, cols)
         chosen = jnp.dot(flat, sel, preferred_element_type=jnp.float32)
         picked_ref[plane] = chosen.astype(picked_ref.dtype).reshape(rows, chans, 3 * cols_out)
-    kpart = kbig_ref[:, first_tap * 9 * chans:(first_tap + planes) * 9 * chans]
+    kpart = kbig_ref[...]
     zero = jnp.zeros((chans, cols_out), picked_ref.dtype)
     for i in range(rows_out):
         pieces = []
@@ -89,12 +89,12 @@
 
 
 def forward_local_rows(vol_ref, kbig_ref, acc_ref, picked_ref):
-    forward_taps([vol_ref.at[0], vol_ref.at[1]], kbig_ref, None, [acc_ref], picked_ref, 1)
+    forward_taps([vol_ref.at[0], vol_ref.at[1]], kbig_ref, None, [acc_ref], picked_ref)
 
 
 def forward_halo_rows(halo_ref, acc_ref, kbig_ref, *refs):
     out_refs, picked_ref = refs[:-1], refs[-1]
-    forward_taps([halo_ref], kbig_ref, acc_ref, list(out_refs), picked_ref, 0)
+    forward_taps([halo_ref], kbig_ref, acc_ref, list(out_refs), picked_ref)
 
 
 def forward_partial(halo, vol, kernel, groups):
@@ -112,7 +112,7 @@
         out_specs=vmem,
         scratch_shapes=[pltpu.VMEM((planes, rows, chans, 3 * cols_out), vol.dtype)],
         cost_estimate=pl.CostEstimate(flops=planes * per_plane, bytes_accessed=2 * vol.size + 4 * rows_out * chans_out * cols_out, transcendentals=0),
-    )(vol, kbig)
+    )(vol, kbig[:, 9 * chans:])
     return pl.pallas_call(
         forward_halo_rows,
         out_shape=[jax.ShapeDtypeStruct((rows_out, share, cols_out), jnp.float32)] * groups,
@@ -120,7 +120,7 @@
         out_specs=[vmem] * groups,
         scratch_shapes=[pltpu.VMEM((1, rows, chans, 3 * cols_out), vol.dtype)],
         cost_estimate=pl.CostEstimate(flops=per_plane, bytes_accessed=2 * halo.size + 8 * rows_out * chans_out * cols_out, transcendentals=0),
-    )(halo, acc, kbig)
+    )(halo, acc, kbig[:, :9 * chans])
 
 
 def backward_rows(*refs):

time: 57.9 us -> 57.8 us (level)
  waiting for transfers between devices: 9.38 us -> 7.98 us
  local copies, waits for them, and re-layouts: 3.82 us -> 5.21 us
    unnamed x18 -> x20, local copies, waits for them, and re-layouts: 1.98 us -> 4.18 us
    ppermute x2, waiting for transfers between devices: 7.26 us -> 5.87 us  [from_behind(): return lax.ppermute(block, axis, route)]
    reshape x1 -> x0, local copies, waits for them, and re-layouts: 0.83 us -> none  [forward_partial(): kbig = jnp.transpose(kernel, (2, 0, 1)).reshape(chans_out, taps * chans)]
  transfers between devices with their start and end apart: 8 -> 8, of which waited for: 2 -> 2; matrix products, arithmetic and copies ran while one was open for 2% -> 3% of each run, Pallas kernels for 13% -> 13%
where the time goes in v14:
time: 57.8 us; the launch traced here: 57.4 us
  starting transfers between devices  32.5 us (56%)
  Pallas kernels  9.95 us (17%)
  waiting for transfers between devices  7.98 us (14%)
  local copies, waits for them, and re-layouts  5.21 us (9%)
  other arithmetic  0.91 us (2%)
  between operations  0.85 us (1%)
    ppermute x6, starting transfers between devices, chan_shift(): lax.ppermute(block, 'chan', [(i, (i + shift) % size) for i in range(size)])  18.5 us
    ppermute x2, starting transfers between devices, from_behind(): return lax.ppermute(block, axis, route)  14 us
    ppermute x2, waiting for transfers between devices, from_behind(): return lax.ppermute(block, axis, route)  5.87 us
    pallas_call x1, Pallas kernels, backward_grad(): pl.pallas_call(backward_rows, out_shape=jax.ShapeDtypeStruct((2, rows, ch...  4.81 us
    unnamed x20, local copies, waits for them, and re-layouts  4.18 us
    pallas_call x1, Pallas kernels, forward_partial(): pl.pallas_call(forward_local_rows, out_shape=jax.ShapeDtypeStruct((rows_o...  2.69 us
    pallas_call x1, Pallas kernels, forward_partial(): pl.pallas_call(forward_halo_rows, out_shape=[jax.ShapeDtypeStruct((rows_o...  2.45 us
    ppermute x6, waiting for transfers between devices, chan_shift(): lax.ppermute(block, 'chan', [(i, (i + shift) % size) for i in range(size)])  2.11 us
  transfers between devices with their start and end apart: 8, of which 2 were waited for; matrix products, arithmetic and copies ran while one was open for 3% of the time, Pallas kernels for 13%

profile of v14, /device:TPU:512, one launch (start us, length us, event | category | flops | bytes accessed | tf_op | source)
XLA Modules:
  0.0 57.4 jit_solution(1564356262371633439)
XLA Ops:
  0.6 0.0 copy-start.5
  0.6 0.0 copy-start.2
  0.6 1.0 %slice.9 = bf16[1,1,16,32,256]{4,3,2,1,0:T(8,128)(2,1)S(1)} slice(bf16[1,2,16,32,256]{4,3,2,1,0:T(8,128)(2,1)} %param.3), slice={[0:1], [1:2], [0:16], [0:32], [0:256]} | slice | bytes 524288 | tf_op jit(solution)/shard_map/slice | solution.py:187
  1.7 3.4 %collective-permute-start = (bf16[1,1,16,32,256]{4,3,2,1,0:T(8,128)(2,1)S(1)}, bf16[1,1,16,32,256]{4,3,2,1,0:T(8,128)(2,1)S(1)}, u32[]{:S(2)}, u32[]{:S(2)}) collective-permute-start(bf16[1,1,16,32,256]{4,3,2,1,0:T(8,128)(2,1)S(1)} %slice.9), channel_id=1, source_target_pairs={{0,8},{8,16},{16,24},{24,32},{32,40},{40,48},{48,56},{56,64},{64,7... | collective-permute-start | bytes 786440 | tf_op jit(solution)/shard_map/ppermute | solution.py:12
  5.1 0.0 copy-done.5
  5.1 10.6 %collective-permute-start.1 = (bf16[1,1,8,32,128]{4,3,2,1,0:T(8,128)(2,1)S(1)}, bf16[1,1,8,32,128]{4,3,2,1,0:T(8,128)(2,1)S(1)}, u32[]{:S(2)}, u32[]{:S(2)}) collective-permute-start(bf16[1,1,8,32,128]{4,3,2,1,0:T(8,128)(2,1)S(1)} %copy-done.5), channel_id=1, source_target_pairs={{8,0},{16,8},{24,16},{32,24},{40,32},{48,40},{56,48},{64,56},{72,6... | collective-permute-start | bytes 196616 | tf_op jit(solution)/shard_map/ppermute | solution.py:12
  15.7 0.0 copy-done.2
  15.7 0.2 fusion.refs_4_
  15.9 0.0 copy-start
  16.0 0.6 %copy-done = bf16[27,32,128]{2,1,0:T(8,128)(2,1)} copy-done((bf16[27,32,128]{2,1,0:T(8,128)(2,1)}, bf16[27,32,128]{2,1,0:T(8,128)(2,1)S(1)}, u32[]{:S(2)}) %copy-start) | copy-done | bytes 221208
  16.6 0.8 %copy.7.kbig_ref = bf16[128,576]{1,0:T(8,128)(2,1)} copy(bf16[128,576]{0,1:T(8,128)(2,1)S(1)} %slice.12) | data formatting | bytes 294912
  17.4 0.7 %copy.8.kbig_ref = bf16[128,288]{1,0:T(8,128)(2,1)} copy(bf16[128,288]{0,1:T(8,128)(2,1)S(1)} %slice.13) | data formatting | bytes 147456
  18.2 2.7 %shard_map.50.acc_ref = f32[8,128,128]{2,1,0:T(8,128)} custom-call(bf16[2,16,32,256]{3,2,1,0:T(8,128)(2,1)} %bitcast.12, bf16[128,576]{1,0:T(8,128)(2,1)} %copy.7.kbig_ref), custom_call_target="tpu_custom_call" | custom-call | flops 352321536 | bytes 1048576 | tf_op jit(solution)/shard_map/pallas_call | solution.py:108
  20.9 0.0 collective-permute-done.1
  20.9 0.0 copy-start.3
  20.9 5.9 %collective-permute-done = bf16[1,1,16,32,256]{4,3,2,1,0:T(8,128)(2,1)S(1)} collective-permute-done((bf16[1,1,16,32,256]{4,3,2,1,0:T(8,128)(2,1)S(1)}, bf16[1,1,16,32,256]{4,3,2,1,0:T(8,128)(2,1)S(1)}, u32[]{:S(2)}, u32[]{:S(2)}) %collective-permute-start) | collective-permute-done | bytes 262176 | tf_op jit(solution)/shard_map/ppermute | solution.py:12
  26.8 0.0 copy-start.1
  26.8 0.7 %copy-done.1 = bf16[1,1,16,32,256]{4,3,2,1,0:T(8,128)(2,1)} copy-done((bf16[1,1,16,32,256]{4,3,2,1,0:T(8,128)(2,1)}, bf16[1,1,16,32,256]{4,3,2,1,0:T(8,128)(2,1)S(1)}, u32[]{:S(2)}) %copy-start.1) | copy-done | bytes 262168
  27.4 2.5 %shard_map.51 = (f32[8,32,128]{2,1,0:T(8,128)}, f32[8,32,128]{2,1,0:T(8,128)}, f32[8,32,128]{2,1,0:T(8,128)}, f32[8,32,128]{2,1,0:T(8,128)}) custom-call(bf16[16,32,256]{2,1,0:T(8,128)(2,1)} %bitcast.11, f32[8,128,128]{2,1,0:T(8,128)} %shard_map.50.acc_ref, bf16[128,288]{1,0:T(8,128)(2,1)} %copy.8.kbig_ref), custom_call_target="tpu_custom_call" | custom-call | flops 176160768 | bytes 1310720 | tf_op jit(solution)/shard_map/pallas_call | solution.py:116
  29.9 0.0 copy-start.4
  29.9 3.9 %collective-permute-start.5 = (bf16[2,8,32,128]{3,2,1,0:T(8,128)(2,1)S(1)}, bf16[2,8,32,128]{3,2,1,0:T(8,128)(2,1)S(1)}, u32[]{:S(2)}, u32[]{:S(2)}) collective-permute-start(bf16[2,8,32,128]{3,2,1,0:T(8,128)(2,1)S(1)} %bitcast.13), channel_id=1, source_target_pairs={{0,6},{2,0},{4,2},{6,4},{1,7},{3,1},{5,3},{7,5},{8,14},{10,8},{12,... | collective-permute-start | bytes 393224 | tf_op jit(solution)/shard_map/ppermute | solution.py:174
  33.8 2.3 %collective-permute-start.6 = (bf16[2,8,32,128]{3,2,1,0:T(8,128)(2,1)S(1)}, bf16[2,8,32,128]{3,2,1,0:T(8,128)(2,1)S(1)}, u32[]{:S(2)}, u32[]{:S(2)}) collective-permute-start(bf16[2,8,32,128]{3,2,1,0:T(8,128)(2,1)S(1)} %bitcast.14), channel_id=1, source_target_pairs={{0,4},{2,6},{4,0},{6,2},{1,5},{3,7},{5,1},{7,3},{8,12},{10,14},{12... | collective-permute-start | bytes 393224 | tf_op jit(solution)/shard_map/ppermute | solution.py:174
  36.1 0.0 copy-done.3
  36.1 3.9 %collective-permute-start.7 = (bf16[2,8,32,128]{3,2,1,0:T(8,128)(2,1)S(1)}, bf16[2,8,32,128]{3,2,1,0:T(8,128)(2,1)S(1)}, u32[]{:S(2)}, u32[]{:S(2)}) collective-permute-start(bf16[2,8,32,128]{3,2,1,0:T(8,128)(2,1)S(1)} %bitcast.15), channel_id=1, source_target_pairs={{0,2},{2,4},{4,6},{6,0},{1,3},{3,5},{5,7},{7,1},{8,10},{10,12},{12... | collective-permute-start | bytes 393224 | tf_op jit(solution)/shard_map/ppermute | solution.py:174
  40.0 3.7 %collective-permute-start.4 = (f32[8,32,128]{2,1,0:T(8,128)}, f32[8,32,128]{2,1,0:T(8,128)S(1)}, u32[]{:S(2)}, u32[]{:S(2)}) collective-permute-start(f32[8,32,128]{2,1,0:T(8,128)} %get-tuple-element.18), channel_id=1, source_target_pairs={{0,6},{2,0},{4,2},{6,4},{1,7},{3,1},{5,3},{7,5},{8,14},{10,8},{12,... | collective-permute-start | bytes 393224 | tf_op jit(solution)/shard_map/ppermute | solution.py:174
  43.7 2.7 %collective-permute-start.3 = (f32[8,32,128]{2,1,0:T(8,128)}, f32[8,32,128]{2,1,0:T(8,128)S(1)}, u32[]{:S(2)}, u32[]{:S(2)}) collective-permute-start(f32[8,32,128]{2,1,0:T(8,128)} %get-tuple-element.17), channel_id=1, source_target_pairs={{0,4},{2,6},{4,0},{6,2},{1,5},{3,7},{5,1},{7,3},{8,12},{10,14},{12... | collective-permute-start | bytes 393224 | tf_op jit(solution)/shard_map/ppermute | solution.py:174
  46.4 0.0 collective-permute-done.5.refs_1_
  46.5 0.0 copy-start.6
  46.5 2.1 %collective-permute-start.2 = (f32[8,32,128]{2,1,0:T(8,128)}, f32[8,32,128]{2,1,0:T(8,128)S(1)}, u32[]{:S(2)}, u32[]{:S(2)}) collective-permute-start(f32[8,32,128]{2,1,0:T(8,128)} %get-tuple-element.16), channel_id=1, source_target_pairs={{0,2},{2,4},{4,6},{6,0},{1,3},{3,5},{5,7},{7,1},{8,10},{10,12},{12... | collective-permute-start | bytes 393224 | tf_op jit(solution)/shard_map/ppermute | solution.py:174
  48.5 0.0 collective-permute-done.6.refs_2_
  48.5 0.0 copy-start.7
  48.5 0.0 collective-permute-done.7.refs_3_
  48.6 0.0 copy-done.6
  48.6 0.6 %copy-done.7 = bf16[2,8,32,128]{3,2,1,0:T(8,128)(2,1)} copy-done((bf16[2,8,32,128]{3,2,1,0:T(8,128)(2,1)}, bf16[2,8,32,128]{3,2,1,0:T(8,128)(2,1)S(1)}, u32[]{:S(2)}) %copy-start.7) | copy-done | bytes 131096
  49.2 0.0 copy-start.8
  49.2 0.7 %copy-done.8 = bf16[2,8,32,128]{3,2,1,0:T(8,128)(2,1)} copy-done((bf16[2,8,32,128]{3,2,1,0:T(8,128)(2,1)}, bf16[2,8,32,128]{3,2,1,0:T(8,128)(2,1)S(1)}, u32[]{:S(2)}) %copy-start.8) | copy-done | bytes 131096
  49.8 4.8 %shard_map.52 = bf16[2,16,32,256]{3,2,1,0:T(8,128)(2,1)} custom-call(bf16[2,8,32,128]{3,2,1,0:T(8,128)(2,1)} %bitcast.16, bf16[2,8,32,128]{3,2,1,0:T(8,128)(2,1)} %copy-done.6, bf16[2,8,32,128]{3,2,1,0:T(8,128)(2,1)} %copy-done.7, bf16[2,8,32,128]{3,2,1,0:T(8,128)(2,1)} %copy-done.8, bf16[27,32,128]{2,1,0:T(8,128)(2,1)} %copy-done), custom_call_target="tpu_custom_call" | custom-call | flops 1006632960 | bytes 1048576 | tf_op jit(solution)/shard_map/pallas_call | solution.py:162
  54.6 0.0 collective-permute-done.4
  54.6 2.1 %collective-permute-done.3 = f32[8,32,128]{2,1,0:T(8,128)S(1)} collective-permute-done((f32[8,32,128]{2,1,0:T(8,128)}, f32[8,32,128]{2,1,0:T(8,128)S(1)}, u32[]{:S(2)}, u32[]{:S(2)}) %collective-permute-start.3) | collective-permute-done | bytes 131104 | tf_op jit(solution)/shard_map/ppermute | solution.py:174
  56.7 0.0 collective-permute-done.2
  56.8 0.0 copy-done.4
  56.8 0.7 %fusion.1 = bf16[1,1,8,32,128]{4,3,2,1,0:T(8,128)(2,1)} fusion(f32[8,32,128]{2,1,0:T(8,128)S(1)} %collective-permute-done.4, f32[8,32,128]{2,1,0:T(8,128)S(1)} %collective-permute-done.3, f32[8,32,128]{2,1,0:T(8,128)S(1)} %copy-done.4, f32[8,32,128]{2,1,0:T(8,128)S(1)} %collective-permute-done.2), kind=kLoop, calls=%fused_computation.5 | loop fusion | flops 131072 | bytes 589824 | tf_op jit(solution)/shard_map/reshape | solution.py:194
  (3 shorter events, 0.0 us)
Async XLA Ops:
  0.6 4.5 %copy-start.5 = (bf16[1,1,8,32,128]{4,3,2,1,0:T(8,128)(2,1)S(1)}, bf16[1,1,8,32,128]{4,3,2,1,0:T(8,128)(2,1)}, u32[]{:S(2)}) copy-start(bf16[1,1,8,32,128]{4,3,2,1,0:T(8,128)(2,1)} %param.5) | copy-start | bytes 196612
  0.6 15.0 %copy-start.2 = (bf16[27,32,128]{2,1,0:T(8,128)(2,1)S(1)}, bf16[27,32,128]{2,1,0:T(8,128)(2,1)}, u32[]{:S(2)}) copy-start(bf16[27,32,128]{2,1,0:T(8,128)(2,1)} %param.4) | copy-start | bytes 663556
  1.7 25.1 %collective-permute-start = (bf16[1,1,16,32,256]{4,3,2,1,0:T(8,128)(2,1)S(1)}, bf16[1,1,16,32,256]{4,3,2,1,0:T(8,128)(2,1)S(1)}, u32[]{:S(2)}, u32[]{:S(2)}) collective-permute-start(bf16[1,1,16,32,256]{4,3,2,1,0:T(8,128)(2,1)S(1)} %slice.9), channel_id=1, source_target_pairs={{0,8},{8,16},{16,24},{24,32},{32,40},{40,48},{48,56},{56,64},{64,7... | collective-permute-start | bytes 786440 | tf_op jit(solution)/shard_map/ppermute | solution.py:12
  5.1 15.8 %collective-permute-start.1 = (bf16[1,1,8,32,128]{4,3,2,1,0:T(8,128)(2,1)S(1)}, bf16[1,1,8,32,128]{4,3,2,1,0:T(8,128)(2,1)S(1)}, u32[]{:S(2)}, u32[]{:S(2)}) collective-permute-start(bf16[1,1,8,32,128]{4,3,2,1,0:T(8,128)(2,1)S(1)} %copy-done.5), channel_id=1, source_target_pairs={{8,0},{16,8},{24,16},{32,24},{40,32},{48,40},{56,48},{64,56},{72,6... | collective-permute-start | bytes 196616 | tf_op jit(solution)/shard_map/ppermute | solution.py:12
  15.9 0.7 %copy-start = (bf16[27,32,128]{2,1,0:T(8,128)(2,1)}, bf16[27,32,128]{2,1,0:T(8,128)(2,1)S(1)}, u32[]{:S(2)}) copy-start(bf16[27,32,128]{2,1,0:T(8,128)(2,1)S(1)} %fusion.refs_4_) | copy-start | bytes 663556
  20.9 15.2 %copy-start.3 = (bf16[1,2,8,32,128]{4,3,2,1,0:T(8,128)(2,1)}, bf16[1,2,8,32,128]{4,3,2,1,0:T(8,128)(2,1)S(1)}, u32[]{:S(2)}) copy-start(bf16[1,2,8,32,128]{4,3,2,1,0:T(8,128)(2,1)S(1)} %pad_maximum_fusion) | copy-start | bytes 393220
  26.8 0.7 %copy-start.1 = (bf16[1,1,16,32,256]{4,3,2,1,0:T(8,128)(2,1)}, bf16[1,1,16,32,256]{4,3,2,1,0:T(8,128)(2,1)S(1)}, u32[]{:S(2)}) copy-start(bf16[1,1,16,32,256]{4,3,2,1,0:T(8,128)(2,1)S(1)} %collective-permute-done) | copy-start | bytes 786436
  29.9 26.9 %copy-start.4 = (f32[8,32,128]{2,1,0:T(8,128)S(1)}, f32[8,32,128]{2,1,0:T(8,128)}, u32[]{:S(2)}) copy-start(f32[8,32,128]{2,1,0:T(8,128)} %get-tuple-element.15) | copy-start | bytes 393220
  29.9 16.5 %collective-permute-start.5 = (bf16[2,8,32,128]{3,2,1,0:T(8,128)(2,1)S(1)}, bf16[2,8,32,128]{3,2,1,0:T(8,128)(2,1)S(1)}, u32[]{:S(2)}, u32[]{:S(2)}) collective-permute-start(bf16[2,8,32,128]{3,2,1,0:T(8,128)(2,1)S(1)} %bitcast.13), channel_id=1, source_target_pairs={{0,6},{2,0},{4,2},{6,4},{1,7},{3,1},{5,3},{7,5},{8,14},{10,8},{12,... | collective-permute-start | bytes 393224 | tf_op jit(solution)/shard_map/ppermute | solution.py:174
  33.8 14.7 %collective-permute-start.6 = (bf16[2,8,32,128]{3,2,1,0:T(8,128)(2,1)S(1)}, bf16[2,8,32,128]{3,2,1,0:T(8,128)(2,1)S(1)}, u32[]{:S(2)}, u32[]{:S(2)}) collective-permute-start(bf16[2,8,32,128]{3,2,1,0:T(8,128)(2,1)S(1)} %bitcast.14), channel_id=1, source_target_pairs={{0,4},{2,6},{4,0},{6,2},{1,5},{3,7},{5,1},{7,3},{8,12},{10,14},{12... | collective-permute-start | bytes 393224 | tf_op jit(solution)/shard_map/ppermute | solution.py:174
  36.1 12.5 %collective-permute-start.7 = (bf16[2,8,32,128]{3,2,1,0:T(8,128)(2,1)S(1)}, bf16[2,8,32,128]{3,2,1,0:T(8,128)(2,1)S(1)}, u32[]{:S(2)}, u32[]{:S(2)}) collective-permute-start(bf16[2,8,32,128]{3,2,1,0:T(8,128)(2,1)S(1)} %bitcast.15), channel_id=1, source_target_pairs={{0,2},{2,4},{4,6},{6,0},{1,3},{3,5},{5,7},{7,1},{8,10},{10,12},{12... | collective-permute-start | bytes 393224 | tf_op jit(solution)/shard_map/ppermute | solution.py:174
  40.0 14.6 %collective-permute-start.4 = (f32[8,32,128]{2,1,0:T(8,128)}, f32[8,32,128]{2,1,0:T(8,128)S(1)}, u32[]{:S(2)}, u32[]{:S(2)}) collective-permute-start(f32[8,32,128]{2,1,0:T(8,128)} %get-tuple-element.18), channel_id=1, source_target_pairs={{0,6},{2,0},{4,2},{6,4},{1,7},{3,1},{5,3},{7,5},{8,14},{10,8},{12,... | collective-permute-start | bytes 393224 | tf_op jit(solution)/shard_map/ppermute | solution.py:174
  43.7 13.0 %collective-permute-start.3 = (f32[8,32,128]{2,1,0:T(8,128)}, f32[8,32,128]{2,1,0:T(8,128)S(1)}, u32[]{:S(2)}, u32[]{:S(2)}) collective-permute-start(f32[8,32,128]{2,1,0:T(8,128)} %get-tuple-element.17), channel_id=1, source_target_pairs={{0,4},{2,6},{4,0},{6,2},{1,5},{3,7},{5,1},{7,3},{8,12},{10,14},{12... | collective-permute-start | bytes 393224 | tf_op jit(solution)/shard_map/ppermute | solution.py:174
  46.5 2.1 %copy-start.6 = (bf16[2,8,32,128]{3,2,1,0:T(8,128)(2,1)}, bf16[2,8,32,128]{3,2,1,0:T(8,128)(2,1)S(1)}, u32[]{:S(2)}) copy-start(bf16[2,8,32,128]{3,2,1,0:T(8,128)(2,1)S(1)} %collective-permute-done.5.refs_1_) | copy-start | bytes 393220
  46.5 10.3 %collective-permute-start.2 = (f32[8,32,128]{2,1,0:T(8,128)}, f32[8,32,128]{2,1,0:T(8,128)S(1)}, u32[]{:S(2)}, u32[]{:S(2)}) collective-permute-start(f32[8,32,128]{2,1,0:T(8,128)} %get-tuple-element.16), channel_id=1, source_target_pairs={{0,2},{2,4},{4,6},{6,0},{1,3},{3,5},{5,7},{7,1},{8,10},{10,12},{12... | collective-permute-start | bytes 393224 | tf_op jit(solution)/shard_map/ppermute | solution.py:174
  48.5 0.6 %copy-start.7 = (bf16[2,8,32,128]{3,2,1,0:T(8,128)(2,1)}, bf16[2,8,32,128]{3,2,1,0:T(8,128)(2,1)S(1)}, u32[]{:S(2)}) copy-start(bf16[2,8,32,128]{3,2,1,0:T(8,128)(2,1)S(1)} %collective-permute-done.6.refs_2_) | copy-start | bytes 393220
  49.2 0.7 %copy-start.8 = (bf16[2,8,32,128]{3,2,1,0:T(8,128)(2,1)}, bf16[2,8,32,128]{3,2,1,0:T(8,128)(2,1)S(1)}, u32[]{:S(2)}) copy-start(bf16[2,8,32,128]{3,2,1,0:T(8,128)(2,1)S(1)} %collective-permute-done.7.refs_3_) | copy-start | bytes 393220

commit v15 on v10

--- a/solution.py
+++ b/solution.py
@@ -120,7 +120,7 @@
         out_specs=[vmem] * groups,
         scratch_shapes=[pltpu.VMEM((1, rows, chans, 3 * cols_out), vol.dtype)],
         cost_estimate=pl.CostEstimate(flops=per_plane, bytes_accessed=2 * halo.size + 8 * rows_out * chans_out * cols_out, transcendentals=0),
-    )(halo, acc, kbig)
+    )(pltpu.with_memory_space_constraint(halo, pltpu.MemorySpace.VMEM), acc, kbig)
 
 
 def backward_rows(*refs):

time: 57.9 us -> 57.1 us (0.986)
  local copies, waits for them, and re-layouts: 3.82 us -> 3.16 us
    unnamed x18 -> x16, local copies, waits for them, and re-layouts: 1.98 us -> 1.31 us
where the time goes in v15:
time: 57.1 us; the launch traced here: 56.7 us
  starting transfers between devices  32.5 us (57%)
  Pallas kernels  9.94 us (17%)
  waiting for transfers between devices  9.35 us (16%)
  local copies, waits for them, and re-layouts  3.16 us (6%)
  other arithmetic  0.91 us (2%)
  between operations  0.84 us (1%)
    ppermute x6, starting transfers between devices, chan_shift(): lax.ppermute(block, 'chan', [(i, (i + shift) % size) for i in range(size)])  18.5 us
    ppermute x2, starting transfers between devices, from_behind(): return lax.ppermute(block, axis, route)  14 us
    ppermute x2, waiting for transfers between devices, from_behind(): return lax.ppermute(block, axis, route)  7.25 us
    pallas_call x1, Pallas kernels, backward_grad(): pl.pallas_call(backward_rows, out_shape=jax.ShapeDtypeStruct((2, rows, ch...  4.81 us
    pallas_call x1, Pallas kernels, forward_partial(): pl.pallas_call(forward_local_rows, out_shape=jax.ShapeDtypeStruct((rows_o...  2.71 us
    pallas_call x1, Pallas kernels, forward_partial(): pl.pallas_call(forward_halo_rows, out_shape=[jax.ShapeDtypeStruct((rows_o...  2.42 us
    ppermute x6, waiting for transfers between devices, chan_shift(): lax.ppermute(block, 'chan', [(i, (i + shift) % size) for i in range(size)])  2.1 us
    unnamed x16, local copies, waits for them, and re-layouts  1.31 us
  transfers between devices with their start and end apart: 8, of which 2 were waited for; matrix products, arithmetic and copies ran while one was open for 2% of the time, Pallas kernels for 13%

profile of v15, /device:TPU:512, one launch (start us, length us, event | category | flops | bytes accessed | tf_op | source)
XLA Modules:
  0.0 56.7 jit_solution(4075796131052992993)
XLA Ops:
  0.6 0.0 copy-start.4
  0.6 0.0 copy-start.1
  0.6 1.0 %slice.3 = bf16[1,1,16,32,256]{4,3,2,1,0:T(8,128)(2,1)S(1)} slice(bf16[1,2,16,32,256]{4,3,2,1,0:T(8,128)(2,1)} %param.3), slice={[0:1], [1:2], [0:16], [0:32], [0:256]} | slice | bytes 524288 | tf_op jit(solution)/shard_map/slice | solution.py:187
  1.7 3.4 %collective-permute-start = (bf16[1,1,16,32,256]{4,3,2,1,0:T(8,128)(2,1)S(1)}, bf16[1,1,16,32,256]{4,3,2,1,0:T(8,128)(2,1)S(1)}, u32[]{:S(2)}, u32[]{:S(2)}) collective-permute-start(bf16[1,1,16,32,256]{4,3,2,1,0:T(8,128)(2,1)S(1)} %slice.3), channel_id=1, source_target_pairs={{0,8},{8,16},{16,24},{24,32},{32,40},{40,48},{48,56},{56,64},{64,7... | collective-permute-start | bytes 786440 | tf_op jit(solution)/shard_map/ppermute | solution.py:12
  5.1 0.0 copy-done.4
  5.1 10.6 %collective-permute-start.1 = (bf16[1,1,8,32,128]{4,3,2,1,0:T(8,128)(2,1)S(1)}, bf16[1,1,8,32,128]{4,3,2,1,0:T(8,128)(2,1)S(1)}, u32[]{:S(2)}, u32[]{:S(2)}) collective-permute-start(bf16[1,1,8,32,128]{4,3,2,1,0:T(8,128)(2,1)S(1)} %copy-done.4), channel_id=1, source_target_pairs={{8,0},{16,8},{24,16},{32,24},{40,32},{48,40},{56,48},{64,56},{72,6... | collective-permute-start | bytes 196616 | tf_op jit(solution)/shard_map/ppermute | solution.py:12
  15.7 0.0 copy-done.1
  15.7 0.2 fusion.refs_4_
  15.9 0.0 copy-start
  15.9 0.8 %copy.5.kbig_ref = bf16[128,864]{1,0:T(8,128)(2,1)} copy(bf16[128,864]{0,1:T(8,128)(2,1)S(1)} %bitcast.10) | data formatting | bytes 442368 | tf_op jit(solution)/shard_map/reshape | solution.py:105
  16.8 0.0 copy-done
  16.8 2.7 %shard_map.50.acc_ref = f32[8,128,128]{2,1,0:T(8,128)} custom-call(bf16[2,16,32,256]{3,2,1,0:T(8,128)(2,1)} %bitcast.11, bf16[128,864]{1,0:T(8,128)(2,1)} %copy.5.kbig_ref), custom_call_target="tpu_custom_call" | custom-call | flops 352321536 | bytes 1048576 | tf_op jit(solution)/shard_map/pallas_call | solution.py:108
  19.5 0.0 collective-permute-done.1
  19.5 0.0 copy-start.2
  19.5 7.2 %collective-permute-done = bf16[1,1,16,32,256]{4,3,2,1,0:T(8,128)(2,1)S(1)} collective-permute-done((bf16[1,1,16,32,256]{4,3,2,1,0:T(8,128)(2,1)S(1)}, bf16[1,1,16,32,256]{4,3,2,1,0:T(8,128)(2,1)S(1)}, u32[]{:S(2)}, u32[]{:S(2)}) %collective-permute-start) | collective-permute-done | bytes 262176 | tf_op jit(solution)/shard_map/ppermute | solution.py:12
  26.8 2.4 %shard_map.51 = (f32[8,32,128]{2,1,0:T(8,128)}, f32[8,32,128]{2,1,0:T(8,128)}, f32[8,32,128]{2,1,0:T(8,128)}, f32[8,32,128]{2,1,0:T(8,128)}) custom-call(bf16[16,32,256]{2,1,0:T(8,128)(2,1)S(1)} %bitcast.9, f32[8,128,128]{2,1,0:T(8,128)} %shard_map.50.acc_ref, bf16[128,864]{1,0:T(8,128)(2,1)} %copy.5.kbig_ref), custom_call_target="tpu_custom_call" | custom-call | flops 176160768 | bytes 1310720 | tf_op jit(solution)/shard_map/pallas_call | solution.py:116
  29.2 0.0 copy-start.3
  29.2 3.9 %collective-permute-start.5 = (bf16[2,8,32,128]{3,2,1,0:T(8,128)(2,1)S(1)}, bf16[2,8,32,128]{3,2,1,0:T(8,128)(2,1)S(1)}, u32[]{:S(2)}, u32[]{:S(2)}) collective-permute-start(bf16[2,8,32,128]{3,2,1,0:T(8,128)(2,1)S(1)} %bitcast.12), channel_id=1, source_target_pairs={{0,6},{2,0},{4,2},{6,4},{1,7},{3,1},{5,3},{7,5},{8,14},{10,8},{12,... | collective-permute-start | bytes 393224 | tf_op jit(solution)/shard_map/ppermute | solution.py:174
  33.1 2.3 %collective-permute-start.6 = (bf16[2,8,32,128]{3,2,1,0:T(8,128)(2,1)S(1)}, bf16[2,8,32,128]{3,2,1,0:T(8,128)(2,1)S(1)}, u32[]{:S(2)}, u32[]{:S(2)}) collective-permute-start(bf16[2,8,32,128]{3,2,1,0:T(8,128)(2,1)S(1)} %bitcast.13), channel_id=1, source_target_pairs={{0,4},{2,6},{4,0},{6,2},{1,5},{3,7},{5,1},{7,3},{8,12},{10,14},{12... | collective-permute-start | bytes 393224 | tf_op jit(solution)/shard_map/ppermute | solution.py:174
  35.4 0.0 copy-done.2
  35.4 3.9 %collective-permute-start.7 = (bf16[2,8,32,128]{3,2,1,0:T(8,128)(2,1)S(1)}, bf16[2,8,32,128]{3,2,1,0:T(8,128)(2,1)S(1)}, u32[]{:S(2)}, u32[]{:S(2)}) collective-permute-start(bf16[2,8,32,128]{3,2,1,0:T(8,128)(2,1)S(1)} %bitcast.14), channel_id=1, source_target_pairs={{0,2},{2,4},{4,6},{6,0},{1,3},{3,5},{5,7},{7,1},{8,10},{10,12},{12... | collective-permute-start | bytes 393224 | tf_op jit(solution)/shard_map/ppermute | solution.py:174
  39.3 3.7 %collective-permute-start.4 = (f32[8,32,128]{2,1,0:T(8,128)}, f32[8,32,128]{2,1,0:T(8,128)S(1)}, u32[]{:S(2)}, u32[]{:S(2)}) collective-permute-start(f32[8,32,128]{2,1,0:T(8,128)} %get-tuple-element.18), channel_id=1, source_target_pairs={{0,6},{2,0},{4,2},{6,4},{1,7},{3,1},{5,3},{7,5},{8,14},{10,8},{12,... | collective-permute-start | bytes 393224 | tf_op jit(solution)/shard_map/ppermute | solution.py:174
  43.0 2.7 %collective-permute-start.3 = (f32[8,32,128]{2,1,0:T(8,128)}, f32[8,32,128]{2,1,0:T(8,128)S(1)}, u32[]{:S(2)}, u32[]{:S(2)}) collective-permute-start(f32[8,32,128]{2,1,0:T(8,128)} %get-tuple-element.17), channel_id=1, source_target_pairs={{0,4},{2,6},{4,0},{6,2},{1,5},{3,7},{5,1},{7,3},{8,12},{10,14},{12... | collective-permute-start | bytes 393224 | tf_op jit(solution)/shard_map/ppermute | solution.py:174
  45.7 0.0 collective-permute-done.5.refs_1_
  45.7 0.0 copy-start.5
  45.7 2.1 %collective-permute-start.2 = (f32[8,32,128]{2,1,0:T(8,128)}, f32[8,32,128]{2,1,0:T(8,128)S(1)}, u32[]{:S(2)}, u32[]{:S(2)}) collective-permute-start(f32[8,32,128]{2,1,0:T(8,128)} %get-tuple-element.16), channel_id=1, source_target_pairs={{0,2},{2,4},{4,6},{6,0},{1,3},{3,5},{5,7},{7,1},{8,10},{10,12},{12... | collective-permute-start | bytes 393224 | tf_op jit(solution)/shard_map/ppermute | solution.py:174
  47.8 0.0 collective-permute-done.6.refs_2_
  47.8 0.0 copy-start.6
  47.8 0.0 collective-permute-done.7.refs_3_
  47.8 0.0 copy-done.5
  47.8 0.6 %copy-done.6 = bf16[2,8,32,128]{3,2,1,0:T(8,128)(2,1)} copy-done((bf16[2,8,32,128]{3,2,1,0:T(8,128)(2,1)}, bf16[2,8,32,128]{3,2,1,0:T(8,128)(2,1)S(1)}, u32[]{:S(2)}) %copy-start.6) | copy-done | bytes 131096
  48.5 0.0 copy-start.7
  48.5 0.7 %copy-done.7 = bf16[2,8,32,128]{3,2,1,0:T(8,128)(2,1)} copy-done((bf16[2,8,32,128]{3,2,1,0:T(8,128)(2,1)}, bf16[2,8,32,128]{3,2,1,0:T(8,128)(2,1)S(1)}, u32[]{:S(2)}) %copy-start.7) | copy-done | bytes 131096
  49.1 4.8 %shard_map.52 = bf16[2,16,32,256]{3,2,1,0:T(8,128)(2,1)} custom-call(bf16[2,8,32,128]{3,2,1,0:T(8,128)(2,1)} %bitcast.15, bf16[2,8,32,128]{3,2,1,0:T(8,128)(2,1)} %copy-done.5, bf16[2,8,32,128]{3,2,1,0:T(8,128)(2,1)} %copy-done.6, bf16[2,8,32,128]{3,2,1,0:T(8,128)(2,1)} %copy-done.7, bf16[27,32,128]{2,1,0:T(8,128)(2,1)} %copy-done), custom_call_target="tpu_custom_call" | custom-call | flops 1006632960 | bytes 1048576 | tf_op jit(solution)/shard_map/pallas_call | solution.py:162
  53.9 0.0 collective-permute-done.4
  53.9 2.1 %collective-permute-done.3 = f32[8,32,128]{2,1,0:T(8,128)S(1)} collective-permute-done((f32[8,32,128]{2,1,0:T(8,128)}, f32[8,32,128]{2,1,0:T(8,128)S(1)}, u32[]{:S(2)}, u32[]{:S(2)}) %collective-permute-start.3) | collective-permute-done | bytes 131104 | tf_op jit(solution)/shard_map/ppermute | solution.py:174
  56.0 0.0 collective-permute-done.2
  56.0 0.0 copy-done.3
  56.0 0.7 %fusion.1 = bf16[1,1,8,32,128]{4,3,2,1,0:T(8,128)(2,1)} fusion(f32[8,32,128]{2,1,0:T(8,128)S(1)} %collective-permute-done.4, f32[8,32,128]{2,1,0:T(8,128)S(1)} %collective-permute-done.3, f32[8,32,128]{2,1,0:T(8,128)S(1)} %copy-done.3, f32[8,32,128]{2,1,0:T(8,128)S(1)} %collective-permute-done.2), kind=kLoop, calls=%fused_computation.5 | loop fusion | flops 131072 | bytes 589824 | tf_op jit(solution)/shard_map/reshape | solution.py:194
  (1 shorter events, 0.0 us)
Async XLA Ops:
  0.6 4.5 %copy-start.4 = (bf16[1,1,8,32,128]{4,3,2,1,0:T(8,128)(2,1)S(1)}, bf16[1,1,8,32,128]{4,3,2,1,0:T(8,128)(2,1)}, u32[]{:S(2)}) copy-start(bf16[1,1,8,32,128]{4,3,2,1,0:T(8,128)(2,1)} %param.5) | copy-start | bytes 196612
  0.6 15.0 %copy-start.1 = (bf16[27,32,128]{2,1,0:T(8,128)(2,1)S(1)}, bf16[27,32,128]{2,1,0:T(8,128)(2,1)}, u32[]{:S(2)}) copy-start(bf16[27,32,128]{2,1,0:T(8,128)(2,1)} %param.4) | copy-start | bytes 663556
  1.7 25.1 %collective-permute-start = (bf16[1,1,16,32,256]{4,3,2,1,0:T(8,128)(2,1)S(1)}, bf16[1,1,16,32,256]{4,3,2,1,0:T(8,128)(2,1)S(1)}, u32[]{:S(2)}, u32[]{:S(2)}) collective-permute-start(bf16[1,1,16,32,256]{4,3,2,1,0:T(8,128)(2,1)S(1)} %slice.3), channel_id=1, source_target_pairs={{0,8},{8,16},{16,24},{24,32},{32,40},{40,48},{48,56},{56,64},{64,7... | collective-permute-start | bytes 786440 | tf_op jit(solution)/shard_map/ppermute | solution.py:12
  5.1 14.4 %collective-permute-start.1 = (bf16[1,1,8,32,128]{4,3,2,1,0:T(8,128)(2,1)S(1)}, bf16[1,1,8,32,128]{4,3,2,1,0:T(8,128)(2,1)S(1)}, u32[]{:S(2)}, u32[]{:S(2)}) collective-permute-start(bf16[1,1,8,32,128]{4,3,2,1,0:T(8,128)(2,1)S(1)} %copy-done.4), channel_id=1, source_target_pairs={{8,0},{16,8},{24,16},{32,24},{40,32},{48,40},{56,48},{64,56},{72,6... | collective-permute-start | bytes 196616 | tf_op jit(solution)/shard_map/ppermute | solution.py:12
  15.9 0.8 %copy-start = (bf16[27,32,128]{2,1,0:T(8,128)(2,1)}, bf16[27,32,128]{2,1,0:T(8,128)(2,1)S(1)}, u32[]{:S(2)}) copy-start(bf16[27,32,128]{2,1,0:T(8,128)(2,1)S(1)} %fusion.refs_4_) | copy-start | bytes 663556
  19.5 15.9 %copy-start.2 = (bf16[1,2,8,32,128]{4,3,2,1,0:T(8,128)(2,1)}, bf16[1,2,8,32,128]{4,3,2,1,0:T(8,128)(2,1)S(1)}, u32[]{:S(2)}) copy-start(bf16[1,2,8,32,128]{4,3,2,1,0:T(8,128)(2,1)S(1)} %pad_maximum_fusion) | copy-start | bytes 393220
  29.2 26.9 %copy-start.3 = (f32[8,32,128]{2,1,0:T(8,128)S(1)}, f32[8,32,128]{2,1,0:T(8,128)}, u32[]{:S(2)}) copy-start(f32[8,32,128]{2,1,0:T(8,128)} %get-tuple-element.15) | copy-start | bytes 393220
  29.2 16.5 %collective-permute-start.5 = (bf16[2,8,32,128]{3,2,1,0:T(8,128)(2,1)S(1)}, bf16[2,8,32,128]{3,2,1,0:T(8,128)(2,1)S(1)}, u32[]{:S(2)}, u32[]{:S(2)}) collective-permute-start(bf16[2,8,32,128]{3,2,1,0:T(8,128)(2,1)S(1)} %bitcast.12), channel_id=1, source_target_pairs={{0,6},{2,0},{4,2},{6,4},{1,7},{3,1},{5,3},{7,5},{8,14},{10,8},{12,... | collective-permute-start | bytes 393224 | tf_op jit(solution)/shard_map/ppermute | solution.py:174
  33.1 14.7 %collective-permute-start.6 = (bf16[2,8,32,128]{3,2,1,0:T(8,128)(2,1)S(1)}, bf16[2,8,32,128]{3,2,1,0:T(8,128)(2,1)S(1)}, u32[]{:S(2)}, u32[]{:S(2)}) collective-permute-start(bf16[2,8,32,128]{3,2,1,0:T(8,128)(2,1)S(1)} %bitcast.13), channel_id=1, source_target_pairs={{0,4},{2,6},{4,0},{6,2},{1,5},{3,7},{5,1},{7,3},{8,12},{10,14},{12... | collective-permute-start | bytes 393224 | tf_op jit(solution)/shard_map/ppermute | solution.py:174
  35.4 12.5 %collective-permute-start.7 = (bf16[2,8,32,128]{3,2,1,0:T(8,128)(2,1)S(1)}, bf16[2,8,32,128]{3,2,1,0:T(8,128)(2,1)S(1)}, u32[]{:S(2)}, u32[]{:S(2)}) collective-permute-start(bf16[2,8,32,128]{3,2,1,0:T(8,128)(2,1)S(1)} %bitcast.14), channel_id=1, source_target_pairs={{0,2},{2,4},{4,6},{6,0},{1,3},{3,5},{5,7},{7,1},{8,10},{10,12},{12... | collective-permute-start | bytes 393224 | tf_op jit(solution)/shard_map/ppermute | solution.py:174
  39.3 14.6 %collective-permute-start.4 = (f32[8,32,128]{2,1,0:T(8,128)}, f32[8,32,128]{2,1,0:T(8,128)S(1)}, u32[]{:S(2)}, u32[]{:S(2)}) collective-permute-start(f32[8,32,128]{2,1,0:T(8,128)} %get-tuple-element.18), channel_id=1, source_target_pairs={{0,6},{2,0},{4,2},{6,4},{1,7},{3,1},{5,3},{7,5},{8,14},{10,8},{12,... | collective-permute-start | bytes 393224 | tf_op jit(solution)/shard_map/ppermute | solution.py:174
  43.0 13.0 %collective-permute-start.3 = (f32[8,32,128]{2,1,0:T(8,128)}, f32[8,32,128]{2,1,0:T(8,128)S(1)}, u32[]{:S(2)}, u32[]{:S(2)}) collective-permute-start(f32[8,32,128]{2,1,0:T(8,128)} %get-tuple-element.17), channel_id=1, source_target_pairs={{0,4},{2,6},{4,0},{6,2},{1,5},{3,7},{5,1},{7,3},{8,12},{10,14},{12... | collective-permute-start | bytes 393224 | tf_op jit(solution)/shard_map/ppermute | solution.py:174
  45.7 2.1 %copy-start.5 = (bf16[2,8,32,128]{3,2,1,0:T(8,128)(2,1)}, bf16[2,8,32,128]{3,2,1,0:T(8,128)(2,1)S(1)}, u32[]{:S(2)}) copy-start(bf16[2,8,32,128]{3,2,1,0:T(8,128)(2,1)S(1)} %collective-permute-done.5.refs_1_) | copy-start | bytes 393220
  45.7 10.3 %collective-permute-start.2 = (f32[8,32,128]{2,1,0:T(8,128)}, f32[8,32,128]{2,1,0:T(8,128)S(1)}, u32[]{:S(2)}, u32[]{:S(2)}) collective-permute-start(f32[8,32,128]{2,1,0:T(8,128)} %get-tuple-element.16), channel_id=1, source_target_pairs={{0,2},{2,4},{4,6},{6,0},{1,3},{3,5},{5,7},{7,1},{8,10},{10,12},{12... | collective-permute-start | bytes 393224 | tf_op jit(solution)/shard_map/ppermute | solution.py:174
  47.8 0.7 %copy-start.6 = (bf16[2,8,32,128]{3,2,1,0:T(8,128)(2,1)}, bf16[2,8,32,128]{3,2,1,0:T(8,128)(2,1)S(1)}, u32[]{:S(2)}) copy-start(bf16[2,8,32,128]{3,2,1,0:T(8,128)(2,1)S(1)} %collective-permute-done.6.refs_2_) | copy-start | bytes 393220
  48.5 0.7 %copy-start.7 = (bf16[2,8,32,128]{3,2,1,0:T(8,128)(2,1)}, bf16[2,8,32,128]{3,2,1,0:T(8,128)(2,1)S(1)}, u32[]{:S(2)}) copy-start(bf16[2,8,32,128]{3,2,1,0:T(8,128)(2,1)S(1)} %collective-permute-done.7.refs_3_) | copy-start | bytes 393220

commit v16 on v15

--- a/solution.py
+++ b/solution.py
@@ -166,7 +166,7 @@
         out_specs=pl.BlockSpec(memory_space=pltpu.VMEM),
         scratch_shapes=[pltpu.VMEM((planes, rows_out, chans_out, 3 * cols), kernel.dtype)],
         cost_estimate=pl.CostEstimate(flops=flops, bytes_accessed=2 * planes * rows_out * chans_out * cols_out + 2 * 2 * rows * chans * cols, transcendentals=0),
-    )(*pieces, kernel)
+    )(*[pltpu.with_memory_space_constraint(piece, pltpu.MemorySpace.VMEM) for piece in pieces], kernel)
 
 
 def chan_shift(block, shift):

time: 57.1 us -> 57.1 us (level)
  waiting for transfers between devices: 9.35 us -> 10.9 us
  local copies, waits for them, and re-layouts: 3.16 us -> 1.88 us
    ppermute x6, waiting for transfers between devices: 2.1 us -> 3.68 us  [chan_shift(): lax.ppermute(block, 'chan', [(i, (i + shift) % size) for i in range(size)])]
    unnamed x16 -> x8, local copies, waits for them, and re-layouts: 1.31 us -> 0.02 us
where the time goes in v16:
time: 57.1 us; the launch traced here: 56.7 us
  starting transfers between devices  32.5 us (57%)
  waiting for transfers between devices  10.9 us (19%)
  Pallas kernels  9.68 us (17%)
  local copies, waits for them, and re-layouts  1.88 us (3%)
  other arithmetic  0.91 us (2%)
  between operations  0.79 us (1%)
    ppermute x6, starting transfers between devices, chan_shift(): lax.ppermute(block, 'chan', [(i, (i + shift) % size) for i in range(size)])  18.5 us
    ppermute x2, starting transfers between devices, from_behind(): return lax.ppermute(block, axis, route)  14 us
    ppermute x2, waiting for transfers between devices, from_behind(): return lax.ppermute(block, axis, route)  7.24 us
    pallas_call x1, Pallas kernels, backward_grad(): pl.pallas_call(backward_rows, out_shape=jax.ShapeDtypeStruct((2, rows, ch...  4.56 us
    ppermute x6, waiting for transfers between devices, chan_shift(): lax.ppermute(block, 'chan', [(i, (i + shift) % size) for i in range(size)])  3.68 us
    pallas_call x1, Pallas kernels, forward_partial(): pl.pallas_call(forward_local_rows, out_shape=jax.ShapeDtypeStruct((rows_o...  2.71 us
    pallas_call x1, Pallas kernels, forward_partial(): pl.pallas_call(forward_halo_rows, out_shape=[jax.ShapeDtypeStruct((rows_o...  2.42 us
  transfers between devices with their start and end apart: 8, of which 2 were waited for; matrix products, arithmetic and copies ran while one was open for 2% of the time, Pallas kernels for 13%

profile of v16, /device:TPU:512, one launch (start us, length us, event | category | flops | bytes accessed | tf_op | source)
XLA Modules:
  0.0 56.7 jit_solution(13463255766210457503)
XLA Ops:
  0.6 0.0 copy-start.3
  0.6 0.0 copy-start.1
  0.6 1.0 %slice.3 = bf16[1,1,16,32,256]{4,3,2,1,0:T(8,128)(2,1)S(1)} slice(bf16[1,2,16,32,256]{4,3,2,1,0:T(8,128)(2,1)} %param.3), slice={[0:1], [1:2], [0:16], [0:32], [0:256]} | slice | bytes 524288 | tf_op jit(solution)/shard_map/slice | solution.py:187
  1.7 3.4 %collective-permute-start = (bf16[1,1,16,32,256]{4,3,2,1,0:T(8,128)(2,1)S(1)}, bf16[1,1,16,32,256]{4,3,2,1,0:T(8,128)(2,1)S(1)}, u32[]{:S(2)}, u32[]{:S(2)}) collective-permute-start(bf16[1,1,16,32,256]{4,3,2,1,0:T(8,128)(2,1)S(1)} %slice.3), channel_id=1, source_target_pairs={{0,8},{8,16},{16,24},{24,32},{32,40},{40,48},{48,56},{56,64},{64,7... | collective-permute-start | bytes 786440 | tf_op jit(solution)/shard_map/ppermute | solution.py:12
  5.1 0.0 copy-done.3
  5.1 10.6 %collective-permute-start.1 = (bf16[1,1,8,32,128]{4,3,2,1,0:T(8,128)(2,1)S(1)}, bf16[1,1,8,32,128]{4,3,2,1,0:T(8,128)(2,1)S(1)}, u32[]{:S(2)}, u32[]{:S(2)}) collective-permute-start(bf16[1,1,8,32,128]{4,3,2,1,0:T(8,128)(2,1)S(1)} %copy-done.3), channel_id=1, source_target_pairs={{8,0},{16,8},{24,16},{32,24},{40,32},{48,40},{56,48},{64,56},{72,6... | collective-permute-start | bytes 196616 | tf_op jit(solution)/shard_map/ppermute | solution.py:12
  15.7 0.0 copy-done.1
  15.7 0.2 fusion.refs_4_
  15.9 0.0 copy-start
  15.9 0.9 %copy.5.kbig_ref = bf16[128,864]{1,0:T(8,128)(2,1)} copy(bf16[128,864]{0,1:T(8,128)(2,1)S(1)} %bitcast.14) | data formatting | bytes 442368 | tf_op jit(solution)/shard_map/reshape | solution.py:105
  16.8 0.0 copy-done
  16.8 2.7 %shard_map.50.acc_ref = f32[8,128,128]{2,1,0:T(8,128)} custom-call(bf16[2,16,32,256]{3,2,1,0:T(8,128)(2,1)} %bitcast.15, bf16[128,864]{1,0:T(8,128)(2,1)} %copy.5.kbig_ref), custom_call_target="tpu_custom_call" | custom-call | flops 352321536 | bytes 1048576 | tf_op jit(solution)/shard_map/pallas_call | solution.py:108
  19.5 0.0 collective-permute-done.1
  19.5 7.2 %collective-permute-done = bf16[1,1,16,32,256]{4,3,2,1,0:T(8,128)(2,1)S(1)} collective-permute-done((bf16[1,1,16,32,256]{4,3,2,1,0:T(8,128)(2,1)S(1)}, bf16[1,1,16,32,256]{4,3,2,1,0:T(8,128)(2,1)S(1)}, u32[]{:S(2)}, u32[]{:S(2)}) %collective-permute-start) | collective-permute-done | bytes 262176 | tf_op jit(solution)/shard_map/ppermute | solution.py:12
  26.8 2.4 %shard_map.51 = (f32[8,32,128]{2,1,0:T(8,128)}, f32[8,32,128]{2,1,0:T(8,128)}, f32[8,32,128]{2,1,0:T(8,128)}, f32[8,32,128]{2,1,0:T(8,128)}) custom-call(bf16[16,32,256]{2,1,0:T(8,128)(2,1)S(1)} %bitcast.9, f32[8,128,128]{2,1,0:T(8,128)} %shard_map.50.acc_ref, bf16[128,864]{1,0:T(8,128)(2,1)} %copy.5.kbig_ref), custom_call_target="tpu_custom_call" | custom-call | flops 176160768 | bytes 1310720 | tf_op jit(solution)/shard_map/pallas_call | solution.py:116
  29.2 0.0 copy-start.2
  29.2 3.9 %collective-permute-start.5 = (bf16[2,8,32,128]{3,2,1,0:T(8,128)(2,1)S(1)}, bf16[2,8,32,128]{3,2,1,0:T(8,128)(2,1)S(1)}, u32[]{:S(2)}, u32[]{:S(2)}) collective-permute-start(bf16[2,8,32,128]{3,2,1,0:T(8,128)(2,1)S(1)} %bitcast.10), channel_id=1, source_target_pairs={{0,6},{2,0},{4,2},{6,4},{1,7},{3,1},{5,3},{7,5},{8,14},{10,8},{12,... | collective-permute-start | bytes 393224 | tf_op jit(solution)/shard_map/ppermute | solution.py:174
  33.1 2.3 %collective-permute-start.6 = (bf16[2,8,32,128]{3,2,1,0:T(8,128)(2,1)S(1)}, bf16[2,8,32,128]{3,2,1,0:T(8,128)(2,1)S(1)}, u32[]{:S(2)}, u32[]{:S(2)}) collective-permute-start(bf16[2,8,32,128]{3,2,1,0:T(8,128)(2,1)S(1)} %bitcast.11), channel_id=1, source_target_pairs={{0,4},{2,6},{4,0},{6,2},{1,5},{3,7},{5,1},{7,3},{8,12},{10,14},{12... | collective-permute-start | bytes 393224 | tf_op jit(solution)/shard_map/ppermute | solution.py:174
  35.4 3.9 %collective-permute-start.7 = (bf16[2,8,32,128]{3,2,1,0:T(8,128)(2,1)S(1)}, bf16[2,8,32,128]{3,2,1,0:T(8,128)(2,1)S(1)}, u32[]{:S(2)}, u32[]{:S(2)}) collective-permute-start(bf16[2,8,32,128]{3,2,1,0:T(8,128)(2,1)S(1)} %bitcast.12), channel_id=1, source_target_pairs={{0,2},{2,4},{4,6},{6,0},{1,3},{3,5},{5,7},{7,1},{8,10},{10,12},{12... | collective-permute-start | bytes 393224 | tf_op jit(solution)/shard_map/ppermute | solution.py:174
  39.3 3.7 %collective-permute-start.4 = (f32[8,32,128]{2,1,0:T(8,128)}, f32[8,32,128]{2,1,0:T(8,128)S(1)}, u32[]{:S(2)}, u32[]{:S(2)}) collective-permute-start(f32[8,32,128]{2,1,0:T(8,128)} %get-tuple-element.18), channel_id=1, source_target_pairs={{0,6},{2,0},{4,2},{6,4},{1,7},{3,1},{5,3},{7,5},{8,14},{10,8},{12,... | collective-permute-start | bytes 393224 | tf_op jit(solution)/shard_map/ppermute | solution.py:174
  43.0 2.7 %collective-permute-start.3 = (f32[8,32,128]{2,1,0:T(8,128)}, f32[8,32,128]{2,1,0:T(8,128)S(1)}, u32[]{:S(2)}, u32[]{:S(2)}) collective-permute-start(f32[8,32,128]{2,1,0:T(8,128)} %get-tuple-element.17), channel_id=1, source_target_pairs={{0,4},{2,6},{4,0},{6,2},{1,5},{3,7},{5,1},{7,3},{8,12},{10,14},{12... | collective-permute-start | bytes 393224 | tf_op jit(solution)/shard_map/ppermute | solution.py:174
  45.7 0.0 collective-permute-done.5.refs_1_
  45.7 2.1 %collective-permute-start.2 = (f32[8,32,128]{2,1,0:T(8,128)}, f32[8,32,128]{2,1,0:T(8,128)S(1)}, u32[]{:S(2)}, u32[]{:S(2)}) collective-permute-start(f32[8,32,128]{2,1,0:T(8,128)} %get-tuple-element.16), channel_id=1, source_target_pairs={{0,2},{2,4},{4,6},{6,0},{1,3},{3,5},{5,7},{7,1},{8,10},{10,12},{12... | collective-permute-start | bytes 393224 | tf_op jit(solution)/shard_map/ppermute | solution.py:174
  47.8 0.0 collective-permute-done.6.refs_2_
  47.8 0.0 collective-permute-done.7.refs_3_
  47.8 4.6 %shard_map.52 = bf16[2,16,32,256]{3,2,1,0:T(8,128)(2,1)} custom-call(bf16[2,8,32,128]{3,2,1,0:T(8,128)(2,1)S(1)} %bitcast.13, bf16[2,8,32,128]{3,2,1,0:T(8,128)(2,1)S(1)} %collective-permute-done.5.refs_1_, bf16[2,8,32,128]{3,2,1,0:T(8,128)(2,1)S(1)} %collective-permute-done.6.refs_2_, bf16[2,8,32,128]{3,2,1,0:T(8,128)(2,1)S(1)} %collective-permute-done.7.refs_3_, ...), custom_call_target="tpu_custom_call" | custom-call | flops 1006632960 | bytes 1048576 | tf_op jit(solution)/shard_map/pallas_call | solution.py:162
  52.4 0.0 collective-permute-done.4
  52.4 3.7 %collective-permute-done.3 = f32[8,32,128]{2,1,0:T(8,128)S(1)} collective-permute-done((f32[8,32,128]{2,1,0:T(8,128)}, f32[8,32,128]{2,1,0:T(8,128)S(1)}, u32[]{:S(2)}, u32[]{:S(2)}) %collective-permute-start.3) | collective-permute-done | bytes 131104 | tf_op jit(solution)/shard_map/ppermute | solution.py:174
  56.0 0.0 collective-permute-done.2
  56.0 0.0 copy-done.2
  56.0 0.7 %fusion.1 = bf16[1,1,8,32,128]{4,3,2,1,0:T(8,128)(2,1)} fusion(f32[8,32,128]{2,1,0:T(8,128)S(1)} %collective-permute-done.4, f32[8,32,128]{2,1,0:T(8,128)S(1)} %collective-permute-done.3, f32[8,32,128]{2,1,0:T(8,128)S(1)} %copy-done.2, f32[8,32,128]{2,1,0:T(8,128)S(1)} %collective-permute-done.2), kind=kLoop, calls=%fused_computation.5 | loop fusion | flops 131072 | bytes 589824 | tf_op jit(solution)/shard_map/reshape | solution.py:194
  (1 shorter events, 0.0 us)
Async XLA Ops:
  0.6 4.5 %copy-start.3 = (bf16[1,1,8,32,128]{4,3,2,1,0:T(8,128)(2,1)S(1)}, bf16[1,1,8,32,128]{4,3,2,1,0:T(8,128)(2,1)}, u32[]{:S(2)}) copy-start(bf16[1,1,8,32,128]{4,3,2,1,0:T(8,128)(2,1)} %param.5) | copy-start | bytes 196612
  0.6 15.0 %copy-start.1 = (bf16[27,32,128]{2,1,0:T(8,128)(2,1)S(1)}, bf16[27,32,128]{2,1,0:T(8,128)(2,1)}, u32[]{:S(2)}) copy-start(bf16[27,32,128]{2,1,0:T(8,128)(2,1)} %param.4) | copy-start | bytes 663556
  1.7 25.1 %collective-permute-start = (bf16[1,1,16,32,256]{4,3,2,1,0:T(8,128)(2,1)S(1)}, bf16[1,1,16,32,256]{4,3,2,1,0:T(8,128)(2,1)S(1)}, u32[]{:S(2)}, u32[]{:S(2)}) collective-permute-start(bf16[1,1,16,32,256]{4,3,2,1,0:T(8,128)(2,1)S(1)} %slice.3), channel_id=1, source_target_pairs={{0,8},{8,16},{16,24},{24,32},{32,40},{40,48},{48,56},{56,64},{64,7... | collective-permute-start | bytes 786440 | tf_op jit(solution)/shard_map/ppermute | solution.py:12
  5.1 14.4 %collective-permute-start.1 = (bf16[1,1,8,32,128]{4,3,2,1,0:T(8,128)(2,1)S(1)}, bf16[1,1,8,32,128]{4,3,2,1,0:T(8,128)(2,1)S(1)}, u32[]{:S(2)}, u32[]{:S(2)}) collective-permute-start(bf16[1,1,8,32,128]{4,3,2,1,0:T(8,128)(2,1)S(1)} %copy-done.3), channel_id=1, source_target_pairs={{8,0},{16,8},{24,16},{32,24},{40,32},{48,40},{56,48},{64,56},{72,6... | collective-permute-start | bytes 196616 | tf_op jit(solution)/shard_map/ppermute | solution.py:12
  15.9 0.9 %copy-start = (bf16[27,32,128]{2,1,0:T(8,128)(2,1)}, bf16[27,32,128]{2,1,0:T(8,128)(2,1)S(1)}, u32[]{:S(2)}) copy-start(bf16[27,32,128]{2,1,0:T(8,128)(2,1)S(1)} %fusion.refs_4_) | copy-start | bytes 663556
  29.2 26.9 %copy-start.2 = (f32[8,32,128]{2,1,0:T(8,128)S(1)}, f32[8,32,128]{2,1,0:T(8,128)}, u32[]{:S(2)}) copy-start(f32[8,32,128]{2,1,0:T(8,128)} %get-tuple-element.15) | copy-start | bytes 393220
  29.2 16.5 %collective-permute-start.5 = (bf16[2,8,32,128]{3,2,1,0:T(8,128)(2,1)S(1)}, bf16[2,8,32,128]{3,2,1,0:T(8,128)(2,1)S(1)}, u32[]{:S(2)}, u32[]{:S(2)}) collective-permute-start(bf16[2,8,32,128]{3,2,1,0:T(8,128)(2,1)S(1)} %bitcast.10), channel_id=1, source_target_pairs={{0,6},{2,0},{4,2},{6,4},{1,7},{3,1},{5,3},{7,5},{8,14},{10,8},{12,... | collective-permute-start | bytes 393224 | tf_op jit(solution)/shard_map/ppermute | solution.py:174
  33.1 14.7 %collective-permute-start.6 = (bf16[2,8,32,128]{3,2,1,0:T(8,128)(2,1)S(1)}, bf16[2,8,32,128]{3,2,1,0:T(8,128)(2,1)S(1)}, u32[]{:S(2)}, u32[]{:S(2)}) collective-permute-start(bf16[2,8,32,128]{3,2,1,0:T(8,128)(2,1)S(1)} %bitcast.11), channel_id=1, source_target_pairs={{0,4},{2,6},{4,0},{6,2},{1,5},{3,7},{5,1},{7,3},{8,12},{10,14},{12... | collective-permute-start | bytes 393224 | tf_op jit(solution)/shard_map/ppermute | solution.py:174
  35.4 12.4 %collective-permute-start.7 = (bf16[2,8,32,128]{3,2,1,0:T(8,128)(2,1)S(1)}, bf16[2,8,32,128]{3,2,1,0:T(8,128)(2,1)S(1)}, u32[]{:S(2)}, u32[]{:S(2)}) collective-permute-start(bf16[2,8,32,128]{3,2,1,0:T(8,128)(2,1)S(1)} %bitcast.12), channel_id=1, source_target_pairs={{0,2},{2,4},{4,6},{6,0},{1,3},{3,5},{5,7},{7,1},{8,10},{10,12},{12... | collective-permute-start | bytes 393224 | tf_op jit(solution)/shard_map/ppermute | solution.py:174
  39.3 13.1 %collective-permute-start.4 = (f32[8,32,128]{2,1,0:T(8,128)}, f32[8,32,128]{2,1,0:T(8,128)S(1)}, u32[]{:S(2)}, u32[]{:S(2)}) collective-permute-start(f32[8,32,128]{2,1,0:T(8,128)} %get-tuple-element.18), channel_id=1, source_target_pairs={{0,6},{2,0},{4,2},{6,4},{1,7},{3,1},{5,3},{7,5},{8,14},{10,8},{12,... | collective-permute-start | bytes 393224 | tf_op jit(solution)/shard_map/ppermute | solution.py:174
  43.0 13.0 %collective-permute-start.3 = (f32[8,32,128]{2,1,0:T(8,128)}, f32[8,32,128]{2,1,0:T(8,128)S(1)}, u32[]{:S(2)}, u32[]{:S(2)}) collective-permute-start(f32[8,32,128]{2,1,0:T(8,128)} %get-tuple-element.17), channel_id=1, source_target_pairs={{0,4},{2,6},{4,0},{6,2},{1,5},{3,7},{5,1},{7,3},{8,12},{10,14},{12... | collective-permute-start | bytes 393224 | tf_op jit(solution)/shard_map/ppermute | solution.py:174
  45.7 10.3 %collective-permute-start.2 = (f32[8,32,128]{2,1,0:T(8,128)}, f32[8,32,128]{2,1,0:T(8,128)S(1)}, u32[]{:S(2)}, u32[]{:S(2)}) collective-permute-start(f32[8,32,128]{2,1,0:T(8,128)} %get-tuple-element.16), channel_id=1, source_target_pairs={{0,2},{2,4},{4,6},{6,0},{1,3},{3,5},{5,7},{7,1},{8,10},{10,12},{12... | collective-permute-start | bytes 393224 | tf_op jit(solution)/shard_map/ppermute | solution.py:174

commit v17 on v15

--- a/solution.py
+++ b/solution.py
@@ -169,6 +169,14 @@
     )(*pieces, kernel)
 
 
+def sum_parts(*refs):
+    out_ref = refs[-1]
+    total = refs[0][...]
+    for ref in refs[1:-1]:
+        total = total + ref[...]
+    out_ref[...] = total.astype(out_ref.dtype)
+
+
 def chan_shift(block, shift):
     size = lax.axis_size("chan")
     return lax.ppermute(block, "chan", [(i, (i + shift) % size) for i in range(size)])
@@ -188,10 +196,14 @@
     chunks = forward_partial(below[0, 0], volume[0], kernel, groups)
     pair = jnp.concatenate([cotangent, from_behind(cotangent, "space", -1)], axis=1)
     chunks, pair = lax.optimization_barrier((chunks, pair))
-    total = chunks[0]
-    for k in range(1, groups):
-        total = total + chan_shift(chunks[k], k)
-    response = total.astype(jnp.bfloat16).reshape(count, planes_out, rows_out, share, cols_out)
+    parts = [chunks[0]] + [chan_shift(chunks[k], k) for k in range(1, groups)]
+    response = pl.pallas_call(
+        sum_parts,
+        out_shape=jax.ShapeDtypeStruct(parts[0].shape, jnp.bfloat16),
+        in_specs=[pl.BlockSpec(memory_space=pltpu.VMEM)] * groups,
+        out_specs=pl.BlockSpec(memory_space=pltpu.VMEM),
+    )(*[pltpu.with_memory_space_constraint(part, pltpu.MemorySpace.VMEM) for part in parts])
+    response = response.reshape(count, planes_out, rows_out, share, cols_out)
     pieces = [pair[0]] + [chan_shift(pair[0], -k) for k in range(1, groups)]
     volume_grad = backward_grad(pieces, kernel).reshape(count, planes_in, rows_in, chans_in, cols_in)
     return (response, volume_grad)

time: 57.1 us -> 58.8 us (1.030)
  starting transfers between devices: 32.5 us -> 33.6 us
  other arithmetic: 0.91 us -> 0.24 us
  Pallas kernels: 9.94 us -> 10.6 us
  waiting for transfers between devices: 9.35 us -> 9.97 us
    ppermute x6, starting transfers between devices: 18.5 us -> 19.7 us  [chan_shift(): lax.ppermute(block, 'chan', [(i, (i + shift) % size) for i in range(size)])]
    reshape x1 -> x0, other arithmetic: 0.67 us -> none  [per_device(): total.astype(jnp.bfloat16)]
    pallas_call x0 -> x1, Pallas kernels: none -> 0.66 us  [per_device(): pl.pallas_call(sum_parts, out_shape=jax.ShapeDtypeStruct(parts[0].shape,...]
    ppermute x6, waiting for transfers between devices: 2.1 us -> 2.72 us  [chan_shift(): lax.ppermute(block, 'chan', [(i, (i + shift) % size) for i in range(size)])]
where the time goes in v17:
time: 58.8 us; the launch traced here: 58.4 us
  starting transfers between devices  33.6 us (57%)
  Pallas kernels  10.6 us (18%)
  waiting for transfers between devices  9.97 us (17%)
  local copies, waits for them, and re-layouts  3.18 us (5%)
  between operations  0.82 us (1%)
    ppermute x6, starting transfers between devices, chan_shift(): lax.ppermute(block, 'chan', [(i, (i + shift) % size) for i in range(size)])  19.7 us
    ppermute x2, starting transfers between devices, from_behind(): return lax.ppermute(block, axis, route)  14 us
    ppermute x2, waiting for transfers between devices, from_behind(): return lax.ppermute(block, axis, route)  7.25 us
    pallas_call x1, Pallas kernels, backward_grad(): pl.pallas_call(backward_rows, out_shape=jax.ShapeDtypeStruct((2, rows, ch...  4.81 us
    ppermute x6, waiting for transfers between devices, chan_shift(): lax.ppermute(block, 'chan', [(i, (i + shift) % size) for i in range(size)])  2.72 us
    pallas_call x1, Pallas kernels, forward_partial(): pl.pallas_call(forward_local_rows, out_shape=jax.ShapeDtypeStruct((rows_o...  2.71 us
    pallas_call x1, Pallas kernels, forward_partial(): pl.pallas_call(forward_halo_rows, out_shape=[jax.ShapeDtypeStruct((rows_o...  2.42 us
    unnamed x16, local copies, waits for them, and re-layouts  1.33 us
  transfers between devices with their start and end apart: 8, of which 2 were waited for; matrix products, arithmetic and copies ran while one was open for 2% of the time, Pallas kernels for 13%

profile of v17, /device:TPU:512, one launch (start us, length us, event | category | flops | bytes accessed | tf_op | source)
XLA Modules:
  0.0 58.4 jit_solution(697223019642076072)
XLA Ops:
  0.6 0.0 copy-start.4
  0.6 0.0 copy-start.2
  0.6 1.0 %slice.3 = bf16[1,1,16,32,256]{4,3,2,1,0:T(8,128)(2,1)S(1)} slice(bf16[1,2,16,32,256]{4,3,2,1,0:T(8,128)(2,1)} %param.3), slice={[0:1], [1:2], [0:16], [0:32], [0:256]} | slice | bytes 524288 | tf_op jit(solution)/shard_map/slice | solution.py:195
  1.7 3.4 %collective-permute-start = (bf16[1,1,16,32,256]{4,3,2,1,0:T(8,128)(2,1)S(1)}, bf16[1,1,16,32,256]{4,3,2,1,0:T(8,128)(2,1)S(1)}, u32[]{:S(2)}, u32[]{:S(2)}) collective-permute-start(bf16[1,1,16,32,256]{4,3,2,1,0:T(8,128)(2,1)S(1)} %slice.3), channel_id=1, source_target_pairs={{0,8},{8,16},{16,24},{24,32},{32,40},{40,48},{48,56},{56,64},{64,7... | collective-permute-start | bytes 786440 | tf_op jit(solution)/shard_map/ppermute | solution.py:12
  5.1 0.0 copy-done.4
  5.1 10.6 %collective-permute-start.1 = (bf16[1,1,8,32,128]{4,3,2,1,0:T(8,128)(2,1)S(1)}, bf16[1,1,8,32,128]{4,3,2,1,0:T(8,128)(2,1)S(1)}, u32[]{:S(2)}, u32[]{:S(2)}) collective-permute-start(bf16[1,1,8,32,128]{4,3,2,1,0:T(8,128)(2,1)S(1)} %copy-done.4), channel_id=1, source_target_pairs={{8,0},{16,8},{24,16},{32,24},{40,32},{48,40},{56,48},{64,56},{72,6... | collective-permute-start | bytes 196616 | tf_op jit(solution)/shard_map/ppermute | solution.py:12
  15.7 0.0 copy-done.2
  15.7 0.2 fusion.refs_4_
  15.9 0.0 copy-start.1
  15.9 0.8 %copy.5.kbig_ref = bf16[128,864]{1,0:T(8,128)(2,1)} copy(bf16[128,864]{0,1:T(8,128)(2,1)S(1)} %bitcast.9) | data formatting | bytes 442368 | tf_op jit(solution)/shard_map/reshape | solution.py:105
  16.8 0.0 copy-done.1
  16.8 2.7 %shard_map.50.acc_ref = f32[8,128,128]{2,1,0:T(8,128)} custom-call(bf16[2,16,32,256]{3,2,1,0:T(8,128)(2,1)} %bitcast.10, bf16[128,864]{1,0:T(8,128)(2,1)} %copy.5.kbig_ref), custom_call_target="tpu_custom_call" | custom-call | flops 352321536 | bytes 1048576 | tf_op jit(solution)/shard_map/pallas_call | solution.py:108
  19.5 0.0 collective-permute-done.1
  19.5 0.0 copy-start.3
  19.5 7.2 %collective-permute-done = bf16[1,1,16,32,256]{4,3,2,1,0:T(8,128)(2,1)S(1)} collective-permute-done((bf16[1,1,16,32,256]{4,3,2,1,0:T(8,128)(2,1)S(1)}, bf16[1,1,16,32,256]{4,3,2,1,0:T(8,128)(2,1)S(1)}, u32[]{:S(2)}, u32[]{:S(2)}) %collective-permute-start) | collective-permute-done | bytes 262176 | tf_op jit(solution)/shard_map/ppermute | solution.py:12
  26.8 2.4 %shard_map.51 = (f32[8,32,128]{2,1,0:T(8,128)}, f32[8,32,128]{2,1,0:T(8,128)}, f32[8,32,128]{2,1,0:T(8,128)}, f32[8,32,128]{2,1,0:T(8,128)}) custom-call(bf16[16,32,256]{2,1,0:T(8,128)(2,1)S(1)} %bitcast.8, f32[8,128,128]{2,1,0:T(8,128)} %shard_map.50.acc_ref, bf16[128,864]{1,0:T(8,128)(2,1)} %copy.5.kbig_ref), custom_call_target="tpu_custom_call" | custom-call | flops 176160768 | bytes 1310720 | tf_op jit(solution)/shard_map/pallas_call | solution.py:116
  29.2 0.0 copy-start
  29.2 3.9 %collective-permute-start.5 = (bf16[2,8,32,128]{3,2,1,0:T(8,128)(2,1)S(1)}, bf16[2,8,32,128]{3,2,1,0:T(8,128)(2,1)S(1)}, u32[]{:S(2)}, u32[]{:S(2)}) collective-permute-start(bf16[2,8,32,128]{3,2,1,0:T(8,128)(2,1)S(1)} %bitcast.11), channel_id=1, source_target_pairs={{0,6},{2,0},{4,2},{6,4},{1,7},{3,1},{5,3},{7,5},{8,14},{10,8},{12,... | collective-permute-start | bytes 393224 | tf_op jit(solution)/shard_map/ppermute | solution.py:182
  33.1 2.3 %collective-permute-start.6 = (bf16[2,8,32,128]{3,2,1,0:T(8,128)(2,1)S(1)}, bf16[2,8,32,128]{3,2,1,0:T(8,128)(2,1)S(1)}, u32[]{:S(2)}, u32[]{:S(2)}) collective-permute-start(bf16[2,8,32,128]{3,2,1,0:T(8,128)(2,1)S(1)} %bitcast.12), channel_id=1, source_target_pairs={{0,4},{2,6},{4,0},{6,2},{1,5},{3,7},{5,1},{7,3},{8,12},{10,14},{12... | collective-permute-start | bytes 393224 | tf_op jit(solution)/shard_map/ppermute | solution.py:182
  35.4 0.0 copy-done.3
  35.4 3.9 %collective-permute-start.7 = (bf16[2,8,32,128]{3,2,1,0:T(8,128)(2,1)S(1)}, bf16[2,8,32,128]{3,2,1,0:T(8,128)(2,1)S(1)}, u32[]{:S(2)}, u32[]{:S(2)}) collective-permute-start(bf16[2,8,32,128]{3,2,1,0:T(8,128)(2,1)S(1)} %bitcast.13), channel_id=1, source_target_pairs={{0,2},{2,4},{4,6},{6,0},{1,3},{3,5},{5,7},{7,1},{8,10},{10,12},{12... | collective-permute-start | bytes 393224 | tf_op jit(solution)/shard_map/ppermute | solution.py:182
  39.3 3.0 %collective-permute-start.2 = (f32[8,32,128]{2,1,0:T(8,128)}, f32[8,32,128]{2,1,0:T(8,128)S(1)}, u32[]{:S(2)}, u32[]{:S(2)}) collective-permute-start(f32[8,32,128]{2,1,0:T(8,128)} %get-tuple-element.16), channel_id=1, source_target_pairs={{0,2},{2,4},{4,6},{6,0},{1,3},{3,5},{5,7},{7,1},{8,10},{10,12},{12... | collective-permute-start | bytes 393224 | tf_op jit(solution)/shard_map/ppermute | solution.py:182
  42.3 3.2 %collective-permute-start.3 = (f32[8,32,128]{2,1,0:T(8,128)}, f32[8,32,128]{2,1,0:T(8,128)S(1)}, u32[]{:S(2)}, u32[]{:S(2)}) collective-permute-start(f32[8,32,128]{2,1,0:T(8,128)} %get-tuple-element.17), channel_id=1, source_target_pairs={{0,4},{2,6},{4,0},{6,2},{1,5},{3,7},{5,1},{7,3},{8,12},{10,14},{12... | collective-permute-start | bytes 393224 | tf_op jit(solution)/shard_map/ppermute | solution.py:182
  45.5 0.0 collective-permute-done.5.refs_1_
  45.5 0.0 copy-start.5
  45.5 3.4 %collective-permute-start.4 = (f32[8,32,128]{2,1,0:T(8,128)}, f32[8,32,128]{2,1,0:T(8,128)S(1)}, u32[]{:S(2)}, u32[]{:S(2)}) collective-permute-start(f32[8,32,128]{2,1,0:T(8,128)} %get-tuple-element.18), channel_id=1, source_target_pairs={{0,6},{2,0},{4,2},{6,4},{1,7},{3,1},{5,3},{7,5},{8,14},{10,8},{12,... | collective-permute-start | bytes 393224 | tf_op jit(solution)/shard_map/ppermute | solution.py:182
  48.9 2.7 %collective-permute-done.6.refs_2_ = bf16[2,8,32,128]{3,2,1,0:T(8,128)(2,1)S(1)} collective-permute-done((bf16[2,8,32,128]{3,2,1,0:T(8,128)(2,1)S(1)}, bf16[2,8,32,128]{3,2,1,0:T(8,128)(2,1)S(1)}, u32[]{:S(2)}, u32[]{:S(2)}) %collective-permute-start.6) | collective-permute-done | bytes 131104 | tf_op jit(solution)/shard_map/ppermute | solution.py:182
  51.6 0.0 copy-start.6
  51.6 0.0 collective-permute-done.7.refs_3_
  51.6 0.0 copy-done.5
  51.6 0.6 %copy-done.6 = bf16[2,8,32,128]{3,2,1,0:T(8,128)(2,1)} copy-done((bf16[2,8,32,128]{3,2,1,0:T(8,128)(2,1)}, bf16[2,8,32,128]{3,2,1,0:T(8,128)(2,1)S(1)}, u32[]{:S(2)}) %copy-start.6) | copy-done | bytes 131096
  52.3 0.0 copy-start.7
  52.3 0.7 %copy-done.7 = bf16[2,8,32,128]{3,2,1,0:T(8,128)(2,1)} copy-done((bf16[2,8,32,128]{3,2,1,0:T(8,128)(2,1)}, bf16[2,8,32,128]{3,2,1,0:T(8,128)(2,1)S(1)}, u32[]{:S(2)}) %copy-start.7) | copy-done | bytes 131096
  52.9 4.8 %shard_map.53 = bf16[2,16,32,256]{3,2,1,0:T(8,128)(2,1)} custom-call(bf16[2,8,32,128]{3,2,1,0:T(8,128)(2,1)} %bitcast.14, bf16[2,8,32,128]{3,2,1,0:T(8,128)(2,1)} %copy-done.5, bf16[2,8,32,128]{3,2,1,0:T(8,128)(2,1)} %copy-done.6, bf16[2,8,32,128]{3,2,1,0:T(8,128)(2,1)} %copy-done.7, bf16[27,32,128]{2,1,0:T(8,128)(2,1)} %copy-done.1), custom_call_target="tpu_custom_call" | custom-call | flops 1006632960 | bytes 1048576 | tf_op jit(solution)/shard_map/pallas_call | solution.py:162
  57.7 0.0 collective-permute-done.2.refs_1_
  57.7 0.0 collective-permute-done.3.refs_2_
  57.7 0.0 collective-permute-done.4.refs_3_
  57.8 0.0 copy-done
  57.8 0.7 %shard_map.52 = bf16[8,32,128]{2,1,0:T(8,128)(2,1)} custom-call(f32[8,32,128]{2,1,0:T(8,128)S(1)} %copy-done, f32[8,32,128]{2,1,0:T(8,128)S(1)} %collective-permute-done.2.refs_1_, f32[8,32,128]{2,1,0:T(8,128)S(1)} %collective-permute-done.3.refs_2_, f32[8,32,128]{2,1,0:T(8,128)S(1)} %collective-permute-done.4.refs_3_), custom_call_target="tpu_custom_call" | custom-call | tf_op jit(solution)/shard_map/pallas_call | solution.py:200
  (1 shorter events, 0.0 us)
Async XLA Ops:
  0.6 4.5 %copy-start.4 = (bf16[1,1,8,32,128]{4,3,2,1,0:T(8,128)(2,1)S(1)}, bf16[1,1,8,32,128]{4,3,2,1,0:T(8,128)(2,1)}, u32[]{:S(2)}) copy-start(bf16[1,1,8,32,128]{4,3,2,1,0:T(8,128)(2,1)} %param.5) | copy-start | bytes 196612
  0.6 15.0 %copy-start.2 = (bf16[27,32,128]{2,1,0:T(8,128)(2,1)S(1)}, bf16[27,32,128]{2,1,0:T(8,128)(2,1)}, u32[]{:S(2)}) copy-start(bf16[27,32,128]{2,1,0:T(8,128)(2,1)} %param.4) | copy-start | bytes 663556
  1.7 25.1 %collective-permute-start = (bf16[1,1,16,32,256]{4,3,2,1,0:T(8,128)(2,1)S(1)}, bf16[1,1,16,32,256]{4,3,2,1,0:T(8,128)(2,1)S(1)}, u32[]{:S(2)}, u32[]{:S(2)}) collective-permute-start(bf16[1,1,16,32,256]{4,3,2,1,0:T(8,128)(2,1)S(1)} %slice.3), channel_id=1, source_target_pairs={{0,8},{8,16},{16,24},{24,32},{32,40},{40,48},{48,56},{56,64},{64,7... | collective-permute-start | bytes 786440 | tf_op jit(solution)/shard_map/ppermute | solution.py:12
  5.1 14.4 %collective-permute-start.1 = (bf16[1,1,8,32,128]{4,3,2,1,0:T(8,128)(2,1)S(1)}, bf16[1,1,8,32,128]{4,3,2,1,0:T(8,128)(2,1)S(1)}, u32[]{:S(2)}, u32[]{:S(2)}) collective-permute-start(bf16[1,1,8,32,128]{4,3,2,1,0:T(8,128)(2,1)S(1)} %copy-done.4), channel_id=1, source_target_pairs={{8,0},{16,8},{24,16},{32,24},{40,32},{48,40},{56,48},{64,56},{72,6... | collective-permute-start | bytes 196616 | tf_op jit(solution)/shard_map/ppermute | solution.py:12
  15.9 0.8 %copy-start.1 = (bf16[27,32,128]{2,1,0:T(8,128)(2,1)}, bf16[27,32,128]{2,1,0:T(8,128)(2,1)S(1)}, u32[]{:S(2)}) copy-start(bf16[27,32,128]{2,1,0:T(8,128)(2,1)S(1)} %fusion.refs_4_) | copy-start | bytes 663556
  19.5 15.9 %copy-start.3 = (bf16[1,2,8,32,128]{4,3,2,1,0:T(8,128)(2,1)}, bf16[1,2,8,32,128]{4,3,2,1,0:T(8,128)(2,1)S(1)}, u32[]{:S(2)}) copy-start(bf16[1,2,8,32,128]{4,3,2,1,0:T(8,128)(2,1)S(1)} %pad_maximum_fusion) | copy-start | bytes 393220
  29.2 28.6 %copy-start = (f32[8,32,128]{2,1,0:T(8,128)S(1)}, f32[8,32,128]{2,1,0:T(8,128)}, u32[]{:S(2)}) copy-start(f32[8,32,128]{2,1,0:T(8,128)} %get-tuple-element.15.refs_0_) | copy-start | bytes 393220
  29.2 16.3 %collective-permute-start.5 = (bf16[2,8,32,128]{3,2,1,0:T(8,128)(2,1)S(1)}, bf16[2,8,32,128]{3,2,1,0:T(8,128)(2,1)S(1)}, u32[]{:S(2)}, u32[]{:S(2)}) collective-permute-start(bf16[2,8,32,128]{3,2,1,0:T(8,128)(2,1)S(1)} %bitcast.11), channel_id=1, source_target_pairs={{0,6},{2,0},{4,2},{6,4},{1,7},{3,1},{5,3},{7,5},{8,14},{10,8},{12,... | collective-permute-start | bytes 393224 | tf_op jit(solution)/shard_map/ppermute | solution.py:182
  33.1 18.5 %collective-permute-start.6 = (bf16[2,8,32,128]{3,2,1,0:T(8,128)(2,1)S(1)}, bf16[2,8,32,128]{3,2,1,0:T(8,128)(2,1)S(1)}, u32[]{:S(2)}, u32[]{:S(2)}) collective-permute-start(bf16[2,8,32,128]{3,2,1,0:T(8,128)(2,1)S(1)} %bitcast.12), channel_id=1, source_target_pairs={{0,4},{2,6},{4,0},{6,2},{1,5},{3,7},{5,1},{7,3},{8,12},{10,14},{12... | collective-permute-start | bytes 393224 | tf_op jit(solution)/shard_map/ppermute | solution.py:182
  35.4 16.2 %collective-permute-start.7 = (bf16[2,8,32,128]{3,2,1,0:T(8,128)(2,1)S(1)}, bf16[2,8,32,128]{3,2,1,0:T(8,128)(2,1)S(1)}, u32[]{:S(2)}, u32[]{:S(2)}) collective-permute-start(bf16[2,8,32,128]{3,2,1,0:T(8,128)(2,1)S(1)} %bitcast.13), channel_id=1, source_target_pairs={{0,2},{2,4},{4,6},{6,0},{1,3},{3,5},{5,7},{7,1},{8,10},{10,12},{12... | collective-permute-start | bytes 393224 | tf_op jit(solution)/shard_map/ppermute | solution.py:182
  39.3 18.4 %collective-permute-start.2 = (f32[8,32,128]{2,1,0:T(8,128)}, f32[8,32,128]{2,1,0:T(8,128)S(1)}, u32[]{:S(2)}, u32[]{:S(2)}) collective-permute-start(f32[8,32,128]{2,1,0:T(8,128)} %get-tuple-element.16), channel_id=1, source_target_pairs={{0,2},{2,4},{4,6},{6,0},{1,3},{3,5},{5,7},{7,1},{8,10},{10,12},{12... | collective-permute-start | bytes 393224 | tf_op jit(solution)/shard_map/ppermute | solution.py:182
  42.3 15.4 %collective-permute-start.3 = (f32[8,32,128]{2,1,0:T(8,128)}, f32[8,32,128]{2,1,0:T(8,128)S(1)}, u32[]{:S(2)}, u32[]{:S(2)}) collective-permute-start(f32[8,32,128]{2,1,0:T(8,128)} %get-tuple-element.17), channel_id=1, source_target_pairs={{0,4},{2,6},{4,0},{6,2},{1,5},{3,7},{5,1},{7,3},{8,12},{10,14},{12... | collective-permute-start | bytes 393224 | tf_op jit(solution)/shard_map/ppermute | solution.py:182
  45.5 6.1 %copy-start.5 = (bf16[2,8,32,128]{3,2,1,0:T(8,128)(2,1)}, bf16[2,8,32,128]{3,2,1,0:T(8,128)(2,1)S(1)}, u32[]{:S(2)}) copy-start(bf16[2,8,32,128]{3,2,1,0:T(8,128)(2,1)S(1)} %collective-permute-done.5.refs_1_) | copy-start | bytes 393220
  45.5 12.2 %collective-permute-start.4 = (f32[8,32,128]{2,1,0:T(8,128)}, f32[8,32,128]{2,1,0:T(8,128)S(1)}, u32[]{:S(2)}, u32[]{:S(2)}) collective-permute-start(f32[8,32,128]{2,1,0:T(8,128)} %get-tuple-element.18), channel_id=1, source_target_pairs={{0,6},{2,0},{4,2},{6,4},{1,7},{3,1},{5,3},{7,5},{8,14},{10,8},{12,... | collective-permute-start | bytes 393224 | tf_op jit(solution)/shard_map/ppermute | solution.py:182
  51.6 0.7 %copy-start.6 = (bf16[2,8,32,128]{3,2,1,0:T(8,128)(2,1)}, bf16[2,8,32,128]{3,2,1,0:T(8,128)(2,1)S(1)}, u32[]{:S(2)}) copy-start(bf16[2,8,32,128]{3,2,1,0:T(8,128)(2,1)S(1)} %collective-permute-done.6.refs_2_) | copy-start | bytes 393220
  52.3 0.7 %copy-start.7 = (bf16[2,8,32,128]{3,2,1,0:T(8,128)(2,1)}, bf16[2,8,32,128]{3,2,1,0:T(8,128)(2,1)S(1)}, u32[]{:S(2)}) copy-start(bf16[2,8,32,128]{3,2,1,0:T(8,128)(2,1)S(1)} %collective-permute-done.7.refs_3_) | copy-start | bytes 393220
